TPU v7x, 32 devices: a whole 2x2x4 slice. The times are simulated.
32 devices in a mesh: blk: 8 (over z, y), face: 4 (over x, core).
Axes of the slice: x: 2, y: 2, z: 4, core: 2. Of those that a mesh axis runs over, the one named last changes fastest.
Arguments:
- forcing: float32 [8, 4, 3, 64, 4096], P('blk', 'face'), may hold values from -6 to 6
- modulus: float32 [8, 4, 3], P('blk', 'face'), may hold values from 0.5 to 4
- orient_codes: int32 [8, 4], P('blk', 'face'), may hold values from 0 to 3
Outputs:
- displacement: float32 [8, 4, 3, 64, 4096], P('blk', 'face')
All inputs are finite; a program needn't handle non-finite values.
Results may differ from a plain program's by a relative error of at most 0.0001.
Values sent between devices are 32-bit elements; how exact they have to be, the bound alone decides.
No kernel may reach another device: no remote copies, remote signals or barrier semaphores. Data moves between devices by JAX's collectives and lax.ppermute only.
A program may use at most 128 MiB of HBM per device.

v0:
```python
import functools
import math

import jax
import jax.numpy as jnp
from jax import lax
from jax.sharding import PartitionSpec as P
from jax.experimental import pallas as pl
from jax.experimental.pallas import tpu as pltpu
import numpy as np

ITERS = 2


mass_shift = 0.02
inject_scale = 2.0
traction_mix = 0.5
penalty_mix = 0.25
lower_edge = 0.3
upper_edge = 1.5
highest = lax.Precision.HIGHEST


def shifted(shard, axis, by):
    length = lax.axis_size(axis)
    pairs = [(i, i + by) for i in range(length) if 0 <= i + by < length]
    return lax.ppermute(shard, axis, pairs)


def shifted_2(shard, axis, by):
    length = lax.axis_size(axis)
    return lax.ppermute(shard, axis, [(i, (i + by) % length) for i in range(length)])


def tables(extent):
    node_index = jnp.arange(extent, dtype=jnp.float32) + 1.0
    basis = math.sqrt(2.0 / (extent + 1)) * jnp.sin(
        math.pi * node_index[:, None] * node_index[None, :] / (extent + 1)
    )
    eigenvalues = 2.0 - 2.0 * jnp.cos(math.pi * node_index / (extent + 1))
    return (basis, eigenvalues)


def tangent_matrix(extent):
    node_index = jnp.arange(extent, dtype=jnp.int32)
    distance = jnp.abs(node_index[:, None] - node_index[None, :])
    end_rows = ((node_index == 0) | (node_index == extent - 1)).astype(jnp.float32)
    adjacent = (distance == 1).astype(jnp.float32)
    diagonal_part = (distance == 0).astype(jnp.float32) * (2.0 - end_rows[:, None])
    return adjacent - diagonal_part


def step_weights(step_count):
    midpoint = 0.5 * (upper_edge + lower_edge)
    radius = 0.5 * (upper_edge - lower_edge)
    return [
        1.0 / (midpoint + radius * math.cos(math.pi * (2 * turn_index + 1) / (2 * step_count)))
        for turn_index in range(step_count)
    ]


def divisor(moduli, eigenvalues):
    extent = eigenvalues.shape[0]
    summed = eigenvalues[:, None, None] + eigenvalues[None, :, None] + eigenvalues[None, None, :]
    scaled = moduli[..., None, None, None] * summed + mass_shift
    return scaled.reshape(moduli.shape + (extent, extent * extent))


def body_transform(field_data, basis, paired_basis):
    extent = basis.shape[0]
    full_shape = field_data.shape
    pair_width = paired_basis.shape[0]
    sectioned = jnp.einsum("ix,bcxm->bcim", basis, field_data, precision=highest)
    sectioned = sectioned.reshape(full_shape[:-1] + (full_shape[-1] // pair_width, pair_width))
    sectioned = jnp.einsum("bcxpz,kz->bcxpk", sectioned, paired_basis, precision=highest)
    sectioned = sectioned.reshape(full_shape[:-1] + (extent, extent))
    sectioned = jnp.einsum("jy,bcxyz->bcxjz", basis, sectioned, precision=highest)
    return sectioned.reshape(full_shape)


def body_solve(right_side, scale_table, basis, paired_basis):
    return body_transform(
        body_transform(right_side, basis, paired_basis) / scale_table, basis, paired_basis
    )


HI = lax.Precision.HIGHEST
f32 = jnp.float32


def np_tables(n):
    g = np.float32
    idx = np.arange(n, dtype=g) + g(1.0)
    arg = (g(math.pi) * idx[:, None]) * idx[None, :] / g(n + 1)
    q = g(math.sqrt(2.0 / (n + 1))) * np.sin(arg)
    e = g(2.0) - g(2.0) * np.cos(g(math.pi) * idx / g(n + 1))
    return q.astype(g), e.astype(g)

def consts(n):
    q, e = np_tables(n)
    h = n // 2
    p = np.kron(np.eye(2, dtype=np.float32), q.T)
    qe = q[0::2]; qo = q[1::2]
    q00 = qe[:, 0::2]; q01 = qe[:, 1::2]; q10 = qo[:, 0::2]; q11 = qo[:, 1::2]
    mst = np.concatenate([np.concatenate([q00, q01], 1), np.concatenate([q11, q10], 1)], 0)
    lane = np.arange(2 * n) % n
    hh = np.arange(2 * n) // n
    ej = e[2 * np.arange(h)[:, None] + hh[None, :]]
    ek = np.ascontiguousarray(np.broadcast_to(e[lane][None, :], (h, 2 * n)))
    return q, p, mst, ej, ek, e

def solve_kernel(*refs, with_faces, emit_u, emit_sides):
    it = iter(refs)
    mod_ref, ex_ref, f_ref = next(it), next(it), next(it)
    if with_faces:
        xlo_ref, xhi_ref, yadd_ref = next(it), next(it), next(it)
    q_ref, p_ref, mst_ref, ej_ref, ek_ref = next(it), next(it), next(it), next(it), next(it)
    o_ref = next(it) if emit_u else None
    if emit_sides:
        xf_ref, yf_ref = next(it), next(it)
    s_ref = next(it)
    n = q_ref.shape[0]
    h = n // 2
    w2 = 2 * n
    nn = f_ref.shape[-1]
    nch = nn // w2
    comp = pl.program_id(0)
    m = mod_ref[comp]
    q = q_ref[...]
    r = f_ref[0]
    if with_faces:
        rows = lax.broadcasted_iota(jnp.int32, (n, nn), 0)
        added = jnp.where(rows == 0, xlo_ref[0], 0.0) + jnp.where(rows == n - 1, xhi_ref[0], 0.0)
        lane = lax.broadcasted_iota(jnp.int32, (n, w2), 1)
        yadd = yadd_ref[0]
        first = added[:, :w2] + jnp.where(lane < n, yadd, 0.0)
        last = added[:, nn - w2:] + jnp.where(lane >= n, yadd, 0.0)
        added = jnp.concatenate([first, added[:, w2:nn - w2], last], 1)
        r = r + (2.0 * m) * added
    a = jnp.dot(q, r, precision=HI, preferred_element_type=f32)
    for c in range(nch):
        s_ref[c * n:(c + 1) * n, :] = a[:, c * w2:(c + 1) * w2]
    s_ref[...] = jnp.dot(s_ref[...], p_ref[...], precision=HI, preferred_element_type=f32)
    mst = mst_ref[...]
    ej = ej_ref[...]
    ek = ek_ref[...]
    lane_lo = lax.broadcasted_iota(jnp.int32, (h, w2), 1) < n
    G = 8

    def ycon(ys):
        zs = [jnp.concatenate([y, pltpu.roll(y, n, 1)], 0) for y in ys]
        w = jnp.dot(mst, jnp.concatenate(zs, 1), precision=HI, preferred_element_type=f32)
        out = []
        for t in range(len(ys)):
            wt = w[:, t * w2:(t + 1) * w2]
            out.append(jnp.where(lane_lo, wt[:h], wt[h:]))
        return out

    def body(g, carry):
        xs = [g * G + t for t in range(G)]
        ys = [s_ref[pl.ds(x, h, stride=n), :] for x in xs]
        ws = ycon(ys)
        ws = [w / (m * ((ex_ref[x] + ej) + ek) + 0.02) for w, x in zip(ws, xs)]
        ws = ycon(ws)
        for x, w in zip(xs, ws):
            s_ref[pl.ds(x, h, stride=n), :] = w
        return carry
    lax.fori_loop(0, n // G, body, 0)
    s_ref[...] = jnp.dot(s_ref[...], p_ref[...], precision=HI, preferred_element_type=f32)
    b = jnp.concatenate([s_ref[c * n:(c + 1) * n, :] for c in range(nch)], 1)
    u = jnp.dot(q, b, precision=HI, preferred_element_type=f32)
    if emit_u:
        o_ref[0] = u

    def slope(p0, p1, p2, p3):
        return m * (11.0 / 6.0 * p0 - 3.0 * p1 + 1.5 * p2 - p3 / 3.0)
    if emit_sides:
        xf_ref[0, 0:1, :] = u[n - 1:n]
        xf_ref[0, 1:2, :] = slope(u[n - 1:n], u[n - 2:n - 1], u[n - 3:n - 2], u[n - 4:n - 3])
        xf_ref[0, 2:3, :] = u[0:1]
        xf_ref[0, 3:4, :] = slope(u[0:1], u[1:2], u[2:3], u[3:4])
        c_hi = u[:, nn - w2:]
        c_hi2 = u[:, nn - 2 * w2:nn - w2]
        yf_ref[0, 0] = c_hi
        yf_ref[0, 1] = slope(c_hi, pltpu.roll(c_hi, n, 1), c_hi2, pltpu.roll(c_hi2, n, 1))
        c_lo = u[:, :w2]
        c_lo2 = u[:, w2:2 * w2]
        yf_ref[0, 2] = c_lo
        yf_ref[0, 3] = slope(c_lo, pltpu.roll(c_lo, n, 1), c_lo2, pltpu.roll(c_lo2, n, 1))


def kernel_sweep(rhs, moduli, faces=None, emit_u=True, emit_sides=False):
    ncomp, n, nn = rhs.shape
    q, p, mst, ej, ek, e = consts(n)
    full = lambda shp: pl.BlockSpec(shp, lambda c: (0,) * len(shp))
    comp3 = lambda shp: pl.BlockSpec((1,) + shp, lambda c: (c,) + (0,) * len(shp))
    smem = pl.BlockSpec(memory_space=pltpu.SMEM)
    in_specs = [smem, smem, comp3((n, nn))]
    args = [moduli, e, rhs]
    if faces is not None:
        xlo, xhi, yadd = faces
        in_specs += [comp3((1, nn)), comp3((1, nn)), comp3((n, 2 * n))]
        args += [xlo.reshape(ncomp, 1, nn), xhi.reshape(ncomp, 1, nn), yadd]
    in_specs += [full(q.shape), full(p.shape), full(mst.shape), full(ej.shape), full(ek.shape)]
    args += [q, p, mst, ej, ek]
    out_specs, out_shape = [], []
    if emit_u:
        out_specs.append(comp3((n, nn)))
        out_shape.append(jax.ShapeDtypeStruct(rhs.shape, f32))
    if emit_sides:
        out_specs += [comp3((4, nn)), comp3((4, n, 2 * n))]
        out_shape += [jax.ShapeDtypeStruct((ncomp, 4, nn), f32), jax.ShapeDtypeStruct((ncomp, 4, n, 2 * n), f32)]
    kernel = functools.partial(solve_kernel, with_faces=faces is not None, emit_u=emit_u, emit_sides=emit_sides)
    return pl.pallas_call(
        kernel,
        grid=(ncomp,),
        in_specs=in_specs,
        out_specs=out_specs,
        out_shape=out_shape,
        scratch_shapes=[pltpu.VMEM((nn // 2, 2 * n), f32)],
    )(*args)


def orient(face_field, code_table, extent):
    square = face_field.reshape(face_field.shape[:-1] + (extent, extent))
    flip_rows = (code_table % 2 == 1)[..., None, None, None]
    flip_cols = (code_table // 2 == 1)[..., None, None, None]
    square = jnp.where(flip_rows, jnp.flip(square, -2), square)
    square = jnp.where(flip_cols, jnp.flip(square, -1), square)
    return square.reshape(face_field.shape)


def face_data(solution, moduli):
    extent = solution.shape[-2]
    cube_view = solution.reshape(solution.shape[:-1] + (extent, extent))
    flat_shape = solution.shape[:-2] + (extent * extent,)

    def pack_side(planes):
        normal_slope = 11.0 / 6.0 * planes[0] - 3.0 * planes[1] + 1.5 * planes[2] - planes[3] / 3.0
        return (planes[0], moduli[..., None] * normal_slope)

    x_high = pack_side([solution[..., extent - 1 - plane_depth, :] for plane_depth in range(4)])
    x_low = pack_side([solution[..., plane_depth, :] for plane_depth in range(4)])
    y_high = pack_side(
        [
            cube_view[..., extent - 1 - plane_depth, :].reshape(flat_shape)
            for plane_depth in range(4)
        ]
    )
    y_low = pack_side(
        [cube_view[..., plane_depth, :].reshape(flat_shape) for plane_depth in range(4)]
    )
    return (x_high, x_low, y_high, y_low)


def place_faces(source_field, moduli, x_low, x_high, y_low, y_high):
    extent = source_field.shape[-2]
    added = jnp.zeros_like(source_field)
    added = added.at[..., 0, :].add(x_low)
    added = added.at[..., extent - 1, :].add(x_high)
    cube_view = added.reshape(added.shape[:-1] + (extent, extent))
    low_square = y_low.reshape(y_low.shape[:-1] + (extent, extent))
    high_square = y_high.reshape(y_high.shape[:-1] + (extent, extent))
    cube_view = cube_view.at[..., 0, :].add(low_square)
    cube_view = cube_view.at[..., extent - 1, :].add(high_square)
    added = cube_view.reshape(source_field.shape)
    return source_field + inject_scale * moduli[..., None, None] * added


def trace_update(current, side_a, side_b, moduli_a, moduli_b, omega_step, tangent):
    extent = tangent.shape[0]
    weight_a = moduli_a[..., None]
    weight_b = moduli_b[..., None]
    residue = (
        weight_a * side_a[0] + weight_b * side_b[0] + traction_mix * (side_a[1] + side_b[1])
    ) / (weight_a + weight_b) - current
    rows_view = residue.reshape(residue.shape[:-1] + (residue.shape[-1] // extent, extent))
    smoothed = rows_view + penalty_mix * jnp.einsum(
        "...z,zk->...k", rows_view, tangent, precision=highest
    )
    return current + omega_step * smoothed.reshape(residue.shape)


def shards(forcing, modulus, orient_codes):
    extent = forcing.shape[3]
    blocks = forcing.shape[1]
    flat = extent * extent
    source_field = forcing[0]
    moduli = modulus[0]
    codes_here = orient_codes[0]
    tangent = tangent_matrix(extent)
    omegas = step_weights(ITERS)
    slab_count = lax.axis_size("blk")
    slab_index = lax.axis_index("blk")
    face_zeros = jnp.zeros((blocks, 3, flat), jnp.float32)
    lam_x = face_zeros
    lam_y = face_zeros
    live_slab = (slab_index < slab_count - 1).astype(jnp.float32)
    faces = [None] * blocks
    for sweep in range(ITERS + 1):
        last = sweep == ITERS
        outs = [
            kernel_sweep(source_field[b], moduli[b], faces[b], emit_u=last, emit_sides=not last)
            for b in range(blocks)
        ]
        if last:
            return jnp.stack([o[0] for o in outs], 0)[None]
        xf = jnp.stack([o[0] for o in outs], 0)
        yf = jnp.stack([o[1] for o in outs], 0)
        x_high_side = (xf[:, :, 0], xf[:, :, 1])
        x_low_side = (xf[:, :, 2], xf[:, :, 3])
        y_high_side = tuple(yf[:, :, k, :, extent:].reshape(blocks, 3, flat) for k in (0, 1))
        y_low_side = tuple(yf[:, :, k, :, :extent].reshape(blocks, 3, flat) for k in (2, 3))
        upper_value, upper_slope, upper_moduli = shifted(
            (x_low_side[0], x_low_side[1], moduli), "blk", -1
        )
        upper_value = orient(upper_value, codes_here, extent)
        upper_slope = orient(upper_slope, codes_here, extent)
        lam_x = (
            trace_update(
                lam_x,
                x_high_side,
                (upper_value, upper_slope),
                moduli,
                upper_moduli,
                omegas[sweep],
                tangent,
            )
            * live_slab
        )
        x_high = lam_x
        x_low = shifted(orient(lam_x, codes_here, extent), "blk", 1)
        next_value, next_slope, next_moduli = shifted_2(
            (y_low_side[0][0], y_low_side[1][0], moduli[0]), "face", -1
        )
        beside_value = jnp.concatenate([y_low_side[0][1:], next_value[None]], 0)
        beside_slope = jnp.concatenate([y_low_side[1][1:], next_slope[None]], 0)
        beside_moduli = jnp.concatenate([moduli[1:], next_moduli[None]], 0)
        lam_y = trace_update(
            lam_y,
            y_high_side,
            (beside_value, beside_slope),
            moduli,
            beside_moduli,
            omegas[sweep],
            tangent,
        )
        previous_trace = shifted_2(lam_y[blocks - 1], "face", 1)
        y_high = lam_y
        y_low = jnp.concatenate([previous_trace[None], lam_y[:-1]], 0)
        yadd = jnp.concatenate(
            [y_low.reshape(blocks, 3, extent, extent), y_high.reshape(blocks, 3, extent, extent)], -1
        )
        faces = [(x_low[b], x_high[b], yadd[b]) for b in range(blocks)]


def solution(mesh):
    placed = (P("blk", "face", None, None, None), P("blk", "face", None), P("blk", "face"))
    return jax.shard_map(
        shards,
        mesh=mesh,
        in_specs=placed,
        out_specs=P("blk", "face", None, None, None),
        check_vma=False,
    )
```

profile of v0, /device:TPU:24, one launch (start us, length us, event | category | flops | bytes accessed | tf_op | source)
XLA Modules:
  0.0 160.9 jit_solution(5076497894936532951)
XLA Ops:
  0.0 3.4 %collective-permute-start = (f32[1,3]{1,0:T(1,128)}, f32[1,3]{1,0:T(1,128)S(1)}, u32[]{:S(2)}, u32[]{:S(2)}) collective-permute-start(f32[1,3]{1,0:T(1,128)} %bitcast.132), channel_id=1, source_target_pairs={{4,0},{8,4},{12,8},{16,12},{20,16},{24,20},{28,24},{5,1},{9,5},{13... | collective-permute-start | bytes 44 | tf_op jit(solution)/shard_map/ppermute | solution.py:27
  3.4 0.7 collective-permute-start.4
  4.1 36.6 %shard_map.199 = (f32[3,4,4096]{2,1,0:T(4,128)}, f32[3,4,64,128]{3,2,1,0:T(8,128)}) custom-call(f32[3]{0:T(128)} %bitcast.134, f32[64]{0:T(128)} %constant.98.clone.refs_1_, f32[3,64,4096]{2,1,0:T(8,128)} %bitcast.122, f32[64,64]{1,0:T(8,128)} %constant.99.clone.refs_3_.refs_6_, f32[128,128]{1,0:T(8,128)} %constant.100.clone.refs_4_.refs_7_, ...), custom_call_target="tpu_custom_call" | custom-call | tf_op jit(solution)/shard_map/pallas_call | solution.py:214
  40.8 1.6 %slice_bitcast_fusion.3 = (f32[1,3,4096]{2,0,1:T(1,128)S(1)}, f32[1,3,4096]{2,0,1:T(1,128)S(1)}, f32[3,4096]{1,0:T(4,128)S(1)}, f32[3,4096]{1,0:T(4,128)S(1)}) fusion(f32[1,3,4,4096]{3,2,1,0:T(4,128)} %bitcast.129), kind=kLoop, calls=%fused_computation.58 | loop fusion | bytes 393216 | tf_op jit(solution)/shard_map/squeeze | solution.py:311
  42.4 2.4 %collective-permute-start.1 = (f32[1,3,4096]{2,0,1:T(1,128)S(1)}, f32[1,3,4096]{2,0,1:T(1,128)S(1)}, u32[]{:S(2)}, u32[]{:S(2)}) collective-permute-start(f32[1,3,4096]{2,0,1:T(1,128)S(1)} %get-tuple-element.31), channel_id=1, source_target_pairs={{4,0},{8,4},{12,8},{16,12},{20,16},{24,20},{28,24},{5,1},{9,5},{13... | collective-permute-start | bytes 147464 | tf_op jit(solution)/shard_map/ppermute | solution.py:27
  44.8 3.3 %collective-permute-start.2 = (f32[1,3,4096]{2,0,1:T(1,128)S(1)}, f32[1,3,4096]{2,0,1:T(1,128)S(1)}, u32[]{:S(2)}, u32[]{:S(2)}) collective-permute-start(f32[1,3,4096]{2,0,1:T(1,128)S(1)} %get-tuple-element.32), channel_id=1, source_target_pairs={{4,0},{8,4},{12,8},{16,12},{20,16},{24,20},{28,24},{5,1},{9,5},{13... | collective-permute-start | bytes 147464 | tf_op jit(solution)/shard_map/ppermute | solution.py:27
  48.2 1.2 fusion.96
  49.3 0.1 squeeze_reshape_squeeze.12
  49.4 0.4 collective-permute-start.5
  50.6 0.1 squeeze.53
  50.7 0.1 squeeze.50
  50.8 0.1 squeeze.52
  50.9 0.1 squeeze.47
  51.1 0.1 reshape_squeeze.21
  51.3 0.1 reshape_squeeze.22
  51.4 0.7 collective-permute-start.6
  52.1 0.1 reduce.1
  52.2 0.1 reshape.353
  52.3 0.1 reduce.3
  52.4 0.1 reshape.355
  52.6 1.4 collective-permute-done.6
  54.0 0.1 reshape.359
  54.2 0.3 fusion.3
  54.5 0.1 mul.288
  54.6 1.4 collective-permute-start.7
  56.2 0.3 fusion.16
  56.7 0.7 mul.311.refs_4_
  57.4 0.1 reshape.368
  57.5 2.7 %collective-permute-start.3 = (f32[1,3,4096]{2,0,1:T(1,128)S(1)}, f32[1,3,4096]{2,0,1:T(1,128)S(1)}, u32[]{:S(2)}, u32[]{:S(2)}) collective-permute-start(f32[1,3,4096]{2,0,1:T(1,128)S(1)} %reshape.368), channel_id=1, source_target_pairs={{0,4},{4,8},{8,12},{12,16},{16,20},{20,24},{24,28},{1,5},{5,9},{9,... | collective-permute-start | bytes 147464 | tf_op jit(solution)/shard_map/ppermute | solution.py:27
  60.2 0.1 reshape_broadcast_in_dim.6
  60.3 0.7 maximum_bitcast_fusion.refs_5_
  61.1 3.3 %collective-permute-done.3 = f32[1,3,4096]{2,0,1:T(1,128)S(1)} collective-permute-done((f32[1,3,4096]{2,0,1:T(1,128)S(1)}, f32[1,3,4096]{2,0,1:T(1,128)S(1)}, u32[]{:S(2)}, u32[]{:S(2)}) %collective-permute-start.3) | collective-permute-done | bytes 49184 | tf_op jit(solution)/shard_map/ppermute | solution.py:27
  64.4 0.6 copy-done.2
  65.0 36.9 %shard_map.200 = (f32[3,4,4096]{2,1,0:T(4,128)}, f32[3,4,64,128]{3,2,1,0:T(8,128)}) custom-call(f32[3]{0:T(128)} %bitcast.135, f32[64]{0:T(128)} %constant.98.clone.refs_1_, f32[3,64,4096]{2,1,0:T(8,128)} %bitcast.123, f32[3,1,4096]{2,1,0:T(1,128)} %bitcast.131, f32[3,1,4096]{2,1,0:T(1,128)} %mul.311.refs_4_, f32[3,64,128]{2,1,0:T(8,128)} %maximum_bitcast_fusion.refs_5_, ...), custom_call_target="tpu_custom_call" | custom-call | tf_op jit(solution)/shard_map/pallas_call | solution.py:214
  101.9 1.1 fusion.95
  103.0 0.1 squeeze_reshape_squeeze.15
  103.3 1.0 collective-permute-start.12
  104.3 1.6 %slice_bitcast_fusion.1 = (f32[1,3,4096]{2,0,1:T(1,128)S(1)}, f32[1,3,4096]{2,0,1:T(1,128)S(1)}, f32[3,4096]{1,0:T(4,128)S(1)}, f32[3,4096]{1,0:T(4,128)S(1)}) fusion(f32[1,3,4,4096]{3,2,1,0:T(4,128)} %bitcast.128), kind=kLoop, calls=%fused_computation.54 | loop fusion | bytes 393216 | tf_op jit(solution)/shard_map/squeeze | solution.py:311
  105.9 0.1 squeeze.60
  106.1 0.1 squeeze.57
  106.2 0.1 squeeze.59
  106.3 0.1 squeeze.55
  106.5 1.9 %collective-permute-start.8 = (f32[1,3,4096]{2,0,1:T(1,128)S(1)}, f32[1,3,4096]{2,0,1:T(1,128)S(1)}, u32[]{:S(2)}, u32[]{:S(2)}) collective-permute-start(f32[1,3,4096]{2,0,1:T(1,128)S(1)} %get-tuple-element.27), channel_id=1, source_target_pairs={{4,0},{8,4},{12,8},{16,12},{20,16},{24,20},{28,24},{5,1},{9,5},{13... | collective-permute-start | bytes 147464 | tf_op jit(solution)/shard_map/ppermute | solution.py:27
  108.4 3.8 %collective-permute-start.9 = (f32[1,3,4096]{2,0,1:T(1,128)S(1)}, f32[1,3,4096]{2,0,1:T(1,128)S(1)}, u32[]{:S(2)}, u32[]{:S(2)}) collective-permute-start(f32[1,3,4096]{2,0,1:T(1,128)S(1)} %get-tuple-element.28), channel_id=1, source_target_pairs={{4,0},{8,4},{12,8},{16,12},{20,16},{24,20},{28,24},{5,1},{9,5},{13... | collective-permute-start | bytes 147464 | tf_op jit(solution)/shard_map/ppermute | solution.py:27
  112.3 0.1 reshape_squeeze.25
  112.4 0.1 divide_subtract_fusion
  112.5 0.1 reshape.366
  112.6 0.3 fusion.1
  112.9 0.1 mul.309
  113.1 0.1 reduce.7
  113.2 0.1 reshape.360
  113.3 1.1 collective-permute-done.9
  114.4 0.1 reduce.9
  114.5 0.1 reshape.362
  115.0 0.3 fusion.97
  115.3 0.1 mul.310
  115.5 0.7 add_multiply_fusion.refs_4_
  116.3 0.1 reshape.369
  116.4 2.1 %collective-permute-start.10 = (f32[1,3,4096]{2,0,1:T(1,128)S(1)}, f32[1,3,4096]{2,0,1:T(1,128)S(1)}, u32[]{:S(2)}, u32[]{:S(2)}) collective-permute-start(f32[1,3,4096]{2,0,1:T(1,128)S(1)} %reshape.369), channel_id=1, source_target_pairs={{0,4},{4,8},{8,12},{12,16},{16,20},{20,24},{24,28},{1,5},{5,9},{9,... | collective-permute-start | bytes 147464 | tf_op jit(solution)/shard_map/ppermute | solution.py:27
  118.6 0.1 reshape_broadcast_in_dim.7
  118.7 0.7 maximum_bitcast_fusion.1.refs_5_
  119.4 4.0 %collective-permute-done.10 = f32[1,3,4096]{2,0,1:T(1,128)S(1)} collective-permute-done((f32[1,3,4096]{2,0,1:T(1,128)S(1)}, f32[1,3,4096]{2,0,1:T(1,128)S(1)}, u32[]{:S(2)}, u32[]{:S(2)}) %collective-permute-start.10) | collective-permute-done | bytes 49184 | tf_op jit(solution)/shard_map/ppermute | solution.py:27
  123.5 0.6 copy-done.1
  124.1 36.9 %shard_map.201 = f32[3,64,4096]{2,1,0:T(8,128)} custom-call(f32[3]{0:T(128)} %bitcast.136, f32[64]{0:T(128)} %constant.98.clone.refs_1_, f32[3,64,4096]{2,1,0:T(8,128)} %bitcast.124, f32[3,1,4096]{2,1,0:T(1,128)} %bitcast.130, f32[3,1,4096]{2,1,0:T(1,128)} %add_multiply_fusion.refs_4_, f32[3,64,128]{2,1,0:T(8,128)} %maximum_bitcast_fusion.1.refs_5_, ...), custom_call_target="tpu_custom_call" | custom-call | tf_op jit(solution)/shard_map/pallas_call | solution.py:214
  (48 shorter events, 1.3 us)
Async XLA Ops:
  0.0 52.0 %copy-start.3 = (f32[1,1,3]{2,1,0:T(1,128)S(1)}, f32[1,1,3]{2,1,0:T(1,128)}, u32[]{:S(2)}) copy-start(f32[1,1,3]{2,1,0:T(1,128)} %param.22) | copy-start | bytes 40
  0.0 51.4 %collective-permute-start = (f32[1,3]{1,0:T(1,128)}, f32[1,3]{1,0:T(1,128)S(1)}, u32[]{:S(2)}, u32[]{:S(2)}) collective-permute-start(f32[1,3]{1,0:T(1,128)} %bitcast.132), channel_id=1, source_target_pairs={{4,0},{8,4},{12,8},{16,12},{20,16},{24,20},{28,24},{5,1},{9,5},{13... | collective-permute-start | bytes 44 | tf_op jit(solution)/shard_map/ppermute | solution.py:27
  3.4 48.6 %collective-permute-start.4 = (f32[3]{0:T(128)}, f32[3]{0:T(128)S(1)}, u32[]{:S(2)}, u32[]{:S(2)}) collective-permute-start(f32[3]{0:T(128)} %bitcast.133), channel_id=1, source_target_pairs={{0,3},{1,0},{2,1},{3,2},{4,7},{5,4},{6,5},{7,6},{8,11},{9,8},{10,9... | collective-permute-start | bytes 44 | tf_op jit(solution)/shard_map/ppermute | solution.py:32
  42.4 9.6 %collective-permute-start.1 = (f32[1,3,4096]{2,0,1:T(1,128)S(1)}, f32[1,3,4096]{2,0,1:T(1,128)S(1)}, u32[]{:S(2)}, u32[]{:S(2)}) collective-permute-start(f32[1,3,4096]{2,0,1:T(1,128)S(1)} %get-tuple-element.31), channel_id=1, source_target_pairs={{4,0},{8,4},{12,8},{16,12},{20,16},{24,20},{28,24},{5,1},{9,5},{13... | collective-permute-start | bytes 147464 | tf_op jit(solution)/shard_map/ppermute | solution.py:27
  44.8 7.5 %collective-permute-start.2 = (f32[1,3,4096]{2,0,1:T(1,128)S(1)}, f32[1,3,4096]{2,0,1:T(1,128)S(1)}, u32[]{:S(2)}, u32[]{:S(2)}) collective-permute-start(f32[1,3,4096]{2,0,1:T(1,128)S(1)} %get-tuple-element.32), channel_id=1, source_target_pairs={{4,0},{8,4},{12,8},{16,12},{20,16},{24,20},{28,24},{5,1},{9,5},{13... | collective-permute-start | bytes 147464 | tf_op jit(solution)/shard_map/ppermute | solution.py:27
  49.4 3.1 %collective-permute-start.5 = (f32[3,4096]{1,0:T(4,128)S(1)}, f32[3,4096]{1,0:T(4,128)S(1)}, u32[]{:S(2)}, u32[]{:S(2)}) collective-permute-start(f32[3,4096]{1,0:T(4,128)S(1)} %squeeze_reshape_squeeze.12), channel_id=1, source_target_pairs={{0,3},{1,0},{2,1},{3,2},{4,7},{5,4},{6,5},{7,6},{8,11},{9,8},{10,9... | collective-permute-start | bytes 147464 | tf_op jit(solution)/shard_map/ppermute | solution.py:32
  51.4 2.6 %collective-permute-start.6 = (f32[3,4096]{1,0:T(4,128)S(1)}, f32[3,4096]{1,0:T(4,128)S(1)}, u32[]{:S(2)}, u32[]{:S(2)}) collective-permute-start(f32[3,4096]{1,0:T(4,128)S(1)} %squeeze_reshape_squeeze.13), channel_id=1, source_target_pairs={{0,3},{1,0},{2,1},{3,2},{4,7},{5,4},{6,5},{7,6},{8,11},{9,8},{10,9... | collective-permute-start | bytes 147464 | tf_op jit(solution)/shard_map/ppermute | solution.py:32
  54.6 5.6 %collective-permute-start.7 = (f32[3,4096]{1,0:T(4,128)S(1)}, f32[3,4096]{1,0:T(4,128)S(1)}, u32[]{:S(2)}, u32[]{:S(2)}) collective-permute-start(f32[3,4096]{1,0:T(4,128)S(1)} %mul.288), channel_id=1, source_target_pairs={{0,1},{1,2},{2,3},{3,0},{4,5},{5,6},{6,7},{7,4},{8,9},{9,10},{10,1... | collective-permute-start | bytes 147464 | tf_op jit(solution)/shard_map/ppermute | solution.py:32
  57.5 6.9 %collective-permute-start.3 = (f32[1,3,4096]{2,0,1:T(1,128)S(1)}, f32[1,3,4096]{2,0,1:T(1,128)S(1)}, u32[]{:S(2)}, u32[]{:S(2)}) collective-permute-start(f32[1,3,4096]{2,0,1:T(1,128)S(1)} %reshape.368), channel_id=1, source_target_pairs={{0,4},{4,8},{8,12},{12,16},{16,20},{20,24},{24,28},{1,5},{5,9},{9,... | collective-permute-start | bytes 147464 | tf_op jit(solution)/shard_map/ppermute | solution.py:27
  60.3 52.0 %copy-start.4 = (f32[1,1,3]{2,1,0:T(1,128)S(1)}, f32[1,1,3]{2,1,0:T(1,128)}, u32[]{:S(2)}) copy-start(f32[1,1,3]{2,1,0:T(1,128)} %param.22) | copy-start | bytes 40
  64.4 0.6 copy-start.2
  103.3 9.1 %collective-permute-start.11 = (f32[3,4096]{1,0:T(4,128)S(1)}, f32[3,4096]{1,0:T(4,128)S(1)}, u32[]{:S(2)}, u32[]{:S(2)}) collective-permute-start(f32[3,4096]{1,0:T(4,128)S(1)} %squeeze_reshape_squeeze.14), channel_id=1, source_target_pairs={{0,3},{1,0},{2,1},{3,2},{4,7},{5,4},{6,5},{7,6},{8,11},{9,8},{10,9... | collective-permute-start | bytes 147464 | tf_op jit(solution)/shard_map/ppermute | solution.py:32
  103.3 9.1 %collective-permute-start.12 = (f32[3,4096]{1,0:T(4,128)S(1)}, f32[3,4096]{1,0:T(4,128)S(1)}, u32[]{:S(2)}, u32[]{:S(2)}) collective-permute-start(f32[3,4096]{1,0:T(4,128)S(1)} %squeeze_reshape_squeeze.15), channel_id=1, source_target_pairs={{0,3},{1,0},{2,1},{3,2},{4,7},{5,4},{6,5},{7,6},{8,11},{9,8},{10,9... | collective-permute-start | bytes 147464 | tf_op jit(solution)/shard_map/ppermute | solution.py:32
  104.3 11.2 %copy-start = (f32[3,1,4096]{2,1,0:T(1,128)S(1)}, f32[3,1,4096]{2,1,0:T(1,128)}, u32[]{:S(2)}) copy-start(f32[3,1,4096]{2,1,0:T(1,128)} %mul.311.refs_4_) | copy-start | bytes 147460
  106.5 6.5 %collective-permute-start.8 = (f32[1,3,4096]{2,0,1:T(1,128)S(1)}, f32[1,3,4096]{2,0,1:T(1,128)S(1)}, u32[]{:S(2)}, u32[]{:S(2)}) collective-permute-start(f32[1,3,4096]{2,0,1:T(1,128)S(1)} %get-tuple-element.27), channel_id=1, source_target_pairs={{4,0},{8,4},{12,8},{16,12},{20,16},{24,20},{28,24},{5,1},{9,5},{13... | collective-permute-start | bytes 147464 | tf_op jit(solution)/shard_map/ppermute | solution.py:27
  108.4 6.0 %collective-permute-start.9 = (f32[1,3,4096]{2,0,1:T(1,128)S(1)}, f32[1,3,4096]{2,0,1:T(1,128)S(1)}, u32[]{:S(2)}, u32[]{:S(2)}) collective-permute-start(f32[1,3,4096]{2,0,1:T(1,128)S(1)} %get-tuple-element.28), channel_id=1, source_target_pairs={{4,0},{8,4},{12,8},{16,12},{20,16},{24,20},{28,24},{5,1},{9,5},{13... | collective-permute-start | bytes 147464 | tf_op jit(solution)/shard_map/ppermute | solution.py:27
  114.7 3.9 %collective-permute-start.13 = (f32[3,4096]{1,0:T(4,128)S(1)}, f32[3,4096]{1,0:T(4,128)S(1)}, u32[]{:S(2)}, u32[]{:S(2)}) collective-permute-start(f32[3,4096]{1,0:T(4,128)S(1)} %add.180), channel_id=1, source_target_pairs={{0,1},{1,2},{2,3},{3,0},{4,5},{5,6},{6,7},{7,4},{8,9},{9,10},{10,1... | collective-permute-start | bytes 147464 | tf_op jit(solution)/shard_map/ppermute | solution.py:32
  116.4 7.1 %collective-permute-start.10 = (f32[1,3,4096]{2,0,1:T(1,128)S(1)}, f32[1,3,4096]{2,0,1:T(1,128)S(1)}, u32[]{:S(2)}, u32[]{:S(2)}) collective-permute-start(f32[1,3,4096]{2,0,1:T(1,128)S(1)} %reshape.369), channel_id=1, source_target_pairs={{0,4},{4,8},{8,12},{12,16},{16,20},{20,24},{24,28},{1,5},{5,9},{9,... | collective-permute-start | bytes 147464 | tf_op jit(solution)/shard_map/ppermute | solution.py:27
  123.5 0.6 copy-start.1
where the time goes:
time: 162 us; the launch traced here: 161 us
  Pallas kernels  110 us (68%)
  starting transfers between devices  24 us (15%)
  local copies, waits for them, and re-layouts  11.3 us (7%)
  waiting for transfers between devices  9.86 us (6%)
  other arithmetic  3.02 us (2%)
    pallas_call x3, Pallas kernels, kernel_sweep(): pl.pallas_call(kernel, grid=(ncomp,), in_specs=in_specs, out_specs=out_sp...  110 us
    ppermute x7, starting transfers between devices, shifted(): return lax.ppermute(shard, axis, pairs)  19.7 us
    ppermute x7, waiting for transfers between devices, shifted(): return lax.ppermute(shard, axis, pairs)  8.46 us
    ppermute x7, starting transfers between devices, shifted_2(): lax.ppermute(shard, axis, [(i, (i + by) % length) for i in range(length)])  4.25 us
    squeeze x2, local copies, waits for them, and re-layouts, shards(): x_low_side = (xf[:, :, 2], xf[:, :, 3])  3.26 us
  transfers between devices with their start and end apart: 14, of which 4 were waited for; matrix products, arithmetic and copies ran while one was open for 7% of the time, Pallas kernels for 23%

commit v1 on v0

--- a/solution.py
+++ b/solution.py
@@ -8,6 +8,7 @@
 from jax.experimental import pallas as pl
 from jax.experimental.pallas import tpu as pltpu
 import numpy as np
+import ml_dtypes
 
 ITERS = 2
 
@@ -84,7 +85,6 @@
     )
 
 
-HI = lax.Precision.HIGHEST
 f32 = jnp.float32
 
 
@@ -96,34 +96,81 @@
     e = g(2.0) - g(2.0) * np.cos(g(math.pi) * idx / g(n + 1))
     return q.astype(g), e.astype(g)
 
+
 def consts(n):
     q, e = np_tables(n)
     h = n // 2
-    p = np.kron(np.eye(2, dtype=np.float32), q.T)
-    qe = q[0::2]; qo = q[1::2]
-    q00 = qe[:, 0::2]; q01 = qe[:, 1::2]; q10 = qo[:, 0::2]; q11 = qo[:, 1::2]
-    mst = np.concatenate([np.concatenate([q00, q01], 1), np.concatenate([q11, q10], 1)], 0)
-    lane = np.arange(2 * n) % n
-    hh = np.arange(2 * n) // n
-    ej = e[2 * np.arange(h)[:, None] + hh[None, :]]
-    ek = np.ascontiguousarray(np.broadcast_to(e[lane][None, :], (h, 2 * n)))
-    return q, p, mst, ej, ek, e
+    p4 = np.kron(np.eye(4, dtype=np.float32), q.T)
+    w = np.zeros((2, 4, h, 2, 4, h), np.float32)
+    qq = q.reshape(h, 2, h, 2)
+    for xl in range(4):
+        w[:, xl, :, :, xl, :] = np.transpose(qq, (3, 2, 1, 0))
+    wy = w.reshape(8 * h, 8 * h)
+    ng = n // 4
+    lane_h = np.arange(8 * h) // (4 * h)
+    lane_xl = (np.arange(8 * h) // h) % 4
+    lane_c = np.arange(8 * h) % h
+    exy = (e[4 * np.arange(ng)[:, None] + lane_xl[None, :]] + e[2 * lane_c + lane_h][None, :]).astype(np.float32)
+    ez = np.ascontiguousarray(np.broadcast_to(e[:, None], (n, 8 * h))).astype(np.float32)
+    return stack_left(q), stack_right(p4), stack_right(wy), exy, ez
+
+
+BF = jnp.bfloat16
+
+def np_split3(w):
+    b = ml_dtypes.bfloat16
+    w1 = w.astype(b)
+    r1 = w - w1.astype(np.float32)
+    w2 = r1.astype(b)
+    w3 = (r1 - w2.astype(np.float32)).astype(b)
+    return w1, w2, w3
+
+
+def stack_right(w):
+    w1, w2, w3 = np_split3(w)
+    return np.concatenate([w1, w2, w3, w1, w2, w1], 0)
+
+
+def stack_left(w):
+    w1, w2, w3 = np_split3(w)
+    return np.concatenate([w1, w2, w3, w1, w2, w1], 1)
+
+
+def split3(d):
+    d1 = d.astype(BF)
+    r1 = d - d1.astype(f32)
+    d2 = r1.astype(BF)
+    d3 = (r1 - d2.astype(f32)).astype(BF)
+    return d1, d2, d3
+
+
+def sdot(d, w6):
+    d1, d2, d3 = split3(d)
+    return jnp.dot(jnp.concatenate([d1, d1, d1, d2, d2, d3], 1), w6, preferred_element_type=f32)
+
+
+def sdot_left(w6, d):
+    d1, d2, d3 = split3(d)
+    return jnp.dot(w6, jnp.concatenate([d1, d1, d1, d2, d2, d3], 0), preferred_element_type=f32)
+
 
 def solve_kernel(*refs, with_faces, emit_u, emit_sides):
     it = iter(refs)
-    mod_ref, ex_ref, f_ref = next(it), next(it), next(it)
+    mod_ref, f_ref = next(it), next(it)
     if with_faces:
         xlo_ref, xhi_ref, yadd_ref = next(it), next(it), next(it)
-    q_ref, p_ref, mst_ref, ej_ref, ek_ref = next(it), next(it), next(it), next(it), next(it)
+    q_ref, p_ref, wy_ref, exy_ref, ez_ref = next(it), next(it), next(it), next(it), next(it)
     o_ref = next(it) if emit_u else None
     if emit_sides:
         xf_ref, yf_ref = next(it), next(it)
-    s_ref = next(it)
+    s_ref, z_ref = next(it), next(it)
     n = q_ref.shape[0]
     h = n // 2
     w2 = 2 * n
+    w4 = 4 * n
     nn = f_ref.shape[-1]
     nch = nn // w2
+    npair = nn // w4
     comp = pl.program_id(0)
     m = mod_ref[comp]
     q = q_ref[...]
@@ -137,38 +184,43 @@
         last = added[:, nn - w2:] + jnp.where(lane >= n, yadd, 0.0)
         added = jnp.concatenate([first, added[:, w2:nn - w2], last], 1)
         r = r + (2.0 * m) * added
-    a = jnp.dot(q, r, precision=HI, preferred_element_type=f32)
-    for c in range(nch):
-        s_ref[c * n:(c + 1) * n, :] = a[:, c * w2:(c + 1) * w2]
-    s_ref[...] = jnp.dot(s_ref[...], p_ref[...], precision=HI, preferred_element_type=f32)
-    mst = mst_ref[...]
-    ej = ej_ref[...]
-    ek = ek_ref[...]
-    lane_lo = lax.broadcasted_iota(jnp.int32, (h, w2), 1) < n
-    G = 8
-
-    def ycon(ys):
-        zs = [jnp.concatenate([y, pltpu.roll(y, n, 1)], 0) for y in ys]
-        w = jnp.dot(mst, jnp.concatenate(zs, 1), precision=HI, preferred_element_type=f32)
-        out = []
-        for t in range(len(ys)):
-            wt = w[:, t * w2:(t + 1) * w2]
-            out.append(jnp.where(lane_lo, wt[:h], wt[h:]))
-        return out
-
-    def body(g, carry):
-        xs = [g * G + t for t in range(G)]
-        ys = [s_ref[pl.ds(x, h, stride=n), :] for x in xs]
-        ws = ycon(ys)
-        ws = [w / (m * ((ex_ref[x] + ej) + ek) + 0.02) for w, x in zip(ws, xs)]
-        ws = ycon(ws)
-        for x, w in zip(xs, ws):
-            s_ref[pl.ds(x, h, stride=n), :] = w
+    a = sdot_left(q, r)
+    for cp in range(npair):
+        z_ref[cp * n:(cp + 1) * n, :] = a[:, cp * w4:(cp + 1) * w4]
+    zo = sdot(z_ref[...], p_ref[...])
+    for cp in range(npair):
+        for cb in range(2):
+            s_ref[(2 * cp + cb) * n:(2 * cp + cb + 1) * n, :] = zo[cp * n:(cp + 1) * n, cb * w2:(cb + 1) * w2]
+    wy = wy_ref[...]
+    ez = ez_ref[...]
+    XG = 4
+    GPI = 4
+
+    def body(it_, carry):
+        lhs = []
+        for gi in range(GPI):
+            g = it_ * GPI + gi
+            blk = jnp.concatenate([s_ref[pl.ds(g * XG + xl, h, stride=n), :] for xl in range(XG)], 0)
+            tb = blk.T
+            lhs.append(jnp.concatenate([tb[:n], tb[n:]], 1))
+        v = sdot(jnp.concatenate(lhs, 0), wy)
+        div = jnp.concatenate([m * (exy_ref[pl.ds(it_ * GPI + gi, 1), :] + ez) + 0.02 for gi in range(GPI)], 0)
+        v = v / div
+        v = sdot(v, wy)
+        for gi in range(GPI):
+            g = it_ * GPI + gi
+            vg = v[gi * n:(gi + 1) * n]
+            tb = jnp.concatenate([vg[:, :w2], vg[:, w2:]], 0).T
+            for xl in range(XG):
+                s_ref[pl.ds(g * XG + xl, h, stride=n), :] = tb[xl * h:(xl + 1) * h]
         return carry
-    lax.fori_loop(0, n // G, body, 0)
-    s_ref[...] = jnp.dot(s_ref[...], p_ref[...], precision=HI, preferred_element_type=f32)
-    b = jnp.concatenate([s_ref[c * n:(c + 1) * n, :] for c in range(nch)], 1)
-    u = jnp.dot(q, b, precision=HI, preferred_element_type=f32)
+    lax.fori_loop(0, n // (XG * GPI), body, 0)
+    for cp in range(npair):
+        z_ref[cp * n:(cp + 1) * n, :] = jnp.concatenate(
+            [s_ref[(2 * cp) * n:(2 * cp + 1) * n, :], s_ref[(2 * cp + 1) * n:(2 * cp + 2) * n, :]], 1)
+    zo = sdot(z_ref[...], p_ref[...])
+    b = jnp.concatenate([zo[cp * n:(cp + 1) * n, :] for cp in range(npair)], 1)
+    u = sdot_left(q, b)
     if emit_u:
         o_ref[0] = u
 
@@ -189,20 +241,20 @@
         yf_ref[0, 3] = slope(c_lo, pltpu.roll(c_lo, n, 1), c_lo2, pltpu.roll(c_lo2, n, 1))
 
 
-def kernel_sweep(rhs, moduli, faces=None, emit_u=True, emit_sides=False):
+def kernel_sweep(rhs, moduli, faces=None, emit_u=True, emit_sides=False, interpret=False):
     ncomp, n, nn = rhs.shape
-    q, p, mst, ej, ek, e = consts(n)
+    q, p4, wy, exy, ez = consts(n)
     full = lambda shp: pl.BlockSpec(shp, lambda c: (0,) * len(shp))
     comp3 = lambda shp: pl.BlockSpec((1,) + shp, lambda c: (c,) + (0,) * len(shp))
     smem = pl.BlockSpec(memory_space=pltpu.SMEM)
-    in_specs = [smem, smem, comp3((n, nn))]
-    args = [moduli, e, rhs]
+    in_specs = [smem, comp3((n, nn))]
+    args = [moduli, rhs]
     if faces is not None:
         xlo, xhi, yadd = faces
         in_specs += [comp3((1, nn)), comp3((1, nn)), comp3((n, 2 * n))]
         args += [xlo.reshape(ncomp, 1, nn), xhi.reshape(ncomp, 1, nn), yadd]
-    in_specs += [full(q.shape), full(p.shape), full(mst.shape), full(ej.shape), full(ek.shape)]
-    args += [q, p, mst, ej, ek]
+    in_specs += [full(q.shape), full(p4.shape), full(wy.shape), full(exy.shape), full(ez.shape)]
+    args += [q, p4, wy, exy, ez]
     out_specs, out_shape = [], []
     if emit_u:
         out_specs.append(comp3((n, nn)))
@@ -217,7 +269,8 @@
         in_specs=in_specs,
         out_specs=out_specs,
         out_shape=out_shape,
-        scratch_shapes=[pltpu.VMEM((nn // 2, 2 * n), f32)],
+        scratch_shapes=[pltpu.VMEM((nn // 2, 2 * n), f32), pltpu.VMEM((nn // 4, 4 * n), f32)],
+        interpret=interpret,
     )(*args)
 
 

time: 162 us -> 142 us (0.88)
  Pallas kernels: 110 us -> 90 us
    pallas_call x3, Pallas kernels: 110 us -> 90 us  [kernel_sweep(): pl.pallas_call(kernel, grid=(ncomp,), in_specs=in_specs, out_specs=out_sp...]
  transfers between devices with their start and end apart: 14 -> 14, of which waited for: 4 -> 5; matrix products, arithmetic and copies ran while one was open for 7% -> 9% of each run, Pallas kernels for 23% -> 21%
where the time goes in v1:
time: 142 us; the launch traced here: 140 us
  Pallas kernels  90 us (63%)
  starting transfers between devices  23.5 us (17%)
  local copies, waits for them, and re-layouts  11.3 us (8%)
  waiting for transfers between devices  10.3 us (7%)
  other arithmetic  3.02 us (2%)
    pallas_call x3, Pallas kernels, kernel_sweep(): pl.pallas_call(kernel, grid=(ncomp,), in_specs=in_specs, out_specs=out_sp...  90 us
    ppermute x7, starting transfers between devices, shifted(): return lax.ppermute(shard, axis, pairs)  19.2 us
    ppermute x7, waiting for transfers between devices, shifted(): return lax.ppermute(shard, axis, pairs)  8.77 us
    ppermute x7, starting transfers between devices, shifted_2(): lax.ppermute(shard, axis, [(i, (i + by) % length) for i in range(length)])  4.26 us
    squeeze x2, local copies, waits for them, and re-layouts, shards(): x_low_side = (xf[:, :, 2], xf[:, :, 3])  3.26 us
  transfers between devices with their start and end apart: 14, of which 5 were waited for; matrix products, arithmetic and copies ran while one was open for 9% of the time, Pallas kernels for 21%

profile of v1, /device:TPU:24, one launch (start us, length us, event | category | flops | bytes accessed | tf_op | source)
XLA Modules:
  0.0 140.4 jit_solution(11063224317272652112)
XLA Ops:
  0.0 3.3 %collective-permute-start = (f32[1,3]{1,0:T(1,128)}, f32[1,3]{1,0:T(1,128)S(1)}, u32[]{:S(2)}, u32[]{:S(2)}) collective-permute-start(f32[1,3]{1,0:T(1,128)} %bitcast.132), channel_id=1, source_target_pairs={{4,0},{8,4},{12,8},{16,12},{20,16},{24,20},{28,24},{5,1},{9,5},{13... | collective-permute-start | bytes 44 | tf_op jit(solution)/shard_map/ppermute | solution.py:28
  3.3 0.7 collective-permute-start.4
  4.0 29.9 %shard_map.172 = (f32[3,4,4096]{2,1,0:T(4,128)}, f32[3,4,64,128]{3,2,1,0:T(8,128)}) custom-call(f32[3]{0:T(128)} %bitcast.134, f32[3,64,4096]{2,1,0:T(8,128)} %bitcast.122, bf16[64,384]{1,0:T(8,128)(2,1)} %constant.96.clone.refs_2_.refs_5_, bf16[1536,256]{1,0:T(8,128)(2,1)} %constant.97.clone.refs_3_.refs_6_, ...), custom_call_target="tpu_custom_call" | custom-call | tf_op jit(solution)/shard_map/pallas_call | solution.py:266
  33.9 1.6 %slice_bitcast_fusion.3 = (f32[1,3,4096]{2,0,1:T(1,128)S(1)}, f32[1,3,4096]{2,0,1:T(1,128)S(1)}, f32[3,4096]{1,0:T(4,128)S(1)}, f32[3,4096]{1,0:T(4,128)S(1)}) fusion(f32[1,3,4,4096]{3,2,1,0:T(4,128)} %bitcast.129), kind=kLoop, calls=%fused_computation.58 | loop fusion | bytes 393216 | tf_op jit(solution)/shard_map/squeeze | solution.py:364
  35.5 2.4 %collective-permute-start.1 = (f32[1,3,4096]{2,0,1:T(1,128)S(1)}, f32[1,3,4096]{2,0,1:T(1,128)S(1)}, u32[]{:S(2)}, u32[]{:S(2)}) collective-permute-start(f32[1,3,4096]{2,0,1:T(1,128)S(1)} %get-tuple-element.31), channel_id=1, source_target_pairs={{4,0},{8,4},{12,8},{16,12},{20,16},{24,20},{28,24},{5,1},{9,5},{13... | collective-permute-start | bytes 147464 | tf_op jit(solution)/shard_map/ppermute | solution.py:28
  37.9 3.3 %collective-permute-start.2 = (f32[1,3,4096]{2,0,1:T(1,128)S(1)}, f32[1,3,4096]{2,0,1:T(1,128)S(1)}, u32[]{:S(2)}, u32[]{:S(2)}) collective-permute-start(f32[1,3,4096]{2,0,1:T(1,128)S(1)} %get-tuple-element.32), channel_id=1, source_target_pairs={{4,0},{8,4},{12,8},{16,12},{20,16},{24,20},{28,24},{5,1},{9,5},{13... | collective-permute-start | bytes 147464 | tf_op jit(solution)/shard_map/ppermute | solution.py:28
  41.3 1.2 fusion.96
  42.4 0.1 squeeze_reshape_squeeze.12
  42.5 0.4 collective-permute-start.5
  43.7 0.1 squeeze.53
  43.8 0.1 squeeze.50
  43.9 0.1 squeeze.52
  44.0 0.1 squeeze.47
  44.2 0.1 reshape_squeeze.21
  44.3 0.1 squeeze_reshape_squeeze.13
  44.4 0.1 reshape_squeeze.22
  44.5 0.7 collective-permute-start.6
  45.2 0.1 reduce.1
  45.3 0.1 reshape.353
  45.4 0.1 reduce.3
  45.6 0.1 reshape.355
  45.7 1.4 collective-permute-done.6
  47.1 0.1 reshape.359
  47.3 0.3 fusion.3
  47.6 0.1 mul.288
  47.7 1.4 collective-permute-start.7
  49.3 0.3 fusion.16
  49.8 0.7 mul.311.refs_3_
  50.5 0.1 reshape.368
  50.6 2.5 %collective-permute-start.3 = (f32[1,3,4096]{2,0,1:T(1,128)S(1)}, f32[1,3,4096]{2,0,1:T(1,128)S(1)}, u32[]{:S(2)}, u32[]{:S(2)}) collective-permute-start(f32[1,3,4096]{2,0,1:T(1,128)S(1)} %reshape.368), channel_id=1, source_target_pairs={{0,4},{4,8},{8,12},{12,16},{16,20},{20,24},{24,28},{1,5},{5,9},{9,... | collective-permute-start | bytes 147464 | tf_op jit(solution)/shard_map/ppermute | solution.py:28
  53.1 0.1 reshape_broadcast_in_dim.6
  53.3 0.7 maximum_bitcast_fusion.refs_4_
  54.0 3.5 %collective-permute-done.3 = f32[1,3,4096]{2,0,1:T(1,128)S(1)} collective-permute-done((f32[1,3,4096]{2,0,1:T(1,128)S(1)}, f32[1,3,4096]{2,0,1:T(1,128)S(1)}, u32[]{:S(2)}, u32[]{:S(2)}) %collective-permute-start.3) | collective-permute-done | bytes 49184 | tf_op jit(solution)/shard_map/ppermute | solution.py:28
  57.5 0.6 copy-done.2
  58.1 30.0 %shard_map.173 = (f32[3,4,4096]{2,1,0:T(4,128)}, f32[3,4,64,128]{3,2,1,0:T(8,128)}) custom-call(f32[3]{0:T(128)} %bitcast.135, f32[3,64,4096]{2,1,0:T(8,128)} %bitcast.123, f32[3,1,4096]{2,1,0:T(1,128)} %bitcast.131, f32[3,1,4096]{2,1,0:T(1,128)} %mul.311.refs_3_, f32[3,64,128]{2,1,0:T(8,128)} %maximum_bitcast_fusion.refs_4_, ...), custom_call_target="tpu_custom_call" | custom-call | tf_op jit(solution)/shard_map/pallas_call | solution.py:266
  88.1 1.1 fusion.95
  89.4 0.1 squeeze_reshape_squeeze.14
  89.6 1.0 collective-permute-start.12
  90.6 1.6 %slice_bitcast_fusion.1 = (f32[1,3,4096]{2,0,1:T(1,128)S(1)}, f32[1,3,4096]{2,0,1:T(1,128)S(1)}, f32[3,4096]{1,0:T(4,128)S(1)}, f32[3,4096]{1,0:T(4,128)S(1)}) fusion(f32[1,3,4,4096]{3,2,1,0:T(4,128)} %bitcast.128), kind=kLoop, calls=%fused_computation.54 | loop fusion | bytes 393216 | tf_op jit(solution)/shard_map/squeeze | solution.py:364
  92.2 0.1 squeeze.60
  92.3 0.1 squeeze.57
  92.4 0.1 squeeze.59
  92.5 0.1 squeeze.55
  92.8 1.9 %collective-permute-start.8 = (f32[1,3,4096]{2,0,1:T(1,128)S(1)}, f32[1,3,4096]{2,0,1:T(1,128)S(1)}, u32[]{:S(2)}, u32[]{:S(2)}) collective-permute-start(f32[1,3,4096]{2,0,1:T(1,128)S(1)} %get-tuple-element.27), channel_id=1, source_target_pairs={{4,0},{8,4},{12,8},{16,12},{20,16},{24,20},{28,24},{5,1},{9,5},{13... | collective-permute-start | bytes 147464 | tf_op jit(solution)/shard_map/ppermute | solution.py:28
  94.7 3.8 %collective-permute-start.9 = (f32[1,3,4096]{2,0,1:T(1,128)S(1)}, f32[1,3,4096]{2,0,1:T(1,128)S(1)}, u32[]{:S(2)}, u32[]{:S(2)}) collective-permute-start(f32[1,3,4096]{2,0,1:T(1,128)S(1)} %get-tuple-element.28), channel_id=1, source_target_pairs={{4,0},{8,4},{12,8},{16,12},{20,16},{24,20},{28,24},{5,1},{9,5},{13... | collective-permute-start | bytes 147464 | tf_op jit(solution)/shard_map/ppermute | solution.py:28
  98.5 0.1 reshape_squeeze.25
  98.7 0.1 divide_subtract_fusion
  98.8 0.1 reshape.366
  98.9 0.3 fusion.1
  99.3 0.1 reduce.7
  99.5 0.1 reshape.360
  99.6 1.1 collective-permute-done.9
  100.7 0.1 reduce.9
  100.8 0.1 reshape.362
  101.3 0.3 fusion.97
  101.6 0.1 mul.310
  101.7 0.7 add_multiply_fusion.refs_3_
  102.5 0.1 reshape.369
  102.7 1.9 %collective-permute-start.10 = (f32[1,3,4096]{2,0,1:T(1,128)S(1)}, f32[1,3,4096]{2,0,1:T(1,128)S(1)}, u32[]{:S(2)}, u32[]{:S(2)}) collective-permute-start(f32[1,3,4096]{2,0,1:T(1,128)S(1)} %reshape.369), channel_id=1, source_target_pairs={{0,4},{4,8},{8,12},{12,16},{16,20},{20,24},{24,28},{1,5},{5,9},{9,... | collective-permute-start | bytes 147464 | tf_op jit(solution)/shard_map/ppermute | solution.py:28
  104.7 0.1 reshape_broadcast_in_dim.7
  104.8 0.7 maximum_bitcast_fusion.1.refs_4_
  105.5 4.2 %collective-permute-done.10 = f32[1,3,4096]{2,0,1:T(1,128)S(1)} collective-permute-done((f32[1,3,4096]{2,0,1:T(1,128)S(1)}, f32[1,3,4096]{2,0,1:T(1,128)S(1)}, u32[]{:S(2)}, u32[]{:S(2)}) %collective-permute-start.10) | collective-permute-done | bytes 49184 | tf_op jit(solution)/shard_map/ppermute | solution.py:28
  109.7 0.6 copy-done.1
  110.3 30.1 %shard_map.174 = f32[3,64,4096]{2,1,0:T(8,128)} custom-call(f32[3]{0:T(128)} %bitcast.136, f32[3,64,4096]{2,1,0:T(8,128)} %bitcast.124, f32[3,1,4096]{2,1,0:T(1,128)} %bitcast.130, f32[3,1,4096]{2,1,0:T(1,128)} %add_multiply_fusion.refs_3_, f32[3,64,128]{2,1,0:T(8,128)} %maximum_bitcast_fusion.1.refs_4_, bf16[64,384]{1,0:T(8,128)(2,1)} %constant.96.clone.refs_2_.refs_5_, ...), custom_call_target="tpu_custom_call" | custom-call | tf_op jit(solution)/shard_map/pallas_call | solution.py:266
  (48 shorter events, 1.4 us)
Async XLA Ops:
  0.0 44.5 %collective-permute-start = (f32[1,3]{1,0:T(1,128)}, f32[1,3]{1,0:T(1,128)S(1)}, u32[]{:S(2)}, u32[]{:S(2)}) collective-permute-start(f32[1,3]{1,0:T(1,128)} %bitcast.132), channel_id=1, source_target_pairs={{4,0},{8,4},{12,8},{16,12},{20,16},{24,20},{28,24},{5,1},{9,5},{13... | collective-permute-start | bytes 44 | tf_op jit(solution)/shard_map/ppermute | solution.py:28
  3.3 41.8 %collective-permute-start.4 = (f32[3]{0:T(128)}, f32[3]{0:T(128)S(1)}, u32[]{:S(2)}, u32[]{:S(2)}) collective-permute-start(f32[3]{0:T(128)} %bitcast.133), channel_id=1, source_target_pairs={{0,3},{1,0},{2,1},{3,2},{4,7},{5,4},{6,5},{7,6},{8,11},{9,8},{10,9... | collective-permute-start | bytes 44 | tf_op jit(solution)/shard_map/ppermute | solution.py:33
  4.0 41.1 %copy-start.3 = (f32[1,1,3]{2,1,0:T(1,128)S(1)}, f32[1,1,3]{2,1,0:T(1,128)}, u32[]{:S(2)}) copy-start(f32[1,1,3]{2,1,0:T(1,128)} %param.19) | copy-start | bytes 40
  35.5 9.6 %collective-permute-start.1 = (f32[1,3,4096]{2,0,1:T(1,128)S(1)}, f32[1,3,4096]{2,0,1:T(1,128)S(1)}, u32[]{:S(2)}, u32[]{:S(2)}) collective-permute-start(f32[1,3,4096]{2,0,1:T(1,128)S(1)} %get-tuple-element.31), channel_id=1, source_target_pairs={{4,0},{8,4},{12,8},{16,12},{20,16},{24,20},{28,24},{5,1},{9,5},{13... | collective-permute-start | bytes 147464 | tf_op jit(solution)/shard_map/ppermute | solution.py:28
  37.9 7.5 %collective-permute-start.2 = (f32[1,3,4096]{2,0,1:T(1,128)S(1)}, f32[1,3,4096]{2,0,1:T(1,128)S(1)}, u32[]{:S(2)}, u32[]{:S(2)}) collective-permute-start(f32[1,3,4096]{2,0,1:T(1,128)S(1)} %get-tuple-element.32), channel_id=1, source_target_pairs={{4,0},{8,4},{12,8},{16,12},{20,16},{24,20},{28,24},{5,1},{9,5},{13... | collective-permute-start | bytes 147464 | tf_op jit(solution)/shard_map/ppermute | solution.py:28
  42.5 3.1 %collective-permute-start.5 = (f32[3,4096]{1,0:T(4,128)S(1)}, f32[3,4096]{1,0:T(4,128)S(1)}, u32[]{:S(2)}, u32[]{:S(2)}) collective-permute-start(f32[3,4096]{1,0:T(4,128)S(1)} %squeeze_reshape_squeeze.12), channel_id=1, source_target_pairs={{0,3},{1,0},{2,1},{3,2},{4,7},{5,4},{6,5},{7,6},{8,11},{9,8},{10,9... | collective-permute-start | bytes 147464 | tf_op jit(solution)/shard_map/ppermute | solution.py:33
  44.5 2.6 %collective-permute-start.6 = (f32[3,4096]{1,0:T(4,128)S(1)}, f32[3,4096]{1,0:T(4,128)S(1)}, u32[]{:S(2)}, u32[]{:S(2)}) collective-permute-start(f32[3,4096]{1,0:T(4,128)S(1)} %squeeze_reshape_squeeze.13), channel_id=1, source_target_pairs={{0,3},{1,0},{2,1},{3,2},{4,7},{5,4},{6,5},{7,6},{8,11},{9,8},{10,9... | collective-permute-start | bytes 147464 | tf_op jit(solution)/shard_map/ppermute | solution.py:33
  47.7 5.5 %collective-permute-start.7 = (f32[3,4096]{1,0:T(4,128)S(1)}, f32[3,4096]{1,0:T(4,128)S(1)}, u32[]{:S(2)}, u32[]{:S(2)}) collective-permute-start(f32[3,4096]{1,0:T(4,128)S(1)} %mul.288), channel_id=1, source_target_pairs={{0,1},{1,2},{2,3},{3,0},{4,5},{5,6},{6,7},{7,4},{8,9},{9,10},{10,1... | collective-permute-start | bytes 147464 | tf_op jit(solution)/shard_map/ppermute | solution.py:33
  50.6 6.9 %collective-permute-start.3 = (f32[1,3,4096]{2,0,1:T(1,128)S(1)}, f32[1,3,4096]{2,0,1:T(1,128)S(1)}, u32[]{:S(2)}, u32[]{:S(2)}) collective-permute-start(f32[1,3,4096]{2,0,1:T(1,128)S(1)} %reshape.368), channel_id=1, source_target_pairs={{0,4},{4,8},{8,12},{12,16},{16,20},{20,24},{24,28},{1,5},{5,9},{9,... | collective-permute-start | bytes 147464 | tf_op jit(solution)/shard_map/ppermute | solution.py:28
  57.5 0.6 copy-start.2
  58.1 40.5 %copy-start.4 = (f32[1,1,3]{2,1,0:T(1,128)S(1)}, f32[1,1,3]{2,1,0:T(1,128)}, u32[]{:S(2)}) copy-start(f32[1,1,3]{2,1,0:T(1,128)} %param.19) | copy-start | bytes 40
  89.5 9.1 %collective-permute-start.11 = (f32[3,4096]{1,0:T(4,128)S(1)}, f32[3,4096]{1,0:T(4,128)S(1)}, u32[]{:S(2)}, u32[]{:S(2)}) collective-permute-start(f32[3,4096]{1,0:T(4,128)S(1)} %squeeze_reshape_squeeze.14), channel_id=1, source_target_pairs={{0,3},{1,0},{2,1},{3,2},{4,7},{5,4},{6,5},{7,6},{8,11},{9,8},{10,9... | collective-permute-start | bytes 147464 | tf_op jit(solution)/shard_map/ppermute | solution.py:33
  89.6 9.1 %collective-permute-start.12 = (f32[3,4096]{1,0:T(4,128)S(1)}, f32[3,4096]{1,0:T(4,128)S(1)}, u32[]{:S(2)}, u32[]{:S(2)}) collective-permute-start(f32[3,4096]{1,0:T(4,128)S(1)} %squeeze_reshape_squeeze.15), channel_id=1, source_target_pairs={{0,3},{1,0},{2,1},{3,2},{4,7},{5,4},{6,5},{7,6},{8,11},{9,8},{10,9... | collective-permute-start | bytes 147464 | tf_op jit(solution)/shard_map/ppermute | solution.py:33
  90.6 11.2 %copy-start = (f32[3,1,4096]{2,1,0:T(1,128)S(1)}, f32[3,1,4096]{2,1,0:T(1,128)}, u32[]{:S(2)}) copy-start(f32[3,1,4096]{2,1,0:T(1,128)} %mul.311.refs_3_) | copy-start | bytes 147460
  92.8 6.6 %collective-permute-start.8 = (f32[1,3,4096]{2,0,1:T(1,128)S(1)}, f32[1,3,4096]{2,0,1:T(1,128)S(1)}, u32[]{:S(2)}, u32[]{:S(2)}) collective-permute-start(f32[1,3,4096]{2,0,1:T(1,128)S(1)} %get-tuple-element.27), channel_id=1, source_target_pairs={{4,0},{8,4},{12,8},{16,12},{20,16},{24,20},{28,24},{5,1},{9,5},{13... | collective-permute-start | bytes 147464 | tf_op jit(solution)/shard_map/ppermute | solution.py:28
  94.7 6.0 %collective-permute-start.9 = (f32[1,3,4096]{2,0,1:T(1,128)S(1)}, f32[1,3,4096]{2,0,1:T(1,128)S(1)}, u32[]{:S(2)}, u32[]{:S(2)}) collective-permute-start(f32[1,3,4096]{2,0,1:T(1,128)S(1)} %get-tuple-element.28), channel_id=1, source_target_pairs={{4,0},{8,4},{12,8},{16,12},{20,16},{24,20},{28,24},{5,1},{9,5},{13... | collective-permute-start | bytes 147464 | tf_op jit(solution)/shard_map/ppermute | solution.py:28
  100.9 3.7 %collective-permute-start.13 = (f32[3,4096]{1,0:T(4,128)S(1)}, f32[3,4096]{1,0:T(4,128)S(1)}, u32[]{:S(2)}, u32[]{:S(2)}) collective-permute-start(f32[3,4096]{1,0:T(4,128)S(1)} %add.180), channel_id=1, source_target_pairs={{0,1},{1,2},{2,3},{3,0},{4,5},{5,6},{6,7},{7,4},{8,9},{9,10},{10,1... | collective-permute-start | bytes 147464 | tf_op jit(solution)/shard_map/ppermute | solution.py:33
  102.7 7.1 %collective-permute-start.10 = (f32[1,3,4096]{2,0,1:T(1,128)S(1)}, f32[1,3,4096]{2,0,1:T(1,128)S(1)}, u32[]{:S(2)}, u32[]{:S(2)}) collective-permute-start(f32[1,3,4096]{2,0,1:T(1,128)S(1)} %reshape.369), channel_id=1, source_target_pairs={{0,4},{4,8},{8,12},{12,16},{16,20},{20,24},{24,28},{1,5},{5,9},{9,... | collective-permute-start | bytes 147464 | tf_op jit(solution)/shard_map/ppermute | solution.py:28
  109.7 0.6 copy-start.1

commit v2 on v1

--- a/solution.py
+++ b/solution.py
@@ -334,6 +334,18 @@
     return current + omega_step * smoothed.reshape(residue.shape)
 
 
+def pack_side(side):
+    return jnp.stack(side, 1)
+
+
+def unpack_side(packed):
+    return (packed[:, 0], packed[:, 1])
+
+
+def oriented(side, codes, extent):
+    return (orient(side[0], codes, extent), orient(side[1], codes, extent))
+
+
 def shards(forcing, modulus, orient_codes):
     extent = forcing.shape[3]
     blocks = forcing.shape[1]
@@ -345,10 +357,17 @@
     omegas = step_weights(ITERS)
     slab_count = lax.axis_size("blk")
     slab_index = lax.axis_index("blk")
+    has_up = (slab_index < slab_count - 1).astype(jnp.float32)
+    has_down = (slab_index > 0).astype(jnp.float32)
+    moduli_up = shifted(moduli, "blk", -1)
+    moduli_down, codes_down = shifted((moduli, codes_here), "blk", 1)
+    moduli_next = jnp.concatenate([moduli[1:], shifted_2(moduli[:1], "face", -1)], 0)
+    moduli_prev = jnp.concatenate([shifted_2(moduli[-1:], "face", 1), moduli[:-1]], 0)
     face_zeros = jnp.zeros((blocks, 3, flat), jnp.float32)
-    lam_x = face_zeros
-    lam_y = face_zeros
-    live_slab = (slab_index < slab_count - 1).astype(jnp.float32)
+    lam_x_up = face_zeros
+    lam_x_down = face_zeros
+    lam_y_next = face_zeros
+    lam_y_prev = face_zeros
     faces = [None] * blocks
     for sweep in range(ITERS + 1):
         last = sweep == ITERS
@@ -360,51 +379,51 @@
             return jnp.stack([o[0] for o in outs], 0)[None]
         xf = jnp.stack([o[0] for o in outs], 0)
         yf = jnp.stack([o[1] for o in outs], 0)
-        x_high_side = (xf[:, :, 0], xf[:, :, 1])
-        x_low_side = (xf[:, :, 2], xf[:, :, 3])
-        y_high_side = tuple(yf[:, :, k, :, extent:].reshape(blocks, 3, flat) for k in (0, 1))
-        y_low_side = tuple(yf[:, :, k, :, :extent].reshape(blocks, 3, flat) for k in (2, 3))
-        upper_value, upper_slope, upper_moduli = shifted(
-            (x_low_side[0], x_low_side[1], moduli), "blk", -1
-        )
-        upper_value = orient(upper_value, codes_here, extent)
-        upper_slope = orient(upper_slope, codes_here, extent)
-        lam_x = (
+        x_high_side = xf[:, :, 0:2].transpose(0, 2, 1, 3)
+        x_low_side = xf[:, :, 2:4].transpose(0, 2, 1, 3)
+        y_high_side = yf[:, :, 0:2, :, extent:].transpose(0, 2, 1, 3, 4).reshape(blocks, 2, 3, flat)
+        y_low_side = yf[:, :, 2:4, :, :extent].transpose(0, 2, 1, 3, 4).reshape(blocks, 2, 3, flat)
+        upper_side = shifted(x_low_side, "blk", -1)
+        lower_side = shifted(x_high_side, "blk", 1)
+        next_side = jnp.concatenate([y_low_side[1:], shifted_2(y_low_side[:1], "face", -1)], 0)
+        prev_side = jnp.concatenate([shifted_2(y_high_side[-1:], "face", 1), y_high_side[:-1]], 0)
+        lam_x_up = (
             trace_update(
-                lam_x,
-                x_high_side,
-                (upper_value, upper_slope),
+                lam_x_up,
+                unpack_side(x_high_side),
+                oriented(unpack_side(upper_side), codes_here, extent),
                 moduli,
-                upper_moduli,
+                moduli_up,
                 omegas[sweep],
                 tangent,
             )
-            * live_slab
+            * has_up
         )
-        x_high = lam_x
-        x_low = shifted(orient(lam_x, codes_here, extent), "blk", 1)
-        next_value, next_slope, next_moduli = shifted_2(
-            (y_low_side[0][0], y_low_side[1][0], moduli[0]), "face", -1
+        lam_x_down = (
+            trace_update(
+                lam_x_down,
+                unpack_side(lower_side),
+                oriented(unpack_side(x_low_side), codes_down, extent),
+                moduli_down,
+                moduli,
+                omegas[sweep],
+                tangent,
+            )
+            * has_down
         )
-        beside_value = jnp.concatenate([y_low_side[0][1:], next_value[None]], 0)
-        beside_slope = jnp.concatenate([y_low_side[1][1:], next_slope[None]], 0)
-        beside_moduli = jnp.concatenate([moduli[1:], next_moduli[None]], 0)
-        lam_y = trace_update(
-            lam_y,
-            y_high_side,
-            (beside_value, beside_slope),
-            moduli,
-            beside_moduli,
-            omegas[sweep],
-            tangent,
+        lam_y_next = trace_update(
+            lam_y_next, unpack_side(y_high_side), unpack_side(next_side), moduli, moduli_next,
+            omegas[sweep], tangent,
         )
-        previous_trace = shifted_2(lam_y[blocks - 1], "face", 1)
-        y_high = lam_y
-        y_low = jnp.concatenate([previous_trace[None], lam_y[:-1]], 0)
+        lam_y_prev = trace_update(
+            lam_y_prev, unpack_side(prev_side), unpack_side(y_low_side), moduli_prev, moduli,
+            omegas[sweep], tangent,
+        )
+        x_low = orient(lam_x_down, codes_down, extent)
         yadd = jnp.concatenate(
-            [y_low.reshape(blocks, 3, extent, extent), y_high.reshape(blocks, 3, extent, extent)], -1
+            [lam_y_prev.reshape(blocks, 3, extent, extent), lam_y_next.reshape(blocks, 3, extent, extent)], -1
         )
-        faces = [(x_low[b], x_high[b], yadd[b]) for b in range(blocks)]
+        faces = [(x_low[b], lam_x_up[b], yadd[b]) for b in range(blocks)]
 
 
 def solution(mesh):

time: 142 us -> 145 us (1.021)
  local copies, waits for them, and re-layouts: 11.3 us -> 14.9 us
  waiting for transfers between devices: 10.3 us -> 6.79 us
  between operations: 1.15 us -> 3.76 us
    ppermute x7, waiting for transfers between devices: 8.77 us -> 3.63 us  [shifted(): return lax.ppermute(shard, axis, pairs)]
    transpose x0 -> x4, local copies, waits for them, and re-layouts: none -> 4.5 us  [the longest x2 2.27 us: shards(): yf[:, :, 0:2, :, extent:].transpose(0, 2, 1, 3, 4)]
    ppermute x7 -> x6, waiting for transfers between devices: 1.49 us -> 3.16 us  [shifted_2(): lax.ppermute(shard, axis, [(i, (i + by) % length) for i in range(length)])]
    squeeze x10 -> x24, local copies, waits for them, and re-layouts: 4.19 us -> 2.78 us  [unpack_side(): return (packed[:, 0], packed[:, 1])]
    ppermute x7 -> x6, starting transfers between devices: 4.26 us -> 3.05 us  [shifted_2(): lax.ppermute(shard, axis, [(i, (i + by) % length) for i in range(length)])]
  transfers between devices with their start and end apart: 14 -> 13, of which waited for: 5 -> 3; matrix products, arithmetic and copies ran while one was open for 9% -> 9% of each run, Pallas kernels for 21% -> 21%
where the time goes in v2:
time: 145 us; the launch traced here: 144 us
  Pallas kernels  90 us (62%)
  starting transfers between devices  23.4 us (16%)
  local copies, waits for them, and re-layouts  14.9 us (10%)
  waiting for transfers between devices  6.79 us (5%)
  between operations  3.76 us (3%)
  other arithmetic  2.49 us (2%)
  matrix products  2.4 us (2%)
    pallas_call x3, Pallas kernels, kernel_sweep(): pl.pallas_call(kernel, grid=(ncomp,), in_specs=in_specs, out_specs=out_sp...  90 us
    ppermute x7, starting transfers between devices, shifted(): return lax.ppermute(shard, axis, pairs)  20.3 us
    ppermute x7, waiting for transfers between devices, shifted(): return lax.ppermute(shard, axis, pairs)  3.63 us
    ppermute x6, waiting for transfers between devices, shifted_2(): lax.ppermute(shard, axis, [(i, (i + by) % length) for i in range(length)])  3.16 us
    ppermute x6, starting transfers between devices, shifted_2(): lax.ppermute(shard, axis, [(i, (i + by) % length) for i in range(length)])  3.05 us
  transfers between devices with their start and end apart: 13, of which 3 were waited for; matrix products, arithmetic and copies ran while one was open for 9% of the time, Pallas kernels for 21%

profile of v2, /device:TPU:24, one launch (start us, length us, event | category | flops | bytes accessed | tf_op | source)
XLA Modules:
  0.0 143.7 jit_solution(7207567519817971588)
XLA Ops:
  0.0 0.9 collective-permute-start.7
  0.9 3.3 %collective-permute-start.3 = (f32[1,3]{1,0:T(1,128)}, f32[1,3]{1,0:T(1,128)S(1)}, u32[]{:S(2)}, u32[]{:S(2)}) collective-permute-start(f32[1,3]{1,0:T(1,128)} %bitcast.209), channel_id=1, source_target_pairs={{4,0},{8,4},{12,8},{16,12},{20,16},{24,20},{28,24},{5,1},{9,5},{13... | collective-permute-start | bytes 44 | tf_op jit(solution)/shard_map/ppermute | solution.py:28
  4.2 2.5 %collective-permute-start.1 = (f32[1,3]{1,0:T(1,128)}, f32[1,3]{1,0:T(1,128)S(1)}, u32[]{:S(2)}, u32[]{:S(2)}) collective-permute-start(f32[1,3]{1,0:T(1,128)} %bitcast.210), channel_id=1, source_target_pairs={{0,4},{4,8},{8,12},{12,16},{16,20},{20,24},{24,28},{1,5},{5,9},{9,... | collective-permute-start | bytes 44 | tf_op jit(solution)/shard_map/ppermute | solution.py:28
  6.8 1.9 %collective-permute-start = (s32[1]{0:T(128)}, s32[1]{0:T(128)}, u32[]{:S(2)}, u32[]{:S(2)}) collective-permute-start(s32[1]{0:T(128)} %bitcast.2), channel_id=1, source_target_pairs={{0,4},{4,8},{8,12},{12,16},{16,20},{20,24},{24,28},{1,5},{5,9},{9,... | collective-permute-start | bytes 20 | tf_op jit(solution)/shard_map/ppermute | solution.py:28
  9.4 29.9 %shard_map.172 = (f32[3,4,4096]{2,1,0:T(4,128)}, f32[3,4,64,128]{3,2,1,0:T(8,128)}) custom-call(f32[3]{0:T(128)} %bitcast.211, f32[3,64,4096]{2,1,0:T(8,128)} %bitcast.198, bf16[64,384]{1,0:T(8,128)(2,1)} %constant.127.clone.refs_2_.refs_5_, bf16[1536,256]{1,0:T(8,128)(2,1)} %constant.128.clone.refs_3_.refs_6_, ...), custom_call_target="tpu_custom_call" | custom-call | tf_op jit(solution)/shard_map/pallas_call | solution.py:266
  39.3 1.1 slice_bitcast_fusion.6
  40.4 0.6 slice_reduce_fusion.11
  41.0 0.1 squeeze.92
  41.2 0.1 squeeze.93
  41.3 0.1 squeeze.91
  41.5 1.1 slice_bitcast_fusion.3
  42.6 0.1 reshape.803
  42.8 0.1 reshape.804
  43.0 0.1 reshape_squeeze.27
  43.3 4.8 %collective-permute-start.4 = (f32[1,2,3,4096]{3,1,2,0:T(2,128)S(1)}, f32[1,2,3,4096]{3,1,2,0:T(2,128)S(1)}, u32[]{:S(2)}, u32[]{:S(2)}) collective-permute-start(f32[1,2,3,4096]{3,1,2,0:T(2,128)S(1)} %get-tuple-element.35), channel_id=1, source_target_pairs={{4,0},{8,4},{12,8},{16,12},{20,16},{24,20},{28,24},{5,1},{9,5},{13... | collective-permute-start | bytes 294920 | tf_op jit(solution)/shard_map/ppermute | solution.py:28
  50.9 1.9 %collective-permute-start.2 = (f32[1,2,3,4096]{3,1,2,0:T(2,128)S(1)}, f32[1,2,3,4096]{3,1,2,0:T(2,128)S(1)}, u32[]{:S(2)}, u32[]{:S(2)}) collective-permute-start(f32[1,2,3,4096]{3,1,2,0:T(2,128)S(1)} %get-tuple-element.36), channel_id=1, source_target_pairs={{0,4},{4,8},{8,12},{12,16},{16,20},{20,24},{24,28},{1,5},{5,9},{9,... | collective-permute-start | bytes 294920 | tf_op jit(solution)/shard_map/ppermute | solution.py:28
  52.8 0.7 collective-permute-start.8
  53.5 0.3 slice_reduce_fusion.10
  53.8 0.1 reshape_squeeze.28
  53.9 0.1 reshape_squeeze.29
  54.1 3.2 %collective-permute-done.8 = f32[1,2,3,4096]{3,2,1,0:T(4,128)S(1)} collective-permute-done((f32[1,2,3,4096]{3,2,1,0:T(4,128)S(1)}, f32[1,2,3,4096]{3,2,1,0:T(4,128)S(1)}, u32[]{:S(2)}, u32[]{:S(2)}) %collective-permute-start.8) | collective-permute-done | bytes 98336 | tf_op jit(solution)/shard_map/ppermute | solution.py:33
  57.3 1.0 collective-permute-done.2
  58.3 0.3 slice_reduce_fusion.15
  58.6 0.1 squeeze.88
  58.7 0.1 squeeze.86
  59.2 0.1 squeeze.96
  59.3 0.1 mul.568
  59.4 0.1 squeeze.97
  59.6 0.1 squeeze.94
  59.7 0.1 mul.559
  60.0 0.3 fusion.40
  60.4 0.7 reshape_squeeze_reshape.8.refs_2_
  61.2 0.3 fusion.34
  61.5 0.7 mul.608.refs_3_
  62.2 0.3 fusion.5
  62.5 0.3 fusion.7
  62.8 0.7 maximum_bitcast_fusion.refs_4_
  63.5 30.0 %shard_map.173 = (f32[3,4,4096]{2,1,0:T(4,128)}, f32[3,4,64,128]{3,2,1,0:T(8,128)}) custom-call(f32[3]{0:T(128)} %bitcast.212, f32[3,64,4096]{2,1,0:T(8,128)} %bitcast.199, f32[3,1,4096]{2,1,0:T(1,128)} %reshape_squeeze_reshape.8.refs_2_, f32[3,1,4096]{2,1,0:T(1,128)} %mul.608.refs_3_, f32[3,64,128]{2,1,0:T(8,128)} %maximum_bitcast_fusion.refs_4_, ...), custom_call_target="tpu_custom_call" | custom-call | tf_op jit(solution)/shard_map/pallas_call | solution.py:266
  93.5 1.1 slice_bitcast_fusion.4
  94.7 3.6 %collective-permute-start.10 = (f32[1,2,3,4096]{3,1,2,0:T(2,128)S(1)}, f32[1,2,3,4096]{3,1,2,0:T(2,128)S(1)}, u32[]{:S(2)}, u32[]{:S(2)}) collective-permute-start(f32[1,2,3,4096]{3,1,2,0:T(2,128)S(1)} %get-tuple-element.33), channel_id=1, source_target_pairs={{4,0},{8,4},{12,8},{16,12},{20,16},{24,20},{28,24},{5,1},{9,5},{13... | collective-permute-start | bytes 294920 | tf_op jit(solution)/shard_map/ppermute | solution.py:28
  98.2 0.3 slice_reduce_fusion.6
  98.5 1.1 slice_bitcast_fusion.1
  99.6 2.3 %collective-permute-start.9 = (f32[1,2,3,4096]{3,1,2,0:T(2,128)S(1)}, f32[1,2,3,4096]{3,1,2,0:T(2,128)S(1)}, u32[]{:S(2)}, u32[]{:S(2)}) collective-permute-start(f32[1,2,3,4096]{3,1,2,0:T(2,128)S(1)} %get-tuple-element.34), channel_id=1, source_target_pairs={{0,4},{4,8},{8,12},{12,16},{16,20},{20,24},{24,28},{1,5},{5,9},{9,... | collective-permute-start | bytes 294920 | tf_op jit(solution)/shard_map/ppermute | solution.py:28
  101.9 0.1 reshape_squeeze.30
  102.2 0.3 slice_reduce_fusion.3
  102.5 0.1 squeeze.105
  103.0 0.1 reshape.811
  103.2 0.1 reshape.812
  103.6 1.4 collective-permute-start.12
  105.0 2.7 %collective-permute-done.9 = f32[1,2,3,4096]{3,1,2,0:T(2,128)S(1)} collective-permute-done((f32[1,2,3,4096]{3,1,2,0:T(2,128)S(1)}, f32[1,2,3,4096]{3,1,2,0:T(2,128)S(1)}, u32[]{:S(2)}, u32[]{:S(2)}) %collective-permute-start.9) | collective-permute-done | bytes 98336 | tf_op jit(solution)/shard_map/ppermute | solution.py:28
  107.7 0.3 slice_reduce_fusion.7
  107.9 0.1 squeeze.101
  108.4 0.3 slice_reduce_fusion.2
  108.7 0.1 reshape_squeeze.32
  109.2 0.3 fusion.27
  109.5 0.3 fusion.18
  110.0 0.7 reshape_squeeze_reshape.9.refs_2_
  110.9 0.1 squeeze.109
  111.3 0.1 squeeze.107
  111.7 0.7 add_multiply_fusion.refs_3_
  112.3 0.3 fusion.11
  112.6 0.3 fusion.9
  112.9 0.7 maximum_bitcast_fusion.1.refs_4_
  113.7 30.0 %shard_map.174 = f32[3,64,4096]{2,1,0:T(8,128)} custom-call(f32[3]{0:T(128)} %bitcast.213, f32[3,64,4096]{2,1,0:T(8,128)} %bitcast.200, f32[3,1,4096]{2,1,0:T(1,128)} %reshape_squeeze_reshape.9.refs_2_, f32[3,1,4096]{2,1,0:T(1,128)} %add_multiply_fusion.refs_3_, f32[3,64,128]{2,1,0:T(8,128)} %maximum_bitcast_fusion.1.refs_4_, ...), custom_call_target="tpu_custom_call" | custom-call | tf_op jit(solution)/shard_map/pallas_call | solution.py:266
  (78 shorter events, 3.8 us)
Async XLA Ops:
  0.0 50.9 %collective-permute-start.7 = (f32[1,3]{1,0:T(1,128)}, f32[1,3]{1,0:T(1,128)S(1)}, u32[]{:S(2)}, u32[]{:S(2)}) collective-permute-start(f32[1,3]{1,0:T(1,128)} %bitcast.207), channel_id=1, source_target_pairs={{0,3},{1,0},{2,1},{3,2},{4,7},{5,4},{6,5},{7,6},{8,11},{9,8},{10,9... | collective-permute-start | bytes 44 | tf_op jit(solution)/shard_map/ppermute | solution.py:33
  0.9 51.9 %collective-permute-start.5 = (f32[1,3]{1,0:T(1,128)}, f32[1,3]{1,0:T(1,128)S(1)}, u32[]{:S(2)}, u32[]{:S(2)}) collective-permute-start(f32[1,3]{1,0:T(1,128)} %bitcast.208), channel_id=1, source_target_pairs={{0,1},{1,2},{2,3},{3,0},{4,5},{5,6},{6,7},{7,4},{8,9},{9,10},{10,1... | collective-permute-start | bytes 44 | tf_op jit(solution)/shard_map/ppermute | solution.py:33
  0.9 52.6 %collective-permute-start.3 = (f32[1,3]{1,0:T(1,128)}, f32[1,3]{1,0:T(1,128)S(1)}, u32[]{:S(2)}, u32[]{:S(2)}) collective-permute-start(f32[1,3]{1,0:T(1,128)} %bitcast.209), channel_id=1, source_target_pairs={{4,0},{8,4},{12,8},{16,12},{20,16},{24,20},{28,24},{5,1},{9,5},{13... | collective-permute-start | bytes 44 | tf_op jit(solution)/shard_map/ppermute | solution.py:28
  4.2 49.3 %collective-permute-start.1 = (f32[1,3]{1,0:T(1,128)}, f32[1,3]{1,0:T(1,128)S(1)}, u32[]{:S(2)}, u32[]{:S(2)}) collective-permute-start(f32[1,3]{1,0:T(1,128)} %bitcast.210), channel_id=1, source_target_pairs={{0,4},{4,8},{8,12},{12,16},{16,20},{20,24},{24,28},{1,5},{5,9},{9,... | collective-permute-start | bytes 44 | tf_op jit(solution)/shard_map/ppermute | solution.py:28
  6.8 36.5 %collective-permute-start = (s32[1]{0:T(128)}, s32[1]{0:T(128)}, u32[]{:S(2)}, u32[]{:S(2)}) collective-permute-start(s32[1]{0:T(128)} %bitcast.2), channel_id=1, source_target_pairs={{0,4},{4,8},{8,12},{12,16},{16,20},{20,24},{24,28},{1,5},{5,9},{9,... | collective-permute-start | bytes 20 | tf_op jit(solution)/shard_map/ppermute | solution.py:28
  39.3 14.2 %copy-start.1 = (f32[1,1,3]{2,1,0:T(1,128)S(1)}, f32[1,1,3]{2,1,0:T(1,128)}, u32[]{:S(2)}) copy-start(f32[1,1,3]{2,1,0:T(1,128)} %param.19) | copy-start | bytes 40
  43.3 10.2 %collective-permute-start.4 = (f32[1,2,3,4096]{3,1,2,0:T(2,128)S(1)}, f32[1,2,3,4096]{3,1,2,0:T(2,128)S(1)}, u32[]{:S(2)}, u32[]{:S(2)}) collective-permute-start(f32[1,2,3,4096]{3,1,2,0:T(2,128)S(1)} %get-tuple-element.35), channel_id=1, source_target_pairs={{4,0},{8,4},{12,8},{16,12},{20,16},{24,20},{28,24},{5,1},{9,5},{13... | collective-permute-start | bytes 294920 | tf_op jit(solution)/shard_map/ppermute | solution.py:28
  50.9 7.4 %collective-permute-start.2 = (f32[1,2,3,4096]{3,1,2,0:T(2,128)S(1)}, f32[1,2,3,4096]{3,1,2,0:T(2,128)S(1)}, u32[]{:S(2)}, u32[]{:S(2)}) collective-permute-start(f32[1,2,3,4096]{3,1,2,0:T(2,128)S(1)} %get-tuple-element.36), channel_id=1, source_target_pairs={{0,4},{4,8},{8,12},{12,16},{16,20},{20,24},{24,28},{1,5},{5,9},{9,... | collective-permute-start | bytes 294920 | tf_op jit(solution)/shard_map/ppermute | solution.py:28
  52.8 4.4 %collective-permute-start.8 = (f32[1,2,3,4096]{3,2,1,0:T(4,128)S(1)}, f32[1,2,3,4096]{3,2,1,0:T(4,128)S(1)}, u32[]{:S(2)}, u32[]{:S(2)}) collective-permute-start(f32[1,2,3,4096]{3,2,1,0:T(4,128)S(1)} %copy.37), channel_id=1, source_target_pairs={{0,3},{1,0},{2,1},{3,2},{4,7},{5,4},{6,5},{7,6},{8,11},{9,8},{10,9... | collective-permute-start | bytes 294920 | tf_op jit(solution)/shard_map/ppermute | solution.py:33
  53.5 6.1 %collective-permute-start.6 = (f32[1,2,3,4096]{3,2,1,0:T(4,128)S(1)}, f32[1,2,3,4096]{3,2,1,0:T(4,128)S(1)}, u32[]{:S(2)}, u32[]{:S(2)}) collective-permute-start(f32[1,2,3,4096]{3,2,1,0:T(4,128)S(1)} %copy.36), channel_id=1, source_target_pairs={{0,1},{1,2},{2,3},{3,0},{4,5},{5,6},{6,7},{7,4},{8,9},{9,10},{10,1... | collective-permute-start | bytes 294920 | tf_op jit(solution)/shard_map/ppermute | solution.py:33
  94.7 13.8 %collective-permute-start.10 = (f32[1,2,3,4096]{3,1,2,0:T(2,128)S(1)}, f32[1,2,3,4096]{3,1,2,0:T(2,128)S(1)}, u32[]{:S(2)}, u32[]{:S(2)}) collective-permute-start(f32[1,2,3,4096]{3,1,2,0:T(2,128)S(1)} %get-tuple-element.33), channel_id=1, source_target_pairs={{4,0},{8,4},{12,8},{16,12},{20,16},{24,20},{28,24},{5,1},{9,5},{13... | collective-permute-start | bytes 294920 | tf_op jit(solution)/shard_map/ppermute | solution.py:28
  99.6 8.0 %collective-permute-start.9 = (f32[1,2,3,4096]{3,1,2,0:T(2,128)S(1)}, f32[1,2,3,4096]{3,1,2,0:T(2,128)S(1)}, u32[]{:S(2)}, u32[]{:S(2)}) collective-permute-start(f32[1,2,3,4096]{3,1,2,0:T(2,128)S(1)} %get-tuple-element.34), channel_id=1, source_target_pairs={{0,4},{4,8},{8,12},{12,16},{16,20},{20,24},{24,28},{1,5},{5,9},{9,... | collective-permute-start | bytes 294920 | tf_op jit(solution)/shard_map/ppermute | solution.py:28
  102.0 7.2 %copy-start.2 = (f32[1,1,3]{2,1,0:T(1,128)S(1)}, f32[1,1,3]{2,1,0:T(1,128)}, u32[]{:S(2)}) copy-start(f32[1,1,3]{2,1,0:T(1,128)} %param.19) | copy-start | bytes 40
  103.6 6.4 %collective-permute-start.12 = (f32[1,2,3,4096]{3,2,1,0:T(4,128)S(1)}, f32[1,2,3,4096]{3,2,1,0:T(4,128)S(1)}, u32[]{:S(2)}, u32[]{:S(2)}) collective-permute-start(f32[1,2,3,4096]{3,2,1,0:T(4,128)S(1)} %copy.47), channel_id=1, source_target_pairs={{0,3},{1,0},{2,1},{3,2},{4,7},{5,4},{6,5},{7,6},{8,11},{9,8},{10,9... | collective-permute-start | bytes 294920 | tf_op jit(solution)/shard_map/ppermute | solution.py:33
  105.0 6.2 %collective-permute-start.11 = (f32[1,2,3,4096]{3,2,1,0:T(4,128)S(1)}, f32[1,2,3,4096]{3,2,1,0:T(4,128)S(1)}, u32[]{:S(2)}, u32[]{:S(2)}) collective-permute-start(f32[1,2,3,4096]{3,2,1,0:T(4,128)S(1)} %copy.46), channel_id=1, source_target_pairs={{0,1},{1,2},{2,3},{3,0},{4,5},{5,6},{6,7},{7,4},{8,9},{9,10},{10,1... | collective-permute-start | bytes 294920 | tf_op jit(solution)/shard_map/ppermute | solution.py:33
  109.1 2.6 %copy-start = (f32[3,1,4096]{2,1,0:T(1,128)S(1)}, f32[3,1,4096]{2,1,0:T(1,128)}, u32[]{:S(2)}) copy-start(f32[3,1,4096]{2,1,0:T(1,128)} %mul.608.refs_3_) | copy-start | bytes 147460

commit v3 on v2

--- a/solution.py
+++ b/solution.py
@@ -154,43 +154,38 @@
     return jnp.dot(w6, jnp.concatenate([d1, d1, d1, d2, d2, d3], 0), preferred_element_type=f32)
 
 
-def solve_kernel(*refs, with_faces, emit_u, emit_sides):
-    it = iter(refs)
-    mod_ref, f_ref = next(it), next(it)
-    if with_faces:
-        xlo_ref, xhi_ref, yadd_ref = next(it), next(it), next(it)
-    q_ref, p_ref, wy_ref, exy_ref, ez_ref = next(it), next(it), next(it), next(it), next(it)
-    o_ref = next(it) if emit_u else None
-    if emit_sides:
-        xf_ref, yf_ref = next(it), next(it)
-    s_ref, z_ref = next(it), next(it)
+def solve_kernel(mod_ref, f_ref, xlo_ref, xhi_ref, yadd_ref, q_ref, p_ref, wy_ref, exy_ref, ez_ref,
+                 o_ref, xf_ref, yf_ref, s_ref):
     n = q_ref.shape[0]
     h = n // 2
     w2 = 2 * n
     w4 = 4 * n
     nn = f_ref.shape[-1]
-    nch = nn // w2
     npair = nn // w4
     comp = pl.program_id(0)
     m = mod_ref[comp]
+    two_m = 2.0 * m
     q = q_ref[...]
-    r = f_ref[0]
-    if with_faces:
-        rows = lax.broadcasted_iota(jnp.int32, (n, nn), 0)
-        added = jnp.where(rows == 0, xlo_ref[0], 0.0) + jnp.where(rows == n - 1, xhi_ref[0], 0.0)
-        lane = lax.broadcasted_iota(jnp.int32, (n, w2), 1)
-        yadd = yadd_ref[0]
-        first = added[:, :w2] + jnp.where(lane < n, yadd, 0.0)
-        last = added[:, nn - w2:] + jnp.where(lane >= n, yadd, 0.0)
-        added = jnp.concatenate([first, added[:, w2:nn - w2], last], 1)
-        r = r + (2.0 * m) * added
-    a = sdot_left(q, r)
-    for cp in range(npair):
-        z_ref[cp * n:(cp + 1) * n, :] = a[:, cp * w4:(cp + 1) * w4]
-    zo = sdot(z_ref[...], p_ref[...])
-    for cp in range(npair):
-        for cb in range(2):
-            s_ref[(2 * cp + cb) * n:(2 * cp + cb + 1) * n, :] = zo[cp * n:(cp + 1) * n, cb * w2:(cb + 1) * w2]
+    p = p_ref[...]
+    rows = lax.broadcasted_iota(jnp.int32, (n, w4), 0)
+    lane4 = lax.broadcasted_iota(jnp.int32, (n, w4), 1)
+    yadd = yadd_ref[0]
+    yadd2 = jnp.concatenate([yadd, yadd], 1)
+    y_first = jnp.where(lane4 < n, yadd2, 0.0)
+    y_last = jnp.where(lane4 >= w4 - n, yadd2, 0.0)
+
+    def stage_in(cp, carry):
+        off = pl.multiple_of(cp * w4, w4)
+        r = f_ref[0, :, pl.ds(off, w4)]
+        added = jnp.where(rows == 0, xlo_ref[0, :, pl.ds(off, w4)], 0.0) + jnp.where(
+            rows == n - 1, xhi_ref[0, :, pl.ds(off, w4)], 0.0)
+        added = added + jnp.where(cp == 0, y_first, 0.0) + jnp.where(cp == npair - 1, y_last, 0.0)
+        r = r + two_m * added
+        zc = sdot(sdot_left(q, r), p)
+        s_ref[pl.ds(2 * cp * n, n), :] = zc[:, :w2]
+        s_ref[pl.ds((2 * cp + 1) * n, n), :] = zc[:, w2:]
+        return carry
+    lax.fori_loop(0, npair, stage_in, 0)
     wy = wy_ref[...]
     ez = ez_ref[...]
     XG = 4
@@ -215,62 +210,51 @@
                 s_ref[pl.ds(g * XG + xl, h, stride=n), :] = tb[xl * h:(xl + 1) * h]
         return carry
     lax.fori_loop(0, n // (XG * GPI), body, 0)
-    for cp in range(npair):
-        z_ref[cp * n:(cp + 1) * n, :] = jnp.concatenate(
-            [s_ref[(2 * cp) * n:(2 * cp + 1) * n, :], s_ref[(2 * cp + 1) * n:(2 * cp + 2) * n, :]], 1)
-    zo = sdot(z_ref[...], p_ref[...])
-    b = jnp.concatenate([zo[cp * n:(cp + 1) * n, :] for cp in range(npair)], 1)
-    u = sdot_left(q, b)
-    if emit_u:
-        o_ref[0] = u
 
     def slope(p0, p1, p2, p3):
         return m * (11.0 / 6.0 * p0 - 3.0 * p1 + 1.5 * p2 - p3 / 3.0)
-    if emit_sides:
-        xf_ref[0, 0:1, :] = u[n - 1:n]
-        xf_ref[0, 1:2, :] = slope(u[n - 1:n], u[n - 2:n - 1], u[n - 3:n - 2], u[n - 4:n - 3])
-        xf_ref[0, 2:3, :] = u[0:1]
-        xf_ref[0, 3:4, :] = slope(u[0:1], u[1:2], u[2:3], u[3:4])
-        c_hi = u[:, nn - w2:]
-        c_hi2 = u[:, nn - 2 * w2:nn - w2]
-        yf_ref[0, 0] = c_hi
-        yf_ref[0, 1] = slope(c_hi, pltpu.roll(c_hi, n, 1), c_hi2, pltpu.roll(c_hi2, n, 1))
-        c_lo = u[:, :w2]
-        c_lo2 = u[:, w2:2 * w2]
-        yf_ref[0, 2] = c_lo
-        yf_ref[0, 3] = slope(c_lo, pltpu.roll(c_lo, n, 1), c_lo2, pltpu.roll(c_lo2, n, 1))
-
-
-def kernel_sweep(rhs, moduli, faces=None, emit_u=True, emit_sides=False, interpret=False):
+
+    def stage_out(cp, carry):
+        off = pl.multiple_of(cp * w4, w4)
+        zin = jnp.concatenate([s_ref[pl.ds(2 * cp * n, n), :], s_ref[pl.ds((2 * cp + 1) * n, n), :]], 1)
+        u = sdot_left(q, sdot(zin, p))
+        o_ref[0, :, pl.ds(off, w4)] = u
+        xf_ref[0, 0:1, pl.ds(off, w4)] = u[n - 1:n]
+        xf_ref[0, 1:2, pl.ds(off, w4)] = slope(u[n - 1:n], u[n - 2:n - 1], u[n - 3:n - 2], u[n - 4:n - 3])
+        xf_ref[0, 2:3, pl.ds(off, w4)] = u[0:1]
+        xf_ref[0, 3:4, pl.ds(off, w4)] = slope(u[0:1], u[1:2], u[2:3], u[3:4])
+        return carry
+    lax.fori_loop(0, npair, stage_out, 0)
+    c_hi = o_ref[0, :, nn - w2:]
+    c_hi2 = o_ref[0, :, nn - 2 * w2:nn - w2]
+    yf_ref[0, 0] = c_hi
+    yf_ref[0, 1] = slope(c_hi, pltpu.roll(c_hi, n, 1), c_hi2, pltpu.roll(c_hi2, n, 1))
+    c_lo = o_ref[0, :, :w2]
+    c_lo2 = o_ref[0, :, w2:2 * w2]
+    yf_ref[0, 2] = c_lo
+    yf_ref[0, 3] = slope(c_lo, pltpu.roll(c_lo, n, 1), c_lo2, pltpu.roll(c_lo2, n, 1))
+
+
+def kernel_sweep(rhs, moduli, faces):
     ncomp, n, nn = rhs.shape
     q, p4, wy, exy, ez = consts(n)
     full = lambda shp: pl.BlockSpec(shp, lambda c: (0,) * len(shp))
     comp3 = lambda shp: pl.BlockSpec((1,) + shp, lambda c: (c,) + (0,) * len(shp))
     smem = pl.BlockSpec(memory_space=pltpu.SMEM)
-    in_specs = [smem, comp3((n, nn))]
-    args = [moduli, rhs]
-    if faces is not None:
-        xlo, xhi, yadd = faces
-        in_specs += [comp3((1, nn)), comp3((1, nn)), comp3((n, 2 * n))]
-        args += [xlo.reshape(ncomp, 1, nn), xhi.reshape(ncomp, 1, nn), yadd]
-    in_specs += [full(q.shape), full(p4.shape), full(wy.shape), full(exy.shape), full(ez.shape)]
-    args += [q, p4, wy, exy, ez]
-    out_specs, out_shape = [], []
-    if emit_u:
-        out_specs.append(comp3((n, nn)))
-        out_shape.append(jax.ShapeDtypeStruct(rhs.shape, f32))
-    if emit_sides:
-        out_specs += [comp3((4, nn)), comp3((4, n, 2 * n))]
-        out_shape += [jax.ShapeDtypeStruct((ncomp, 4, nn), f32), jax.ShapeDtypeStruct((ncomp, 4, n, 2 * n), f32)]
-    kernel = functools.partial(solve_kernel, with_faces=faces is not None, emit_u=emit_u, emit_sides=emit_sides)
+    xlo, xhi, yadd = faces
+    in_specs = [smem, comp3((n, nn)), comp3((1, nn)), comp3((1, nn)), comp3((n, 2 * n)),
+                full(q.shape), full(p4.shape), full(wy.shape), full(exy.shape), full(ez.shape)]
+    args = [moduli, rhs, xlo.reshape(ncomp, 1, nn), xhi.reshape(ncomp, 1, nn), yadd, q, p4, wy, exy, ez]
+    out_specs = [comp3((n, nn)), comp3((4, nn)), comp3((4, n, 2 * n))]
+    out_shape = [jax.ShapeDtypeStruct(rhs.shape, f32), jax.ShapeDtypeStruct((ncomp, 4, nn), f32),
+                 jax.ShapeDtypeStruct((ncomp, 4, n, 2 * n), f32)]
     return pl.pallas_call(
-        kernel,
+        solve_kernel,
         grid=(ncomp,),
         in_specs=in_specs,
         out_specs=out_specs,
         out_shape=out_shape,
-        scratch_shapes=[pltpu.VMEM((nn // 2, 2 * n), f32), pltpu.VMEM((nn // 4, 4 * n), f32)],
-        interpret=interpret,
+        scratch_shapes=[pltpu.VMEM((nn // 2, 2 * n), f32)],
     )(*args)
 
 
@@ -368,17 +352,14 @@
     lam_x_down = face_zeros
     lam_y_next = face_zeros
     lam_y_prev = face_zeros
-    faces = [None] * blocks
+    faces = [(face_zeros[b], face_zeros[b], jnp.zeros((3, extent, 2 * extent), jnp.float32)) for b in range(blocks)]
     for sweep in range(ITERS + 1):
         last = sweep == ITERS
-        outs = [
-            kernel_sweep(source_field[b], moduli[b], faces[b], emit_u=last, emit_sides=not last)
-            for b in range(blocks)
-        ]
+        outs = [kernel_sweep(source_field[b], moduli[b], faces[b]) for b in range(blocks)]
         if last:
             return jnp.stack([o[0] for o in outs], 0)[None]
-        xf = jnp.stack([o[0] for o in outs], 0)
-        yf = jnp.stack([o[1] for o in outs], 0)
+        xf = jnp.stack([o[1] for o in outs], 0)
+        yf = jnp.stack([o[2] for o in outs], 0)
         x_high_side = xf[:, :, 0:2].transpose(0, 2, 1, 3)
         x_low_side = xf[:, :, 2:4].transpose(0, 2, 1, 3)
         y_high_side = yf[:, :, 0:2, :, extent:].transpose(0, 2, 1, 3, 4).reshape(blocks, 2, 3, flat)

time: 145 us -> 246 us (1.70)
  Pallas kernels: 90 us -> 190 us
    pallas_call x3, Pallas kernels: 90 us -> 190 us  [kernel_sweep(): pl.pallas_call(solve_kernel, grid=(ncomp,), in_specs=in_specs, out_specs=...]
  transfers between devices with their start and end apart: 13 -> 13, of which waited for: 3 -> 3; matrix products, arithmetic and copies ran while one was open for 9% -> 6% of each run, Pallas kernels for 21% -> 26%
where the time goes in v3:
time: 246 us; the launch traced here: 245 us
  Pallas kernels  190 us (77%)
  starting transfers between devices  23.5 us (10%)
  local copies, waits for them, and re-layouts  16.2 us (7%)
  waiting for transfers between devices  6.62 us (3%)
  between operations  3.88 us (2%)
  other arithmetic  2.51 us (1%)
    pallas_call x3, Pallas kernels, kernel_sweep(): pl.pallas_call(solve_kernel, grid=(ncomp,), in_specs=in_specs, out_specs=...  190 us
    ppermute x7, starting transfers between devices, shifted(): return lax.ppermute(shard, axis, pairs)  20.3 us
  transfers between devices with their start and end apart: 13, of which 3 were waited for; matrix products, arithmetic and copies ran while one was open for 6% of the time, Pallas kernels for 26%

profile of v3, /device:TPU:24, one launch (start us, length us, event | category | flops | bytes accessed | tf_op | source)
XLA Modules:
  0.0 244.6 jit_solution(10518386649201019824)
XLA Ops:
  0.0 0.9 collective-permute-start.7
  0.9 3.3 %collective-permute-start.3 = (f32[1,3]{1,0:T(1,128)}, f32[1,3]{1,0:T(1,128)S(1)}, u32[]{:S(2)}, u32[]{:S(2)}) collective-permute-start(f32[1,3]{1,0:T(1,128)} %bitcast.209), channel_id=1, source_target_pairs={{4,0},{8,4},{12,8},{16,12},{20,16},{24,20},{28,24},{5,1},{9,5},{13... | collective-permute-start | bytes 44 | tf_op jit(solution)/shard_map/ppermute | solution.py:28
  4.2 2.5 %collective-permute-start.1 = (f32[1,3]{1,0:T(1,128)}, f32[1,3]{1,0:T(1,128)S(1)}, u32[]{:S(2)}, u32[]{:S(2)}) collective-permute-start(f32[1,3]{1,0:T(1,128)} %bitcast.210), channel_id=1, source_target_pairs={{0,4},{4,8},{8,12},{12,16},{16,20},{20,24},{24,28},{1,5},{5,9},{9,... | collective-permute-start | bytes 44 | tf_op jit(solution)/shard_map/ppermute | solution.py:28
  6.8 1.9 collective-permute-start
  9.4 0.6 broadcast_9_xlo_ref_xhi_ref.2.xlo_ref.xhi_ref
  10.0 0.6 broadcast_in_dim.121.yadd_ref
  10.7 63.2 %shard_map.172 = (f32[3,64,4096]{2,1,0:T(8,128)}, f32[3,4,4096]{2,1,0:T(4,128)}, f32[3,4,64,128]{3,2,1,0:T(8,128)}) custom-call(f32[3]{0:T(128)} %bitcast.211, f32[3,64,4096]{2,1,0:T(8,128)} %bitcast.198, f32[3,1,4096]{2,1,0:T(1,128)} %broadcast_9_xlo_ref_xhi_ref.2.xlo_ref.xhi_ref, f32[3,1,4096]{2,1,0:T(1,128)} %broadcast_9_xlo_ref_xhi_ref.2.xlo_ref.xhi_ref, ...), custom_call_target="tpu_custom_call" | custom-call | tf_op jit(solution)/shard_map/pallas_call | solution.py:251
  73.9 1.1 slice_bitcast_fusion.6
  75.0 0.6 slice_reduce_fusion.11
  75.5 0.1 squeeze.92
  76.0 1.1 slice_bitcast_fusion.3
  77.2 0.1 reshape.803
  77.4 0.1 reshape.804
  77.6 0.1 reshape_squeeze.27
  77.9 4.8 %collective-permute-start.4 = (f32[1,2,3,4096]{3,1,2,0:T(2,128)S(1)}, f32[1,2,3,4096]{3,1,2,0:T(2,128)S(1)}, u32[]{:S(2)}, u32[]{:S(2)}) collective-permute-start(f32[1,2,3,4096]{3,1,2,0:T(2,128)S(1)} %get-tuple-element.37), channel_id=1, source_target_pairs={{4,0},{8,4},{12,8},{16,12},{20,16},{24,20},{28,24},{5,1},{9,5},{13... | collective-permute-start | bytes 294920 | tf_op jit(solution)/shard_map/ppermute | solution.py:28
  85.4 1.9 collective-permute-start.2
  87.4 0.7 collective-permute-start.8
  88.1 0.3 slice_reduce_fusion.10
  88.4 0.1 reshape_squeeze.28
  88.5 0.1 reshape_squeeze.29
  88.6 3.3 %collective-permute-done.8 = f32[1,2,3,4096]{3,2,1,0:T(4,128)S(1)} collective-permute-done((f32[1,2,3,4096]{3,2,1,0:T(4,128)S(1)}, f32[1,2,3,4096]{3,2,1,0:T(4,128)S(1)}, u32[]{:S(2)}, u32[]{:S(2)}) %collective-permute-start.8) | collective-permute-done | bytes 98336 | tf_op jit(solution)/shard_map/ppermute | solution.py:33
  92.0 0.8 collective-permute-done.2
  92.8 0.3 slice_reduce_fusion.15
  93.1 0.1 squeeze.88
  93.3 0.1 squeeze.89
  93.5 0.1 squeeze.87
  93.8 0.1 squeeze.96
  94.2 0.1 squeeze.94
  94.4 0.1 squeeze.95
  94.5 0.3 fusion.40
  95.0 0.7 reshape_squeeze_reshape.8.xlo_ref
  95.7 0.3 fusion.34
  96.0 0.7 mul.608.xhi_ref
  96.7 0.3 fusion.5
  97.0 0.3 fusion.7
  97.3 0.7 maximum_bitcast_fusion.yadd_ref
  98.1 63.2 %shard_map.173 = (f32[3,64,4096]{2,1,0:T(8,128)}, f32[3,4,4096]{2,1,0:T(4,128)}, f32[3,4,64,128]{3,2,1,0:T(8,128)}) custom-call(f32[3]{0:T(128)} %bitcast.212, f32[3,64,4096]{2,1,0:T(8,128)} %bitcast.199, f32[3,1,4096]{2,1,0:T(1,128)} %reshape_squeeze_reshape.8.xlo_ref, f32[3,1,4096]{2,1,0:T(1,128)} %mul.608.xhi_ref, ...), custom_call_target="tpu_custom_call" | custom-call | tf_op jit(solution)/shard_map/pallas_call | solution.py:251
  161.3 1.1 slice_bitcast_fusion.4
  162.4 3.5 %collective-permute-start.10 = (f32[1,2,3,4096]{3,1,2,0:T(2,128)S(1)}, f32[1,2,3,4096]{3,1,2,0:T(2,128)S(1)}, u32[]{:S(2)}, u32[]{:S(2)}) collective-permute-start(f32[1,2,3,4096]{3,1,2,0:T(2,128)S(1)} %get-tuple-element.35), channel_id=1, source_target_pairs={{4,0},{8,4},{12,8},{16,12},{20,16},{24,20},{28,24},{5,1},{9,5},{13... | collective-permute-start | bytes 294920 | tf_op jit(solution)/shard_map/ppermute | solution.py:28
  165.9 0.3 slice_reduce_fusion.6
  166.2 1.1 slice_bitcast_fusion.1
  167.3 2.3 collective-permute-start.9
  169.6 0.1 reshape_squeeze.30
  169.8 0.1 reshape_squeeze.31
  170.0 0.3 slice_reduce_fusion.3
  170.2 0.1 squeeze.105
  170.7 0.1 reshape.811
  170.9 0.1 reshape.812
  171.3 1.6 collective-permute-start.12
  172.9 2.5 %collective-permute-done.9 = f32[1,2,3,4096]{3,1,2,0:T(2,128)S(1)} collective-permute-done((f32[1,2,3,4096]{3,1,2,0:T(2,128)S(1)}, f32[1,2,3,4096]{3,1,2,0:T(2,128)S(1)}, u32[]{:S(2)}, u32[]{:S(2)}) %collective-permute-start.9) | collective-permute-done | bytes 98336 | tf_op jit(solution)/shard_map/ppermute | solution.py:28
  175.3 0.3 slice_reduce_fusion.7
  175.6 0.1 squeeze.101
  176.1 0.3 slice_reduce_fusion.2
  176.4 0.1 reshape_squeeze.32
  176.9 0.3 fusion.27
  177.2 0.3 fusion.18
  177.7 0.7 reshape_squeeze_reshape.9.xlo_ref
  178.6 0.1 squeeze.109
  179.0 0.1 squeeze.107
  179.3 0.7 add_multiply_fusion.xhi_ref
  180.0 0.3 fusion.11
  180.3 0.3 fusion.9
  180.6 0.7 maximum_bitcast_fusion.1.yadd_ref
  181.3 63.2 %shard_map.174 = (f32[3,64,4096]{2,1,0:T(8,128)}, f32[3,4,4096]{2,1,0:T(4,128)}, f32[3,4,64,128]{3,2,1,0:T(8,128)}) custom-call(f32[3]{0:T(128)} %bitcast.213, f32[3,64,4096]{2,1,0:T(8,128)} %bitcast.200, f32[3,1,4096]{2,1,0:T(1,128)} %reshape_squeeze_reshape.9.xlo_ref, f32[3,1,4096]{2,1,0:T(1,128)} %add_multiply_fusion.xhi_ref, ...), custom_call_target="tpu_custom_call" | custom-call | tf_op jit(solution)/shard_map/pallas_call | solution.py:251
  (80 shorter events, 4.0 us)
Async XLA Ops:
  0.0 85.4 %collective-permute-start.7 = (f32[1,3]{1,0:T(1,128)}, f32[1,3]{1,0:T(1,128)S(1)}, u32[]{:S(2)}, u32[]{:S(2)}) collective-permute-start(f32[1,3]{1,0:T(1,128)} %bitcast.207), channel_id=1, source_target_pairs={{0,3},{1,0},{2,1},{3,2},{4,7},{5,4},{6,5},{7,6},{8,11},{9,8},{10,9... | collective-permute-start | bytes 44 | tf_op jit(solution)/shard_map/ppermute | solution.py:33
  0.9 86.4 %collective-permute-start.5 = (f32[1,3]{1,0:T(1,128)}, f32[1,3]{1,0:T(1,128)S(1)}, u32[]{:S(2)}, u32[]{:S(2)}) collective-permute-start(f32[1,3]{1,0:T(1,128)} %bitcast.208), channel_id=1, source_target_pairs={{0,1},{1,2},{2,3},{3,0},{4,5},{5,6},{6,7},{7,4},{8,9},{9,10},{10,1... | collective-permute-start | bytes 44 | tf_op jit(solution)/shard_map/ppermute | solution.py:33
  0.9 87.1 %collective-permute-start.3 = (f32[1,3]{1,0:T(1,128)}, f32[1,3]{1,0:T(1,128)S(1)}, u32[]{:S(2)}, u32[]{:S(2)}) collective-permute-start(f32[1,3]{1,0:T(1,128)} %bitcast.209), channel_id=1, source_target_pairs={{4,0},{8,4},{12,8},{16,12},{20,16},{24,20},{28,24},{5,1},{9,5},{13... | collective-permute-start | bytes 44 | tf_op jit(solution)/shard_map/ppermute | solution.py:28
  4.2 83.8 %collective-permute-start.1 = (f32[1,3]{1,0:T(1,128)}, f32[1,3]{1,0:T(1,128)S(1)}, u32[]{:S(2)}, u32[]{:S(2)}) collective-permute-start(f32[1,3]{1,0:T(1,128)} %bitcast.210), channel_id=1, source_target_pairs={{0,4},{4,8},{8,12},{12,16},{16,20},{20,24},{24,28},{1,5},{5,9},{9,... | collective-permute-start | bytes 44 | tf_op jit(solution)/shard_map/ppermute | solution.py:28
  6.8 71.1 %collective-permute-start = (s32[1]{0:T(128)}, s32[1]{0:T(128)}, u32[]{:S(2)}, u32[]{:S(2)}) collective-permute-start(s32[1]{0:T(128)} %bitcast.2), channel_id=1, source_target_pairs={{0,4},{4,8},{8,12},{12,16},{16,20},{20,24},{24,28},{1,5},{5,9},{9,... | collective-permute-start | bytes 20 | tf_op jit(solution)/shard_map/ppermute | solution.py:28
  73.9 14.2 %copy-start.1 = (f32[1,1,3]{2,1,0:T(1,128)S(1)}, f32[1,1,3]{2,1,0:T(1,128)}, u32[]{:S(2)}) copy-start(f32[1,1,3]{2,1,0:T(1,128)} %param.19) | copy-start | bytes 40
  77.9 10.2 %collective-permute-start.4 = (f32[1,2,3,4096]{3,1,2,0:T(2,128)S(1)}, f32[1,2,3,4096]{3,1,2,0:T(2,128)S(1)}, u32[]{:S(2)}, u32[]{:S(2)}) collective-permute-start(f32[1,2,3,4096]{3,1,2,0:T(2,128)S(1)} %get-tuple-element.37), channel_id=1, source_target_pairs={{4,0},{8,4},{12,8},{16,12},{20,16},{24,20},{28,24},{5,1},{9,5},{13... | collective-permute-start | bytes 294920 | tf_op jit(solution)/shard_map/ppermute | solution.py:28
  85.4 7.4 %collective-permute-start.2 = (f32[1,2,3,4096]{3,1,2,0:T(2,128)S(1)}, f32[1,2,3,4096]{3,1,2,0:T(2,128)S(1)}, u32[]{:S(2)}, u32[]{:S(2)}) collective-permute-start(f32[1,2,3,4096]{3,1,2,0:T(2,128)S(1)} %get-tuple-element.38), channel_id=1, source_target_pairs={{0,4},{4,8},{8,12},{12,16},{16,20},{20,24},{24,28},{1,5},{5,9},{9,... | collective-permute-start | bytes 294920 | tf_op jit(solution)/shard_map/ppermute | solution.py:28
  87.4 4.5 %collective-permute-start.8 = (f32[1,2,3,4096]{3,2,1,0:T(4,128)S(1)}, f32[1,2,3,4096]{3,2,1,0:T(4,128)S(1)}, u32[]{:S(2)}, u32[]{:S(2)}) collective-permute-start(f32[1,2,3,4096]{3,2,1,0:T(4,128)S(1)} %copy.37), channel_id=1, source_target_pairs={{0,3},{1,0},{2,1},{3,2},{4,7},{5,4},{6,5},{7,6},{8,11},{9,8},{10,9... | collective-permute-start | bytes 294920 | tf_op jit(solution)/shard_map/ppermute | solution.py:33
  88.0 6.1 %collective-permute-start.6 = (f32[1,2,3,4096]{3,2,1,0:T(4,128)S(1)}, f32[1,2,3,4096]{3,2,1,0:T(4,128)S(1)}, u32[]{:S(2)}, u32[]{:S(2)}) collective-permute-start(f32[1,2,3,4096]{3,2,1,0:T(4,128)S(1)} %copy.36), channel_id=1, source_target_pairs={{0,1},{1,2},{2,3},{3,0},{4,5},{5,6},{6,7},{7,4},{8,9},{9,10},{10,1... | collective-permute-start | bytes 294920 | tf_op jit(solution)/shard_map/ppermute | solution.py:33
  162.4 13.7 %collective-permute-start.10 = (f32[1,2,3,4096]{3,1,2,0:T(2,128)S(1)}, f32[1,2,3,4096]{3,1,2,0:T(2,128)S(1)}, u32[]{:S(2)}, u32[]{:S(2)}) collective-permute-start(f32[1,2,3,4096]{3,1,2,0:T(2,128)S(1)} %get-tuple-element.35), channel_id=1, source_target_pairs={{4,0},{8,4},{12,8},{16,12},{20,16},{24,20},{28,24},{5,1},{9,5},{13... | collective-permute-start | bytes 294920 | tf_op jit(solution)/shard_map/ppermute | solution.py:28
  167.3 8.0 %collective-permute-start.9 = (f32[1,2,3,4096]{3,1,2,0:T(2,128)S(1)}, f32[1,2,3,4096]{3,1,2,0:T(2,128)S(1)}, u32[]{:S(2)}, u32[]{:S(2)}) collective-permute-start(f32[1,2,3,4096]{3,1,2,0:T(2,128)S(1)} %get-tuple-element.36), channel_id=1, source_target_pairs={{0,4},{4,8},{8,12},{12,16},{16,20},{20,24},{24,28},{1,5},{5,9},{9,... | collective-permute-start | bytes 294920 | tf_op jit(solution)/shard_map/ppermute | solution.py:28
  169.8 7.1 %copy-start.2 = (f32[1,1,3]{2,1,0:T(1,128)S(1)}, f32[1,1,3]{2,1,0:T(1,128)}, u32[]{:S(2)}) copy-start(f32[1,1,3]{2,1,0:T(1,128)} %param.19) | copy-start | bytes 40
  171.3 6.3 %collective-permute-start.12 = (f32[1,2,3,4096]{3,2,1,0:T(4,128)S(1)}, f32[1,2,3,4096]{3,2,1,0:T(4,128)S(1)}, u32[]{:S(2)}, u32[]{:S(2)}) collective-permute-start(f32[1,2,3,4096]{3,2,1,0:T(4,128)S(1)} %copy.47), channel_id=1, source_target_pairs={{0,3},{1,0},{2,1},{3,2},{4,7},{5,4},{6,5},{7,6},{8,11},{9,8},{10,9... | collective-permute-start | bytes 294920 | tf_op jit(solution)/shard_map/ppermute | solution.py:33
  172.9 6.1 %collective-permute-start.11 = (f32[1,2,3,4096]{3,2,1,0:T(4,128)S(1)}, f32[1,2,3,4096]{3,2,1,0:T(4,128)S(1)}, u32[]{:S(2)}, u32[]{:S(2)}) collective-permute-start(f32[1,2,3,4096]{3,2,1,0:T(4,128)S(1)} %copy.46), channel_id=1, source_target_pairs={{0,1},{1,2},{2,3},{3,0},{4,5},{5,6},{6,7},{7,4},{8,9},{9,10},{10,1... | collective-permute-start | bytes 294920 | tf_op jit(solution)/shard_map/ppermute | solution.py:33
  176.7 2.6 %copy-start = (f32[3,1,4096]{2,1,0:T(1,128)S(1)}, f32[3,1,4096]{2,1,0:T(1,128)}, u32[]{:S(2)}) copy-start(f32[3,1,4096]{2,1,0:T(1,128)} %mul.608.xhi_ref) | copy-start | bytes 147460

commit v4 on v1

--- a/solution.py
+++ b/solution.py
@@ -128,12 +128,12 @@
 
 def stack_right(w):
     w1, w2, w3 = np_split3(w)
-    return np.concatenate([w1, w2, w3, w1, w2, w1], 0)
+    return np.concatenate([w1, w2, w1, w1], 0)
 
 
 def stack_left(w):
     w1, w2, w3 = np_split3(w)
-    return np.concatenate([w1, w2, w3, w1, w2, w1], 1)
+    return np.concatenate([w1, w2, w1, w1], 1)
 
 
 def split3(d):
@@ -146,12 +146,12 @@
 
 def sdot(d, w6):
     d1, d2, d3 = split3(d)
-    return jnp.dot(jnp.concatenate([d1, d1, d1, d2, d2, d3], 1), w6, preferred_element_type=f32)
+    return jnp.dot(jnp.concatenate([d1, d1, d2, d3], 1), w6, preferred_element_type=f32)
 
 
 def sdot_left(w6, d):
     d1, d2, d3 = split3(d)
-    return jnp.dot(w6, jnp.concatenate([d1, d1, d1, d2, d2, d3], 0), preferred_element_type=f32)
+    return jnp.dot(w6, jnp.concatenate([d1, d1, d2, d3], 0), preferred_element_type=f32)
 
 
 def solve_kernel(*refs, with_faces, emit_u, emit_sides):

time: 142 us -> 121 us (0.85)
  Pallas kernels: 90 us -> 69.2 us
    pallas_call x3, Pallas kernels: 90 us -> 69.2 us  [kernel_sweep(): pl.pallas_call(kernel, grid=(ncomp,), in_specs=in_specs, out_specs=out_sp...]
  transfers between devices with their start and end apart: 14 -> 14, of which waited for: 5 -> 5; matrix products, arithmetic and copies ran while one was open for 9% -> 10% of each run, Pallas kernels for 21% -> 19%
where the time goes in v4:
time: 121 us; the launch traced here: 120 us
  Pallas kernels  69.2 us (57%)
  starting transfers between devices  23.6 us (20%)
  local copies, waits for them, and re-layouts  11.3 us (9%)
  waiting for transfers between devices  10.3 us (9%)
  other arithmetic  3.02 us (2%)
  matrix products  1.21 us (1%)
    pallas_call x3, Pallas kernels, kernel_sweep(): pl.pallas_call(kernel, grid=(ncomp,), in_specs=in_specs, out_specs=out_sp...  69.2 us
    ppermute x7, starting transfers between devices, shifted(): return lax.ppermute(shard, axis, pairs)  19.2 us
    ppermute x7, waiting for transfers between devices, shifted(): return lax.ppermute(shard, axis, pairs)  8.79 us
    ppermute x7, starting transfers between devices, shifted_2(): lax.ppermute(shard, axis, [(i, (i + by) % length) for i in range(length)])  4.44 us
    squeeze x2, local copies, waits for them, and re-layouts, shards(): x_low_side = (xf[:, :, 2], xf[:, :, 3])  3.26 us
  transfers between devices with their start and end apart: 14, of which 5 were waited for; matrix products, arithmetic and copies ran while one was open for 10% of the time, Pallas kernels for 19%

profile of v4, /device:TPU:24, one launch (start us, length us, event | category | flops | bytes accessed | tf_op | source)
XLA Modules:
  0.0 119.8 jit_solution(15218318969957159957)
XLA Ops:
  0.0 3.3 %collective-permute-start = (f32[1,3]{1,0:T(1,128)}, f32[1,3]{1,0:T(1,128)S(1)}, u32[]{:S(2)}, u32[]{:S(2)}) collective-permute-start(f32[1,3]{1,0:T(1,128)} %bitcast.132), channel_id=1, source_target_pairs={{4,0},{8,4},{12,8},{16,12},{20,16},{24,20},{28,24},{5,1},{9,5},{13... | collective-permute-start | bytes 44 | tf_op jit(solution)/shard_map/ppermute | solution.py:28
  3.3 0.7 collective-permute-start.4
  4.0 23.0 %shard_map.172 = (f32[3,4,4096]{2,1,0:T(4,128)}, f32[3,4,64,128]{3,2,1,0:T(8,128)}) custom-call(f32[3]{0:T(128)} %bitcast.134, f32[3,64,4096]{2,1,0:T(8,128)} %bitcast.122, bf16[64,256]{1,0:T(8,128)(2,1)} %constant.96.clone.refs_2_.refs_5_, bf16[1024,256]{1,0:T(8,128)(2,1)} %constant.97.clone.refs_3_.refs_6_, ...), custom_call_target="tpu_custom_call" | custom-call | tf_op jit(solution)/shard_map/pallas_call | solution.py:266
  27.0 1.6 %slice_bitcast_fusion.3 = (f32[1,3,4096]{2,0,1:T(1,128)S(1)}, f32[1,3,4096]{2,0,1:T(1,128)S(1)}, f32[3,4096]{1,0:T(4,128)S(1)}, f32[3,4096]{1,0:T(4,128)S(1)}) fusion(f32[1,3,4,4096]{3,2,1,0:T(4,128)} %bitcast.129), kind=kLoop, calls=%fused_computation.58 | loop fusion | bytes 393216 | tf_op jit(solution)/shard_map/squeeze | solution.py:364
  28.7 2.4 %collective-permute-start.1 = (f32[1,3,4096]{2,0,1:T(1,128)S(1)}, f32[1,3,4096]{2,0,1:T(1,128)S(1)}, u32[]{:S(2)}, u32[]{:S(2)}) collective-permute-start(f32[1,3,4096]{2,0,1:T(1,128)S(1)} %get-tuple-element.31), channel_id=1, source_target_pairs={{4,0},{8,4},{12,8},{16,12},{20,16},{24,20},{28,24},{5,1},{9,5},{13... | collective-permute-start | bytes 147464 | tf_op jit(solution)/shard_map/ppermute | solution.py:28
  31.1 3.3 %collective-permute-start.2 = (f32[1,3,4096]{2,0,1:T(1,128)S(1)}, f32[1,3,4096]{2,0,1:T(1,128)S(1)}, u32[]{:S(2)}, u32[]{:S(2)}) collective-permute-start(f32[1,3,4096]{2,0,1:T(1,128)S(1)} %get-tuple-element.32), channel_id=1, source_target_pairs={{4,0},{8,4},{12,8},{16,12},{20,16},{24,20},{28,24},{5,1},{9,5},{13... | collective-permute-start | bytes 147464 | tf_op jit(solution)/shard_map/ppermute | solution.py:28
  34.4 1.2 fusion.96
  35.6 0.1 squeeze_reshape_squeeze.12
  35.7 0.4 collective-permute-start.5
  36.8 0.1 squeeze.53
  36.9 0.1 squeeze.50
  37.0 0.1 squeeze.52
  37.2 0.1 squeeze.47
  37.3 0.1 reshape_squeeze.21
  37.4 0.1 squeeze_reshape_squeeze.13
  37.6 0.7 collective-permute-start.6
  38.3 0.1 reduce.1
  38.4 0.1 reshape.353
  38.6 0.1 reduce.3
  38.7 0.1 reshape.355
  38.8 1.4 %collective-permute-done.6 = f32[3,4096]{1,0:T(4,128)S(1)} collective-permute-done((f32[3,4096]{1,0:T(4,128)S(1)}, f32[3,4096]{1,0:T(4,128)S(1)}, u32[]{:S(2)}, u32[]{:S(2)}) %collective-permute-start.6) | collective-permute-done | bytes 49184 | tf_op jit(solution)/shard_map/ppermute | solution.py:33
  40.3 0.1 reshape.359
  40.4 0.3 fusion.3
  40.7 0.1 mul.288
  40.8 1.4 %collective-permute-start.7 = (f32[3,4096]{1,0:T(4,128)S(1)}, f32[3,4096]{1,0:T(4,128)S(1)}, u32[]{:S(2)}, u32[]{:S(2)}) collective-permute-start(f32[3,4096]{1,0:T(4,128)S(1)} %mul.288), channel_id=1, source_target_pairs={{0,1},{1,2},{2,3},{3,0},{4,5},{5,6},{6,7},{7,4},{8,9},{9,10},{10,1... | collective-permute-start | bytes 147464 | tf_op jit(solution)/shard_map/ppermute | solution.py:33
  42.4 0.3 fusion.16
  42.9 0.7 mul.311.refs_3_
  43.6 0.1 reshape.368
  43.7 2.5 %collective-permute-start.3 = (f32[1,3,4096]{2,0,1:T(1,128)S(1)}, f32[1,3,4096]{2,0,1:T(1,128)S(1)}, u32[]{:S(2)}, u32[]{:S(2)}) collective-permute-start(f32[1,3,4096]{2,0,1:T(1,128)S(1)} %reshape.368), channel_id=1, source_target_pairs={{0,4},{4,8},{8,12},{12,16},{16,20},{20,24},{24,28},{1,5},{5,9},{9,... | collective-permute-start | bytes 147464 | tf_op jit(solution)/shard_map/ppermute | solution.py:28
  46.3 0.1 reshape_broadcast_in_dim.6
  46.4 0.7 maximum_bitcast_fusion.refs_4_
  47.1 3.5 %collective-permute-done.3 = f32[1,3,4096]{2,0,1:T(1,128)S(1)} collective-permute-done((f32[1,3,4096]{2,0,1:T(1,128)S(1)}, f32[1,3,4096]{2,0,1:T(1,128)S(1)}, u32[]{:S(2)}, u32[]{:S(2)}) %collective-permute-start.3) | collective-permute-done | bytes 49184 | tf_op jit(solution)/shard_map/ppermute | solution.py:28
  50.6 0.6 copy-done.2
  51.3 23.1 %shard_map.173 = (f32[3,4,4096]{2,1,0:T(4,128)}, f32[3,4,64,128]{3,2,1,0:T(8,128)}) custom-call(f32[3]{0:T(128)} %bitcast.135, f32[3,64,4096]{2,1,0:T(8,128)} %bitcast.123, f32[3,1,4096]{2,1,0:T(1,128)} %bitcast.131, f32[3,1,4096]{2,1,0:T(1,128)} %mul.311.refs_3_, f32[3,64,128]{2,1,0:T(8,128)} %maximum_bitcast_fusion.refs_4_, ...), custom_call_target="tpu_custom_call" | custom-call | tf_op jit(solution)/shard_map/pallas_call | solution.py:266
  74.3 1.1 fusion.95
  75.5 0.1 squeeze_reshape_squeeze.15
  75.6 0.1 squeeze_reshape_squeeze.14
  75.8 1.0 collective-permute-start.12
  76.7 1.6 %slice_bitcast_fusion.1 = (f32[1,3,4096]{2,0,1:T(1,128)S(1)}, f32[1,3,4096]{2,0,1:T(1,128)S(1)}, f32[3,4096]{1,0:T(4,128)S(1)}, f32[3,4096]{1,0:T(4,128)S(1)}) fusion(f32[1,3,4,4096]{3,2,1,0:T(4,128)} %bitcast.128), kind=kLoop, calls=%fused_computation.54 | loop fusion | bytes 393216 | tf_op jit(solution)/shard_map/squeeze | solution.py:364
  78.4 0.1 squeeze.60
  78.5 0.1 squeeze.57
  78.6 0.1 squeeze.59
  78.7 0.1 squeeze.55
  78.9 1.9 %collective-permute-start.8 = (f32[1,3,4096]{2,0,1:T(1,128)S(1)}, f32[1,3,4096]{2,0,1:T(1,128)S(1)}, u32[]{:S(2)}, u32[]{:S(2)}) collective-permute-start(f32[1,3,4096]{2,0,1:T(1,128)S(1)} %get-tuple-element.27), channel_id=1, source_target_pairs={{4,0},{8,4},{12,8},{16,12},{20,16},{24,20},{28,24},{5,1},{9,5},{13... | collective-permute-start | bytes 147464 | tf_op jit(solution)/shard_map/ppermute | solution.py:28
  80.9 3.8 %collective-permute-start.9 = (f32[1,3,4096]{2,0,1:T(1,128)S(1)}, f32[1,3,4096]{2,0,1:T(1,128)S(1)}, u32[]{:S(2)}, u32[]{:S(2)}) collective-permute-start(f32[1,3,4096]{2,0,1:T(1,128)S(1)} %get-tuple-element.28), channel_id=1, source_target_pairs={{4,0},{8,4},{12,8},{16,12},{20,16},{24,20},{28,24},{5,1},{9,5},{13... | collective-permute-start | bytes 147464 | tf_op jit(solution)/shard_map/ppermute | solution.py:28
  84.8 0.1 divide_subtract_fusion
  84.9 0.1 reshape.366
  85.0 0.3 fusion.1
  85.5 0.1 reduce.7
  85.6 0.1 reshape.360
  85.7 1.1 collective-permute-done.9
  86.9 0.1 reduce.9
  87.0 0.1 reshape.362
  87.1 0.2 collective-permute-start.13
  87.6 0.3 fusion.97
  88.0 0.1 mul.310
  88.1 0.7 add_multiply_fusion.refs_3_
  88.9 0.1 reshape.369
  89.0 1.9 %collective-permute-start.10 = (f32[1,3,4096]{2,0,1:T(1,128)S(1)}, f32[1,3,4096]{2,0,1:T(1,128)S(1)}, u32[]{:S(2)}, u32[]{:S(2)}) collective-permute-start(f32[1,3,4096]{2,0,1:T(1,128)S(1)} %reshape.369), channel_id=1, source_target_pairs={{0,4},{4,8},{8,12},{12,16},{16,20},{20,24},{24,28},{1,5},{5,9},{9,... | collective-permute-start | bytes 147464 | tf_op jit(solution)/shard_map/ppermute | solution.py:28
  91.1 0.1 reshape_broadcast_in_dim.7
  91.2 0.7 maximum_bitcast_fusion.1.refs_4_
  91.9 4.2 %collective-permute-done.10 = f32[1,3,4096]{2,0,1:T(1,128)S(1)} collective-permute-done((f32[1,3,4096]{2,0,1:T(1,128)S(1)}, f32[1,3,4096]{2,0,1:T(1,128)S(1)}, u32[]{:S(2)}, u32[]{:S(2)}) %collective-permute-start.10) | collective-permute-done | bytes 49184 | tf_op jit(solution)/shard_map/ppermute | solution.py:28
  96.1 0.6 copy-done.1
  96.7 23.1 %shard_map.174 = f32[3,64,4096]{2,1,0:T(8,128)} custom-call(f32[3]{0:T(128)} %bitcast.136, f32[3,64,4096]{2,1,0:T(8,128)} %bitcast.124, f32[3,1,4096]{2,1,0:T(1,128)} %bitcast.130, f32[3,1,4096]{2,1,0:T(1,128)} %add_multiply_fusion.refs_3_, f32[3,64,128]{2,1,0:T(8,128)} %maximum_bitcast_fusion.1.refs_4_, bf16[64,256]{1,0:T(8,128)(2,1)} %constant.96.clone.refs_2_.refs_5_, ...), custom_call_target="tpu_custom_call" | custom-call | tf_op jit(solution)/shard_map/pallas_call | solution.py:266
  (48 shorter events, 1.4 us)
Async XLA Ops:
  0.0 37.6 %collective-permute-start = (f32[1,3]{1,0:T(1,128)}, f32[1,3]{1,0:T(1,128)S(1)}, u32[]{:S(2)}, u32[]{:S(2)}) collective-permute-start(f32[1,3]{1,0:T(1,128)} %bitcast.132), channel_id=1, source_target_pairs={{4,0},{8,4},{12,8},{16,12},{20,16},{24,20},{28,24},{5,1},{9,5},{13... | collective-permute-start | bytes 44 | tf_op jit(solution)/shard_map/ppermute | solution.py:28
  3.3 35.0 %collective-permute-start.4 = (f32[3]{0:T(128)}, f32[3]{0:T(128)S(1)}, u32[]{:S(2)}, u32[]{:S(2)}) collective-permute-start(f32[3]{0:T(128)} %bitcast.133), channel_id=1, source_target_pairs={{0,3},{1,0},{2,1},{3,2},{4,7},{5,4},{6,5},{7,6},{8,11},{9,8},{10,9... | collective-permute-start | bytes 44 | tf_op jit(solution)/shard_map/ppermute | solution.py:33
  4.0 34.3 %copy-start.3 = (f32[1,1,3]{2,1,0:T(1,128)S(1)}, f32[1,1,3]{2,1,0:T(1,128)}, u32[]{:S(2)}) copy-start(f32[1,1,3]{2,1,0:T(1,128)} %param.19) | copy-start | bytes 40
  28.7 9.6 %collective-permute-start.1 = (f32[1,3,4096]{2,0,1:T(1,128)S(1)}, f32[1,3,4096]{2,0,1:T(1,128)S(1)}, u32[]{:S(2)}, u32[]{:S(2)}) collective-permute-start(f32[1,3,4096]{2,0,1:T(1,128)S(1)} %get-tuple-element.31), channel_id=1, source_target_pairs={{4,0},{8,4},{12,8},{16,12},{20,16},{24,20},{28,24},{5,1},{9,5},{13... | collective-permute-start | bytes 147464 | tf_op jit(solution)/shard_map/ppermute | solution.py:28
  31.1 7.5 %collective-permute-start.2 = (f32[1,3,4096]{2,0,1:T(1,128)S(1)}, f32[1,3,4096]{2,0,1:T(1,128)S(1)}, u32[]{:S(2)}, u32[]{:S(2)}) collective-permute-start(f32[1,3,4096]{2,0,1:T(1,128)S(1)} %get-tuple-element.32), channel_id=1, source_target_pairs={{4,0},{8,4},{12,8},{16,12},{20,16},{24,20},{28,24},{5,1},{9,5},{13... | collective-permute-start | bytes 147464 | tf_op jit(solution)/shard_map/ppermute | solution.py:28
  35.7 3.1 %collective-permute-start.5 = (f32[3,4096]{1,0:T(4,128)S(1)}, f32[3,4096]{1,0:T(4,128)S(1)}, u32[]{:S(2)}, u32[]{:S(2)}) collective-permute-start(f32[3,4096]{1,0:T(4,128)S(1)} %squeeze_reshape_squeeze.12), channel_id=1, source_target_pairs={{0,3},{1,0},{2,1},{3,2},{4,7},{5,4},{6,5},{7,6},{8,11},{9,8},{10,9... | collective-permute-start | bytes 147464 | tf_op jit(solution)/shard_map/ppermute | solution.py:33
  37.6 2.6 %collective-permute-start.6 = (f32[3,4096]{1,0:T(4,128)S(1)}, f32[3,4096]{1,0:T(4,128)S(1)}, u32[]{:S(2)}, u32[]{:S(2)}) collective-permute-start(f32[3,4096]{1,0:T(4,128)S(1)} %squeeze_reshape_squeeze.13), channel_id=1, source_target_pairs={{0,3},{1,0},{2,1},{3,2},{4,7},{5,4},{6,5},{7,6},{8,11},{9,8},{10,9... | collective-permute-start | bytes 147464 | tf_op jit(solution)/shard_map/ppermute | solution.py:33
  40.8 5.5 %collective-permute-start.7 = (f32[3,4096]{1,0:T(4,128)S(1)}, f32[3,4096]{1,0:T(4,128)S(1)}, u32[]{:S(2)}, u32[]{:S(2)}) collective-permute-start(f32[3,4096]{1,0:T(4,128)S(1)} %mul.288), channel_id=1, source_target_pairs={{0,1},{1,2},{2,3},{3,0},{4,5},{5,6},{6,7},{7,4},{8,9},{9,10},{10,1... | collective-permute-start | bytes 147464 | tf_op jit(solution)/shard_map/ppermute | solution.py:33
  43.7 6.9 %collective-permute-start.3 = (f32[1,3,4096]{2,0,1:T(1,128)S(1)}, f32[1,3,4096]{2,0,1:T(1,128)S(1)}, u32[]{:S(2)}, u32[]{:S(2)}) collective-permute-start(f32[1,3,4096]{2,0,1:T(1,128)S(1)} %reshape.368), channel_id=1, source_target_pairs={{0,4},{4,8},{8,12},{12,16},{16,20},{20,24},{24,28},{1,5},{5,9},{9,... | collective-permute-start | bytes 147464 | tf_op jit(solution)/shard_map/ppermute | solution.py:28
  50.6 0.6 copy-start.2
  51.2 33.6 %copy-start.4 = (f32[1,1,3]{2,1,0:T(1,128)S(1)}, f32[1,1,3]{2,1,0:T(1,128)}, u32[]{:S(2)}) copy-start(f32[1,1,3]{2,1,0:T(1,128)} %param.19) | copy-start | bytes 40
  75.7 9.1 %collective-permute-start.11 = (f32[3,4096]{1,0:T(4,128)S(1)}, f32[3,4096]{1,0:T(4,128)S(1)}, u32[]{:S(2)}, u32[]{:S(2)}) collective-permute-start(f32[3,4096]{1,0:T(4,128)S(1)} %squeeze_reshape_squeeze.14), channel_id=1, source_target_pairs={{0,3},{1,0},{2,1},{3,2},{4,7},{5,4},{6,5},{7,6},{8,11},{9,8},{10,9... | collective-permute-start | bytes 147464 | tf_op jit(solution)/shard_map/ppermute | solution.py:33
  75.8 9.0 %collective-permute-start.12 = (f32[3,4096]{1,0:T(4,128)S(1)}, f32[3,4096]{1,0:T(4,128)S(1)}, u32[]{:S(2)}, u32[]{:S(2)}) collective-permute-start(f32[3,4096]{1,0:T(4,128)S(1)} %squeeze_reshape_squeeze.15), channel_id=1, source_target_pairs={{0,3},{1,0},{2,1},{3,2},{4,7},{5,4},{6,5},{7,6},{8,11},{9,8},{10,9... | collective-permute-start | bytes 147464 | tf_op jit(solution)/shard_map/ppermute | solution.py:33
  76.7 11.4 %copy-start = (f32[3,1,4096]{2,1,0:T(1,128)S(1)}, f32[3,1,4096]{2,1,0:T(1,128)}, u32[]{:S(2)}) copy-start(f32[3,1,4096]{2,1,0:T(1,128)} %mul.311.refs_3_) | copy-start | bytes 147460
  78.9 6.5 %collective-permute-start.8 = (f32[1,3,4096]{2,0,1:T(1,128)S(1)}, f32[1,3,4096]{2,0,1:T(1,128)S(1)}, u32[]{:S(2)}, u32[]{:S(2)}) collective-permute-start(f32[1,3,4096]{2,0,1:T(1,128)S(1)} %get-tuple-element.27), channel_id=1, source_target_pairs={{4,0},{8,4},{12,8},{16,12},{20,16},{24,20},{28,24},{5,1},{9,5},{13... | collective-permute-start | bytes 147464 | tf_op jit(solution)/shard_map/ppermute | solution.py:28
  80.9 6.0 %collective-permute-start.9 = (f32[1,3,4096]{2,0,1:T(1,128)S(1)}, f32[1,3,4096]{2,0,1:T(1,128)S(1)}, u32[]{:S(2)}, u32[]{:S(2)}) collective-permute-start(f32[1,3,4096]{2,0,1:T(1,128)S(1)} %get-tuple-element.28), channel_id=1, source_target_pairs={{4,0},{8,4},{12,8},{16,12},{20,16},{24,20},{28,24},{5,1},{9,5},{13... | collective-permute-start | bytes 147464 | tf_op jit(solution)/shard_map/ppermute | solution.py:28
  87.1 3.9 %collective-permute-start.13 = (f32[3,4096]{1,0:T(4,128)S(1)}, f32[3,4096]{1,0:T(4,128)S(1)}, u32[]{:S(2)}, u32[]{:S(2)}) collective-permute-start(f32[3,4096]{1,0:T(4,128)S(1)} %add.180), channel_id=1, source_target_pairs={{0,1},{1,2},{2,3},{3,0},{4,5},{5,6},{6,7},{7,4},{8,9},{9,10},{10,1... | collective-permute-start | bytes 147464 | tf_op jit(solution)/shard_map/ppermute | solution.py:33
  89.0 7.1 %collective-permute-start.10 = (f32[1,3,4096]{2,0,1:T(1,128)S(1)}, f32[1,3,4096]{2,0,1:T(1,128)S(1)}, u32[]{:S(2)}, u32[]{:S(2)}) collective-permute-start(f32[1,3,4096]{2,0,1:T(1,128)S(1)} %reshape.369), channel_id=1, source_target_pairs={{0,4},{4,8},{8,12},{12,16},{16,20},{20,24},{24,28},{1,5},{5,9},{9,... | collective-permute-start | bytes 147464 | tf_op jit(solution)/shard_map/ppermute | solution.py:28
  96.1 0.6 copy-start.1

commit v5 on v2

--- a/solution.py
+++ b/solution.py
@@ -128,12 +128,12 @@
 
 def stack_right(w):
     w1, w2, w3 = np_split3(w)
-    return np.concatenate([w1, w2, w3, w1, w2, w1], 0)
+    return np.concatenate([w1, w2, w1, w1], 0)
 
 
 def stack_left(w):
     w1, w2, w3 = np_split3(w)
-    return np.concatenate([w1, w2, w3, w1, w2, w1], 1)
+    return np.concatenate([w1, w2, w1, w1], 1)
 
 
 def split3(d):
@@ -146,12 +146,12 @@
 
 def sdot(d, w6):
     d1, d2, d3 = split3(d)
-    return jnp.dot(jnp.concatenate([d1, d1, d1, d2, d2, d3], 1), w6, preferred_element_type=f32)
+    return jnp.dot(jnp.concatenate([d1, d1, d2, d3], 1), w6, preferred_element_type=f32)
 
 
 def sdot_left(w6, d):
     d1, d2, d3 = split3(d)
-    return jnp.dot(w6, jnp.concatenate([d1, d1, d1, d2, d2, d3], 0), preferred_element_type=f32)
+    return jnp.dot(w6, jnp.concatenate([d1, d1, d2, d3], 0), preferred_element_type=f32)
 
 
 def solve_kernel(*refs, with_faces, emit_u, emit_sides):
@@ -359,10 +359,8 @@
     slab_index = lax.axis_index("blk")
     has_up = (slab_index < slab_count - 1).astype(jnp.float32)
     has_down = (slab_index > 0).astype(jnp.float32)
-    moduli_up = shifted(moduli, "blk", -1)
-    moduli_down, codes_down = shifted((moduli, codes_here), "blk", 1)
-    moduli_next = jnp.concatenate([moduli[1:], shifted_2(moduli[:1], "face", -1)], 0)
-    moduli_prev = jnp.concatenate([shifted_2(moduli[-1:], "face", 1), moduli[:-1]], 0)
+    moduli_rows = jnp.broadcast_to(moduli[:, None, :, None], (blocks, 1, 3, flat))
+    codes_rows = jnp.broadcast_to(codes_here.astype(jnp.float32)[:, None, None, None], (blocks, 1, 3, flat))
     face_zeros = jnp.zeros((blocks, 3, flat), jnp.float32)
     lam_x_up = face_zeros
     lam_x_down = face_zeros
@@ -383,10 +381,22 @@
         x_low_side = xf[:, :, 2:4].transpose(0, 2, 1, 3)
         y_high_side = yf[:, :, 0:2, :, extent:].transpose(0, 2, 1, 3, 4).reshape(blocks, 2, 3, flat)
         y_low_side = yf[:, :, 2:4, :, :extent].transpose(0, 2, 1, 3, 4).reshape(blocks, 2, 3, flat)
+        first = sweep == 0
+        if first:
+            x_low_side = jnp.concatenate([x_low_side, moduli_rows], 1)
+            x_high_side = jnp.concatenate([x_high_side, moduli_rows, codes_rows], 1)
+            y_low_side = jnp.concatenate([y_low_side, moduli_rows], 1)
+            y_high_side = jnp.concatenate([y_high_side, moduli_rows], 1)
         upper_side = shifted(x_low_side, "blk", -1)
         lower_side = shifted(x_high_side, "blk", 1)
         next_side = jnp.concatenate([y_low_side[1:], shifted_2(y_low_side[:1], "face", -1)], 0)
         prev_side = jnp.concatenate([shifted_2(y_high_side[-1:], "face", 1), y_high_side[:-1]], 0)
+        if first:
+            moduli_up = upper_side[:, 2, :, 0]
+            moduli_down = lower_side[:, 2, :, 0]
+            codes_down = lower_side[:, 3, 0, 0].astype(jnp.int32)
+            moduli_next = next_side[:, 2, :, 0]
+            moduli_prev = prev_side[:, 2, :, 0]
         lam_x_up = (
             trace_update(
                 lam_x_up,

time: 145 us -> 115 us (0.79)
  Pallas kernels: 90 us -> 69.2 us
  starting transfers between devices: 23.4 us -> 15.6 us
  between operations: 3.76 us -> 1.92 us
  waiting for transfers between devices: 6.79 us -> 5.09 us
    pallas_call x3, Pallas kernels: 90 us -> 69.2 us  [kernel_sweep(): pl.pallas_call(kernel, grid=(ncomp,), in_specs=in_specs, out_specs=out_sp...]
    ppermute x7 -> x4, starting transfers between devices: 20.3 us -> 12.2 us  [shifted(): return lax.ppermute(shard, axis, pairs)]
    ppermute x7 -> x4, waiting for transfers between devices: 3.63 us -> 2.58 us  [shifted(): return lax.ppermute(shard, axis, pairs)]
    ppermute x6 -> x4, waiting for transfers between devices: 3.16 us -> 2.5 us  [shifted_2(): lax.ppermute(shard, axis, [(i, (i + by) % length) for i in range(length)])]
    ppermute x6 -> x4, starting transfers between devices: 3.05 us -> 3.47 us  [shifted_2(): lax.ppermute(shard, axis, [(i, (i + by) % length) for i in range(length)])]
  transfers between devices with their start and end apart: 13 -> 8, of which waited for: 3 -> 3; matrix products, arithmetic and copies ran while one was open for 9% -> 10% of each run, Pallas kernels for 21% -> 0%
where the time goes in v5:
time: 115 us; the launch traced here: 113 us
  Pallas kernels  69.2 us (60%)
  local copies, waits for them, and re-layouts  15.9 us (14%)
  starting transfers between devices  15.6 us (14%)
  waiting for transfers between devices  5.09 us (4%)
  other arithmetic  2.78 us (2%)
  matrix products  2.4 us (2%)
  between operations  1.92 us (2%)
    pallas_call x3, Pallas kernels, kernel_sweep(): pl.pallas_call(kernel, grid=(ncomp,), in_specs=in_specs, out_specs=out_sp...  69.2 us
    ppermute x4, starting transfers between devices, shifted(): return lax.ppermute(shard, axis, pairs)  12.2 us
    ppermute x4, starting transfers between devices, shifted_2(): lax.ppermute(shard, axis, [(i, (i + by) % length) for i in range(length)])  3.47 us
    squeeze x24, local copies, waits for them, and re-layouts, unpack_side(): return (packed[:, 0], packed[:, 1])  2.78 us
    ppermute x4, waiting for transfers between devices, shifted(): return lax.ppermute(shard, axis, pairs)  2.58 us
    ppermute x4, waiting for transfers between devices, shifted_2(): lax.ppermute(shard, axis, [(i, (i + by) % length) for i in range(length)])  2.5 us
    dot_general x8, matrix products, trace_update(): jnp.einsum('...z,zk->...k', rows_view, tangent, precision=highest)  2.4 us
  transfers between devices with their start and end apart: 8, of which 3 were waited for; matrix products, arithmetic and copies ran while one was open for 10% of the time, Pallas kernels for 0%

profile of v5, /device:TPU:24, one launch (start us, length us, event | category | flops | bytes accessed | tf_op | source)
XLA Modules:
  0.0 113.0 jit_solution(12020339283426634892)
XLA Ops:
  0.0 23.0 %shard_map.172 = (f32[3,4,4096]{2,1,0:T(4,128)}, f32[3,4,64,128]{3,2,1,0:T(8,128)}) custom-call(f32[3]{0:T(128)} %bitcast.187, f32[3,64,4096]{2,1,0:T(8,128)} %bitcast.178, bf16[64,256]{1,0:T(8,128)(2,1)} %constant.127.clone.refs_2_.refs_5_, bf16[1024,256]{1,0:T(8,128)(2,1)} %constant.128.clone.refs_3_.refs_6_, ...), custom_call_target="tpu_custom_call" | custom-call | tf_op jit(solution)/shard_map/pallas_call | solution.py:266
  23.0 1.1 slice_bitcast_fusion.6
  24.3 3.3 %collective-permute-start.1 = (f32[1,3,3,4096]{3,1,2,0:T(4,128)S(1)}, f32[1,3,3,4096]{3,1,2,0:T(4,128)S(1)}, u32[]{:S(2)}, u32[]{:S(2)}) collective-permute-start(f32[1,3,3,4096]{3,1,2,0:T(4,128)S(1)} %pad_maximum_fusion.2), channel_id=1, source_target_pairs={{4,0},{8,4},{12,8},{16,12},{20,16},{24,20},{28,24},{5,1},{9,5},{13... | collective-permute-start | bytes 442376 | tf_op jit(solution)/shard_map/ppermute | solution.py:28
  28.5 2.5 %collective-permute-start = (f32[1,4,3,4096]{3,1,2,0:T(4,128)S(1)}, f32[1,4,3,4096]{3,1,2,0:T(4,128)S(1)}, u32[]{:S(2)}, u32[]{:S(2)}) collective-permute-start(f32[1,4,3,4096]{3,1,2,0:T(4,128)S(1)} %maximum_maximum_fusion), channel_id=1, source_target_pairs={{0,4},{4,8},{8,12},{12,16},{16,20},{20,24},{24,28},{1,5},{5,9},{9,... | collective-permute-start | bytes 589832 | tf_op jit(solution)/shard_map/ppermute | solution.py:28
  31.1 1.1 %slice_bitcast_fusion.3 = (f32[1,2,3,64,64]{4,3,1,2,0:T(8,128)S(1)}, f32[1,2,3,64,64]{4,3,1,2,0:T(8,128)S(1)}) fusion(f32[1,3,4,64,128]{4,3,2,1,0:T(8,128)} %bitcast.181), kind=kLoop, calls=%fused_computation.30 | loop fusion | bytes 393216 | tf_op jit(solution)/shard_map/transpose | solution.py:382
  32.2 0.1 reshape.814
  32.4 0.1 reshape.815
  32.8 1.7 %collective-permute-start.3 = (f32[1,3,3,4096]{3,2,1,0:T(4,128)S(1)}, f32[1,3,3,4096]{3,2,1,0:T(4,128)S(1)}, u32[]{:S(2)}, u32[]{:S(2)}) collective-permute-start(f32[1,3,3,4096]{3,2,1,0:T(4,128)S(1)} %get-tuple-element.50), channel_id=1, source_target_pairs={{0,3},{1,0},{2,1},{3,2},{4,7},{5,4},{6,5},{7,6},{8,11},{9,8},{10,9... | collective-permute-start | bytes 442376 | tf_op jit(solution)/shard_map/ppermute | solution.py:33
  34.6 0.6 slice_reduce_fusion.11
  35.2 0.1 squeeze.89
  35.5 0.1 squeeze.88
  35.7 0.1 reshape_squeeze.27
  35.8 0.1 reshape_squeeze.26
  35.9 2.2 %collective-permute-done.2 = f32[1,3,3,4096]{3,2,1,0:T(4,128)S(1)} collective-permute-done((f32[1,3,3,4096]{3,2,1,0:T(4,128)S(1)}, f32[1,3,3,4096]{3,2,1,0:T(4,128)S(1)}, u32[]{:S(2)}, u32[]{:S(2)}) %collective-permute-start.2) | collective-permute-done | bytes 147488 | tf_op jit(solution)/shard_map/ppermute | solution.py:33
  38.2 0.3 slice_reduce_fusion.10
  38.5 0.1 reshape_squeeze.28
  38.8 0.3 collective-permute-done.3
  39.3 0.1 squeeze.91
  39.5 0.1 squeeze.92
  39.7 0.1 squeeze.94
  39.8 0.1 mul.568
  40.0 0.1 slice_reduce_fusion.16
  40.2 0.5 slice.181
  41.4 0.3 slice_reduce_fusion.15
  41.6 0.1 squeeze.85
  41.8 0.1 squeeze.83
  42.5 0.3 fusion.34
  42.8 0.7 mul.608.refs_3_
  43.5 0.3 fusion.40
  44.0 0.7 reshape_squeeze_reshape.8.refs_2_
  44.7 0.3 fusion.9
  45.0 0.3 fusion.7
  45.3 0.7 maximum_bitcast_fusion.refs_4_
  46.0 23.1 %shard_map.173 = (f32[3,4,4096]{2,1,0:T(4,128)}, f32[3,4,64,128]{3,2,1,0:T(8,128)}) custom-call(f32[3]{0:T(128)} %bitcast.188, f32[3,64,4096]{2,1,0:T(8,128)} %bitcast.179, f32[3,1,4096]{2,1,0:T(1,128)} %reshape_squeeze_reshape.8.refs_2_, f32[3,1,4096]{2,1,0:T(1,128)} %mul.608.refs_3_, f32[3,64,128]{2,1,0:T(8,128)} %maximum_bitcast_fusion.refs_4_, ...), custom_call_target="tpu_custom_call" | custom-call | tf_op jit(solution)/shard_map/pallas_call | solution.py:266
  69.1 1.1 slice_bitcast_fusion.4
  70.2 4.2 %collective-permute-start.5 = (f32[1,2,3,4096]{3,1,2,0:T(2,128)S(1)}, f32[1,2,3,4096]{3,1,2,0:T(2,128)S(1)}, u32[]{:S(2)}, u32[]{:S(2)}) collective-permute-start(f32[1,2,3,4096]{3,1,2,0:T(2,128)S(1)} %get-tuple-element.33), channel_id=1, source_target_pairs={{4,0},{8,4},{12,8},{16,12},{20,16},{24,20},{28,24},{5,1},{9,5},{13... | collective-permute-start | bytes 294920 | tf_op jit(solution)/shard_map/ppermute | solution.py:28
  74.4 0.3 slice_reduce_fusion.6
  74.7 1.1 %slice_bitcast_fusion.1 = (f32[1,2,3,64,64]{4,3,1,2,0:T(8,128)S(1)}, f32[1,2,3,64,64]{4,3,1,2,0:T(8,128)S(1)}) fusion(f32[1,3,4,64,128]{4,3,2,1,0:T(8,128)} %bitcast.182), kind=kLoop, calls=%fused_computation.28 | loop fusion | bytes 393216 | tf_op jit(solution)/shard_map/transpose | solution.py:382
  75.8 2.1 %collective-permute-start.4 = (f32[1,2,3,4096]{3,1,2,0:T(2,128)S(1)}, f32[1,2,3,4096]{3,1,2,0:T(2,128)S(1)}, u32[]{:S(2)}, u32[]{:S(2)}) collective-permute-start(f32[1,2,3,4096]{3,1,2,0:T(2,128)S(1)} %get-tuple-element.34), channel_id=1, source_target_pairs={{0,4},{4,8},{8,12},{12,16},{16,20},{20,24},{24,28},{1,5},{5,9},{9,... | collective-permute-start | bytes 294920 | tf_op jit(solution)/shard_map/ppermute | solution.py:28
  77.9 0.1 reshape_squeeze.30
  78.3 0.3 slice_reduce_fusion.3
  78.5 0.1 squeeze.102
  78.8 0.1 squeeze.103
  78.9 0.1 squeeze.101
  79.0 0.1 reshape.822
  79.2 0.1 reshape.823
  79.6 1.7 %collective-permute-start.7 = (f32[1,2,3,4096]{3,2,1,0:T(4,128)S(1)}, f32[1,2,3,4096]{3,2,1,0:T(4,128)S(1)}, u32[]{:S(2)}, u32[]{:S(2)}) collective-permute-start(f32[1,2,3,4096]{3,2,1,0:T(4,128)S(1)} %copy.78), channel_id=1, source_target_pairs={{0,3},{1,0},{2,1},{3,2},{4,7},{5,4},{6,5},{7,6},{8,11},{9,8},{10,9... | collective-permute-start | bytes 294920 | tf_op jit(solution)/shard_map/ppermute | solution.py:33
  81.3 2.6 %collective-permute-done.4 = f32[1,2,3,4096]{3,1,2,0:T(2,128)S(1)} collective-permute-done((f32[1,2,3,4096]{3,1,2,0:T(2,128)S(1)}, f32[1,2,3,4096]{3,1,2,0:T(2,128)S(1)}, u32[]{:S(2)}, u32[]{:S(2)}) %collective-permute-start.4) | collective-permute-done | bytes 98336 | tf_op jit(solution)/shard_map/ppermute | solution.py:28
  83.9 0.3 slice_reduce_fusion.7
  84.1 0.1 squeeze.98
  84.6 0.3 slice_reduce_fusion.2
  84.9 0.1 reshape_squeeze.32
  85.0 0.1 reshape_squeeze.33
  85.4 0.3 fusion.11
  85.7 0.3 fusion.12
  86.2 0.7 reshape_squeeze_reshape.9.refs_2_
  87.1 0.1 squeeze.106
  87.2 0.1 mul.604
  87.5 0.1 squeeze.104
  87.8 0.7 add_multiply_fusion.refs_3_
  88.5 0.3 fusion.16
  88.8 0.3 fusion.14
  89.1 0.7 maximum_bitcast_fusion.1.refs_4_
  89.8 23.1 %shard_map.174 = f32[3,64,4096]{2,1,0:T(8,128)} custom-call(f32[3]{0:T(128)} %bitcast.189, f32[3,64,4096]{2,1,0:T(8,128)} %bitcast.180, f32[3,1,4096]{2,1,0:T(1,128)} %reshape_squeeze_reshape.9.refs_2_, f32[3,1,4096]{2,1,0:T(1,128)} %add_multiply_fusion.refs_3_, f32[3,64,128]{2,1,0:T(8,128)} %maximum_bitcast_fusion.1.refs_4_, ...), custom_call_target="tpu_custom_call" | custom-call | tf_op jit(solution)/shard_map/pallas_call | solution.py:266
  (77 shorter events, 4.2 us)
Async XLA Ops:
  0.0 24.1 %copy-start.1 = (f32[1,1,3]{2,1,0:T(1,128)S(1)}, f32[1,1,3]{2,1,0:T(1,128)}, u32[]{:S(2)}) copy-start(f32[1,1,3]{2,1,0:T(1,128)} %param.19) | copy-start | bytes 40
  24.3 13.9 %collective-permute-start.1 = (f32[1,3,3,4096]{3,1,2,0:T(4,128)S(1)}, f32[1,3,3,4096]{3,1,2,0:T(4,128)S(1)}, u32[]{:S(2)}, u32[]{:S(2)}) collective-permute-start(f32[1,3,3,4096]{3,1,2,0:T(4,128)S(1)} %pad_maximum_fusion.2), channel_id=1, source_target_pairs={{4,0},{8,4},{12,8},{16,12},{20,16},{24,20},{28,24},{5,1},{9,5},{13... | collective-permute-start | bytes 442376 | tf_op jit(solution)/shard_map/ppermute | solution.py:28
  28.5 11.7 %collective-permute-start = (f32[1,4,3,4096]{3,1,2,0:T(4,128)S(1)}, f32[1,4,3,4096]{3,1,2,0:T(4,128)S(1)}, u32[]{:S(2)}, u32[]{:S(2)}) collective-permute-start(f32[1,4,3,4096]{3,1,2,0:T(4,128)S(1)} %maximum_maximum_fusion), channel_id=1, source_target_pairs={{0,4},{4,8},{8,12},{12,16},{16,20},{20,24},{24,28},{1,5},{5,9},{9,... | collective-permute-start | bytes 589832 | tf_op jit(solution)/shard_map/ppermute | solution.py:28
  32.8 5.4 %collective-permute-start.2 = (f32[1,3,3,4096]{3,2,1,0:T(4,128)S(1)}, f32[1,3,3,4096]{3,2,1,0:T(4,128)S(1)}, u32[]{:S(2)}, u32[]{:S(2)}) collective-permute-start(f32[1,3,3,4096]{3,2,1,0:T(4,128)S(1)} %get-tuple-element.49), channel_id=1, source_target_pairs={{0,1},{1,2},{2,3},{3,0},{4,5},{5,6},{6,7},{7,4},{8,9},{9,10},{10,1... | collective-permute-start | bytes 442376 | tf_op jit(solution)/shard_map/ppermute | solution.py:33
  32.8 6.2 %collective-permute-start.3 = (f32[1,3,3,4096]{3,2,1,0:T(4,128)S(1)}, f32[1,3,3,4096]{3,2,1,0:T(4,128)S(1)}, u32[]{:S(2)}, u32[]{:S(2)}) collective-permute-start(f32[1,3,3,4096]{3,2,1,0:T(4,128)S(1)} %get-tuple-element.50), channel_id=1, source_target_pairs={{0,3},{1,0},{2,1},{3,2},{4,7},{5,4},{6,5},{7,6},{8,11},{9,8},{10,9... | collective-permute-start | bytes 442376 | tf_op jit(solution)/shard_map/ppermute | solution.py:33
  70.2 14.4 %collective-permute-start.5 = (f32[1,2,3,4096]{3,1,2,0:T(2,128)S(1)}, f32[1,2,3,4096]{3,1,2,0:T(2,128)S(1)}, u32[]{:S(2)}, u32[]{:S(2)}) collective-permute-start(f32[1,2,3,4096]{3,1,2,0:T(2,128)S(1)} %get-tuple-element.33), channel_id=1, source_target_pairs={{4,0},{8,4},{12,8},{16,12},{20,16},{24,20},{28,24},{5,1},{9,5},{13... | collective-permute-start | bytes 294920 | tf_op jit(solution)/shard_map/ppermute | solution.py:28
  75.8 8.0 %collective-permute-start.4 = (f32[1,2,3,4096]{3,1,2,0:T(2,128)S(1)}, f32[1,2,3,4096]{3,1,2,0:T(2,128)S(1)}, u32[]{:S(2)}, u32[]{:S(2)}) collective-permute-start(f32[1,2,3,4096]{3,1,2,0:T(2,128)S(1)} %get-tuple-element.34), channel_id=1, source_target_pairs={{0,4},{4,8},{8,12},{12,16},{16,20},{20,24},{24,28},{1,5},{5,9},{9,... | collective-permute-start | bytes 294920 | tf_op jit(solution)/shard_map/ppermute | solution.py:28
  78.1 7.3 %copy-start.2 = (f32[1,1,3]{2,1,0:T(1,128)S(1)}, f32[1,1,3]{2,1,0:T(1,128)}, u32[]{:S(2)}) copy-start(f32[1,1,3]{2,1,0:T(1,128)} %param.19) | copy-start | bytes 40
  79.6 6.5 %collective-permute-start.7 = (f32[1,2,3,4096]{3,2,1,0:T(4,128)S(1)}, f32[1,2,3,4096]{3,2,1,0:T(4,128)S(1)}, u32[]{:S(2)}, u32[]{:S(2)}) collective-permute-start(f32[1,2,3,4096]{3,2,1,0:T(4,128)S(1)} %copy.78), channel_id=1, source_target_pairs={{0,3},{1,0},{2,1},{3,2},{4,7},{5,4},{6,5},{7,6},{8,11},{9,8},{10,9... | collective-permute-start | bytes 294920 | tf_op jit(solution)/shard_map/ppermute | solution.py:33
  81.3 6.2 %collective-permute-start.6 = (f32[1,2,3,4096]{3,2,1,0:T(4,128)S(1)}, f32[1,2,3,4096]{3,2,1,0:T(4,128)S(1)}, u32[]{:S(2)}, u32[]{:S(2)}) collective-permute-start(f32[1,2,3,4096]{3,2,1,0:T(4,128)S(1)} %copy.77), channel_id=1, source_target_pairs={{0,1},{1,2},{2,3},{3,0},{4,5},{5,6},{6,7},{7,4},{8,9},{9,10},{10,1... | collective-permute-start | bytes 294920 | tf_op jit(solution)/shard_map/ppermute | solution.py:33
  85.3 2.6 %copy-start = (f32[3,1,4096]{2,1,0:T(1,128)S(1)}, f32[3,1,4096]{2,1,0:T(1,128)}, u32[]{:S(2)}) copy-start(f32[3,1,4096]{2,1,0:T(1,128)} %mul.608.refs_3_) | copy-start | bytes 147460

commit v6 on v2

--- a/solution.py
+++ b/solution.py
@@ -128,12 +128,12 @@
 
 def stack_right(w):
     w1, w2, w3 = np_split3(w)
-    return np.concatenate([w1, w2, w3, w1, w2, w1], 0)
+    return np.concatenate([w1, w2, w1, w1], 0)
 
 
 def stack_left(w):
     w1, w2, w3 = np_split3(w)
-    return np.concatenate([w1, w2, w3, w1, w2, w1], 1)
+    return np.concatenate([w1, w2, w1, w1], 1)
 
 
 def split3(d):
@@ -146,12 +146,12 @@
 
 def sdot(d, w6):
     d1, d2, d3 = split3(d)
-    return jnp.dot(jnp.concatenate([d1, d1, d1, d2, d2, d3], 1), w6, preferred_element_type=f32)
+    return jnp.dot(jnp.concatenate([d1, d1, d2, d3], 1), w6, preferred_element_type=f32)
 
 
 def sdot_left(w6, d):
     d1, d2, d3 = split3(d)
-    return jnp.dot(w6, jnp.concatenate([d1, d1, d1, d2, d2, d3], 0), preferred_element_type=f32)
+    return jnp.dot(w6, jnp.concatenate([d1, d1, d2, d3], 0), preferred_element_type=f32)
 
 
 def solve_kernel(*refs, with_faces, emit_u, emit_sides):
@@ -160,9 +160,10 @@
     if with_faces:
         xlo_ref, xhi_ref, yadd_ref = next(it), next(it), next(it)
     q_ref, p_ref, wy_ref, exy_ref, ez_ref = next(it), next(it), next(it), next(it), next(it)
+    code_ref = next(it)
     o_ref = next(it) if emit_u else None
     if emit_sides:
-        xf_ref, yf_ref = next(it), next(it)
+        xh_ref, xl_ref, yh_ref, yl_ref = next(it), next(it), next(it), next(it)
     s_ref, z_ref = next(it), next(it)
     n = q_ref.shape[0]
     h = n // 2
@@ -227,21 +228,28 @@
     def slope(p0, p1, p2, p3):
         return m * (11.0 / 6.0 * p0 - 3.0 * p1 + 1.5 * p2 - p3 / 3.0)
     if emit_sides:
-        xf_ref[0, 0:1, :] = u[n - 1:n]
-        xf_ref[0, 1:2, :] = slope(u[n - 1:n], u[n - 2:n - 1], u[n - 3:n - 2], u[n - 4:n - 3])
-        xf_ref[0, 2:3, :] = u[0:1]
-        xf_ref[0, 3:4, :] = slope(u[0:1], u[1:2], u[2:3], u[3:4])
+        m_row = jnp.full((1, nn), m, f32)
+        xh_ref[0, 0:1, :] = u[n - 1:n]
+        xh_ref[0, 1:2, :] = slope(u[n - 1:n], u[n - 2:n - 1], u[n - 3:n - 2], u[n - 4:n - 3])
+        xh_ref[0, 2:3, :] = m_row
+        xh_ref[0, 3:4, :] = jnp.full((1, nn), code_ref[0], f32)
+        xl_ref[0, 0:1, :] = u[0:1]
+        xl_ref[0, 1:2, :] = slope(u[0:1], u[1:2], u[2:3], u[3:4])
+        xl_ref[0, 2:3, :] = m_row
+        m_sq = jnp.full((n, w2), m, f32)
         c_hi = u[:, nn - w2:]
         c_hi2 = u[:, nn - 2 * w2:nn - w2]
-        yf_ref[0, 0] = c_hi
-        yf_ref[0, 1] = slope(c_hi, pltpu.roll(c_hi, n, 1), c_hi2, pltpu.roll(c_hi2, n, 1))
+        yh_ref[0, 0] = c_hi
+        yh_ref[0, 1] = slope(c_hi, pltpu.roll(c_hi, n, 1), c_hi2, pltpu.roll(c_hi2, n, 1))
+        yh_ref[0, 2] = m_sq
         c_lo = u[:, :w2]
         c_lo2 = u[:, w2:2 * w2]
-        yf_ref[0, 2] = c_lo
-        yf_ref[0, 3] = slope(c_lo, pltpu.roll(c_lo, n, 1), c_lo2, pltpu.roll(c_lo2, n, 1))
-
-
-def kernel_sweep(rhs, moduli, faces=None, emit_u=True, emit_sides=False, interpret=False):
+        yl_ref[0, 0] = c_lo
+        yl_ref[0, 1] = slope(c_lo, pltpu.roll(c_lo, n, 1), c_lo2, pltpu.roll(c_lo2, n, 1))
+        yl_ref[0, 2] = m_sq
+
+
+def kernel_sweep(rhs, moduli, code, faces=None, emit_u=True, emit_sides=False, interpret=False):
     ncomp, n, nn = rhs.shape
     q, p4, wy, exy, ez = consts(n)
     full = lambda shp: pl.BlockSpec(shp, lambda c: (0,) * len(shp))
@@ -253,15 +261,16 @@
         xlo, xhi, yadd = faces
         in_specs += [comp3((1, nn)), comp3((1, nn)), comp3((n, 2 * n))]
         args += [xlo.reshape(ncomp, 1, nn), xhi.reshape(ncomp, 1, nn), yadd]
-    in_specs += [full(q.shape), full(p4.shape), full(wy.shape), full(exy.shape), full(ez.shape)]
-    args += [q, p4, wy, exy, ez]
+    in_specs += [full(q.shape), full(p4.shape), full(wy.shape), full(exy.shape), full(ez.shape), smem]
+    args += [q, p4, wy, exy, ez, code]
     out_specs, out_shape = [], []
     if emit_u:
         out_specs.append(comp3((n, nn)))
         out_shape.append(jax.ShapeDtypeStruct(rhs.shape, f32))
     if emit_sides:
-        out_specs += [comp3((4, nn)), comp3((4, n, 2 * n))]
-        out_shape += [jax.ShapeDtypeStruct((ncomp, 4, nn), f32), jax.ShapeDtypeStruct((ncomp, 4, n, 2 * n), f32)]
+        out_specs += [comp3((4, nn)), comp3((3, nn)), comp3((3, n, 2 * n)), comp3((3, n, 2 * n))]
+        out_shape += [jax.ShapeDtypeStruct((ncomp, 4, nn), f32), jax.ShapeDtypeStruct((ncomp, 3, nn), f32),
+                      jax.ShapeDtypeStruct((ncomp, 3, n, 2 * n), f32), jax.ShapeDtypeStruct((ncomp, 3, n, 2 * n), f32)]
     kernel = functools.partial(solve_kernel, with_faces=faces is not None, emit_u=emit_u, emit_sides=emit_sides)
     return pl.pallas_call(
         kernel,
@@ -334,16 +343,28 @@
     return current + omega_step * smoothed.reshape(residue.shape)
 
 
-def pack_side(side):
-    return jnp.stack(side, 1)
-
-
-def unpack_side(packed):
-    return (packed[:, 0], packed[:, 1])
+def x_side(packet):
+    return (packet[:, :, 0], packet[:, :, 1])
+
+
+def y_side(packet, low):
+    extent = packet.shape[-2]
+    part = packet[..., :extent] if low else packet[..., extent:]
+    return (part[:, :, 0], part[:, :, 1])
 
 
 def oriented(side, codes, extent):
     return (orient(side[0], codes, extent), orient(side[1], codes, extent))
+
+
+def square_update(current, side_a, side_b, moduli_a, moduli_b, omega_step, tangent):
+    weight_a = moduli_a[..., None, None]
+    weight_b = moduli_b[..., None, None]
+    residue = (
+        weight_a * side_a[0] + weight_b * side_b[0] + traction_mix * (side_a[1] + side_b[1])
+    ) / (weight_a + weight_b) - current
+    smoothed = residue + penalty_mix * jnp.einsum("...z,zk->...k", residue, tangent, precision=highest)
+    return current + omega_step * smoothed
 
 
 def shards(forcing, modulus, orient_codes):
@@ -353,76 +374,59 @@
     source_field = forcing[0]
     moduli = modulus[0]
     codes_here = orient_codes[0]
+    code_values = codes_here.astype(jnp.float32)
     tangent = tangent_matrix(extent)
     omegas = step_weights(ITERS)
     slab_count = lax.axis_size("blk")
     slab_index = lax.axis_index("blk")
     has_up = (slab_index < slab_count - 1).astype(jnp.float32)
     has_down = (slab_index > 0).astype(jnp.float32)
-    moduli_up = shifted(moduli, "blk", -1)
-    moduli_down, codes_down = shifted((moduli, codes_here), "blk", 1)
-    moduli_next = jnp.concatenate([moduli[1:], shifted_2(moduli[:1], "face", -1)], 0)
-    moduli_prev = jnp.concatenate([shifted_2(moduli[-1:], "face", 1), moduli[:-1]], 0)
-    face_zeros = jnp.zeros((blocks, 3, flat), jnp.float32)
-    lam_x_up = face_zeros
-    lam_x_down = face_zeros
-    lam_y_next = face_zeros
-    lam_y_prev = face_zeros
+    lam_x_up = jnp.zeros((blocks, 3, flat), jnp.float32)
+    lam_x_down = lam_x_up
+    lam_y_next = jnp.zeros((blocks, 3, extent, extent), jnp.float32)
+    lam_y_prev = lam_y_next
     faces = [None] * blocks
     for sweep in range(ITERS + 1):
         last = sweep == ITERS
         outs = [
-            kernel_sweep(source_field[b], moduli[b], faces[b], emit_u=last, emit_sides=not last)
+            kernel_sweep(source_field[b], moduli[b], code_values[b:b + 1], faces[b], emit_u=last, emit_sides=not last)
             for b in range(blocks)
         ]
         if last:
             return jnp.stack([o[0] for o in outs], 0)[None]
-        xf = jnp.stack([o[0] for o in outs], 0)
-        yf = jnp.stack([o[1] for o in outs], 0)
-        x_high_side = xf[:, :, 0:2].transpose(0, 2, 1, 3)
-        x_low_side = xf[:, :, 2:4].transpose(0, 2, 1, 3)
-        y_high_side = yf[:, :, 0:2, :, extent:].transpose(0, 2, 1, 3, 4).reshape(blocks, 2, 3, flat)
-        y_low_side = yf[:, :, 2:4, :, :extent].transpose(0, 2, 1, 3, 4).reshape(blocks, 2, 3, flat)
-        upper_side = shifted(x_low_side, "blk", -1)
-        lower_side = shifted(x_high_side, "blk", 1)
-        next_side = jnp.concatenate([y_low_side[1:], shifted_2(y_low_side[:1], "face", -1)], 0)
-        prev_side = jnp.concatenate([shifted_2(y_high_side[-1:], "face", 1), y_high_side[:-1]], 0)
+        xh, xl, yh, yl = (jnp.stack([o[k] for o in outs], 0) for k in range(4))
+        upper = shifted(xl, "blk", -1)
+        lower = shifted(xh, "blk", 1)
+        nxt = jnp.concatenate([yl[1:], shifted_2(yl[:1], "face", -1)], 0)
+        prv = jnp.concatenate([shifted_2(yh[-1:], "face", 1), yh[:-1]], 0)
+        if sweep == 0:
+            moduli_up = upper[:, :, 2, 0]
+            moduli_down = lower[:, :, 2, 0]
+            codes_down = lower[:, 0, 3, 0].astype(jnp.int32)
+            moduli_next = nxt[:, :, 2, 0, 0]
+            moduli_prev = prv[:, :, 2, 0, 0]
         lam_x_up = (
             trace_update(
-                lam_x_up,
-                unpack_side(x_high_side),
-                oriented(unpack_side(upper_side), codes_here, extent),
-                moduli,
-                moduli_up,
-                omegas[sweep],
-                tangent,
+                lam_x_up, x_side(xh), oriented(x_side(upper), codes_here, extent),
+                moduli, moduli_up, omegas[sweep], tangent,
             )
             * has_up
         )
         lam_x_down = (
             trace_update(
-                lam_x_down,
-                unpack_side(lower_side),
-                oriented(unpack_side(x_low_side), codes_down, extent),
-                moduli_down,
-                moduli,
-                omegas[sweep],
-                tangent,
+                lam_x_down, x_side(lower), oriented(x_side(xl), codes_down, extent),
+                moduli_down, moduli, omegas[sweep], tangent,
             )
             * has_down
         )
-        lam_y_next = trace_update(
-            lam_y_next, unpack_side(y_high_side), unpack_side(next_side), moduli, moduli_next,
-            omegas[sweep], tangent,
+        lam_y_next = square_update(
+            lam_y_next, y_side(yh, False), y_side(nxt, True), moduli, moduli_next, omegas[sweep], tangent
         )
-        lam_y_prev = trace_update(
-            lam_y_prev, unpack_side(prev_side), unpack_side(y_low_side), moduli_prev, moduli,
-            omegas[sweep], tangent,
+        lam_y_prev = square_update(
+            lam_y_prev, y_side(prv, False), y_side(yl, True), moduli_prev, moduli, omegas[sweep], tangent
         )
         x_low = orient(lam_x_down, codes_down, extent)
-        yadd = jnp.concatenate(
-            [lam_y_prev.reshape(blocks, 3, extent, extent), lam_y_next.reshape(blocks, 3, extent, extent)], -1
-        )
+        yadd = jnp.concatenate([lam_y_prev, lam_y_next], -1)
         faces = [(x_low[b], lam_x_up[b], yadd[b]) for b in range(blocks)]
 
 

time: 145 us -> 113 us (0.78)
  Pallas kernels: 90 us -> 69.3 us
  starting transfers between devices: 23.4 us -> 13.3 us
  between operations: 3.76 us -> 1.81 us
  local copies, waits for them, and re-layouts: 14.9 us -> 16.4 us
    pallas_call x3, Pallas kernels: 90 us -> 69.3 us  [kernel_sweep(): pl.pallas_call(kernel, grid=(ncomp,), in_specs=in_specs, out_specs=out_sp...]
    ppermute x7 -> x4, starting transfers between devices: 20.3 us -> 12.1 us  [shifted(): return lax.ppermute(shard, axis, pairs)]
    slice x7 -> x13, local copies, waits for them, and re-layouts: 2.18 us -> 7.35 us  [the longest x8 6.39 us: x_side(): return (packet[:, :, 0], packet[:, :, 1])]
    transpose x4 -> x0, local copies, waits for them, and re-layouts: 4.5 us -> none  [the longest x2 2.27 us: shards(): yf[:, :, 0:2, :, extent:].transpose(0, 2, 1, 3, 4)]
    pallas_call x0 -> x4, local copies, waits for them, and re-layouts: none -> 2.98 us  [kernel_sweep(): pl.pallas_call(kernel, grid=(ncomp,), in_specs=in_specs, out_specs=out_sp...]
    ppermute x6 -> x4, waiting for transfers between devices: 3.16 us -> 0.92 us  [shifted_2(): lax.ppermute(shard, axis, [(i, (i + by) % length) for i in range(length)])]
    ppermute x6 -> x4, starting transfers between devices: 3.05 us -> 1.18 us  [shifted_2(): lax.ppermute(shard, axis, [(i, (i + by) % length) for i in range(length)])]
    ppermute x7 -> x4, waiting for transfers between devices: 3.63 us -> 4.74 us  [shifted(): return lax.ppermute(shard, axis, pairs)]
  transfers between devices with their start and end apart: 13 -> 8, of which waited for: 3 -> 4; matrix products, arithmetic and copies ran while one was open for 9% -> 12% of each run, Pallas kernels for 21% -> 0%
where the time goes in v6:
time: 113 us; the launch traced here: 111 us
  Pallas kernels  69.3 us (61%)
  local copies, waits for them, and re-layouts  16.4 us (15%)
  starting transfers between devices  13.3 us (12%)
  waiting for transfers between devices  5.67 us (5%)
  matrix products  2.51 us (2%)
  other arithmetic  2.3 us (2%)
  between operations  1.81 us (2%)
    pallas_call x3, Pallas kernels, kernel_sweep(): pl.pallas_call(kernel, grid=(ncomp,), in_specs=in_specs, out_specs=out_sp...  69.3 us
    ppermute x4, starting transfers between devices, shifted(): return lax.ppermute(shard, axis, pairs)  12.1 us
    slice x8, local copies, waits for them, and re-layouts, x_side(): return (packet[:, :, 0], packet[:, :, 1])  6.39 us
    ppermute x4, waiting for transfers between devices, shifted(): return lax.ppermute(shard, axis, pairs)  4.74 us
    pallas_call x4, local copies, waits for them, and re-layouts, kernel_sweep(): pl.pallas_call(kernel, grid=(ncomp,), in_specs=in_specs, out_specs=out_sp...  2.98 us
  transfers between devices with their start and end apart: 8, of which 4 were waited for; matrix products, arithmetic and copies ran while one was open for 12% of the time, Pallas kernels for 0%

profile of v6, /device:TPU:24, one launch (start us, length us, event | category | flops | bytes accessed | tf_op | source)
XLA Modules:
  0.0 111.3 jit_solution(9716516098102772074)
XLA Ops:
  0.7 23.1 %shard_map.172 = (f32[3,4,4096]{2,1,0:T(4,128)}, f32[3,3,4096]{2,1,0:T(4,128)}, f32[3,3,64,128]{3,2,1,0:T(8,128)}, f32[3,3,64,128]{3,2,1,0:T(8,128)}) custom-call(f32[3]{0:T(128)} %bitcast.310, f32[3,64,4096]{2,1,0:T(8,128)} %bitcast.289, bf16[64,256]{1,0:T(8,128)(2,1)} %constant.130.clone.refs_2_.refs_5_, ...), custom_call_target="tpu_custom_call" | custom-call | tf_op jit(solution)/shard_map/pallas_call | solution.py:275
  23.7 3.3 %collective-permute-start.1 = (f32[1,3,3,4096]{3,2,1,0:T(4,128)}, f32[1,3,3,4096]{3,2,1,0:T(4,128)S(1)}, u32[]{:S(2)}, u32[]{:S(2)}) collective-permute-start(f32[1,3,3,4096]{3,2,1,0:T(4,128)} %bitcast.304), channel_id=1, source_target_pairs={{4,0},{8,4},{12,8},{16,12},{20,16},{24,20},{28,24},{5,1},{9,5},{13... | collective-permute-start | bytes 442376 | tf_op jit(solution)/shard_map/ppermute | solution.py:28
  27.0 2.5 %collective-permute-start = (f32[1,3,4,4096]{3,2,1,0:T(4,128)}, f32[1,3,4,4096]{3,2,1,0:T(4,128)S(1)}, u32[]{:S(2)}, u32[]{:S(2)}) collective-permute-start(f32[1,3,4,4096]{3,2,1,0:T(4,128)} %bitcast.302), channel_id=1, source_target_pairs={{0,4},{4,8},{8,12},{12,16},{16,20},{20,24},{24,28},{1,5},{5,9},{9,... | collective-permute-start | bytes 589832 | tf_op jit(solution)/shard_map/ppermute | solution.py:28
  29.6 1.0 copy.43
  30.6 0.4 collective-permute-start.3
  31.0 1.0 copy.44
  32.0 0.2 collective-permute-start.2
  32.2 1.3 %slice_reduce_fusion.14 = (f32[3,4096]{1,0:T(4,128)S(1)}, f32[3,4096]{1,0:T(4,128)S(1)}) fusion(f32[1,3,3,4096]{3,2,1,0:T(4,128)} %bitcast.305), kind=kLoop, calls=%fused_computation.165 | loop fusion | bytes 196608 | tf_op jit(solution)/shard_map/slice | solution.py:347
  33.5 1.3 %slice_reduce_fusion.11 = (f32[3,4096]{1,0:T(4,128)S(1)}, f32[3,4096]{1,0:T(4,128)S(1)}) fusion(f32[1,3,4,4096]{3,2,1,0:T(4,128)} %bitcast.303), kind=kLoop, calls=%fused_computation.162 | loop fusion | bytes 196608 | tf_op jit(solution)/shard_map/slice | solution.py:347
  34.8 0.1 squeeze.89
  35.0 0.1 squeeze.87
  35.1 0.1 squeeze.90
  35.2 0.1 squeeze.88
  35.3 0.1 reshape_squeeze.26
  35.4 0.1 reshape_squeeze.27
  35.6 1.0 collective-permute-done.1
  36.7 0.3 slice_reduce_fusion.10
  36.9 0.1 reshape_squeeze.28
  37.0 0.1 reshape_squeeze.29
  37.5 0.5 slice.172
  38.8 0.3 slice_reduce_fusion.15
  39.1 0.1 squeeze.85
  39.2 0.1 squeeze.83
  39.3 0.1 squeeze.86
  39.4 0.1 squeeze.84
  40.1 0.3 fusion.80
  40.4 0.7 mul.548.refs_3_
  41.1 0.3 fusion.86
  41.6 0.7 reshape_squeeze_reshape.8.refs_2_
  42.3 0.3 fusion.7
  42.6 0.3 fusion.9
  43.0 0.7 maximum_bitcast_fusion.refs_4_
  43.7 23.1 %shard_map.173 = (f32[3,4,4096]{2,1,0:T(4,128)}, f32[3,3,4096]{2,1,0:T(4,128)}, f32[3,3,64,128]{3,2,1,0:T(8,128)}, f32[3,3,64,128]{3,2,1,0:T(8,128)}) custom-call(f32[3]{0:T(128)} %bitcast.311, f32[3,64,4096]{2,1,0:T(8,128)} %bitcast.290, f32[3,1,4096]{2,1,0:T(1,128)} %reshape_squeeze_reshape.8.refs_2_, f32[3,1,4096]{2,1,0:T(1,128)} %mul.548.refs_3_, ...), custom_call_target="tpu_custom_call" | custom-call | tf_op jit(solution)/shard_map/pallas_call | solution.py:275
  66.8 1.4 %slice_reduce_fusion.3 = (f32[3,4096]{1,0:T(4,128)S(1)}, f32[3,4096]{1,0:T(4,128)S(1)}) fusion(f32[1,3,4,4096]{3,2,1,0:T(4,128)} %bitcast.306), kind=kLoop, calls=%fused_computation.154 | loop fusion | bytes 196608 | tf_op jit(solution)/shard_map/slice | solution.py:347
  68.2 0.1 squeeze.102
  68.3 0.1 squeeze.100
  68.4 0.1 squeeze.103
  68.5 0.1 squeeze.101
  68.6 1.3 %slice_reduce_fusion.6 = (f32[3,4096]{1,0:T(4,128)S(1)}, f32[3,4096]{1,0:T(4,128)S(1)}) fusion(f32[1,3,3,4096]{3,2,1,0:T(4,128)} %bitcast.308), kind=kLoop, calls=%fused_computation.157 | loop fusion | bytes 196608 | tf_op jit(solution)/shard_map/slice | solution.py:347
  70.0 4.3 %collective-permute-start.5 = (f32[1,3,3,4096]{3,2,1,0:T(4,128)}, f32[1,3,3,4096]{3,2,1,0:T(4,128)S(1)}, u32[]{:S(2)}, u32[]{:S(2)}) collective-permute-start(f32[1,3,3,4096]{3,2,1,0:T(4,128)} %bitcast.309), channel_id=1, source_target_pairs={{4,0},{8,4},{12,8},{16,12},{20,16},{24,20},{28,24},{5,1},{9,5},{13... | collective-permute-start | bytes 442376 | tf_op jit(solution)/shard_map/ppermute | solution.py:28
  74.3 1.9 %collective-permute-start.4 = (f32[1,3,4,4096]{3,2,1,0:T(4,128)}, f32[1,3,4,4096]{3,2,1,0:T(4,128)S(1)}, u32[]{:S(2)}, u32[]{:S(2)}) collective-permute-start(f32[1,3,4,4096]{3,2,1,0:T(4,128)} %bitcast.307), channel_id=1, source_target_pairs={{0,4},{4,8},{8,12},{12,16},{16,20},{20,24},{24,28},{1,5},{5,9},{9,... | collective-permute-start | bytes 589832 | tf_op jit(solution)/shard_map/ppermute | solution.py:28
  76.2 0.1 reshape_squeeze.30
  76.4 0.1 reshape_squeeze.31
  76.7 1.0 copy.42
  77.8 0.3 collective-permute-start.7
  78.1 0.2 collective-permute-start.6
  78.3 0.8 collective-permute-done.5
  79.1 0.3 slice_reduce_fusion.2
  79.4 0.1 reshape_squeeze.32
  79.5 0.1 reshape_squeeze.33
  79.9 0.3 fusion.12
  80.3 0.7 add_multiply_fusion.refs_3_
  81.0 2.9 %collective-permute-done.4 = f32[1,3,4,4096]{3,2,1,0:T(4,128)S(1)} collective-permute-done((f32[1,3,4,4096]{3,2,1,0:T(4,128)}, f32[1,3,4,4096]{3,2,1,0:T(4,128)S(1)}, u32[]{:S(2)}, u32[]{:S(2)}) %collective-permute-start.4) | collective-permute-done | bytes 196640 | tf_op jit(solution)/shard_map/ppermute | solution.py:28
  83.9 0.3 slice_reduce_fusion.7
  84.2 0.1 squeeze.98
  84.4 0.1 squeeze.99
  84.5 0.1 squeeze.97
  84.7 0.3 fusion.11
  85.1 0.7 reshape_squeeze_reshape.9.refs_2_
  85.9 0.3 fusion.16
  86.2 0.9 collective-permute-done.6
  87.1 0.3 fusion.14
  87.4 0.7 maximum_bitcast_fusion.1.refs_4_
  88.1 23.1 %shard_map.174 = f32[3,64,4096]{2,1,0:T(8,128)} custom-call(f32[3]{0:T(128)} %bitcast.312, f32[3,64,4096]{2,1,0:T(8,128)} %bitcast.291, f32[3,1,4096]{2,1,0:T(1,128)} %reshape_squeeze_reshape.9.refs_2_, f32[3,1,4096]{2,1,0:T(1,128)} %add_multiply_fusion.refs_3_, f32[3,64,128]{2,1,0:T(8,128)} %maximum_bitcast_fusion.1.refs_4_, ...), custom_call_target="tpu_custom_call" | custom-call | tf_op jit(solution)/shard_map/pallas_call | solution.py:275
  (51 shorter events, 1.9 us)
Async XLA Ops:
  23.7 12.9 %collective-permute-start.1 = (f32[1,3,3,4096]{3,2,1,0:T(4,128)}, f32[1,3,3,4096]{3,2,1,0:T(4,128)S(1)}, u32[]{:S(2)}, u32[]{:S(2)}) collective-permute-start(f32[1,3,3,4096]{3,2,1,0:T(4,128)} %bitcast.304), channel_id=1, source_target_pairs={{4,0},{8,4},{12,8},{16,12},{20,16},{24,20},{28,24},{5,1},{9,5},{13... | collective-permute-start | bytes 442376 | tf_op jit(solution)/shard_map/ppermute | solution.py:28
  27.0 10.5 %collective-permute-start = (f32[1,3,4,4096]{3,2,1,0:T(4,128)}, f32[1,3,4,4096]{3,2,1,0:T(4,128)S(1)}, u32[]{:S(2)}, u32[]{:S(2)}) collective-permute-start(f32[1,3,4,4096]{3,2,1,0:T(4,128)} %bitcast.302), channel_id=1, source_target_pairs={{0,4},{4,8},{8,12},{12,16},{16,20},{20,24},{24,28},{1,5},{5,9},{9,... | collective-permute-start | bytes 589832 | tf_op jit(solution)/shard_map/ppermute | solution.py:28
  30.6 9.3 %collective-permute-start.3 = (f32[1,3,3,64,128]{4,3,1,2,0:T(8,128)S(1)}, f32[1,3,3,64,128]{4,3,1,2,0:T(8,128)S(1)}, u32[]{:S(2)}, u32[]{:S(2)}) collective-permute-start(f32[1,3,3,64,128]{4,3,1,2,0:T(8,128)S(1)} %bitcast.292), channel_id=1, source_target_pairs={{0,3},{1,0},{2,1},{3,2},{4,7},{5,4},{6,5},{7,6},{8,11},{9,8},{10,9... | collective-permute-start | bytes 884744 | tf_op jit(solution)/shard_map/ppermute | solution.py:33
  31.0 9.1 %copy-start.2 = (f32[1,1,3]{2,1,0:T(1,128)S(1)}, f32[1,1,3]{2,1,0:T(1,128)}, u32[]{:S(2)}) copy-start(f32[1,1,3]{2,1,0:T(1,128)} %param.19) | copy-start | bytes 40
  32.0 8.0 %collective-permute-start.2 = (f32[1,3,3,64,128]{4,3,1,2,0:T(8,128)S(1)}, f32[1,3,3,64,128]{4,3,1,2,0:T(8,128)S(1)}, u32[]{:S(2)}, u32[]{:S(2)}) collective-permute-start(f32[1,3,3,64,128]{4,3,1,2,0:T(8,128)S(1)} %bitcast.294), channel_id=1, source_target_pairs={{0,1},{1,2},{2,3},{3,0},{4,5},{5,6},{6,7},{7,4},{8,9},{9,10},{10,1... | collective-permute-start | bytes 884744 | tf_op jit(solution)/shard_map/ppermute | solution.py:33
  66.8 10.9 %copy-start.1 = (f32[3,3,64,128]{3,2,1,0:T(8,128)S(1)}, f32[3,3,64,128]{3,2,1,0:T(8,128)}, u32[]{:S(2)}) copy-start(f32[3,3,64,128]{3,2,1,0:T(8,128)} %get-tuple-element.20) | copy-start | bytes 884740
  66.8 13.0 %copy-start.3 = (f32[1,1,3]{2,1,0:T(1,128)S(1)}, f32[1,1,3]{2,1,0:T(1,128)}, u32[]{:S(2)}) copy-start(f32[1,1,3]{2,1,0:T(1,128)} %param.19) | copy-start | bytes 40
  70.0 10.3 %copy-start = (f32[3,1,4096]{2,1,0:T(1,128)S(1)}, f32[3,1,4096]{2,1,0:T(1,128)}, u32[]{:S(2)}) copy-start(f32[3,1,4096]{2,1,0:T(1,128)} %mul.548.refs_3_) | copy-start | bytes 147460
  70.0 9.1 %collective-permute-start.5 = (f32[1,3,3,4096]{3,2,1,0:T(4,128)}, f32[1,3,3,4096]{3,2,1,0:T(4,128)S(1)}, u32[]{:S(2)}, u32[]{:S(2)}) collective-permute-start(f32[1,3,3,4096]{3,2,1,0:T(4,128)} %bitcast.309), channel_id=1, source_target_pairs={{4,0},{8,4},{12,8},{16,12},{20,16},{24,20},{28,24},{5,1},{9,5},{13... | collective-permute-start | bytes 442376 | tf_op jit(solution)/shard_map/ppermute | solution.py:28
  74.3 9.6 %collective-permute-start.4 = (f32[1,3,4,4096]{3,2,1,0:T(4,128)}, f32[1,3,4,4096]{3,2,1,0:T(4,128)S(1)}, u32[]{:S(2)}, u32[]{:S(2)}) collective-permute-start(f32[1,3,4,4096]{3,2,1,0:T(4,128)} %bitcast.307), channel_id=1, source_target_pairs={{0,4},{4,8},{8,12},{12,16},{16,20},{20,24},{24,28},{1,5},{5,9},{9,... | collective-permute-start | bytes 589832 | tf_op jit(solution)/shard_map/ppermute | solution.py:28
  77.8 8.1 %collective-permute-start.7 = (f32[1,3,3,64,128]{4,3,1,2,0:T(8,128)S(1)}, f32[1,3,3,64,128]{4,3,1,2,0:T(8,128)S(1)}, u32[]{:S(2)}, u32[]{:S(2)}) collective-permute-start(f32[1,3,3,64,128]{4,3,1,2,0:T(8,128)S(1)} %bitcast.296), channel_id=1, source_target_pairs={{0,3},{1,0},{2,1},{3,2},{4,7},{5,4},{6,5},{7,6},{8,11},{9,8},{10,9... | collective-permute-start | bytes 884744 | tf_op jit(solution)/shard_map/ppermute | solution.py:33
  78.1 9.0 %collective-permute-start.6 = (f32[1,3,3,64,128]{4,3,1,2,0:T(8,128)S(1)}, f32[1,3,3,64,128]{4,3,1,2,0:T(8,128)S(1)}, u32[]{:S(2)}, u32[]{:S(2)}) collective-permute-start(f32[1,3,3,64,128]{4,3,1,2,0:T(8,128)S(1)} %bitcast.298), channel_id=1, source_target_pairs={{0,1},{1,2},{2,3},{3,0},{4,5},{5,6},{6,7},{7,4},{8,9},{9,10},{10,1... | collective-permute-start | bytes 884744 | tf_op jit(solution)/shard_map/ppermute | solution.py:33

commit v7 on v6

--- a/solution.py
+++ b/solution.py
@@ -229,24 +229,22 @@
         return m * (11.0 / 6.0 * p0 - 3.0 * p1 + 1.5 * p2 - p3 / 3.0)
     if emit_sides:
         m_row = jnp.full((1, nn), m, f32)
-        xh_ref[0, 0:1, :] = u[n - 1:n]
-        xh_ref[0, 1:2, :] = slope(u[n - 1:n], u[n - 2:n - 1], u[n - 3:n - 2], u[n - 4:n - 3])
-        xh_ref[0, 2:3, :] = m_row
-        xh_ref[0, 3:4, :] = jnp.full((1, nn), code_ref[0], f32)
-        xl_ref[0, 0:1, :] = u[0:1]
-        xl_ref[0, 1:2, :] = slope(u[0:1], u[1:2], u[2:3], u[3:4])
-        xl_ref[0, 2:3, :] = m_row
-        m_sq = jnp.full((n, w2), m, f32)
+        xh_ref[0, 0:1, :] = m * u[n - 1:n] + 0.5 * slope(u[n - 1:n], u[n - 2:n - 1], u[n - 3:n - 2], u[n - 4:n - 3])
+        xh_ref[0, 1:2, :] = m_row
+        xh_ref[0, 2:3, :] = jnp.full((1, nn), code_ref[0], f32)
+        xl_ref[0, 0:1, :] = m * u[0:1] + 0.5 * slope(u[0:1], u[1:2], u[2:3], u[3:4])
+        xl_ref[0, 1:2, :] = m_row
+        m_sq = jnp.full((n, n), m, f32)
         c_hi = u[:, nn - w2:]
         c_hi2 = u[:, nn - 2 * w2:nn - w2]
-        yh_ref[0, 0] = c_hi
-        yh_ref[0, 1] = slope(c_hi, pltpu.roll(c_hi, n, 1), c_hi2, pltpu.roll(c_hi2, n, 1))
-        yh_ref[0, 2] = m_sq
+        s_hi = m * c_hi + 0.5 * slope(c_hi, pltpu.roll(c_hi, n, 1), c_hi2, pltpu.roll(c_hi2, n, 1))
+        yh_ref[0, 0] = pltpu.roll(s_hi, n, 1)[:, :n]
+        yh_ref[0, 1] = m_sq
         c_lo = u[:, :w2]
         c_lo2 = u[:, w2:2 * w2]
-        yl_ref[0, 0] = c_lo
-        yl_ref[0, 1] = slope(c_lo, pltpu.roll(c_lo, n, 1), c_lo2, pltpu.roll(c_lo2, n, 1))
-        yl_ref[0, 2] = m_sq
+        s_lo = m * c_lo + 0.5 * slope(c_lo, pltpu.roll(c_lo, n, 1), c_lo2, pltpu.roll(c_lo2, n, 1))
+        yl_ref[0, 0] = s_lo[:, :n]
+        yl_ref[0, 1] = m_sq
 
 
 def kernel_sweep(rhs, moduli, code, faces=None, emit_u=True, emit_sides=False, interpret=False):
@@ -268,9 +266,9 @@
         out_specs.append(comp3((n, nn)))
         out_shape.append(jax.ShapeDtypeStruct(rhs.shape, f32))
     if emit_sides:
-        out_specs += [comp3((4, nn)), comp3((3, nn)), comp3((3, n, 2 * n)), comp3((3, n, 2 * n))]
-        out_shape += [jax.ShapeDtypeStruct((ncomp, 4, nn), f32), jax.ShapeDtypeStruct((ncomp, 3, nn), f32),
-                      jax.ShapeDtypeStruct((ncomp, 3, n, 2 * n), f32), jax.ShapeDtypeStruct((ncomp, 3, n, 2 * n), f32)]
+        out_specs += [comp3((3, nn)), comp3((2, nn)), comp3((2, n, n)), comp3((2, n, n))]
+        out_shape += [jax.ShapeDtypeStruct((ncomp, 3, nn), f32), jax.ShapeDtypeStruct((ncomp, 2, nn), f32),
+                      jax.ShapeDtypeStruct((ncomp, 2, n, n), f32), jax.ShapeDtypeStruct((ncomp, 2, n, n), f32)]
     kernel = functools.partial(solve_kernel, with_faces=faces is not None, emit_u=emit_u, emit_sides=emit_sides)
     return pl.pallas_call(
         kernel,
@@ -343,26 +341,16 @@
     return current + omega_step * smoothed.reshape(residue.shape)
 
 
-def x_side(packet):
-    return (packet[:, :, 0], packet[:, :, 1])
-
-
-def y_side(packet, low):
-    extent = packet.shape[-2]
-    part = packet[..., :extent] if low else packet[..., extent:]
-    return (part[:, :, 0], part[:, :, 1])
-
-
-def oriented(side, codes, extent):
-    return (orient(side[0], codes, extent), orient(side[1], codes, extent))
-
-
-def square_update(current, side_a, side_b, moduli_a, moduli_b, omega_step, tangent):
-    weight_a = moduli_a[..., None, None]
-    weight_b = moduli_b[..., None, None]
-    residue = (
-        weight_a * side_a[0] + weight_b * side_b[0] + traction_mix * (side_a[1] + side_b[1])
-    ) / (weight_a + weight_b) - current
+def flat_update(current, sum_a, sum_b, moduli_a, moduli_b, omega_step, tangent):
+    extent = tangent.shape[0]
+    residue = (sum_a + sum_b) / (moduli_a + moduli_b)[..., None] - current
+    rows_view = residue.reshape(residue.shape[:-1] + (residue.shape[-1] // extent, extent))
+    smoothed = rows_view + penalty_mix * jnp.einsum("...z,zk->...k", rows_view, tangent, precision=highest)
+    return current + omega_step * smoothed.reshape(residue.shape)
+
+
+def square_update(current, sum_a, sum_b, moduli_a, moduli_b, omega_step, tangent):
+    residue = (sum_a + sum_b) / (moduli_a + moduli_b)[..., None, None] - current
     smoothed = residue + penalty_mix * jnp.einsum("...z,zk->...k", residue, tangent, precision=highest)
     return current + omega_step * smoothed
 
@@ -400,30 +388,30 @@
         nxt = jnp.concatenate([yl[1:], shifted_2(yl[:1], "face", -1)], 0)
         prv = jnp.concatenate([shifted_2(yh[-1:], "face", 1), yh[:-1]], 0)
         if sweep == 0:
-            moduli_up = upper[:, :, 2, 0]
-            moduli_down = lower[:, :, 2, 0]
-            codes_down = lower[:, 0, 3, 0].astype(jnp.int32)
-            moduli_next = nxt[:, :, 2, 0, 0]
-            moduli_prev = prv[:, :, 2, 0, 0]
+            moduli_up = upper[:, :, 1, 0]
+            moduli_down = lower[:, :, 1, 0]
+            codes_down = lower[:, 0, 2, 0].astype(jnp.int32)
+            moduli_next = nxt[:, :, 1, 0, 0]
+            moduli_prev = prv[:, :, 1, 0, 0]
         lam_x_up = (
-            trace_update(
-                lam_x_up, x_side(xh), oriented(x_side(upper), codes_here, extent),
+            flat_update(
+                lam_x_up, xh[:, :, 0], orient(upper[:, :, 0], codes_here, extent),
                 moduli, moduli_up, omegas[sweep], tangent,
             )
             * has_up
         )
         lam_x_down = (
-            trace_update(
-                lam_x_down, x_side(lower), oriented(x_side(xl), codes_down, extent),
+            flat_update(
+                lam_x_down, lower[:, :, 0], orient(xl[:, :, 0], codes_down, extent),
                 moduli_down, moduli, omegas[sweep], tangent,
             )
             * has_down
         )
         lam_y_next = square_update(
-            lam_y_next, y_side(yh, False), y_side(nxt, True), moduli, moduli_next, omegas[sweep], tangent
+            lam_y_next, yh[:, :, 0], nxt[:, :, 0], moduli, moduli_next, omegas[sweep], tangent
         )
         lam_y_prev = square_update(
-            lam_y_prev, y_side(prv, False), y_side(yl, True), moduli_prev, moduli, omegas[sweep], tangent
+            lam_y_prev, prv[:, :, 0], yl[:, :, 0], moduli_prev, moduli, omegas[sweep], tangent
         )
         x_low = orient(lam_x_down, codes_down, extent)
         yadd = jnp.concatenate([lam_y_prev, lam_y_next], -1)

time: 113 us -> 113 us (level)
  waiting for transfers between devices: 5.67 us -> 9.53 us
  local copies, waits for them, and re-layouts: 16.4 us -> 13.8 us
    ppermute x4, waiting for transfers between devices: 0.92 us -> 4.6 us  [shifted_2(): lax.ppermute(shard, axis, [(i, (i + by) % length) for i in range(length)])]
    slice x13, local copies, waits for them, and re-layouts: 7.35 us -> 5.72 us  [the longest x2 2.14 us: shards(): xh[:, :, 0]]
  transfers between devices with their start and end apart: 8 -> 8, of which waited for: 4 -> 3; matrix products, arithmetic and copies ran while one was open for 12% -> 9% of each run, Pallas kernels for 0% -> 0%
where the time goes in v7:
time: 113 us; the launch traced here: 112 us
  Pallas kernels  69.5 us (62%)
  local copies, waits for them, and re-layouts  13.8 us (12%)
  starting transfers between devices  13 us (12%)
  waiting for transfers between devices  9.53 us (8%)
  matrix products  2.39 us (2%)
  other arithmetic  2.24 us (2%)
  between operations  1.74 us (2%)
    pallas_call x3, Pallas kernels, kernel_sweep(): pl.pallas_call(kernel, grid=(ncomp,), in_specs=in_specs, out_specs=out_sp...  69.5 us
    ppermute x4, starting transfers between devices, shifted(): return lax.ppermute(shard, axis, pairs)  11.7 us
    ppermute x4, waiting for transfers between devices, shifted(): return lax.ppermute(shard, axis, pairs)  4.92 us
    ppermute x4, waiting for transfers between devices, shifted_2(): lax.ppermute(shard, axis, [(i, (i + by) % length) for i in range(length)])  4.6 us
    pallas_call x4, local copies, waits for them, and re-layouts, kernel_sweep(): pl.pallas_call(kernel, grid=(ncomp,), in_specs=in_specs, out_specs=out_sp...  3.77 us
  transfers between devices with their start and end apart: 8, of which 3 were waited for; matrix products, arithmetic and copies ran while one was open for 9% of the time, Pallas kernels for 0%

profile of v7, /device:TPU:24, one launch (start us, length us, event | category | flops | bytes accessed | tf_op | source)
XLA Modules:
  0.0 112.1 jit_solution(13515814069908559395)
XLA Ops:
  0.7 23.2 %shard_map.172 = (f32[3,3,4096]{2,1,0:T(4,128)}, f32[3,2,4096]{2,1,0:T(2,128)}, f32[3,2,64,64]{3,2,1,0:T(8,128)}, f32[3,2,64,64]{3,2,1,0:T(8,128)}) custom-call(f32[3]{0:T(128)} %bitcast.174, f32[3,64,4096]{2,1,0:T(8,128)} %bitcast.153, bf16[64,256]{1,0:T(8,128)(2,1)} %constant.107.clone.refs_2_.refs_5_, bf16[1024,256]{1,0:T(8,128)(2,1)} %constant.108.clone.refs_3_.refs_6_, ...), custom_call_target="tpu_custom_call" | custom-call | tf_op jit(solution)/shard_map/pallas_call | solution.py:273
  23.8 3.3 %collective-permute-start.1 = (f32[1,3,2,4096]{3,2,1,0:T(2,128)}, f32[1,3,2,4096]{3,2,1,0:T(2,128)S(1)}, u32[]{:S(2)}, u32[]{:S(2)}) collective-permute-start(f32[1,3,2,4096]{3,2,1,0:T(2,128)} %bitcast.166), channel_id=1, source_target_pairs={{4,0},{8,4},{12,8},{16,12},{20,16},{24,20},{28,24},{5,1},{9,5},{13... | collective-permute-start | bytes 294920 | tf_op jit(solution)/shard_map/ppermute | solution.py:28
  27.1 0.9 copy.43
  28.1 0.7 collective-permute-start.3
  28.8 0.9 copy.44
  29.7 0.1 collective-permute-start.2
  29.8 2.5 %collective-permute-start = (f32[1,3,3,4096]{3,2,1,0:T(4,128)}, f32[1,3,3,4096]{3,2,1,0:T(4,128)S(1)}, u32[]{:S(2)}, u32[]{:S(2)}) collective-permute-start(f32[1,3,3,4096]{3,2,1,0:T(4,128)} %bitcast.170), channel_id=1, source_target_pairs={{0,4},{4,8},{8,12},{12,16},{16,20},{20,24},{24,28},{1,5},{5,9},{9,... | collective-permute-start | bytes 442376 | tf_op jit(solution)/shard_map/ppermute | solution.py:28
  32.4 1.1 slice_reduce_fusion.5
  33.5 1.0 slice_reduce_fusion.6
  34.5 0.1 squeeze.57
  34.6 0.1 squeeze.55
  34.7 0.1 reshape_squeeze.14
  34.9 0.1 slice_reduce_fusion.4
  35.0 0.1 reshape_squeeze.15
  35.2 0.1 slice_reduce_fusion.8
  35.3 0.1 slice_reduce_fusion.10
  35.4 0.1 rev.38
  35.5 0.1 slice_reduce_fusion.9
  35.6 4.9 %collective-permute-done = f32[1,3,3,4096]{3,2,1,0:T(4,128)S(1)} collective-permute-done((f32[1,3,3,4096]{3,2,1,0:T(4,128)}, f32[1,3,3,4096]{3,2,1,0:T(4,128)S(1)}, u32[]{:S(2)}, u32[]{:S(2)}) %collective-permute-start) | collective-permute-done | bytes 147488 | tf_op jit(solution)/shard_map/ppermute | solution.py:28
  40.6 0.5 slice.84
  41.7 0.1 slice_reduce_fusion.7
  41.9 0.1 squeeze.54
  42.0 0.1 squeeze.52
  42.1 0.1 slice_reduce_fusion.11
  42.2 0.3 fusion.44
  42.6 0.7 mul.220.refs_3_
  43.3 0.1 rev.35
  43.4 0.3 fusion.47
  43.7 0.1 reverse.15
  43.9 0.7 reshape_squeeze_reshape.8.refs_2_
  44.6 0.3 fusion.7
  44.9 0.3 fusion.9
  45.2 0.7 maximum_bitcast_fusion.refs_4_
  45.9 23.2 %shard_map.173 = (f32[3,3,4096]{2,1,0:T(4,128)}, f32[3,2,4096]{2,1,0:T(2,128)}, f32[3,2,64,64]{3,2,1,0:T(8,128)}, f32[3,2,64,64]{3,2,1,0:T(8,128)}) custom-call(f32[3]{0:T(128)} %bitcast.175, f32[3,64,4096]{2,1,0:T(8,128)} %bitcast.154, f32[3,1,4096]{2,1,0:T(1,128)} %reshape_squeeze_reshape.8.refs_2_, f32[3,1,4096]{2,1,0:T(1,128)} %mul.220.refs_3_, ...), custom_call_target="tpu_custom_call" | custom-call | tf_op jit(solution)/shard_map/pallas_call | solution.py:273
  69.1 1.1 slice_reduce_fusion.1
  70.2 0.1 squeeze.64
  70.3 0.1 squeeze.63
  70.4 1.0 slice_reduce_fusion.2
  71.5 1.9 %collective-permute-start.5 = (f32[1,3,2,4096]{3,2,1,0:T(2,128)}, f32[1,3,2,4096]{3,2,1,0:T(2,128)S(1)}, u32[]{:S(2)}, u32[]{:S(2)}) collective-permute-start(f32[1,3,2,4096]{3,2,1,0:T(2,128)} %bitcast.169), channel_id=1, source_target_pairs={{4,0},{8,4},{12,8},{16,12},{20,16},{24,20},{28,24},{5,1},{9,5},{13... | collective-permute-start | bytes 294920 | tf_op jit(solution)/shard_map/ppermute | solution.py:28
  73.4 3.9 %collective-permute-start.4 = (f32[1,3,3,4096]{3,2,1,0:T(4,128)}, f32[1,3,3,4096]{3,2,1,0:T(4,128)S(1)}, u32[]{:S(2)}, u32[]{:S(2)}) collective-permute-start(f32[1,3,3,4096]{3,2,1,0:T(4,128)} %bitcast.173), channel_id=1, source_target_pairs={{0,4},{4,8},{8,12},{12,16},{16,20},{20,24},{24,28},{1,5},{5,9},{9,... | collective-permute-start | bytes 442376 | tf_op jit(solution)/shard_map/ppermute | solution.py:28
  77.3 0.1 reshape_squeeze.16
  77.5 0.1 rev.40
  77.6 0.9 copy.42
  78.5 0.9 copy.41
  79.5 0.2 collective-permute-start.7
  79.7 0.4 collective-permute-start.6
  80.0 0.1 slice_reduce_fusion
  80.2 0.1 reshape_squeeze.17
  80.3 0.1 rev.43
  80.4 0.3 fusion.12
  80.7 0.1 mul.219
  80.9 0.7 add_multiply_fusion.refs_3_
  81.5 2.8 %collective-permute-done.7 = f32[1,3,2,64,64]{4,3,1,2,0:T(8,128)S(1)} collective-permute-done((f32[1,3,2,64,64]{4,3,1,2,0:T(8,128)S(1)}, f32[1,3,2,64,64]{4,3,1,2,0:T(8,128)S(1)}, u32[]{:S(2)}, u32[]{:S(2)}) %collective-permute-start.7) | collective-permute-done | bytes 98336 | tf_op jit(solution)/shard_map/ppermute | solution.py:33
  84.3 0.3 fusion.16
  84.6 1.8 %collective-permute-done.6 = f32[1,3,2,64,64]{4,3,1,2,0:T(8,128)S(1)} collective-permute-done((f32[1,3,2,64,64]{4,3,1,2,0:T(8,128)S(1)}, f32[1,3,2,64,64]{4,3,1,2,0:T(8,128)S(1)}, u32[]{:S(2)}, u32[]{:S(2)}) %collective-permute-start.6) | collective-permute-done | bytes 98336 | tf_op jit(solution)/shard_map/ppermute | solution.py:33
  86.4 0.3 fusion.14
  86.7 0.7 maximum_bitcast_fusion.1.refs_4_
  87.5 0.1 slice_reduce_fusion.3
  87.6 0.1 squeeze.62
  87.7 0.1 squeeze.61
  87.8 0.3 fusion.11
  88.2 0.1 reverse.17
  88.3 0.7 reshape_squeeze_reshape.9.refs_2_
  89.0 23.1 %shard_map.174 = f32[3,64,4096]{2,1,0:T(8,128)} custom-call(f32[3]{0:T(128)} %bitcast.176, f32[3,64,4096]{2,1,0:T(8,128)} %bitcast.155, f32[3,1,4096]{2,1,0:T(1,128)} %reshape_squeeze_reshape.9.refs_2_, f32[3,1,4096]{2,1,0:T(1,128)} %add_multiply_fusion.refs_3_, f32[3,64,128]{2,1,0:T(8,128)} %maximum_bitcast_fusion.1.refs_4_, ...), custom_call_target="tpu_custom_call" | custom-call | tf_op jit(solution)/shard_map/pallas_call | solution.py:273
  (25 shorter events, 0.2 us)
Async XLA Ops:
  0.7 41.6 %copy-start.1 = (f32[1,1,3]{2,1,0:T(1,128)S(1)}, f32[1,1,3]{2,1,0:T(1,128)}, u32[]{:S(2)}) copy-start(f32[1,1,3]{2,1,0:T(1,128)} %param.19) | copy-start | bytes 40
  23.8 11.1 %collective-permute-start.1 = (f32[1,3,2,4096]{3,2,1,0:T(2,128)}, f32[1,3,2,4096]{3,2,1,0:T(2,128)S(1)}, u32[]{:S(2)}, u32[]{:S(2)}) collective-permute-start(f32[1,3,2,4096]{3,2,1,0:T(2,128)} %bitcast.166), channel_id=1, source_target_pairs={{4,0},{8,4},{12,8},{16,12},{20,16},{24,20},{28,24},{5,1},{9,5},{13... | collective-permute-start | bytes 294920 | tf_op jit(solution)/shard_map/ppermute | solution.py:28
  28.1 7.1 %collective-permute-start.3 = (f32[1,3,2,64,64]{4,3,1,2,0:T(8,128)S(1)}, f32[1,3,2,64,64]{4,3,1,2,0:T(8,128)S(1)}, u32[]{:S(2)}, u32[]{:S(2)}) collective-permute-start(f32[1,3,2,64,64]{4,3,1,2,0:T(8,128)S(1)} %bitcast.156), channel_id=1, source_target_pairs={{0,3},{1,0},{2,1},{3,2},{4,7},{5,4},{6,5},{7,6},{8,11},{9,8},{10,9... | collective-permute-start | bytes 294920 | tf_op jit(solution)/shard_map/ppermute | solution.py:33
  29.7 5.8 %collective-permute-start.2 = (f32[1,3,2,64,64]{4,3,1,2,0:T(8,128)S(1)}, f32[1,3,2,64,64]{4,3,1,2,0:T(8,128)S(1)}, u32[]{:S(2)}, u32[]{:S(2)}) collective-permute-start(f32[1,3,2,64,64]{4,3,1,2,0:T(8,128)S(1)} %bitcast.158), channel_id=1, source_target_pairs={{0,1},{1,2},{2,3},{3,0},{4,5},{5,6},{6,7},{7,4},{8,9},{9,10},{10,1... | collective-permute-start | bytes 294920 | tf_op jit(solution)/shard_map/ppermute | solution.py:33
  29.8 10.8 %collective-permute-start = (f32[1,3,3,4096]{3,2,1,0:T(4,128)}, f32[1,3,3,4096]{3,2,1,0:T(4,128)S(1)}, u32[]{:S(2)}, u32[]{:S(2)}) collective-permute-start(f32[1,3,3,4096]{3,2,1,0:T(4,128)} %bitcast.170), channel_id=1, source_target_pairs={{0,4},{4,8},{8,12},{12,16},{16,20},{20,24},{24,28},{1,5},{5,9},{9,... | collective-permute-start | bytes 442376 | tf_op jit(solution)/shard_map/ppermute | solution.py:28
  69.1 11.7 %copy-start = (f32[3,1,4096]{2,1,0:T(1,128)S(1)}, f32[3,1,4096]{2,1,0:T(1,128)}, u32[]{:S(2)}) copy-start(f32[3,1,4096]{2,1,0:T(1,128)} %mul.220.refs_3_) | copy-start | bytes 147460
  71.5 8.6 %collective-permute-start.5 = (f32[1,3,2,4096]{3,2,1,0:T(2,128)}, f32[1,3,2,4096]{3,2,1,0:T(2,128)S(1)}, u32[]{:S(2)}, u32[]{:S(2)}) collective-permute-start(f32[1,3,2,4096]{3,2,1,0:T(2,128)} %bitcast.169), channel_id=1, source_target_pairs={{4,0},{8,4},{12,8},{16,12},{20,16},{24,20},{28,24},{5,1},{9,5},{13... | collective-permute-start | bytes 294920 | tf_op jit(solution)/shard_map/ppermute | solution.py:28
  73.4 14.1 %collective-permute-start.4 = (f32[1,3,3,4096]{3,2,1,0:T(4,128)}, f32[1,3,3,4096]{3,2,1,0:T(4,128)S(1)}, u32[]{:S(2)}, u32[]{:S(2)}) collective-permute-start(f32[1,3,3,4096]{3,2,1,0:T(4,128)} %bitcast.173), channel_id=1, source_target_pairs={{0,4},{4,8},{8,12},{12,16},{16,20},{20,24},{24,28},{1,5},{5,9},{9,... | collective-permute-start | bytes 442376 | tf_op jit(solution)/shard_map/ppermute | solution.py:28
  79.5 4.8 %collective-permute-start.7 = (f32[1,3,2,64,64]{4,3,1,2,0:T(8,128)S(1)}, f32[1,3,2,64,64]{4,3,1,2,0:T(8,128)S(1)}, u32[]{:S(2)}, u32[]{:S(2)}) collective-permute-start(f32[1,3,2,64,64]{4,3,1,2,0:T(8,128)S(1)} %bitcast.160), channel_id=1, source_target_pairs={{0,3},{1,0},{2,1},{3,2},{4,7},{5,4},{6,5},{7,6},{8,11},{9,8},{10,9... | collective-permute-start | bytes 294920 | tf_op jit(solution)/shard_map/ppermute | solution.py:33
  79.7 6.8 %collective-permute-start.6 = (f32[1,3,2,64,64]{4,3,1,2,0:T(8,128)S(1)}, f32[1,3,2,64,64]{4,3,1,2,0:T(8,128)S(1)}, u32[]{:S(2)}, u32[]{:S(2)}) collective-permute-start(f32[1,3,2,64,64]{4,3,1,2,0:T(8,128)S(1)} %bitcast.162), channel_id=1, source_target_pairs={{0,1},{1,2},{2,3},{3,0},{4,5},{5,6},{6,7},{7,4},{8,9},{9,10},{10,1... | collective-permute-start | bytes 294920 | tf_op jit(solution)/shard_map/ppermute | solution.py:33

commit v8 on v7

--- a/solution.py
+++ b/solution.py
@@ -195,7 +195,7 @@
     wy = wy_ref[...]
     ez = ez_ref[...]
     XG = 4
-    GPI = 4
+    GPI = 8
 
     def body(it_, carry):
         lhs = []

time: 113 us -> 106 us (0.938)
  Pallas kernels: 69.5 us -> 62.4 us
    pallas_call x3, Pallas kernels: 69.5 us -> 62.4 us  [kernel_sweep(): pl.pallas_call(kernel, grid=(ncomp,), in_specs=in_specs, out_specs=out_sp...]
where the time goes in v8:
time: 106 us; the launch traced here: 105 us
  Pallas kernels  62.4 us (59%)
  local copies, waits for them, and re-layouts  13.8 us (13%)
  starting transfers between devices  13 us (12%)
  waiting for transfers between devices  9.54 us (9%)
  matrix products  2.39 us (2%)
  other arithmetic  2.24 us (2%)
  between operations  1.74 us (2%)
    pallas_call x3, Pallas kernels, kernel_sweep(): pl.pallas_call(kernel, grid=(ncomp,), in_specs=in_specs, out_specs=out_sp...  62.4 us
    ppermute x4, starting transfers between devices, shifted(): return lax.ppermute(shard, axis, pairs)  11.7 us
    ppermute x4, waiting for transfers between devices, shifted(): return lax.ppermute(shard, axis, pairs)  4.93 us
    ppermute x4, waiting for transfers between devices, shifted_2(): lax.ppermute(shard, axis, [(i, (i + by) % length) for i in range(length)])  4.61 us
    pallas_call x4, local copies, waits for them, and re-layouts, kernel_sweep(): pl.pallas_call(kernel, grid=(ncomp,), in_specs=in_specs, out_specs=out_sp...  3.77 us
    slice x2, local copies, waits for them, and re-layouts, shards(): xh[:, :, 0]  2.14 us
  transfers between devices with their start and end apart: 8, of which 3 were waited for; matrix products, arithmetic and copies ran while one was open for 9% of the time, Pallas kernels for 0%

profile of v8, /device:TPU:24, one launch (start us, length us, event | category | flops | bytes accessed | tf_op | source)
XLA Modules:
  0.0 105.1 jit_solution(14190709238835627859)
XLA Ops:
  0.7 20.8 %shard_map.172 = (f32[3,3,4096]{2,1,0:T(4,128)}, f32[3,2,4096]{2,1,0:T(2,128)}, f32[3,2,64,64]{3,2,1,0:T(8,128)}, f32[3,2,64,64]{3,2,1,0:T(8,128)}) custom-call(f32[3]{0:T(128)} %bitcast.174, f32[3,64,4096]{2,1,0:T(8,128)} %bitcast.153, bf16[64,256]{1,0:T(8,128)(2,1)} %constant.107.clone.refs_2_.refs_5_, bf16[1024,256]{1,0:T(8,128)(2,1)} %constant.108.clone.refs_3_.refs_6_, ...), custom_call_target="tpu_custom_call" | custom-call | tf_op jit(solution)/shard_map/pallas_call | solution.py:273
  21.5 3.3 %collective-permute-start.1 = (f32[1,3,2,4096]{3,2,1,0:T(2,128)}, f32[1,3,2,4096]{3,2,1,0:T(2,128)S(1)}, u32[]{:S(2)}, u32[]{:S(2)}) collective-permute-start(f32[1,3,2,4096]{3,2,1,0:T(2,128)} %bitcast.166), channel_id=1, source_target_pairs={{4,0},{8,4},{12,8},{16,12},{20,16},{24,20},{28,24},{5,1},{9,5},{13... | collective-permute-start | bytes 294920 | tf_op jit(solution)/shard_map/ppermute | solution.py:28
  24.8 0.9 copy.43
  25.7 0.7 collective-permute-start.3
  26.4 0.9 copy.44
  27.4 0.1 collective-permute-start.2
  27.4 2.5 %collective-permute-start = (f32[1,3,3,4096]{3,2,1,0:T(4,128)}, f32[1,3,3,4096]{3,2,1,0:T(4,128)S(1)}, u32[]{:S(2)}, u32[]{:S(2)}) collective-permute-start(f32[1,3,3,4096]{3,2,1,0:T(4,128)} %bitcast.170), channel_id=1, source_target_pairs={{0,4},{4,8},{8,12},{12,16},{16,20},{20,24},{24,28},{1,5},{5,9},{9,... | collective-permute-start | bytes 442376 | tf_op jit(solution)/shard_map/ppermute | solution.py:28
  30.0 1.1 %slice_reduce_fusion.5 = f32[3,4096]{1,0:T(4,128)S(1)} fusion(f32[1,3,3,4096]{3,2,1,0:T(4,128)} %bitcast.171), kind=kLoop, calls=%fused_computation.88 | loop fusion | bytes 98304 | tf_op jit(solution)/shard_map/slice | solution.py:398
  31.1 1.0 slice_reduce_fusion.6
  32.1 0.1 squeeze.57
  32.3 0.1 squeeze.55
  32.4 0.1 reshape_squeeze.14
  32.5 0.1 slice_reduce_fusion.4
  32.7 0.1 reshape_squeeze.15
  32.9 0.1 slice_reduce_fusion.8
  33.0 0.1 slice_reduce_fusion.10
  33.1 0.1 rev.38
  33.2 0.1 slice_reduce_fusion.9
  33.3 4.9 %collective-permute-done = f32[1,3,3,4096]{3,2,1,0:T(4,128)S(1)} collective-permute-done((f32[1,3,3,4096]{3,2,1,0:T(4,128)}, f32[1,3,3,4096]{3,2,1,0:T(4,128)S(1)}, u32[]{:S(2)}, u32[]{:S(2)}) %collective-permute-start) | collective-permute-done | bytes 147488 | tf_op jit(solution)/shard_map/ppermute | solution.py:28
  38.2 0.5 slice.84
  39.4 0.1 slice_reduce_fusion.7
  39.5 0.1 squeeze.54
  39.6 0.1 squeeze.52
  39.8 0.1 slice_reduce_fusion.11
  39.9 0.3 fusion.44
  40.2 0.7 mul.220.refs_3_
  40.9 0.1 rev.35
  41.0 0.3 fusion.47
  41.4 0.1 reverse.15
  41.5 0.7 reshape_squeeze_reshape.8.refs_2_
  42.2 0.3 fusion.7
  42.5 0.3 fusion.9
  42.8 0.7 maximum_bitcast_fusion.refs_4_
  43.6 20.8 %shard_map.173 = (f32[3,3,4096]{2,1,0:T(4,128)}, f32[3,2,4096]{2,1,0:T(2,128)}, f32[3,2,64,64]{3,2,1,0:T(8,128)}, f32[3,2,64,64]{3,2,1,0:T(8,128)}) custom-call(f32[3]{0:T(128)} %bitcast.175, f32[3,64,4096]{2,1,0:T(8,128)} %bitcast.154, f32[3,1,4096]{2,1,0:T(1,128)} %reshape_squeeze_reshape.8.refs_2_, f32[3,1,4096]{2,1,0:T(1,128)} %mul.220.refs_3_, ...), custom_call_target="tpu_custom_call" | custom-call | tf_op jit(solution)/shard_map/pallas_call | solution.py:273
  64.4 1.1 %slice_reduce_fusion.1 = f32[3,4096]{1,0:T(4,128)S(1)} fusion(f32[1,3,3,4096]{3,2,1,0:T(4,128)} %bitcast.172), kind=kLoop, calls=%fused_computation.84 | loop fusion | bytes 98304 | tf_op jit(solution)/shard_map/slice | solution.py:398
  65.5 0.1 squeeze.64
  65.6 0.1 squeeze.63
  65.7 1.0 slice_reduce_fusion.2
  66.8 1.9 %collective-permute-start.5 = (f32[1,3,2,4096]{3,2,1,0:T(2,128)}, f32[1,3,2,4096]{3,2,1,0:T(2,128)S(1)}, u32[]{:S(2)}, u32[]{:S(2)}) collective-permute-start(f32[1,3,2,4096]{3,2,1,0:T(2,128)} %bitcast.169), channel_id=1, source_target_pairs={{4,0},{8,4},{12,8},{16,12},{20,16},{24,20},{28,24},{5,1},{9,5},{13... | collective-permute-start | bytes 294920 | tf_op jit(solution)/shard_map/ppermute | solution.py:28
  68.7 3.9 %collective-permute-start.4 = (f32[1,3,3,4096]{3,2,1,0:T(4,128)}, f32[1,3,3,4096]{3,2,1,0:T(4,128)S(1)}, u32[]{:S(2)}, u32[]{:S(2)}) collective-permute-start(f32[1,3,3,4096]{3,2,1,0:T(4,128)} %bitcast.173), channel_id=1, source_target_pairs={{0,4},{4,8},{8,12},{12,16},{16,20},{20,24},{24,28},{1,5},{5,9},{9,... | collective-permute-start | bytes 442376 | tf_op jit(solution)/shard_map/ppermute | solution.py:28
  72.6 0.1 reshape_squeeze.16
  72.8 0.1 rev.40
  72.9 0.9 copy.42
  73.8 0.9 copy.41
  74.8 0.2 collective-permute-start.7
  75.0 0.4 collective-permute-start.6
  75.3 0.1 slice_reduce_fusion
  75.5 0.1 reshape_squeeze.17
  75.6 0.1 rev.43
  75.7 0.3 fusion.12
  76.0 0.1 mul.219
  76.2 0.7 add_multiply_fusion.refs_3_
  76.8 2.8 %collective-permute-done.7 = f32[1,3,2,64,64]{4,3,1,2,0:T(8,128)S(1)} collective-permute-done((f32[1,3,2,64,64]{4,3,1,2,0:T(8,128)S(1)}, f32[1,3,2,64,64]{4,3,1,2,0:T(8,128)S(1)}, u32[]{:S(2)}, u32[]{:S(2)}) %collective-permute-start.7) | collective-permute-done | bytes 98336 | tf_op jit(solution)/shard_map/ppermute | solution.py:33
  79.6 0.3 fusion.16
  79.9 1.8 %collective-permute-done.6 = f32[1,3,2,64,64]{4,3,1,2,0:T(8,128)S(1)} collective-permute-done((f32[1,3,2,64,64]{4,3,1,2,0:T(8,128)S(1)}, f32[1,3,2,64,64]{4,3,1,2,0:T(8,128)S(1)}, u32[]{:S(2)}, u32[]{:S(2)}) %collective-permute-start.6) | collective-permute-done | bytes 98336 | tf_op jit(solution)/shard_map/ppermute | solution.py:33
  81.7 0.3 fusion.14
  82.0 0.7 maximum_bitcast_fusion.1.refs_4_
  82.8 0.1 slice_reduce_fusion.3
  82.9 0.1 squeeze.62
  83.0 0.1 squeeze.61
  83.1 0.3 fusion.11
  83.5 0.1 reverse.17
  83.6 0.7 reshape_squeeze_reshape.9.refs_2_
  84.3 20.8 %shard_map.174 = f32[3,64,4096]{2,1,0:T(8,128)} custom-call(f32[3]{0:T(128)} %bitcast.176, f32[3,64,4096]{2,1,0:T(8,128)} %bitcast.155, f32[3,1,4096]{2,1,0:T(1,128)} %reshape_squeeze_reshape.9.refs_2_, f32[3,1,4096]{2,1,0:T(1,128)} %add_multiply_fusion.refs_3_, f32[3,64,128]{2,1,0:T(8,128)} %maximum_bitcast_fusion.1.refs_4_, ...), custom_call_target="tpu_custom_call" | custom-call | tf_op jit(solution)/shard_map/pallas_call | solution.py:273
  (25 shorter events, 0.2 us)
Async XLA Ops:
  0.7 39.2 %copy-start.1 = (f32[1,1,3]{2,1,0:T(1,128)S(1)}, f32[1,1,3]{2,1,0:T(1,128)}, u32[]{:S(2)}) copy-start(f32[1,1,3]{2,1,0:T(1,128)} %param.19) | copy-start | bytes 40
  21.5 11.1 %collective-permute-start.1 = (f32[1,3,2,4096]{3,2,1,0:T(2,128)}, f32[1,3,2,4096]{3,2,1,0:T(2,128)S(1)}, u32[]{:S(2)}, u32[]{:S(2)}) collective-permute-start(f32[1,3,2,4096]{3,2,1,0:T(2,128)} %bitcast.166), channel_id=1, source_target_pairs={{4,0},{8,4},{12,8},{16,12},{20,16},{24,20},{28,24},{5,1},{9,5},{13... | collective-permute-start | bytes 294920 | tf_op jit(solution)/shard_map/ppermute | solution.py:28
  25.7 7.1 %collective-permute-start.3 = (f32[1,3,2,64,64]{4,3,1,2,0:T(8,128)S(1)}, f32[1,3,2,64,64]{4,3,1,2,0:T(8,128)S(1)}, u32[]{:S(2)}, u32[]{:S(2)}) collective-permute-start(f32[1,3,2,64,64]{4,3,1,2,0:T(8,128)S(1)} %bitcast.156), channel_id=1, source_target_pairs={{0,3},{1,0},{2,1},{3,2},{4,7},{5,4},{6,5},{7,6},{8,11},{9,8},{10,9... | collective-permute-start | bytes 294920 | tf_op jit(solution)/shard_map/ppermute | solution.py:33
  27.4 5.8 %collective-permute-start.2 = (f32[1,3,2,64,64]{4,3,1,2,0:T(8,128)S(1)}, f32[1,3,2,64,64]{4,3,1,2,0:T(8,128)S(1)}, u32[]{:S(2)}, u32[]{:S(2)}) collective-permute-start(f32[1,3,2,64,64]{4,3,1,2,0:T(8,128)S(1)} %bitcast.158), channel_id=1, source_target_pairs={{0,1},{1,2},{2,3},{3,0},{4,5},{5,6},{6,7},{7,4},{8,9},{9,10},{10,1... | collective-permute-start | bytes 294920 | tf_op jit(solution)/shard_map/ppermute | solution.py:33
  27.4 10.8 %collective-permute-start = (f32[1,3,3,4096]{3,2,1,0:T(4,128)}, f32[1,3,3,4096]{3,2,1,0:T(4,128)S(1)}, u32[]{:S(2)}, u32[]{:S(2)}) collective-permute-start(f32[1,3,3,4096]{3,2,1,0:T(4,128)} %bitcast.170), channel_id=1, source_target_pairs={{0,4},{4,8},{8,12},{12,16},{16,20},{20,24},{24,28},{1,5},{5,9},{9,... | collective-permute-start | bytes 442376 | tf_op jit(solution)/shard_map/ppermute | solution.py:28
  64.4 11.7 %copy-start = (f32[3,1,4096]{2,1,0:T(1,128)S(1)}, f32[3,1,4096]{2,1,0:T(1,128)}, u32[]{:S(2)}) copy-start(f32[3,1,4096]{2,1,0:T(1,128)} %mul.220.refs_3_) | copy-start | bytes 147460
  66.8 8.6 %collective-permute-start.5 = (f32[1,3,2,4096]{3,2,1,0:T(2,128)}, f32[1,3,2,4096]{3,2,1,0:T(2,128)S(1)}, u32[]{:S(2)}, u32[]{:S(2)}) collective-permute-start(f32[1,3,2,4096]{3,2,1,0:T(2,128)} %bitcast.169), channel_id=1, source_target_pairs={{4,0},{8,4},{12,8},{16,12},{20,16},{24,20},{28,24},{5,1},{9,5},{13... | collective-permute-start | bytes 294920 | tf_op jit(solution)/shard_map/ppermute | solution.py:28
  68.7 14.1 %collective-permute-start.4 = (f32[1,3,3,4096]{3,2,1,0:T(4,128)}, f32[1,3,3,4096]{3,2,1,0:T(4,128)S(1)}, u32[]{:S(2)}, u32[]{:S(2)}) collective-permute-start(f32[1,3,3,4096]{3,2,1,0:T(4,128)} %bitcast.173), channel_id=1, source_target_pairs={{0,4},{4,8},{8,12},{12,16},{16,20},{20,24},{24,28},{1,5},{5,9},{9,... | collective-permute-start | bytes 442376 | tf_op jit(solution)/shard_map/ppermute | solution.py:28
  74.8 4.9 %collective-permute-start.7 = (f32[1,3,2,64,64]{4,3,1,2,0:T(8,128)S(1)}, f32[1,3,2,64,64]{4,3,1,2,0:T(8,128)S(1)}, u32[]{:S(2)}, u32[]{:S(2)}) collective-permute-start(f32[1,3,2,64,64]{4,3,1,2,0:T(8,128)S(1)} %bitcast.160), channel_id=1, source_target_pairs={{0,3},{1,0},{2,1},{3,2},{4,7},{5,4},{6,5},{7,6},{8,11},{9,8},{10,9... | collective-permute-start | bytes 294920 | tf_op jit(solution)/shard_map/ppermute | solution.py:33
  75.0 6.8 %collective-permute-start.6 = (f32[1,3,2,64,64]{4,3,1,2,0:T(8,128)S(1)}, f32[1,3,2,64,64]{4,3,1,2,0:T(8,128)S(1)}, u32[]{:S(2)}, u32[]{:S(2)}) collective-permute-start(f32[1,3,2,64,64]{4,3,1,2,0:T(8,128)S(1)} %bitcast.162), channel_id=1, source_target_pairs={{0,1},{1,2},{2,3},{3,0},{4,5},{5,6},{6,7},{7,4},{8,9},{9,10},{10,1... | collective-permute-start | bytes 294920 | tf_op jit(solution)/shard_map/ppermute | solution.py:33

commit v9 on v8

--- a/solution.py
+++ b/solution.py
@@ -154,16 +154,21 @@
     return jnp.dot(w6, jnp.concatenate([d1, d1, d2, d3], 0), preferred_element_type=f32)
 
 
-def solve_kernel(*refs, with_faces, emit_u, emit_sides):
+def solve_kernel(*refs, with_faces, emit_u, emit_sides, omega):
     it = iter(refs)
     mod_ref, f_ref = next(it), next(it)
     if with_faces:
-        xlo_ref, xhi_ref, yadd_ref = next(it), next(it), next(it)
+        (nbm_ref, lxu_ref, lxd_ref, ly_ref, sxh_ref, sxl_ref, sy_ref,
+         rup_ref, rdn_ref, ryp_ref, ryn_ref) = (next(it) for _ in range(11))
     q_ref, p_ref, wy_ref, exy_ref, ez_ref = next(it), next(it), next(it), next(it), next(it)
     code_ref = next(it)
     o_ref = next(it) if emit_u else None
     if emit_sides:
-        xh_ref, xl_ref, yh_ref, yl_ref = next(it), next(it), next(it), next(it)
+        xh_ref, xl_ref, y_ref = next(it), next(it), next(it)
+    if with_faces and emit_sides:
+        nlx_ref, nld_ref, nly_ref = next(it), next(it), next(it)
+    elif with_faces:
+        nlx_ref = nld_ref = nly_ref = None
     s_ref, z_ref = next(it), next(it)
     n = q_ref.shape[0]
     h = n // 2
@@ -177,10 +182,41 @@
     q = q_ref[...]
     r = f_ref[0]
     if with_faces:
+        m_up = nbm_ref[0, comp]
+        m_dn = nbm_ref[1, comp]
+        m_prev = nbm_ref[2, comp]
+        m_next = nbm_ref[3, comp]
+        has_up = nbm_ref[4, comp]
+        has_dn = nbm_ref[5, comp]
+        lane_x = lax.broadcasted_iota(jnp.int32, (1, nn), 1) % n
+        lane_y = lax.broadcasted_iota(jnp.int32, (n, w2), 1)
+
+        def smooth(res, lanes, width):
+            left = pltpu.roll(res, 1, 1)
+            right = pltpu.roll(res, width - 1, 1)
+            left = jnp.where(lanes % n == 0, 0.0, left)
+            right = jnp.where(lanes % n == n - 1, 0.0, right)
+            diag = jnp.where((lanes % n == 0) | (lanes % n == n - 1), -1.0, -2.0)
+            return res + 0.25 * ((left + right) + diag * res)
+
+        xu = lxu_ref[0]
+        res = (sxh_ref[0, 0:1, :] + rup_ref[0]) / (m + m_up) - xu
+        xhi_face = (xu + omega * smooth(res, lane_x, nn)) * has_up
+        xd = lxd_ref[0]
+        res = (rdn_ref[0] + sxl_ref[0, 0:1, :]) / (m_dn + m) - xd
+        xlo_face = (xd + omega * smooth(res, lane_x, nn)) * has_dn
+        ly = ly_ref[0]
+        lo = lane_y < n
+        recv = pltpu.roll(jnp.where(lo, ryn_ref[0, 0], ryp_ref[0, 0]), n, 1)
+        res = (sy_ref[0, 0] + recv) / (m + jnp.where(lo, m_prev, m_next)) - ly
+        yadd = ly + omega * smooth(res, lane_y, w2)
+        if nlx_ref is not None:
+            nlx_ref[0] = xhi_face
+            nld_ref[0] = xlo_face
+            nly_ref[0] = yadd
         rows = lax.broadcasted_iota(jnp.int32, (n, nn), 0)
-        added = jnp.where(rows == 0, xlo_ref[0], 0.0) + jnp.where(rows == n - 1, xhi_ref[0], 0.0)
-        lane = lax.broadcasted_iota(jnp.int32, (n, w2), 1)
-        yadd = yadd_ref[0]
+        added = jnp.where(rows == 0, xlo_face, 0.0) + jnp.where(rows == n - 1, xhi_face, 0.0)
+        lane = lane_y
         first = added[:, :w2] + jnp.where(lane < n, yadd, 0.0)
         last = added[:, nn - w2:] + jnp.where(lane >= n, yadd, 0.0)
         added = jnp.concatenate([first, added[:, w2:nn - w2], last], 1)
@@ -234,20 +270,18 @@
         xh_ref[0, 2:3, :] = jnp.full((1, nn), code_ref[0], f32)
         xl_ref[0, 0:1, :] = m * u[0:1] + 0.5 * slope(u[0:1], u[1:2], u[2:3], u[3:4])
         xl_ref[0, 1:2, :] = m_row
-        m_sq = jnp.full((n, n), m, f32)
         c_hi = u[:, nn - w2:]
         c_hi2 = u[:, nn - 2 * w2:nn - w2]
         s_hi = m * c_hi + 0.5 * slope(c_hi, pltpu.roll(c_hi, n, 1), c_hi2, pltpu.roll(c_hi2, n, 1))
-        yh_ref[0, 0] = pltpu.roll(s_hi, n, 1)[:, :n]
-        yh_ref[0, 1] = m_sq
         c_lo = u[:, :w2]
         c_lo2 = u[:, w2:2 * w2]
         s_lo = m * c_lo + 0.5 * slope(c_lo, pltpu.roll(c_lo, n, 1), c_lo2, pltpu.roll(c_lo2, n, 1))
-        yl_ref[0, 0] = s_lo[:, :n]
-        yl_ref[0, 1] = m_sq
-
-
-def kernel_sweep(rhs, moduli, code, faces=None, emit_u=True, emit_sides=False, interpret=False):
+        lane_s = lax.broadcasted_iota(jnp.int32, (n, w2), 1)
+        y_ref[0, 0] = jnp.where(lane_s < n, s_lo, s_hi)
+        y_ref[0, 1] = jnp.full((n, w2), m, f32)
+
+
+def kernel_sweep(rhs, moduli, code, state=None, emit_u=True, emit_sides=False, omega=0.0):
     ncomp, n, nn = rhs.shape
     q, p4, wy, exy, ez = consts(n)
     full = lambda shp: pl.BlockSpec(shp, lambda c: (0,) * len(shp))
@@ -255,10 +289,11 @@
     smem = pl.BlockSpec(memory_space=pltpu.SMEM)
     in_specs = [smem, comp3((n, nn))]
     args = [moduli, rhs]
-    if faces is not None:
-        xlo, xhi, yadd = faces
-        in_specs += [comp3((1, nn)), comp3((1, nn)), comp3((n, 2 * n))]
-        args += [xlo.reshape(ncomp, 1, nn), xhi.reshape(ncomp, 1, nn), yadd]
+    if state is not None:
+        in_specs += [smem, comp3((1, nn)), comp3((1, nn)), comp3((n, 2 * n)),
+                     comp3((3, nn)), comp3((2, nn)), comp3((2, n, 2 * n)),
+                     comp3((1, nn)), comp3((1, nn)), comp3((2, n, 2 * n)), comp3((2, n, 2 * n))]
+        args += list(state)
     in_specs += [full(q.shape), full(p4.shape), full(wy.shape), full(exy.shape), full(ez.shape), smem]
     args += [q, p4, wy, exy, ez, code]
     out_specs, out_shape = [], []
@@ -266,10 +301,15 @@
         out_specs.append(comp3((n, nn)))
         out_shape.append(jax.ShapeDtypeStruct(rhs.shape, f32))
     if emit_sides:
-        out_specs += [comp3((3, nn)), comp3((2, nn)), comp3((2, n, n)), comp3((2, n, n))]
+        out_specs += [comp3((3, nn)), comp3((2, nn)), comp3((2, n, 2 * n))]
         out_shape += [jax.ShapeDtypeStruct((ncomp, 3, nn), f32), jax.ShapeDtypeStruct((ncomp, 2, nn), f32),
-                      jax.ShapeDtypeStruct((ncomp, 2, n, n), f32), jax.ShapeDtypeStruct((ncomp, 2, n, n), f32)]
-    kernel = functools.partial(solve_kernel, with_faces=faces is not None, emit_u=emit_u, emit_sides=emit_sides)
+                      jax.ShapeDtypeStruct((ncomp, 2, n, 2 * n), f32)]
+        if state is not None:
+            out_specs += [comp3((1, nn)), comp3((1, nn)), comp3((n, 2 * n))]
+            out_shape += [jax.ShapeDtypeStruct((ncomp, 1, nn), f32), jax.ShapeDtypeStruct((ncomp, 1, nn), f32),
+                          jax.ShapeDtypeStruct((ncomp, n, 2 * n), f32)]
+    kernel = functools.partial(solve_kernel, with_faces=state is not None, emit_u=emit_u,
+                               emit_sides=emit_sides, omega=omega)
     return pl.pallas_call(
         kernel,
         grid=(ncomp,),
@@ -277,7 +317,6 @@
         out_specs=out_specs,
         out_shape=out_shape,
         scratch_shapes=[pltpu.VMEM((nn // 2, 2 * n), f32), pltpu.VMEM((nn // 4, 4 * n), f32)],
-        interpret=interpret,
     )(*args)
 
 
@@ -363,59 +402,44 @@
     moduli = modulus[0]
     codes_here = orient_codes[0]
     code_values = codes_here.astype(jnp.float32)
-    tangent = tangent_matrix(extent)
     omegas = step_weights(ITERS)
     slab_count = lax.axis_size("blk")
     slab_index = lax.axis_index("blk")
-    has_up = (slab_index < slab_count - 1).astype(jnp.float32)
-    has_down = (slab_index > 0).astype(jnp.float32)
-    lam_x_up = jnp.zeros((blocks, 3, flat), jnp.float32)
+    has_up = jnp.broadcast_to((slab_index < slab_count - 1).astype(jnp.float32), (blocks, 3))
+    has_down = jnp.broadcast_to((slab_index > 0).astype(jnp.float32), (blocks, 3))
+    lam_x_up = jnp.zeros((blocks, 3, 1, flat), jnp.float32)
     lam_x_down = lam_x_up
-    lam_y_next = jnp.zeros((blocks, 3, extent, extent), jnp.float32)
-    lam_y_prev = lam_y_next
-    faces = [None] * blocks
+    lam_y = jnp.zeros((blocks, 3, extent, 2 * extent), jnp.float32)
+    state = [None] * blocks
     for sweep in range(ITERS + 1):
         last = sweep == ITERS
+        omega = omegas[sweep - 1] if sweep > 0 else 0.0
         outs = [
-            kernel_sweep(source_field[b], moduli[b], code_values[b:b + 1], faces[b], emit_u=last, emit_sides=not last)
+            kernel_sweep(source_field[b], moduli[b], code_values[b:b + 1], state[b], emit_u=last,
+                         emit_sides=not last, omega=omega)
             for b in range(blocks)
         ]
         if last:
             return jnp.stack([o[0] for o in outs], 0)[None]
-        xh, xl, yh, yl = (jnp.stack([o[k] for o in outs], 0) for k in range(4))
+        xh, xl, ys = (jnp.stack([o[k] for o in outs], 0) for k in range(3))
+        if sweep > 0:
+            lam_x_up, lam_x_down, lam_y = (jnp.stack([o[k] for o in outs], 0) for k in range(3, 6))
         upper = shifted(xl, "blk", -1)
         lower = shifted(xh, "blk", 1)
-        nxt = jnp.concatenate([yl[1:], shifted_2(yl[:1], "face", -1)], 0)
-        prv = jnp.concatenate([shifted_2(yh[-1:], "face", 1), yh[:-1]], 0)
+        nxt = jnp.concatenate([ys[1:], shifted_2(ys[:1], "face", -1)], 0)
+        prv = jnp.concatenate([shifted_2(ys[-1:], "face", 1), ys[:-1]], 0)
         if sweep == 0:
-            moduli_up = upper[:, :, 1, 0]
-            moduli_down = lower[:, :, 1, 0]
             codes_down = lower[:, 0, 2, 0].astype(jnp.int32)
-            moduli_next = nxt[:, :, 1, 0, 0]
-            moduli_prev = prv[:, :, 1, 0, 0]
-        lam_x_up = (
-            flat_update(
-                lam_x_up, xh[:, :, 0], orient(upper[:, :, 0], codes_here, extent),
-                moduli, moduli_up, omegas[sweep], tangent,
+            neighbour_moduli = jnp.stack(
+                [upper[:, :, 1, 0], lower[:, :, 1, 0], prv[:, :, 1, 0, 0], nxt[:, :, 1, 0, 0], has_up, has_down], 1
             )
-            * has_up
-        )
-        lam_x_down = (
-            flat_update(
-                lam_x_down, lower[:, :, 0], orient(xl[:, :, 0], codes_down, extent),
-                moduli_down, moduli, omegas[sweep], tangent,
-            )
-            * has_down
-        )
-        lam_y_next = square_update(
-            lam_y_next, yh[:, :, 0], nxt[:, :, 0], moduli, moduli_next, omegas[sweep], tangent
-        )
-        lam_y_prev = square_update(
-            lam_y_prev, prv[:, :, 0], yl[:, :, 0], moduli_prev, moduli, omegas[sweep], tangent
-        )
-        x_low = orient(lam_x_down, codes_down, extent)
-        yadd = jnp.concatenate([lam_y_prev, lam_y_next], -1)
-        faces = [(x_low[b], lam_x_up[b], yadd[b]) for b in range(blocks)]
+        up_sum = orient(upper[:, :, 0], codes_here, extent)[:, :, None]
+        down_sum = orient(lower[:, :, 0], codes_down, extent)[:, :, None]
+        state = [
+            (neighbour_moduli[b], lam_x_up[b], lam_x_down[b], lam_y[b], xh[b], xl[b], ys[b],
+             up_sum[b], down_sum[b], prv[b], nxt[b])
+            for b in range(blocks)
+        ]
 
 
 def solution(mesh):

time: 106 us -> 99.4 us (0.938)
  local copies, waits for them, and re-layouts: 13.8 us -> 7.7 us
  waiting for transfers between devices: 9.54 us -> 12.6 us
  matrix products: 2.39 us -> 0 us
  other arithmetic: 2.24 us -> 0.12 us
  Pallas kernels: 62.4 us -> 63.6 us
    ppermute x4, waiting for transfers between devices: 4.93 us -> 12.6 us  [shifted(): return lax.ppermute(shard, axis, pairs)]
    slice x12 -> x4, local copies, waits for them, and re-layouts: 5.21 us -> 0.56 us  [the longest x2 0.28 us: shards(): down_sum = orient(lower[:, :, 0], codes_down, extent)[:, :, None]]
    ppermute x4, waiting for transfers between devices: 4.61 us -> 0.01 us  [shifted_2(): lax.ppermute(shard, axis, [(i, (i + by) % length) for i in range(length)])]
    pallas_call x4 -> x0, local copies, waits for them, and re-layouts: 3.77 us -> none  [kernel_sweep(): pl.pallas_call(kernel, grid=(ncomp,), in_specs=in_specs, out_specs=out_sp...]
    dot_general x8 -> x0, matrix products: 2.39 us -> none  [the longest x4 1.21 us: flat_update(): jnp.einsum('...z,zk->...k', rows_view, tangent, precision=highest)]
    another operation x6 -> x12, local copies, waits for them, and re-layouts: 1.65 us -> 3.67 us  [the longest x2 1.46 us: shards(): down_sum[b]]
    squeeze x2 -> x0, other arithmetic: 1.45 us -> none  [shards(): faces = [(x_low[b], lam_x_up[b], yadd[b]) for b in range(blocks)]]
    pallas_call x3, Pallas kernels: 62.4 us -> 63.6 us  [kernel_sweep(): pl.pallas_call(kernel, grid=(ncomp,), in_specs=in_specs, out_specs=out_sp...]
  transfers between devices with their start and end apart: 8 -> 8, of which waited for: 3 -> 4; matrix products, arithmetic and copies ran while one was open for 9% -> 5% of each run, Pallas kernels for 0% -> 0%
where the time goes in v9:
time: 99.4 us; the launch traced here: 98.9 us
  Pallas kernels  63.6 us (64%)
  starting transfers between devices  13.1 us (13%)
  waiting for transfers between devices  12.6 us (13%)
  local copies, waits for them, and re-layouts  7.7 us (8%)
  between operations  1.73 us (2%)
    pallas_call x3, Pallas kernels, kernel_sweep(): pl.pallas_call(kernel, grid=(ncomp,), in_specs=in_specs, out_specs=out_sp...  63.6 us
    ppermute x4, waiting for transfers between devices, shifted(): return lax.ppermute(shard, axis, pairs)  12.6 us
    ppermute x4, starting transfers between devices, shifted(): return lax.ppermute(shard, axis, pairs)  11.6 us
  transfers between devices with their start and end apart: 8, of which 4 were waited for; matrix products, arithmetic and copies ran while one was open for 5% of the time, Pallas kernels for 0%

profile of v9, /device:TPU:24, one launch (start us, length us, event | category | flops | bytes accessed | tf_op | source)
XLA Modules:
  0.0 98.9 jit_solution(14677167331586289491)
XLA Ops:
  0.7 20.6 %shard_map.172 = (f32[3,3,4096]{2,1,0:T(4,128)}, f32[3,2,4096]{2,1,0:T(2,128)}, f32[3,2,64,128]{3,2,1,0:T(8,128)}) custom-call(f32[3]{0:T(128)} %bitcast.58, f32[3,64,4096]{2,1,0:T(8,128)} %bitcast.41, bf16[64,256]{1,0:T(8,128)(2,1)} %constant.80.clone.refs_2_.refs_13_, bf16[1024,256]{1,0:T(8,128)(2,1)} %constant.81.clone.refs_3_.refs_14_, ...), custom_call_target="tpu_custom_call" | custom-call | tf_op jit(solution)/shard_map/pallas_call | solution.py:313
  21.3 3.3 %collective-permute-start = (f32[1,3,2,4096]{3,2,1,0:T(2,128)}, f32[1,3,2,4096]{3,2,1,0:T(2,128)S(1)}, u32[]{:S(2)}, u32[]{:S(2)}) collective-permute-start(f32[1,3,2,4096]{3,2,1,0:T(2,128)} %bitcast.55), channel_id=1, source_target_pairs={{4,0},{8,4},{12,8},{16,12},{20,16},{24,20},{28,24},{5,1},{9,5},{13... | collective-permute-start | bytes 294920 | tf_op jit(solution)/shard_map/ppermute | solution.py:28
  24.6 0.7 collective-permute-start.3
  25.3 0.0 collective-permute-start.2
  25.3 2.5 %collective-permute-start.1 = (f32[1,3,3,4096]{3,2,1,0:T(4,128)}, f32[1,3,3,4096]{3,2,1,0:T(4,128)S(1)}, u32[]{:S(2)}, u32[]{:S(2)}) collective-permute-start(f32[1,3,3,4096]{3,2,1,0:T(4,128)} %bitcast.46), channel_id=1, source_target_pairs={{0,4},{4,8},{8,12},{12,16},{16,20},{20,24},{24,28},{1,5},{5,9},{9,... | collective-permute-start | bytes 442376 | tf_op jit(solution)/shard_map/ppermute | solution.py:28
  27.9 0.1 collective-permute-done
  28.0 0.1 slice_reduce_fusion.3
  28.2 0.1 reshape_squeeze.12
  28.3 0.1 rev.27
  28.4 0.7 squeeze_broadcast_in_dim_reshape.12.refs_9_
  29.2 6.9 %collective-permute-done.1 = f32[1,3,3,4096]{3,2,1,0:T(4,128)S(1)} collective-permute-done((f32[1,3,3,4096]{3,2,1,0:T(4,128)}, f32[1,3,3,4096]{3,2,1,0:T(4,128)S(1)}, u32[]{:S(2)}, u32[]{:S(2)}) %collective-permute-start.1) | collective-permute-done | bytes 147488 | tf_op jit(solution)/shard_map/ppermute | solution.py:28
  36.0 0.5 slice.41
  37.2 0.1 slice_reduce_fusion.2
  37.3 0.1 reshape_squeeze.13
  37.5 0.1 rev.29
  37.6 0.7 squeeze_broadcast_in_dim_reshape.13.refs_10_
  38.3 0.0 collective-permute-done.3
  38.4 0.0 copy-start
  38.4 0.0 collective-permute-done.2
  38.4 0.0 copy-start.1
  38.4 0.1 stack.24
  38.5 0.7 copy.31
  39.2 0.6 broadcast_1_refs_3__refs_4_.2.refs_3_.refs_4_
  39.9 0.7 squeeze.25.refs_5_
  40.5 0.0 copy-done
  40.5 0.0 copy-done.1
  40.5 21.4 %shard_map.173 = (f32[3,3,4096]{2,1,0:T(4,128)}, f32[3,2,4096]{2,1,0:T(2,128)}, f32[3,2,64,128]{3,2,1,0:T(8,128)}, f32[3,1,4096]{2,1,0:T(1,128)}, f32[3,1,4096]{2,1,0:T(1,128)}, /*index=5*/f32[3,64,128]{2,1,0:T(8,128)}) custom-call(f32[3]{0:T(128)} %bitcast.59, f32[3,64,4096]{2,1,0:T(8,128)} %bitcast.42, f32[6,3]{1,0:T(8,128)} %bitcast.56, ...), custom_call_target="tpu_custom_call" | custom-call | tf_op jit(solution)/shard_map/pallas_call | solution.py:313
  61.9 1.9 %collective-permute-start.4 = (f32[1,3,2,4096]{3,2,1,0:T(2,128)}, f32[1,3,2,4096]{3,2,1,0:T(2,128)S(1)}, u32[]{:S(2)}, u32[]{:S(2)}) collective-permute-start(f32[1,3,2,4096]{3,2,1,0:T(2,128)} %bitcast.54), channel_id=1, source_target_pairs={{4,0},{8,4},{12,8},{16,12},{20,16},{24,20},{28,24},{5,1},{9,5},{13... | collective-permute-start | bytes 294920 | tf_op jit(solution)/shard_map/ppermute | solution.py:28
  63.9 0.8 collective-permute-start.7
  64.7 0.0 collective-permute-start.6
  64.7 3.8 %collective-permute-start.5 = (f32[1,3,3,4096]{3,2,1,0:T(4,128)}, f32[1,3,3,4096]{3,2,1,0:T(4,128)S(1)}, u32[]{:S(2)}, u32[]{:S(2)}) collective-permute-start(f32[1,3,3,4096]{3,2,1,0:T(4,128)} %bitcast.49), channel_id=1, source_target_pairs={{0,4},{4,8},{8,12},{12,16},{16,20},{20,24},{24,28},{1,5},{5,9},{9,... | collective-permute-start | bytes 442376 | tf_op jit(solution)/shard_map/ppermute | solution.py:28
  68.5 0.3 collective-permute-done.4
  68.9 0.1 slice_reduce_fusion.1
  69.0 0.1 reshape_squeeze.14
  69.2 0.1 rev.31
  69.3 0.7 squeeze_broadcast_in_dim_reshape.14.refs_9_
  70.0 5.3 %collective-permute-done.5 = f32[1,3,3,4096]{3,2,1,0:T(4,128)S(1)} collective-permute-done((f32[1,3,3,4096]{3,2,1,0:T(4,128)}, f32[1,3,3,4096]{3,2,1,0:T(4,128)S(1)}, u32[]{:S(2)}, u32[]{:S(2)}) %collective-permute-start.5) | collective-permute-done | bytes 147488 | tf_op jit(solution)/shard_map/ppermute | solution.py:28
  75.3 0.1 slice_reduce_fusion
  75.4 0.1 reshape_squeeze.15
  75.6 0.1 rev.33
  75.7 0.7 squeeze_broadcast_in_dim_reshape.15.refs_10_
  76.4 0.0 collective-permute-done.7
  76.5 0.0 copy-start.2
  76.5 0.0 collective-permute-done.6
  76.5 0.0 copy-start.3
  76.5 0.7 copy-done.2
  77.1 0.1 copy-done.3
  77.2 21.5 %shard_map.174 = f32[3,64,4096]{2,1,0:T(8,128)} custom-call(f32[3]{0:T(128)} %bitcast.60, f32[3,64,4096]{2,1,0:T(8,128)} %bitcast.43, f32[6,3]{1,0:T(8,128)} %bitcast.57, f32[3,1,4096]{2,1,0:T(1,128)} %get-tuple-element.17.refs_3_, f32[3,1,4096]{2,1,0:T(1,128)} %get-tuple-element.18.refs_4_, f32[3,64,128]{2,1,0:T(8,128)} %get-tuple-element.19.refs_5_, ...), custom_call_target="tpu_custom_call" | custom-call | tf_op jit(solution)/shard_map/pallas_call | solution.py:313
  (18 shorter events, 0.2 us)
Async XLA Ops:
  21.3 6.7 %collective-permute-start = (f32[1,3,2,4096]{3,2,1,0:T(2,128)}, f32[1,3,2,4096]{3,2,1,0:T(2,128)S(1)}, u32[]{:S(2)}, u32[]{:S(2)}) collective-permute-start(f32[1,3,2,4096]{3,2,1,0:T(2,128)} %bitcast.55), channel_id=1, source_target_pairs={{4,0},{8,4},{12,8},{16,12},{20,16},{24,20},{28,24},{5,1},{9,5},{13... | collective-permute-start | bytes 294920 | tf_op jit(solution)/shard_map/ppermute | solution.py:28
  24.6 13.7 %collective-permute-start.3 = (f32[1,3,2,64,128]{4,3,2,1,0:T(8,128)}, f32[1,3,2,64,128]{4,3,2,1,0:T(8,128)S(1)}, u32[]{:S(2)}, u32[]{:S(2)}) collective-permute-start(f32[1,3,2,64,128]{4,3,2,1,0:T(8,128)} %bitcast.47), channel_id=1, source_target_pairs={{0,3},{1,0},{2,1},{3,2},{4,7},{5,4},{6,5},{7,6},{8,11},{9,8},{10,9... | collective-permute-start | bytes 589832 | tf_op jit(solution)/shard_map/ppermute | solution.py:33
  25.3 13.1 %collective-permute-start.2 = (f32[1,3,2,64,128]{4,3,2,1,0:T(8,128)}, f32[1,3,2,64,128]{4,3,2,1,0:T(8,128)S(1)}, u32[]{:S(2)}, u32[]{:S(2)}) collective-permute-start(f32[1,3,2,64,128]{4,3,2,1,0:T(8,128)} %bitcast.48), channel_id=1, source_target_pairs={{0,1},{1,2},{2,3},{3,0},{4,5},{5,6},{6,7},{7,4},{8,9},{9,10},{10,1... | collective-permute-start | bytes 589832 | tf_op jit(solution)/shard_map/ppermute | solution.py:33
  25.3 10.7 %collective-permute-start.1 = (f32[1,3,3,4096]{3,2,1,0:T(4,128)}, f32[1,3,3,4096]{3,2,1,0:T(4,128)S(1)}, u32[]{:S(2)}, u32[]{:S(2)}) collective-permute-start(f32[1,3,3,4096]{3,2,1,0:T(4,128)} %bitcast.46), channel_id=1, source_target_pairs={{0,4},{4,8},{8,12},{12,16},{16,20},{20,24},{24,28},{1,5},{5,9},{9,... | collective-permute-start | bytes 442376 | tf_op jit(solution)/shard_map/ppermute | solution.py:28
  38.4 2.2 %copy-start = (f32[1,3,2,64,128]{4,3,2,1,0:T(8,128)}, f32[1,3,2,64,128]{4,3,2,1,0:T(8,128)S(1)}, u32[]{:S(2)}) copy-start(f32[1,3,2,64,128]{4,3,2,1,0:T(8,128)S(1)} %collective-permute-done.3) | copy-start | bytes 589828
  38.4 2.1 %copy-start.1 = (f32[1,3,2,64,128]{4,3,2,1,0:T(8,128)}, f32[1,3,2,64,128]{4,3,2,1,0:T(8,128)S(1)}, u32[]{:S(2)}) copy-start(f32[1,3,2,64,128]{4,3,2,1,0:T(8,128)S(1)} %collective-permute-done.2) | copy-start | bytes 589828
  61.9 6.9 %collective-permute-start.4 = (f32[1,3,2,4096]{3,2,1,0:T(2,128)}, f32[1,3,2,4096]{3,2,1,0:T(2,128)S(1)}, u32[]{:S(2)}, u32[]{:S(2)}) collective-permute-start(f32[1,3,2,4096]{3,2,1,0:T(2,128)} %bitcast.54), channel_id=1, source_target_pairs={{4,0},{8,4},{12,8},{16,12},{20,16},{24,20},{28,24},{5,1},{9,5},{13... | collective-permute-start | bytes 294920 | tf_op jit(solution)/shard_map/ppermute | solution.py:28
  63.9 12.6 %collective-permute-start.7 = (f32[1,3,2,64,128]{4,3,2,1,0:T(8,128)}, f32[1,3,2,64,128]{4,3,2,1,0:T(8,128)S(1)}, u32[]{:S(2)}, u32[]{:S(2)}) collective-permute-start(f32[1,3,2,64,128]{4,3,2,1,0:T(8,128)} %bitcast.50), channel_id=1, source_target_pairs={{0,3},{1,0},{2,1},{3,2},{4,7},{5,4},{6,5},{7,6},{8,11},{9,8},{10,9... | collective-permute-start | bytes 589832 | tf_op jit(solution)/shard_map/ppermute | solution.py:33
  64.7 11.8 %collective-permute-start.6 = (f32[1,3,2,64,128]{4,3,2,1,0:T(8,128)}, f32[1,3,2,64,128]{4,3,2,1,0:T(8,128)S(1)}, u32[]{:S(2)}, u32[]{:S(2)}) collective-permute-start(f32[1,3,2,64,128]{4,3,2,1,0:T(8,128)} %bitcast.51), channel_id=1, source_target_pairs={{0,1},{1,2},{2,3},{3,0},{4,5},{5,6},{6,7},{7,4},{8,9},{9,10},{10,1... | collective-permute-start | bytes 589832 | tf_op jit(solution)/shard_map/ppermute | solution.py:33
  64.7 10.6 %collective-permute-start.5 = (f32[1,3,3,4096]{3,2,1,0:T(4,128)}, f32[1,3,3,4096]{3,2,1,0:T(4,128)S(1)}, u32[]{:S(2)}, u32[]{:S(2)}) collective-permute-start(f32[1,3,3,4096]{3,2,1,0:T(4,128)} %bitcast.49), channel_id=1, source_target_pairs={{0,4},{4,8},{8,12},{12,16},{16,20},{20,24},{24,28},{1,5},{5,9},{9,... | collective-permute-start | bytes 442376 | tf_op jit(solution)/shard_map/ppermute | solution.py:28
  76.5 0.7 copy-start.2
  76.5 0.7 copy-start.3

commit v10 on v9

--- a/solution.py
+++ b/solution.py
@@ -154,12 +154,13 @@
     return jnp.dot(w6, jnp.concatenate([d1, d1, d2, d3], 0), preferred_element_type=f32)
 
 
-def solve_kernel(*refs, with_faces, emit_u, emit_sides, omega):
+def solve_kernel(*refs, with_faces, emit_u, emit_sides, omega, zero_lam):
     it = iter(refs)
     mod_ref, f_ref = next(it), next(it)
     if with_faces:
-        (nbm_ref, lxu_ref, lxd_ref, ly_ref, sxh_ref, sxl_ref, sy_ref,
-         rup_ref, rdn_ref, ryp_ref, ryn_ref) = (next(it) for _ in range(11))
+        nbm_ref = next(it)
+        lxu_ref, lxd_ref, ly_ref = (None, None, None) if zero_lam else (next(it), next(it), next(it))
+        sxh_ref, sxl_ref, sy_ref, rup_ref, rdn_ref, ryp_ref, ryn_ref = (next(it) for _ in range(7))
     q_ref, p_ref, wy_ref, exy_ref, ez_ref = next(it), next(it), next(it), next(it), next(it)
     code_ref = next(it)
     o_ref = next(it) if emit_u else None
@@ -199,13 +200,13 @@
             diag = jnp.where((lanes % n == 0) | (lanes % n == n - 1), -1.0, -2.0)
             return res + 0.25 * ((left + right) + diag * res)
 
-        xu = lxu_ref[0]
+        xu = 0.0 if zero_lam else lxu_ref[0]
         res = (sxh_ref[0, 0:1, :] + rup_ref[0]) / (m + m_up) - xu
         xhi_face = (xu + omega * smooth(res, lane_x, nn)) * has_up
-        xd = lxd_ref[0]
+        xd = 0.0 if zero_lam else lxd_ref[0]
         res = (rdn_ref[0] + sxl_ref[0, 0:1, :]) / (m_dn + m) - xd
         xlo_face = (xd + omega * smooth(res, lane_x, nn)) * has_dn
-        ly = ly_ref[0]
+        ly = 0.0 if zero_lam else ly_ref[0]
         lo = lane_y < n
         recv = pltpu.roll(jnp.where(lo, ryn_ref[0, 0], ryp_ref[0, 0]), n, 1)
         res = (sy_ref[0, 0] + recv) / (m + jnp.where(lo, m_prev, m_next)) - ly
@@ -289,9 +290,14 @@
     smem = pl.BlockSpec(memory_space=pltpu.SMEM)
     in_specs = [smem, comp3((n, nn))]
     args = [moduli, rhs]
+    zero_lam = state is not None and state[1] is None
     if state is not None:
-        in_specs += [smem, comp3((1, nn)), comp3((1, nn)), comp3((n, 2 * n)),
-                     comp3((3, nn)), comp3((2, nn)), comp3((2, n, 2 * n)),
+        if zero_lam:
+            state = state[:1] + state[4:]
+            in_specs += [smem]
+        else:
+            in_specs += [smem, comp3((1, nn)), comp3((1, nn)), comp3((n, 2 * n))]
+        in_specs += [comp3((3, nn)), comp3((2, nn)), comp3((2, n, 2 * n)),
                      comp3((1, nn)), comp3((1, nn)), comp3((2, n, 2 * n)), comp3((2, n, 2 * n))]
         args += list(state)
     in_specs += [full(q.shape), full(p4.shape), full(wy.shape), full(exy.shape), full(ez.shape), smem]
@@ -309,7 +315,7 @@
             out_shape += [jax.ShapeDtypeStruct((ncomp, 1, nn), f32), jax.ShapeDtypeStruct((ncomp, 1, nn), f32),
                           jax.ShapeDtypeStruct((ncomp, n, 2 * n), f32)]
     kernel = functools.partial(solve_kernel, with_faces=state is not None, emit_u=emit_u,
-                               emit_sides=emit_sides, omega=omega)
+                               emit_sides=emit_sides, omega=omega, zero_lam=zero_lam)
     return pl.pallas_call(
         kernel,
         grid=(ncomp,),
@@ -407,9 +413,7 @@
     slab_index = lax.axis_index("blk")
     has_up = jnp.broadcast_to((slab_index < slab_count - 1).astype(jnp.float32), (blocks, 3))
     has_down = jnp.broadcast_to((slab_index > 0).astype(jnp.float32), (blocks, 3))
-    lam_x_up = jnp.zeros((blocks, 3, 1, flat), jnp.float32)
-    lam_x_down = lam_x_up
-    lam_y = jnp.zeros((blocks, 3, extent, 2 * extent), jnp.float32)
+    lam_x_up = lam_x_down = lam_y = [None] * blocks
     state = [None] * blocks
     for sweep in range(ITERS + 1):
         last = sweep == ITERS

time: 99.4 us -> 98.1 us (0.987)
  local copies, waits for them, and re-layouts: 7.7 us -> 6.41 us
where the time goes in v10:
time: 98.1 us; the launch traced here: 97.6 us
  Pallas kernels  63.6 us (65%)
  starting transfers between devices  13.1 us (13%)
  waiting for transfers between devices  12.6 us (13%)
  local copies, waits for them, and re-layouts  6.41 us (7%)
  between operations  1.74 us (2%)
    pallas_call x3, Pallas kernels, kernel_sweep(): pl.pallas_call(kernel, grid=(ncomp,), in_specs=in_specs, out_specs=out_sp...  63.6 us
    ppermute x4, waiting for transfers between devices, shifted(): return lax.ppermute(shard, axis, pairs)  12.6 us
    ppermute x4, starting transfers between devices, shifted(): return lax.ppermute(shard, axis, pairs)  11.6 us
  transfers between devices with their start and end apart: 8, of which 4 were waited for; matrix products, arithmetic and copies ran while one was open for 5% of the time, Pallas kernels for 0%

profile of v10, /device:TPU:24, one launch (start us, length us, event | category | flops | bytes accessed | tf_op | source)
XLA Modules:
  0.0 97.6 jit_solution(15875044387629494429)
XLA Ops:
  0.7 20.6 %shard_map.172 = (f32[3,3,4096]{2,1,0:T(4,128)}, f32[3,2,4096]{2,1,0:T(2,128)}, f32[3,2,64,128]{3,2,1,0:T(8,128)}) custom-call(f32[3]{0:T(128)} %bitcast.58, f32[3,64,4096]{2,1,0:T(8,128)} %bitcast.41, bf16[64,256]{1,0:T(8,128)(2,1)} %constant.77.clone.refs_2_.refs_10_.refs_13_, bf16[1024,256]{1,0:T(8,128)(2,1)} %constant.78.clone.refs_3_.refs_11_.refs_14_, ...), custom_call_target="tpu_custom_call" | custom-call | tf_op jit(solution)/shard_map/pallas_call | solution.py:319
  21.3 3.3 %collective-permute-start = (f32[1,3,2,4096]{3,2,1,0:T(2,128)}, f32[1,3,2,4096]{3,2,1,0:T(2,128)S(1)}, u32[]{:S(2)}, u32[]{:S(2)}) collective-permute-start(f32[1,3,2,4096]{3,2,1,0:T(2,128)} %bitcast.55), channel_id=1, source_target_pairs={{4,0},{8,4},{12,8},{16,12},{20,16},{24,20},{28,24},{5,1},{9,5},{13... | collective-permute-start | bytes 294920 | tf_op jit(solution)/shard_map/ppermute | solution.py:28
  24.6 0.7 collective-permute-start.3
  25.3 0.0 collective-permute-start.2
  25.3 2.5 %collective-permute-start.1 = (f32[1,3,3,4096]{3,2,1,0:T(4,128)}, f32[1,3,3,4096]{3,2,1,0:T(4,128)S(1)}, u32[]{:S(2)}, u32[]{:S(2)}) collective-permute-start(f32[1,3,3,4096]{3,2,1,0:T(4,128)} %bitcast.46), channel_id=1, source_target_pairs={{0,4},{4,8},{8,12},{12,16},{16,20},{20,24},{24,28},{1,5},{5,9},{9,... | collective-permute-start | bytes 442376 | tf_op jit(solution)/shard_map/ppermute | solution.py:28
  27.9 0.1 collective-permute-done
  28.0 0.1 slice_reduce_fusion.3
  28.2 0.1 reshape_squeeze.12
  28.3 0.1 rev.27
  28.4 0.7 squeeze_broadcast_in_dim_reshape.12.refs_6_
  29.1 6.9 %collective-permute-done.1 = f32[1,3,3,4096]{3,2,1,0:T(4,128)S(1)} collective-permute-done((f32[1,3,3,4096]{3,2,1,0:T(4,128)}, f32[1,3,3,4096]{3,2,1,0:T(4,128)S(1)}, u32[]{:S(2)}, u32[]{:S(2)}) %collective-permute-start.1) | collective-permute-done | bytes 147488 | tf_op jit(solution)/shard_map/ppermute | solution.py:28
  36.0 0.5 slice.41
  37.2 0.1 slice_reduce_fusion.2
  37.3 0.1 reshape_squeeze.13
  37.5 0.1 rev.29
  37.6 0.7 squeeze_broadcast_in_dim_reshape.13.refs_7_
  38.3 0.0 collective-permute-done.3
  38.4 0.0 copy-start
  38.4 0.0 collective-permute-done.2
  38.4 0.0 copy-start.1
  38.4 0.1 stack.24
  38.5 0.7 copy.31
  39.2 0.0 copy-done
  39.2 0.0 copy-done.1
  39.2 21.4 %shard_map.173 = (f32[3,3,4096]{2,1,0:T(4,128)}, f32[3,2,4096]{2,1,0:T(2,128)}, f32[3,2,64,128]{3,2,1,0:T(8,128)}, f32[3,1,4096]{2,1,0:T(1,128)}, f32[3,1,4096]{2,1,0:T(1,128)}, /*index=5*/f32[3,64,128]{2,1,0:T(8,128)}) custom-call(f32[3]{0:T(128)} %bitcast.59, f32[3,64,4096]{2,1,0:T(8,128)} %bitcast.42, f32[6,3]{1,0:T(8,128)} %bitcast.56, ...), custom_call_target="tpu_custom_call" | custom-call | tf_op jit(solution)/shard_map/pallas_call | solution.py:319
  60.6 1.9 %collective-permute-start.4 = (f32[1,3,2,4096]{3,2,1,0:T(2,128)}, f32[1,3,2,4096]{3,2,1,0:T(2,128)S(1)}, u32[]{:S(2)}, u32[]{:S(2)}) collective-permute-start(f32[1,3,2,4096]{3,2,1,0:T(2,128)} %bitcast.54), channel_id=1, source_target_pairs={{4,0},{8,4},{12,8},{16,12},{20,16},{24,20},{28,24},{5,1},{9,5},{13... | collective-permute-start | bytes 294920 | tf_op jit(solution)/shard_map/ppermute | solution.py:28
  62.6 0.8 collective-permute-start.7
  63.4 0.0 collective-permute-start.6
  63.4 3.8 %collective-permute-start.5 = (f32[1,3,3,4096]{3,2,1,0:T(4,128)}, f32[1,3,3,4096]{3,2,1,0:T(4,128)S(1)}, u32[]{:S(2)}, u32[]{:S(2)}) collective-permute-start(f32[1,3,3,4096]{3,2,1,0:T(4,128)} %bitcast.49), channel_id=1, source_target_pairs={{0,4},{4,8},{8,12},{12,16},{16,20},{20,24},{24,28},{1,5},{5,9},{9,... | collective-permute-start | bytes 442376 | tf_op jit(solution)/shard_map/ppermute | solution.py:28
  67.2 0.3 collective-permute-done.4
  67.6 0.1 slice_reduce_fusion.1
  67.7 0.1 reshape_squeeze.14
  67.9 0.1 rev.31
  68.0 0.7 squeeze_broadcast_in_dim_reshape.14.refs_9_
  68.7 5.3 %collective-permute-done.5 = f32[1,3,3,4096]{3,2,1,0:T(4,128)S(1)} collective-permute-done((f32[1,3,3,4096]{3,2,1,0:T(4,128)}, f32[1,3,3,4096]{3,2,1,0:T(4,128)S(1)}, u32[]{:S(2)}, u32[]{:S(2)}) %collective-permute-start.5) | collective-permute-done | bytes 147488 | tf_op jit(solution)/shard_map/ppermute | solution.py:28
  74.0 0.1 slice_reduce_fusion
  74.1 0.1 reshape_squeeze.15
  74.3 0.1 rev.33
  74.4 0.7 squeeze_broadcast_in_dim_reshape.15.refs_10_
  75.1 0.0 collective-permute-done.7
  75.1 0.0 copy-start.2
  75.1 0.0 collective-permute-done.6
  75.2 0.0 copy-start.3
  75.2 0.7 copy-done.2
  75.8 0.1 copy-done.3
  75.9 21.5 %shard_map.174 = f32[3,64,4096]{2,1,0:T(8,128)} custom-call(f32[3]{0:T(128)} %bitcast.60, f32[3,64,4096]{2,1,0:T(8,128)} %bitcast.43, f32[6,3]{1,0:T(8,128)} %bitcast.57, f32[3,1,4096]{2,1,0:T(1,128)} %get-tuple-element.17.refs_3_, f32[3,1,4096]{2,1,0:T(1,128)} %get-tuple-element.18.refs_4_, f32[3,64,128]{2,1,0:T(8,128)} %get-tuple-element.19.refs_5_, ...), custom_call_target="tpu_custom_call" | custom-call | tf_op jit(solution)/shard_map/pallas_call | solution.py:319
  (18 shorter events, 0.2 us)
Async XLA Ops:
  21.3 6.7 %collective-permute-start = (f32[1,3,2,4096]{3,2,1,0:T(2,128)}, f32[1,3,2,4096]{3,2,1,0:T(2,128)S(1)}, u32[]{:S(2)}, u32[]{:S(2)}) collective-permute-start(f32[1,3,2,4096]{3,2,1,0:T(2,128)} %bitcast.55), channel_id=1, source_target_pairs={{4,0},{8,4},{12,8},{16,12},{20,16},{24,20},{28,24},{5,1},{9,5},{13... | collective-permute-start | bytes 294920 | tf_op jit(solution)/shard_map/ppermute | solution.py:28
  24.6 13.7 %collective-permute-start.3 = (f32[1,3,2,64,128]{4,3,2,1,0:T(8,128)}, f32[1,3,2,64,128]{4,3,2,1,0:T(8,128)S(1)}, u32[]{:S(2)}, u32[]{:S(2)}) collective-permute-start(f32[1,3,2,64,128]{4,3,2,1,0:T(8,128)} %bitcast.47), channel_id=1, source_target_pairs={{0,3},{1,0},{2,1},{3,2},{4,7},{5,4},{6,5},{7,6},{8,11},{9,8},{10,9... | collective-permute-start | bytes 589832 | tf_op jit(solution)/shard_map/ppermute | solution.py:33
  25.3 13.1 %collective-permute-start.2 = (f32[1,3,2,64,128]{4,3,2,1,0:T(8,128)}, f32[1,3,2,64,128]{4,3,2,1,0:T(8,128)S(1)}, u32[]{:S(2)}, u32[]{:S(2)}) collective-permute-start(f32[1,3,2,64,128]{4,3,2,1,0:T(8,128)} %bitcast.48), channel_id=1, source_target_pairs={{0,1},{1,2},{2,3},{3,0},{4,5},{5,6},{6,7},{7,4},{8,9},{9,10},{10,1... | collective-permute-start | bytes 589832 | tf_op jit(solution)/shard_map/ppermute | solution.py:33
  25.3 10.7 %collective-permute-start.1 = (f32[1,3,3,4096]{3,2,1,0:T(4,128)}, f32[1,3,3,4096]{3,2,1,0:T(4,128)S(1)}, u32[]{:S(2)}, u32[]{:S(2)}) collective-permute-start(f32[1,3,3,4096]{3,2,1,0:T(4,128)} %bitcast.46), channel_id=1, source_target_pairs={{0,4},{4,8},{8,12},{12,16},{16,20},{20,24},{24,28},{1,5},{5,9},{9,... | collective-permute-start | bytes 442376 | tf_op jit(solution)/shard_map/ppermute | solution.py:28
  38.4 0.9 copy-start
  38.4 0.8 copy-start.1
  60.6 6.9 %collective-permute-start.4 = (f32[1,3,2,4096]{3,2,1,0:T(2,128)}, f32[1,3,2,4096]{3,2,1,0:T(2,128)S(1)}, u32[]{:S(2)}, u32[]{:S(2)}) collective-permute-start(f32[1,3,2,4096]{3,2,1,0:T(2,128)} %bitcast.54), channel_id=1, source_target_pairs={{4,0},{8,4},{12,8},{16,12},{20,16},{24,20},{28,24},{5,1},{9,5},{13... | collective-permute-start | bytes 294920 | tf_op jit(solution)/shard_map/ppermute | solution.py:28
  62.6 12.6 %collective-permute-start.7 = (f32[1,3,2,64,128]{4,3,2,1,0:T(8,128)}, f32[1,3,2,64,128]{4,3,2,1,0:T(8,128)S(1)}, u32[]{:S(2)}, u32[]{:S(2)}) collective-permute-start(f32[1,3,2,64,128]{4,3,2,1,0:T(8,128)} %bitcast.50), channel_id=1, source_target_pairs={{0,3},{1,0},{2,1},{3,2},{4,7},{5,4},{6,5},{7,6},{8,11},{9,8},{10,9... | collective-permute-start | bytes 589832 | tf_op jit(solution)/shard_map/ppermute | solution.py:33
  63.4 11.8 %collective-permute-start.6 = (f32[1,3,2,64,128]{4,3,2,1,0:T(8,128)}, f32[1,3,2,64,128]{4,3,2,1,0:T(8,128)S(1)}, u32[]{:S(2)}, u32[]{:S(2)}) collective-permute-start(f32[1,3,2,64,128]{4,3,2,1,0:T(8,128)} %bitcast.51), channel_id=1, source_target_pairs={{0,1},{1,2},{2,3},{3,0},{4,5},{5,6},{6,7},{7,4},{8,9},{9,10},{10,1... | collective-permute-start | bytes 589832 | tf_op jit(solution)/shard_map/ppermute | solution.py:33
  63.4 10.6 %collective-permute-start.5 = (f32[1,3,3,4096]{3,2,1,0:T(4,128)}, f32[1,3,3,4096]{3,2,1,0:T(4,128)S(1)}, u32[]{:S(2)}, u32[]{:S(2)}) collective-permute-start(f32[1,3,3,4096]{3,2,1,0:T(4,128)} %bitcast.49), channel_id=1, source_target_pairs={{0,4},{4,8},{8,12},{12,16},{16,20},{20,24},{24,28},{1,5},{5,9},{9,... | collective-permute-start | bytes 442376 | tf_op jit(solution)/shard_map/ppermute | solution.py:28
  75.1 0.7 copy-start.2
  75.2 0.7 copy-start.3

commit v11 on v10

--- a/solution.py
+++ b/solution.py
@@ -154,7 +154,7 @@
     return jnp.dot(w6, jnp.concatenate([d1, d1, d2, d3], 0), preferred_element_type=f32)
 
 
-def solve_kernel(*refs, with_faces, emit_u, emit_sides, omega, zero_lam):
+def solve_kernel(*refs, with_faces, emit_u, emit_sides, omega, zero_lam, meta):
     it = iter(refs)
     mod_ref, f_ref = next(it), next(it)
     if with_faces:
@@ -267,10 +267,12 @@
     if emit_sides:
         m_row = jnp.full((1, nn), m, f32)
         xh_ref[0, 0:1, :] = m * u[n - 1:n] + 0.5 * slope(u[n - 1:n], u[n - 2:n - 1], u[n - 3:n - 2], u[n - 4:n - 3])
-        xh_ref[0, 1:2, :] = m_row
-        xh_ref[0, 2:3, :] = jnp.full((1, nn), code_ref[0], f32)
+        if meta:
+            xh_ref[0, 1:2, :] = m_row
+            xh_ref[0, 2:3, :] = jnp.full((1, nn), code_ref[0], f32)
         xl_ref[0, 0:1, :] = m * u[0:1] + 0.5 * slope(u[0:1], u[1:2], u[2:3], u[3:4])
-        xl_ref[0, 1:2, :] = m_row
+        if meta:
+            xl_ref[0, 1:2, :] = m_row
         c_hi = u[:, nn - w2:]
         c_hi2 = u[:, nn - 2 * w2:nn - w2]
         s_hi = m * c_hi + 0.5 * slope(c_hi, pltpu.roll(c_hi, n, 1), c_hi2, pltpu.roll(c_hi2, n, 1))
@@ -279,10 +281,11 @@
         s_lo = m * c_lo + 0.5 * slope(c_lo, pltpu.roll(c_lo, n, 1), c_lo2, pltpu.roll(c_lo2, n, 1))
         lane_s = lax.broadcasted_iota(jnp.int32, (n, w2), 1)
         y_ref[0, 0] = jnp.where(lane_s < n, s_lo, s_hi)
-        y_ref[0, 1] = jnp.full((n, w2), m, f32)
-
-
-def kernel_sweep(rhs, moduli, code, state=None, emit_u=True, emit_sides=False, omega=0.0):
+        if meta:
+            y_ref[0, 1] = jnp.full((n, w2), m, f32)
+
+
+def kernel_sweep(rhs, moduli, code, state=None, emit_u=True, emit_sides=False, omega=0.0, meta=False):
     ncomp, n, nn = rhs.shape
     q, p4, wy, exy, ez = consts(n)
     full = lambda shp: pl.BlockSpec(shp, lambda c: (0,) * len(shp))
@@ -297,8 +300,7 @@
             in_specs += [smem]
         else:
             in_specs += [smem, comp3((1, nn)), comp3((1, nn)), comp3((n, 2 * n))]
-        in_specs += [comp3((3, nn)), comp3((2, nn)), comp3((2, n, 2 * n)),
-                     comp3((1, nn)), comp3((1, nn)), comp3((2, n, 2 * n)), comp3((2, n, 2 * n))]
+        in_specs += [comp3(x.shape[1:]) for x in state[-7:]]
         args += list(state)
     in_specs += [full(q.shape), full(p4.shape), full(wy.shape), full(exy.shape), full(ez.shape), smem]
     args += [q, p4, wy, exy, ez, code]
@@ -307,15 +309,16 @@
         out_specs.append(comp3((n, nn)))
         out_shape.append(jax.ShapeDtypeStruct(rhs.shape, f32))
     if emit_sides:
-        out_specs += [comp3((3, nn)), comp3((2, nn)), comp3((2, n, 2 * n))]
-        out_shape += [jax.ShapeDtypeStruct((ncomp, 3, nn), f32), jax.ShapeDtypeStruct((ncomp, 2, nn), f32),
-                      jax.ShapeDtypeStruct((ncomp, 2, n, 2 * n), f32)]
+        rx_h, rx_l, r_y = (3, 2, 2) if meta else (1, 1, 1)
+        out_specs += [comp3((rx_h, nn)), comp3((rx_l, nn)), comp3((r_y, n, 2 * n))]
+        out_shape += [jax.ShapeDtypeStruct((ncomp, rx_h, nn), f32), jax.ShapeDtypeStruct((ncomp, rx_l, nn), f32),
+                      jax.ShapeDtypeStruct((ncomp, r_y, n, 2 * n), f32)]
         if state is not None:
             out_specs += [comp3((1, nn)), comp3((1, nn)), comp3((n, 2 * n))]
             out_shape += [jax.ShapeDtypeStruct((ncomp, 1, nn), f32), jax.ShapeDtypeStruct((ncomp, 1, nn), f32),
                           jax.ShapeDtypeStruct((ncomp, n, 2 * n), f32)]
     kernel = functools.partial(solve_kernel, with_faces=state is not None, emit_u=emit_u,
-                               emit_sides=emit_sides, omega=omega, zero_lam=zero_lam)
+                               emit_sides=emit_sides, omega=omega, zero_lam=zero_lam, meta=meta)
     return pl.pallas_call(
         kernel,
         grid=(ncomp,),
@@ -420,7 +423,7 @@
         omega = omegas[sweep - 1] if sweep > 0 else 0.0
         outs = [
             kernel_sweep(source_field[b], moduli[b], code_values[b:b + 1], state[b], emit_u=last,
-                         emit_sides=not last, omega=omega)
+                         emit_sides=not last, omega=omega, meta=sweep == 0)
             for b in range(blocks)
         ]
         if last:

time: 98.1 us -> 94.2 us (0.960)
  waiting for transfers between devices: 12.6 us -> 9.35 us
    ppermute x4, waiting for transfers between devices: 12.6 us -> 9.34 us  [shifted(): return lax.ppermute(shard, axis, pairs)]
  transfers between devices with their start and end apart: 8 -> 8, of which waited for: 4 -> 3; matrix products, arithmetic and copies ran while one was open for 5% -> 5% of each run, Pallas kernels for 0% -> 0%
where the time goes in v11:
time: 94.2 us; the launch traced here: 94 us
  Pallas kernels  63.5 us (67%)
  starting transfers between devices  12.9 us (14%)
  waiting for transfers between devices  9.35 us (10%)
  local copies, waits for them, and re-layouts  6.09 us (6%)
  between operations  1.74 us (2%)
    pallas_call x3, Pallas kernels, kernel_sweep(): pl.pallas_call(kernel, grid=(ncomp,), in_specs=in_specs, out_specs=out_sp...  63.5 us
    ppermute x4, starting transfers between devices, shifted(): return lax.ppermute(shard, axis, pairs)  11.7 us
    ppermute x4, waiting for transfers between devices, shifted(): return lax.ppermute(shard, axis, pairs)  9.34 us
  transfers between devices with their start and end apart: 8, of which 3 were waited for; matrix products, arithmetic and copies ran while one was open for 5% of the time, Pallas kernels for 0%

profile of v11, /device:TPU:24, one launch (start us, length us, event | category | flops | bytes accessed | tf_op | source)
XLA Modules:
  0.0 94.0 jit_solution(7996874138041374612)
XLA Ops:
  0.7 20.6 %shard_map.172 = (f32[3,3,4096]{2,1,0:T(4,128)}, f32[3,2,4096]{2,1,0:T(2,128)}, f32[3,2,64,128]{3,2,1,0:T(8,128)}) custom-call(f32[3]{0:T(128)} %bitcast.60, f32[3,64,4096]{2,1,0:T(8,128)} %bitcast.43, bf16[64,256]{1,0:T(8,128)(2,1)} %constant.77.clone.refs_2_.refs_10_.refs_13_, bf16[1024,256]{1,0:T(8,128)(2,1)} %constant.78.clone.refs_3_.refs_11_.refs_14_, ...), custom_call_target="tpu_custom_call" | custom-call | tf_op jit(solution)/shard_map/pallas_call | solution.py:322
  21.3 3.3 %collective-permute-start = (f32[1,3,2,4096]{3,2,1,0:T(2,128)}, f32[1,3,2,4096]{3,2,1,0:T(2,128)S(1)}, u32[]{:S(2)}, u32[]{:S(2)}) collective-permute-start(f32[1,3,2,4096]{3,2,1,0:T(2,128)} %bitcast.55), channel_id=1, source_target_pairs={{4,0},{8,4},{12,8},{16,12},{20,16},{24,20},{28,24},{5,1},{9,5},{13... | collective-permute-start | bytes 294920 | tf_op jit(solution)/shard_map/ppermute | solution.py:28
  24.6 0.7 collective-permute-start.3
  25.3 0.0 collective-permute-start.2
  25.3 2.5 %collective-permute-start.1 = (f32[1,3,3,4096]{3,2,1,0:T(4,128)}, f32[1,3,3,4096]{3,2,1,0:T(4,128)S(1)}, u32[]{:S(2)}, u32[]{:S(2)}) collective-permute-start(f32[1,3,3,4096]{3,2,1,0:T(4,128)} %bitcast.48), channel_id=1, source_target_pairs={{0,4},{4,8},{8,12},{12,16},{16,20},{20,24},{24,28},{1,5},{5,9},{9,... | collective-permute-start | bytes 442376 | tf_op jit(solution)/shard_map/ppermute | solution.py:28
  27.9 0.1 collective-permute-done
  28.0 0.1 slice_reduce_fusion.1
  28.2 0.1 reshape_squeeze.12
  28.3 0.1 rev.27
  28.4 0.7 squeeze_broadcast_in_dim_reshape.12.refs_6_
  29.1 6.9 %collective-permute-done.1 = f32[1,3,3,4096]{3,2,1,0:T(4,128)S(1)} collective-permute-done((f32[1,3,3,4096]{3,2,1,0:T(4,128)}, f32[1,3,3,4096]{3,2,1,0:T(4,128)S(1)}, u32[]{:S(2)}, u32[]{:S(2)}) %collective-permute-start.1) | collective-permute-done | bytes 147488 | tf_op jit(solution)/shard_map/ppermute | solution.py:28
  36.0 0.6 slice.33
  37.2 0.1 slice_reduce_fusion
  37.4 0.1 reshape_squeeze.13
  37.5 0.1 rev.29
  37.7 0.7 squeeze_broadcast_in_dim_reshape.13.refs_7_
  38.4 0.0 collective-permute-done.3
  38.4 0.0 copy-start
  38.4 0.0 collective-permute-done.2
  38.4 0.0 copy-start.1
  38.5 0.1 stack.24
  38.6 0.7 copy.34
  39.3 0.0 copy-done
  39.3 0.0 copy-done.1
  39.3 21.4 %shard_map.173 = (f32[3,1,4096]{2,1,0:T(1,128)}, f32[3,1,4096]{2,1,0:T(1,128)}, f32[3,1,64,128]{3,2,1,0:T(8,128)}, f32[3,1,4096]{2,1,0:T(1,128)}, f32[3,1,4096]{2,1,0:T(1,128)}, /*index=5*/f32[3,64,128]{2,1,0:T(8,128)}) custom-call(f32[3]{0:T(128)} %bitcast.61, f32[3,64,4096]{2,1,0:T(8,128)} %bitcast.44, f32[6,3]{1,0:T(8,128)} %bitcast.58, ...), custom_call_target="tpu_custom_call" | custom-call | tf_op jit(solution)/shard_map/pallas_call | solution.py:322
  60.7 1.9 %collective-permute-start.4 = (f32[1,3,1,4096]{3,2,1,0:T(1,128)}, f32[1,3,1,4096]{3,2,1,0:T(1,128)S(1)}, u32[]{:S(2)}, u32[]{:S(2)}) collective-permute-start(f32[1,3,1,4096]{3,2,1,0:T(1,128)} %bitcast.57), channel_id=1, source_target_pairs={{4,0},{8,4},{12,8},{16,12},{20,16},{24,20},{28,24},{5,1},{9,5},{13... | collective-permute-start | bytes 147464 | tf_op jit(solution)/shard_map/ppermute | solution.py:28
  62.6 3.9 %collective-permute-start.5 = (f32[1,3,1,4096]{3,2,1,0:T(1,128)}, f32[1,3,1,4096]{3,2,1,0:T(1,128)S(1)}, u32[]{:S(2)}, u32[]{:S(2)}) collective-permute-start(f32[1,3,1,4096]{3,2,1,0:T(1,128)} %bitcast.56), channel_id=1, source_target_pairs={{0,4},{4,8},{8,12},{12,16},{16,20},{20,24},{24,28},{1,5},{5,9},{9,... | collective-permute-start | bytes 147464 | tf_op jit(solution)/shard_map/ppermute | solution.py:28
  66.5 0.2 collective-permute-start.7
  66.8 0.3 collective-permute-start.6
  67.1 0.0 collective-permute-done.4
  67.1 0.1 reduce.2
  67.2 0.1 reshape_squeeze.14
  67.3 2.3 %collective-permute-done.5 = f32[1,3,1,4096]{3,2,1,0:T(1,128)S(1)} collective-permute-done((f32[1,3,1,4096]{3,2,1,0:T(1,128)}, f32[1,3,1,4096]{3,2,1,0:T(1,128)S(1)}, u32[]{:S(2)}, u32[]{:S(2)}) %collective-permute-start.5) | collective-permute-done | bytes 49184 | tf_op jit(solution)/shard_map/ppermute | solution.py:28
  69.7 0.1 reduce.3
  69.8 0.1 reshape_squeeze.15
  70.0 0.1 rev.33
  70.1 0.1 rev.31
  70.2 0.7 squeeze_broadcast_in_dim_reshape.15.refs_10_
  71.0 0.7 squeeze_broadcast_in_dim_reshape.14.refs_9_
  71.7 0.0 collective-permute-done.7
  71.7 0.0 copy-start.2
  71.7 0.0 collective-permute-done.6
  71.7 0.0 copy-start.3
  71.7 0.6 copy-done.2
  72.3 0.0 copy-done.3
  72.4 21.5 %shard_map.174 = f32[3,64,4096]{2,1,0:T(8,128)} custom-call(f32[3]{0:T(128)} %bitcast.62, f32[3,64,4096]{2,1,0:T(8,128)} %bitcast.45, f32[6,3]{1,0:T(8,128)} %bitcast.59, f32[3,1,4096]{2,1,0:T(1,128)} %get-tuple-element.17.refs_3_, f32[3,1,4096]{2,1,0:T(1,128)} %get-tuple-element.18.refs_4_, f32[3,64,128]{2,1,0:T(8,128)} %get-tuple-element.19.refs_5_, ...), custom_call_target="tpu_custom_call" | custom-call | tf_op jit(solution)/shard_map/pallas_call | solution.py:322
  (18 shorter events, 0.2 us)
Async XLA Ops:
  21.3 6.7 %collective-permute-start = (f32[1,3,2,4096]{3,2,1,0:T(2,128)}, f32[1,3,2,4096]{3,2,1,0:T(2,128)S(1)}, u32[]{:S(2)}, u32[]{:S(2)}) collective-permute-start(f32[1,3,2,4096]{3,2,1,0:T(2,128)} %bitcast.55), channel_id=1, source_target_pairs={{4,0},{8,4},{12,8},{16,12},{20,16},{24,20},{28,24},{5,1},{9,5},{13... | collective-permute-start | bytes 294920 | tf_op jit(solution)/shard_map/ppermute | solution.py:28
  24.6 13.8 %collective-permute-start.3 = (f32[1,3,2,64,128]{4,3,2,1,0:T(8,128)}, f32[1,3,2,64,128]{4,3,2,1,0:T(8,128)S(1)}, u32[]{:S(2)}, u32[]{:S(2)}) collective-permute-start(f32[1,3,2,64,128]{4,3,2,1,0:T(8,128)} %bitcast.49), channel_id=1, source_target_pairs={{0,3},{1,0},{2,1},{3,2},{4,7},{5,4},{6,5},{7,6},{8,11},{9,8},{10,9... | collective-permute-start | bytes 589832 | tf_op jit(solution)/shard_map/ppermute | solution.py:33
  25.3 13.1 %collective-permute-start.2 = (f32[1,3,2,64,128]{4,3,2,1,0:T(8,128)}, f32[1,3,2,64,128]{4,3,2,1,0:T(8,128)S(1)}, u32[]{:S(2)}, u32[]{:S(2)}) collective-permute-start(f32[1,3,2,64,128]{4,3,2,1,0:T(8,128)} %bitcast.50), channel_id=1, source_target_pairs={{0,1},{1,2},{2,3},{3,0},{4,5},{5,6},{6,7},{7,4},{8,9},{9,10},{10,1... | collective-permute-start | bytes 589832 | tf_op jit(solution)/shard_map/ppermute | solution.py:33
  25.3 10.7 %collective-permute-start.1 = (f32[1,3,3,4096]{3,2,1,0:T(4,128)}, f32[1,3,3,4096]{3,2,1,0:T(4,128)S(1)}, u32[]{:S(2)}, u32[]{:S(2)}) collective-permute-start(f32[1,3,3,4096]{3,2,1,0:T(4,128)} %bitcast.48), channel_id=1, source_target_pairs={{0,4},{4,8},{8,12},{12,16},{16,20},{20,24},{24,28},{1,5},{5,9},{9,... | collective-permute-start | bytes 442376 | tf_op jit(solution)/shard_map/ppermute | solution.py:28
  38.4 0.9 copy-start
  38.4 0.8 copy-start.1
  60.7 6.4 %collective-permute-start.4 = (f32[1,3,1,4096]{3,2,1,0:T(1,128)}, f32[1,3,1,4096]{3,2,1,0:T(1,128)S(1)}, u32[]{:S(2)}, u32[]{:S(2)}) collective-permute-start(f32[1,3,1,4096]{3,2,1,0:T(1,128)} %bitcast.57), channel_id=1, source_target_pairs={{4,0},{8,4},{12,8},{16,12},{20,16},{24,20},{28,24},{5,1},{9,5},{13... | collective-permute-start | bytes 147464 | tf_op jit(solution)/shard_map/ppermute | solution.py:28
  62.6 7.1 %collective-permute-start.5 = (f32[1,3,1,4096]{3,2,1,0:T(1,128)}, f32[1,3,1,4096]{3,2,1,0:T(1,128)S(1)}, u32[]{:S(2)}, u32[]{:S(2)}) collective-permute-start(f32[1,3,1,4096]{3,2,1,0:T(1,128)} %bitcast.56), channel_id=1, source_target_pairs={{0,4},{4,8},{8,12},{12,16},{16,20},{20,24},{24,28},{1,5},{5,9},{9,... | collective-permute-start | bytes 147464 | tf_op jit(solution)/shard_map/ppermute | solution.py:28
  66.5 5.2 %collective-permute-start.7 = (f32[1,3,1,64,128]{4,3,1,2,0:T(8,128)}, f32[1,3,1,64,128]{4,3,1,2,0:T(8,128)S(1)}, u32[]{:S(2)}, u32[]{:S(2)}) collective-permute-start(f32[1,3,1,64,128]{4,3,1,2,0:T(8,128)} %bitcast.51), channel_id=1, source_target_pairs={{0,3},{1,0},{2,1},{3,2},{4,7},{5,4},{6,5},{7,6},{8,11},{9,8},{10,9... | collective-permute-start | bytes 294920 | tf_op jit(solution)/shard_map/ppermute | solution.py:33
  66.8 4.9 %collective-permute-start.6 = (f32[1,3,1,64,128]{4,3,1,2,0:T(8,128)}, f32[1,3,1,64,128]{4,3,1,2,0:T(8,128)S(1)}, u32[]{:S(2)}, u32[]{:S(2)}) collective-permute-start(f32[1,3,1,64,128]{4,3,1,2,0:T(8,128)} %bitcast.52), channel_id=1, source_target_pairs={{0,1},{1,2},{2,3},{3,0},{4,5},{5,6},{6,7},{7,4},{8,9},{9,10},{10,1... | collective-permute-start | bytes 294920 | tf_op jit(solution)/shard_map/ppermute | solution.py:33
  71.7 0.6 copy-start.2
  71.7 0.7 copy-start.3

commit v12 on v11

--- a/solution.py
+++ b/solution.py
@@ -201,15 +201,15 @@
             return res + 0.25 * ((left + right) + diag * res)
 
         xu = 0.0 if zero_lam else lxu_ref[0]
-        res = (sxh_ref[0, 0:1, :] + rup_ref[0]) / (m + m_up) - xu
+        res = (sxh_ref[0, 0:1, 0:nn] + rup_ref[0]) / (m + m_up) - xu
         xhi_face = (xu + omega * smooth(res, lane_x, nn)) * has_up
         xd = 0.0 if zero_lam else lxd_ref[0]
-        res = (rdn_ref[0] + sxl_ref[0, 0:1, :]) / (m_dn + m) - xd
+        res = (rdn_ref[0] + sxl_ref[0, 0:1, 0:nn]) / (m_dn + m) - xd
         xlo_face = (xd + omega * smooth(res, lane_x, nn)) * has_dn
         ly = 0.0 if zero_lam else ly_ref[0]
         lo = lane_y < n
-        recv = pltpu.roll(jnp.where(lo, ryn_ref[0, 0], ryp_ref[0, 0]), n, 1)
-        res = (sy_ref[0, 0] + recv) / (m + jnp.where(lo, m_prev, m_next)) - ly
+        recv = pltpu.roll(jnp.where(lo, ryn_ref[0, 0, 0:n], ryp_ref[0, 0, 0:n]), n, 1)
+        res = (sy_ref[0, 0, 0:n] + recv) / (m + jnp.where(lo, m_prev, m_next)) - ly
         yadd = ly + omega * smooth(res, lane_y, w2)
         if nlx_ref is not None:
             nlx_ref[0] = xhi_face
@@ -266,13 +266,13 @@
         return m * (11.0 / 6.0 * p0 - 3.0 * p1 + 1.5 * p2 - p3 / 3.0)
     if emit_sides:
         m_row = jnp.full((1, nn), m, f32)
-        xh_ref[0, 0:1, :] = m * u[n - 1:n] + 0.5 * slope(u[n - 1:n], u[n - 2:n - 1], u[n - 3:n - 2], u[n - 4:n - 3])
+        xh_ref[0, 0:1, 0:nn] = m * u[n - 1:n] + 0.5 * slope(u[n - 1:n], u[n - 2:n - 1], u[n - 3:n - 2], u[n - 4:n - 3])
+        lane_t = lax.broadcasted_iota(jnp.int32, (1, w2), 1)
         if meta:
-            xh_ref[0, 1:2, :] = m_row
-            xh_ref[0, 2:3, :] = jnp.full((1, nn), code_ref[0], f32)
-        xl_ref[0, 0:1, :] = m * u[0:1] + 0.5 * slope(u[0:1], u[1:2], u[2:3], u[3:4])
+            xh_ref[0, 0:1, nn:nn + w2] = jnp.where(lane_t < n, m, code_ref[0])
+        xl_ref[0, 0:1, 0:nn] = m * u[0:1] + 0.5 * slope(u[0:1], u[1:2], u[2:3], u[3:4])
         if meta:
-            xl_ref[0, 1:2, :] = m_row
+            xl_ref[0, 0:1, nn:nn + w2] = jnp.full((1, w2), m, f32)
         c_hi = u[:, nn - w2:]
         c_hi2 = u[:, nn - 2 * w2:nn - w2]
         s_hi = m * c_hi + 0.5 * slope(c_hi, pltpu.roll(c_hi, n, 1), c_hi2, pltpu.roll(c_hi2, n, 1))
@@ -280,9 +280,9 @@
         c_lo2 = u[:, w2:2 * w2]
         s_lo = m * c_lo + 0.5 * slope(c_lo, pltpu.roll(c_lo, n, 1), c_lo2, pltpu.roll(c_lo2, n, 1))
         lane_s = lax.broadcasted_iota(jnp.int32, (n, w2), 1)
-        y_ref[0, 0] = jnp.where(lane_s < n, s_lo, s_hi)
+        y_ref[0, 0, 0:n] = jnp.where(lane_s < n, s_lo, s_hi)
         if meta:
-            y_ref[0, 1] = jnp.full((n, w2), m, f32)
+            y_ref[0, 0, n:n + 8] = jnp.full((8, w2), m, f32)
 
 
 def kernel_sweep(rhs, moduli, code, state=None, emit_u=True, emit_sides=False, omega=0.0, meta=False):
@@ -309,10 +309,10 @@
         out_specs.append(comp3((n, nn)))
         out_shape.append(jax.ShapeDtypeStruct(rhs.shape, f32))
     if emit_sides:
-        rx_h, rx_l, r_y = (3, 2, 2) if meta else (1, 1, 1)
-        out_specs += [comp3((rx_h, nn)), comp3((rx_l, nn)), comp3((r_y, n, 2 * n))]
-        out_shape += [jax.ShapeDtypeStruct((ncomp, rx_h, nn), f32), jax.ShapeDtypeStruct((ncomp, rx_l, nn), f32),
-                      jax.ShapeDtypeStruct((ncomp, r_y, n, 2 * n), f32)]
+        wx, ry = (nn + 2 * n, n + 8) if meta else (nn, n)
+        out_specs += [comp3((1, wx)), comp3((1, wx)), comp3((1, ry, 2 * n))]
+        out_shape += [jax.ShapeDtypeStruct((ncomp, 1, wx), f32), jax.ShapeDtypeStruct((ncomp, 1, wx), f32),
+                      jax.ShapeDtypeStruct((ncomp, 1, ry, 2 * n), f32)]
         if state is not None:
             out_specs += [comp3((1, nn)), comp3((1, nn)), comp3((n, 2 * n))]
             out_shape += [jax.ShapeDtypeStruct((ncomp, 1, nn), f32), jax.ShapeDtypeStruct((ncomp, 1, nn), f32),
@@ -436,12 +436,13 @@
         nxt = jnp.concatenate([ys[1:], shifted_2(ys[:1], "face", -1)], 0)
         prv = jnp.concatenate([shifted_2(ys[-1:], "face", 1), ys[:-1]], 0)
         if sweep == 0:
-            codes_down = lower[:, 0, 2, 0].astype(jnp.int32)
+            codes_down = lower[:, 0, 0, flat + extent].astype(jnp.int32)
             neighbour_moduli = jnp.stack(
-                [upper[:, :, 1, 0], lower[:, :, 1, 0], prv[:, :, 1, 0, 0], nxt[:, :, 1, 0, 0], has_up, has_down], 1
+                [upper[:, :, 0, flat], lower[:, :, 0, flat], prv[:, :, 0, extent, 0], nxt[:, :, 0, extent, 0],
+                 has_up, has_down], 1
             )
-        up_sum = orient(upper[:, :, 0], codes_here, extent)[:, :, None]
-        down_sum = orient(lower[:, :, 0], codes_down, extent)[:, :, None]
+        up_sum = orient(upper[:, :, 0, :flat], codes_here, extent)[:, :, None]
+        down_sum = orient(lower[:, :, 0, :flat], codes_down, extent)[:, :, None]
         state = [
             (neighbour_moduli[b], lam_x_up[b], lam_x_down[b], lam_y[b], xh[b], xl[b], ys[b],
              up_sum[b], down_sum[b], prv[b], nxt[b])

time: 94.2 us -> 92.3 us (0.980)
  waiting for transfers between devices: 9.35 us -> 6.08 us
  starting transfers between devices: 12.9 us -> 14.1 us
    ppermute x4, waiting for transfers between devices: 9.34 us -> 6.07 us  [shifted(): return lax.ppermute(shard, axis, pairs)]
    ppermute x4, starting transfers between devices: 11.7 us -> 12.9 us  [shifted(): return lax.ppermute(shard, axis, pairs)]
  transfers between devices with their start and end apart: 8 -> 8, of which waited for: 3 -> 2; matrix products, arithmetic and copies ran while one was open for 5% -> 6% of each run, Pallas kernels for 0% -> 0%
where the time goes in v12:
time: 92.3 us; the launch traced here: 92 us
  Pallas kernels  63.5 us (69%)
  starting transfers between devices  14.1 us (15%)
  local copies, waits for them, and re-layouts  6.16 us (7%)
  waiting for transfers between devices  6.08 us (7%)
  between operations  1.8 us (2%)
    pallas_call x3, Pallas kernels, kernel_sweep(): pl.pallas_call(kernel, grid=(ncomp,), in_specs=in_specs, out_specs=out_sp...  63.5 us
    ppermute x4, starting transfers between devices, shifted(): return lax.ppermute(shard, axis, pairs)  12.9 us
    ppermute x4, waiting for transfers between devices, shifted(): return lax.ppermute(shard, axis, pairs)  6.07 us
  transfers between devices with their start and end apart: 8, of which 2 were waited for; matrix products, arithmetic and copies ran while one was open for 6% of the time, Pallas kernels for 0%

profile of v12, /device:TPU:24, one launch (start us, length us, event | category | flops | bytes accessed | tf_op | source)
XLA Modules:
  0.0 92.0 jit_solution(16623920101290295494)
XLA Ops:
  0.7 20.7 %shard_map.172 = (f32[3,1,4224]{2,1,0:T(1,128)}, f32[3,1,4224]{2,1,0:T(1,128)}, f32[3,1,72,128]{3,2,1,0:T(8,128)}) custom-call(f32[3]{0:T(128)} %bitcast.62, f32[3,64,4096]{2,1,0:T(8,128)} %bitcast.45, bf16[64,256]{1,0:T(8,128)(2,1)} %constant.77.clone.refs_2_.refs_10_.refs_13_, bf16[1024,256]{1,0:T(8,128)(2,1)} %constant.78.clone.refs_3_.refs_11_.refs_14_, ...), custom_call_target="tpu_custom_call" | custom-call | tf_op jit(solution)/shard_map/pallas_call | solution.py:322
  21.3 3.4 %collective-permute-start.1 = (f32[1,3,1,4224]{3,2,1,0:T(1,128)}, f32[1,3,1,4224]{3,2,1,0:T(1,128)S(1)}, u32[]{:S(2)}, u32[]{:S(2)}) collective-permute-start(f32[1,3,1,4224]{3,2,1,0:T(1,128)} %bitcast.56), channel_id=1, source_target_pairs={{0,4},{4,8},{8,12},{12,16},{16,20},{20,24},{24,28},{1,5},{5,9},{9,... | collective-permute-start | bytes 152072 | tf_op jit(solution)/shard_map/ppermute | solution.py:28
  24.8 0.7 collective-permute-start.3
  25.5 0.0 collective-permute-start.2
  25.5 3.3 %collective-permute-start = (f32[1,3,1,4224]{3,2,1,0:T(1,128)}, f32[1,3,1,4224]{3,2,1,0:T(1,128)S(1)}, u32[]{:S(2)}, u32[]{:S(2)}) collective-permute-start(f32[1,3,1,4224]{3,2,1,0:T(1,128)} %bitcast.57), channel_id=1, source_target_pairs={{4,0},{8,4},{12,8},{16,12},{20,16},{24,20},{28,24},{5,1},{9,5},{13... | collective-permute-start | bytes 152072 | tf_op jit(solution)/shard_map/ppermute | solution.py:28
  28.8 0.0 collective-permute-done.1
  28.8 0.1 slice_reduce_fusion
  29.0 0.6 slice.33
  30.3 0.1 reshape_squeeze.13
  30.4 1.7 %collective-permute-done = f32[1,3,1,4224]{3,2,1,0:T(1,128)S(1)} collective-permute-done((f32[1,3,1,4224]{3,2,1,0:T(1,128)}, f32[1,3,1,4224]{3,2,1,0:T(1,128)S(1)}, u32[]{:S(2)}, u32[]{:S(2)}) %collective-permute-start) | collective-permute-done | bytes 50720 | tf_op jit(solution)/shard_map/ppermute | solution.py:28
  32.2 0.1 slice_reduce_fusion.1
  32.3 0.1 reshape_squeeze.12
  32.5 0.1 rev.27
  32.6 0.1 rev.29
  32.8 0.7 squeeze_broadcast_in_dim_reshape.12.refs_6_
  33.5 0.7 squeeze_broadcast_in_dim_reshape.13.refs_7_
  34.2 0.0 collective-permute-done.3
  34.2 0.0 copy-start
  34.2 0.0 collective-permute-done.2
  34.2 0.0 copy-start.1
  34.3 0.1 stack.24
  34.4 0.7 copy.37
  35.1 0.0 copy-done
  35.1 0.0 copy-done.1
  35.1 21.3 %shard_map.173 = (f32[3,1,4096]{2,1,0:T(1,128)}, f32[3,1,4096]{2,1,0:T(1,128)}, f32[3,1,64,128]{3,2,1,0:T(8,128)}, f32[3,1,4096]{2,1,0:T(1,128)}, f32[3,1,4096]{2,1,0:T(1,128)}, /*index=5*/f32[3,64,128]{2,1,0:T(8,128)}) custom-call(f32[3]{0:T(128)} %bitcast.63, f32[3,64,4096]{2,1,0:T(8,128)} %bitcast.46, f32[6,3]{1,0:T(8,128)} %bitcast.60, ...), custom_call_target="tpu_custom_call" | custom-call | tf_op jit(solution)/shard_map/pallas_call | solution.py:322
  56.4 4.2 %collective-permute-start.4 = (f32[1,3,1,4096]{3,2,1,0:T(1,128)}, f32[1,3,1,4096]{3,2,1,0:T(1,128)S(1)}, u32[]{:S(2)}, u32[]{:S(2)}) collective-permute-start(f32[1,3,1,4096]{3,2,1,0:T(1,128)} %bitcast.59), channel_id=1, source_target_pairs={{4,0},{8,4},{12,8},{16,12},{20,16},{24,20},{28,24},{5,1},{9,5},{13... | collective-permute-start | bytes 147464 | tf_op jit(solution)/shard_map/ppermute | solution.py:28
  60.6 1.9 %collective-permute-start.5 = (f32[1,3,1,4096]{3,2,1,0:T(1,128)}, f32[1,3,1,4096]{3,2,1,0:T(1,128)S(1)}, u32[]{:S(2)}, u32[]{:S(2)}) collective-permute-start(f32[1,3,1,4096]{3,2,1,0:T(1,128)} %bitcast.58), channel_id=1, source_target_pairs={{0,4},{4,8},{8,12},{12,16},{16,20},{20,24},{24,28},{1,5},{5,9},{9,... | collective-permute-start | bytes 147464 | tf_op jit(solution)/shard_map/ppermute | solution.py:28
  62.5 0.5 collective-permute-start.7
  63.1 0.0 collective-permute-start.6
  63.1 0.0 collective-permute-done.4
  63.1 0.1 reduce.2
  63.2 0.1 reshape_squeeze.14
  63.3 4.3 %collective-permute-done.5 = f32[1,3,1,4096]{3,2,1,0:T(1,128)S(1)} collective-permute-done((f32[1,3,1,4096]{3,2,1,0:T(1,128)}, f32[1,3,1,4096]{3,2,1,0:T(1,128)S(1)}, u32[]{:S(2)}, u32[]{:S(2)}) %collective-permute-start.5) | collective-permute-done | bytes 49184 | tf_op jit(solution)/shard_map/ppermute | solution.py:28
  67.7 0.1 reduce.3
  67.8 0.1 reshape_squeeze.15
  68.0 0.1 rev.33
  68.1 0.1 rev.31
  68.2 0.7 squeeze_broadcast_in_dim_reshape.15.refs_10_
  69.0 0.7 squeeze_broadcast_in_dim_reshape.14.refs_9_
  69.7 0.0 collective-permute-done.7
  69.7 0.0 copy-start.2
  69.7 0.0 collective-permute-done.6
  69.7 0.0 copy-start.3
  69.7 0.6 copy-done.2
  70.3 0.0 copy-done.3
  70.4 21.5 %shard_map.174 = f32[3,64,4096]{2,1,0:T(8,128)} custom-call(f32[3]{0:T(128)} %bitcast.64, f32[3,64,4096]{2,1,0:T(8,128)} %bitcast.47, f32[6,3]{1,0:T(8,128)} %bitcast.61, f32[3,1,4096]{2,1,0:T(1,128)} %get-tuple-element.17.refs_3_, f32[3,1,4096]{2,1,0:T(1,128)} %get-tuple-element.18.refs_4_, f32[3,64,128]{2,1,0:T(8,128)} %get-tuple-element.19.refs_5_, ...), custom_call_target="tpu_custom_call" | custom-call | tf_op jit(solution)/shard_map/pallas_call | solution.py:322
  (18 shorter events, 0.2 us)
Async XLA Ops:
  21.3 7.5 %collective-permute-start.1 = (f32[1,3,1,4224]{3,2,1,0:T(1,128)}, f32[1,3,1,4224]{3,2,1,0:T(1,128)S(1)}, u32[]{:S(2)}, u32[]{:S(2)}) collective-permute-start(f32[1,3,1,4224]{3,2,1,0:T(1,128)} %bitcast.56), channel_id=1, source_target_pairs={{0,4},{4,8},{8,12},{12,16},{16,20},{20,24},{24,28},{1,5},{5,9},{9,... | collective-permute-start | bytes 152072 | tf_op jit(solution)/shard_map/ppermute | solution.py:28
  24.8 9.4 %collective-permute-start.3 = (f32[1,3,1,72,128]{4,3,1,2,0:T(8,128)}, f32[1,3,1,72,128]{4,3,1,2,0:T(8,128)S(1)}, u32[]{:S(2)}, u32[]{:S(2)}) collective-permute-start(f32[1,3,1,72,128]{4,3,1,2,0:T(8,128)} %bitcast.50), channel_id=1, source_target_pairs={{0,3},{1,0},{2,1},{3,2},{4,7},{5,4},{6,5},{7,6},{8,11},{9,8},{10,9... | collective-permute-start | bytes 331784 | tf_op jit(solution)/shard_map/ppermute | solution.py:33
  25.5 8.8 %collective-permute-start.2 = (f32[1,3,1,72,128]{4,3,1,2,0:T(8,128)}, f32[1,3,1,72,128]{4,3,1,2,0:T(8,128)S(1)}, u32[]{:S(2)}, u32[]{:S(2)}) collective-permute-start(f32[1,3,1,72,128]{4,3,1,2,0:T(8,128)} %bitcast.51), channel_id=1, source_target_pairs={{0,1},{1,2},{2,3},{3,0},{4,5},{5,6},{6,7},{7,4},{8,9},{9,10},{10,1... | collective-permute-start | bytes 331784 | tf_op jit(solution)/shard_map/ppermute | solution.py:33
  25.5 6.7 %collective-permute-start = (f32[1,3,1,4224]{3,2,1,0:T(1,128)}, f32[1,3,1,4224]{3,2,1,0:T(1,128)S(1)}, u32[]{:S(2)}, u32[]{:S(2)}) collective-permute-start(f32[1,3,1,4224]{3,2,1,0:T(1,128)} %bitcast.57), channel_id=1, source_target_pairs={{4,0},{8,4},{12,8},{16,12},{20,16},{24,20},{28,24},{5,1},{9,5},{13... | collective-permute-start | bytes 152072 | tf_op jit(solution)/shard_map/ppermute | solution.py:28
  34.2 0.9 copy-start
  34.2 0.8 copy-start.1
  56.4 6.7 %collective-permute-start.4 = (f32[1,3,1,4096]{3,2,1,0:T(1,128)}, f32[1,3,1,4096]{3,2,1,0:T(1,128)S(1)}, u32[]{:S(2)}, u32[]{:S(2)}) collective-permute-start(f32[1,3,1,4096]{3,2,1,0:T(1,128)} %bitcast.59), channel_id=1, source_target_pairs={{4,0},{8,4},{12,8},{16,12},{20,16},{24,20},{28,24},{5,1},{9,5},{13... | collective-permute-start | bytes 147464 | tf_op jit(solution)/shard_map/ppermute | solution.py:28
  60.6 7.1 %collective-permute-start.5 = (f32[1,3,1,4096]{3,2,1,0:T(1,128)}, f32[1,3,1,4096]{3,2,1,0:T(1,128)S(1)}, u32[]{:S(2)}, u32[]{:S(2)}) collective-permute-start(f32[1,3,1,4096]{3,2,1,0:T(1,128)} %bitcast.58), channel_id=1, source_target_pairs={{0,4},{4,8},{8,12},{12,16},{16,20},{20,24},{24,28},{1,5},{5,9},{9,... | collective-permute-start | bytes 147464 | tf_op jit(solution)/shard_map/ppermute | solution.py:28
  62.5 7.2 %collective-permute-start.7 = (f32[1,3,1,64,128]{4,3,1,2,0:T(8,128)}, f32[1,3,1,64,128]{4,3,1,2,0:T(8,128)S(1)}, u32[]{:S(2)}, u32[]{:S(2)}) collective-permute-start(f32[1,3,1,64,128]{4,3,1,2,0:T(8,128)} %bitcast.52), channel_id=1, source_target_pairs={{0,3},{1,0},{2,1},{3,2},{4,7},{5,4},{6,5},{7,6},{8,11},{9,8},{10,9... | collective-permute-start | bytes 294920 | tf_op jit(solution)/shard_map/ppermute | solution.py:33
  63.1 6.6 %collective-permute-start.6 = (f32[1,3,1,64,128]{4,3,1,2,0:T(8,128)}, f32[1,3,1,64,128]{4,3,1,2,0:T(8,128)S(1)}, u32[]{:S(2)}, u32[]{:S(2)}) collective-permute-start(f32[1,3,1,64,128]{4,3,1,2,0:T(8,128)} %bitcast.53), channel_id=1, source_target_pairs={{0,1},{1,2},{2,3},{3,0},{4,5},{5,6},{6,7},{7,4},{8,9},{9,10},{10,1... | collective-permute-start | bytes 294920 | tf_op jit(solution)/shard_map/ppermute | solution.py:33
  69.7 0.6 copy-start.2
  69.7 0.7 copy-start.3

commit v13 on v12

--- a/solution.py
+++ b/solution.py
@@ -160,12 +160,12 @@
     if with_faces:
         nbm_ref = next(it)
         lxu_ref, lxd_ref, ly_ref = (None, None, None) if zero_lam else (next(it), next(it), next(it))
-        sxh_ref, sxl_ref, sy_ref, rup_ref, rdn_ref, ryp_ref, ryn_ref = (next(it) for _ in range(7))
+        sxh_ref, sxl_ref, sylo_ref, syhi_ref, rup_ref, rdn_ref, ryp_ref, ryn_ref = (next(it) for _ in range(8))
     q_ref, p_ref, wy_ref, exy_ref, ez_ref = next(it), next(it), next(it), next(it), next(it)
     code_ref = next(it)
     o_ref = next(it) if emit_u else None
     if emit_sides:
-        xh_ref, xl_ref, y_ref = next(it), next(it), next(it)
+        xh_ref, xl_ref, ylo_ref, yhi_ref = next(it), next(it), next(it), next(it)
     if with_faces and emit_sides:
         nlx_ref, nld_ref, nly_ref = next(it), next(it), next(it)
     elif with_faces:
@@ -208,8 +208,9 @@
         xlo_face = (xd + omega * smooth(res, lane_x, nn)) * has_dn
         ly = 0.0 if zero_lam else ly_ref[0]
         lo = lane_y < n
-        recv = pltpu.roll(jnp.where(lo, ryn_ref[0, 0, 0:n], ryp_ref[0, 0, 0:n]), n, 1)
-        res = (sy_ref[0, 0, 0:n] + recv) / (m + jnp.where(lo, m_prev, m_next)) - ly
+        recv = jnp.concatenate([ryp_ref[0, 0, 0:n], ryn_ref[0, 0, 0:n]], 1)
+        own = jnp.concatenate([sylo_ref[0, 0, 0:n], syhi_ref[0, 0, 0:n]], 1)
+        res = (own + recv) / (m + jnp.where(lo, m_prev, m_next)) - ly
         yadd = ly + omega * smooth(res, lane_y, w2)
         if nlx_ref is not None:
             nlx_ref[0] = xhi_face
@@ -280,9 +281,11 @@
         c_lo2 = u[:, w2:2 * w2]
         s_lo = m * c_lo + 0.5 * slope(c_lo, pltpu.roll(c_lo, n, 1), c_lo2, pltpu.roll(c_lo2, n, 1))
         lane_s = lax.broadcasted_iota(jnp.int32, (n, w2), 1)
-        y_ref[0, 0, 0:n] = jnp.where(lane_s < n, s_lo, s_hi)
+        ylo_ref[0, 0, 0:n] = s_lo[:, :n]
+        yhi_ref[0, 0, 0:n] = pltpu.roll(s_hi, n, 1)[:, :n]
         if meta:
-            y_ref[0, 0, n:n + 8] = jnp.full((8, w2), m, f32)
+            ylo_ref[0, 0, n:n + 8] = jnp.full((8, n), m, f32)
+            yhi_ref[0, 0, n:n + 8] = jnp.full((8, n), m, f32)
 
 
 def kernel_sweep(rhs, moduli, code, state=None, emit_u=True, emit_sides=False, omega=0.0, meta=False):
@@ -300,7 +303,7 @@
             in_specs += [smem]
         else:
             in_specs += [smem, comp3((1, nn)), comp3((1, nn)), comp3((n, 2 * n))]
-        in_specs += [comp3(x.shape[1:]) for x in state[-7:]]
+        in_specs += [comp3(x.shape[1:]) for x in state[-8:]]
         args += list(state)
     in_specs += [full(q.shape), full(p4.shape), full(wy.shape), full(exy.shape), full(ez.shape), smem]
     args += [q, p4, wy, exy, ez, code]
@@ -310,9 +313,9 @@
         out_shape.append(jax.ShapeDtypeStruct(rhs.shape, f32))
     if emit_sides:
         wx, ry = (nn + 2 * n, n + 8) if meta else (nn, n)
-        out_specs += [comp3((1, wx)), comp3((1, wx)), comp3((1, ry, 2 * n))]
+        out_specs += [comp3((1, wx)), comp3((1, wx)), comp3((1, ry, n)), comp3((1, ry, n))]
         out_shape += [jax.ShapeDtypeStruct((ncomp, 1, wx), f32), jax.ShapeDtypeStruct((ncomp, 1, wx), f32),
-                      jax.ShapeDtypeStruct((ncomp, 1, ry, 2 * n), f32)]
+                      jax.ShapeDtypeStruct((ncomp, 1, ry, n), f32), jax.ShapeDtypeStruct((ncomp, 1, ry, n), f32)]
         if state is not None:
             out_specs += [comp3((1, nn)), comp3((1, nn)), comp3((n, 2 * n))]
             out_shape += [jax.ShapeDtypeStruct((ncomp, 1, nn), f32), jax.ShapeDtypeStruct((ncomp, 1, nn), f32),
@@ -428,13 +431,13 @@
         ]
         if last:
             return jnp.stack([o[0] for o in outs], 0)[None]
-        xh, xl, ys = (jnp.stack([o[k] for o in outs], 0) for k in range(3))
+        xh, xl, ylo, yhi = (jnp.stack([o[k] for o in outs], 0) for k in range(4))
         if sweep > 0:
-            lam_x_up, lam_x_down, lam_y = (jnp.stack([o[k] for o in outs], 0) for k in range(3, 6))
+            lam_x_up, lam_x_down, lam_y = (jnp.stack([o[k] for o in outs], 0) for k in range(4, 7))
         upper = shifted(xl, "blk", -1)
         lower = shifted(xh, "blk", 1)
-        nxt = jnp.concatenate([ys[1:], shifted_2(ys[:1], "face", -1)], 0)
-        prv = jnp.concatenate([shifted_2(ys[-1:], "face", 1), ys[:-1]], 0)
+        nxt = jnp.concatenate([ylo[1:], shifted_2(ylo[:1], "face", -1)], 0)
+        prv = jnp.concatenate([shifted_2(yhi[-1:], "face", 1), yhi[:-1]], 0)
         if sweep == 0:
             codes_down = lower[:, 0, 0, flat + extent].astype(jnp.int32)
             neighbour_moduli = jnp.stack(
@@ -444,7 +447,7 @@
         up_sum = orient(upper[:, :, 0, :flat], codes_here, extent)[:, :, None]
         down_sum = orient(lower[:, :, 0, :flat], codes_down, extent)[:, :, None]
         state = [
-            (neighbour_moduli[b], lam_x_up[b], lam_x_down[b], lam_y[b], xh[b], xl[b], ys[b],
+            (neighbour_moduli[b], lam_x_up[b], lam_x_down[b], lam_y[b], xh[b], xl[b], ylo[b], yhi[b],
              up_sum[b], down_sum[b], prv[b], nxt[b])
             for b in range(blocks)
         ]

time: 92.3 us -> 91.8 us (level)
  waiting for transfers between devices: 6.08 us -> 4.25 us
    ppermute x4, waiting for transfers between devices: 6.07 us -> 3.51 us  [shifted(): return lax.ppermute(shard, axis, pairs)]
    ppermute x4, starting transfers between devices: 1.27 us -> 2.35 us  [shifted_2(): lax.ppermute(shard, axis, [(i, (i + by) % length) for i in range(length)])]
  transfers between devices with their start and end apart: 8 -> 8, of which waited for: 2 -> 3; matrix products, arithmetic and copies ran while one was open for 6% -> 6% of each run, Pallas kernels for 0% -> 0%
where the time goes in v13:
time: 91.8 us; the launch traced here: 91.1 us
  Pallas kernels  63.8 us (69%)
  starting transfers between devices  14.9 us (16%)
  local copies, waits for them, and re-layouts  6.1 us (7%)
  waiting for transfers between devices  4.25 us (5%)
  between operations  1.7 us (2%)
    pallas_call x3, Pallas kernels, kernel_sweep(): pl.pallas_call(kernel, grid=(ncomp,), in_specs=in_specs, out_specs=out_sp...  63.8 us
    ppermute x4, starting transfers between devices, shifted(): return lax.ppermute(shard, axis, pairs)  12.6 us
    ppermute x4, waiting for transfers between devices, shifted(): return lax.ppermute(shard, axis, pairs)  3.51 us
    ppermute x4, starting transfers between devices, shifted_2(): lax.ppermute(shard, axis, [(i, (i + by) % length) for i in range(length)])  2.35 us
  transfers between devices with their start and end apart: 8, of which 3 were waited for; matrix products, arithmetic and copies ran while one was open for 6% of the time, Pallas kernels for 0%

profile of v13, /device:TPU:24, one launch (start us, length us, event | category | flops | bytes accessed | tf_op | source)
XLA Modules:
  0.0 91.1 jit_solution(6825650425392004993)
XLA Ops:
  0.7 20.8 %shard_map.172 = (f32[3,1,4224]{2,1,0:T(1,128)}, f32[3,1,4224]{2,1,0:T(1,128)}, f32[3,1,72,64]{3,2,1,0:T(8,128)}, f32[3,1,72,64]{3,2,1,0:T(8,128)}) custom-call(f32[3]{0:T(128)} %bitcast.60, f32[3,64,4096]{2,1,0:T(8,128)} %bitcast.43, bf16[64,256]{1,0:T(8,128)(2,1)} %constant.77.clone.refs_2_.refs_11_.refs_14_, ...), custom_call_target="tpu_custom_call" | custom-call | tf_op jit(solution)/shard_map/pallas_call | solution.py:325
  21.5 3.4 %collective-permute-start.1 = (f32[1,3,1,4224]{3,2,1,0:T(1,128)}, f32[1,3,1,4224]{3,2,1,0:T(1,128)S(1)}, u32[]{:S(2)}, u32[]{:S(2)}) collective-permute-start(f32[1,3,1,4224]{3,2,1,0:T(1,128)} %bitcast.54), channel_id=1, source_target_pairs={{0,4},{4,8},{8,12},{12,16},{16,20},{20,24},{24,28},{1,5},{5,9},{9,... | collective-permute-start | bytes 152072 | tf_op jit(solution)/shard_map/ppermute | solution.py:28
  24.9 3.3 %collective-permute-start = (f32[1,3,1,4224]{3,2,1,0:T(1,128)}, f32[1,3,1,4224]{3,2,1,0:T(1,128)S(1)}, u32[]{:S(2)}, u32[]{:S(2)}) collective-permute-start(f32[1,3,1,4224]{3,2,1,0:T(1,128)} %bitcast.55), channel_id=1, source_target_pairs={{4,0},{8,4},{12,8},{16,12},{20,16},{24,20},{28,24},{5,1},{9,5},{13... | collective-permute-start | bytes 152072 | tf_op jit(solution)/shard_map/ppermute | solution.py:28
  28.2 0.4 collective-permute-start.3
  28.7 0.1 collective-permute-start.2
  28.8 0.0 collective-permute-done.1
  28.8 0.1 slice_reduce_fusion
  29.0 0.6 slice.33
  30.2 0.1 reshape_squeeze.13
  30.3 0.8 collective-permute-done
  31.1 0.1 slice_reduce_fusion.1
  31.3 0.1 reshape_squeeze.12
  31.4 0.1 rev.27
  31.6 0.1 rev.29
  31.7 0.7 squeeze_broadcast_in_dim_reshape.12.refs_7_
  32.5 0.7 squeeze_broadcast_in_dim_reshape.13.refs_8_
  33.2 0.0 collective-permute-done.3
  33.2 0.0 copy-start
  33.2 0.7 collective-permute-done.2
  33.9 0.0 copy-start.1
  33.9 0.1 stack.31
  34.0 0.7 copy.31
  34.7 0.0 copy-done
  34.7 0.0 copy-done.1
  34.7 21.5 %shard_map.173 = (f32[3,1,4096]{2,1,0:T(1,128)}, f32[3,1,4096]{2,1,0:T(1,128)}, f32[3,1,64,64]{3,2,1,0:T(8,128)}, f32[3,1,64,64]{3,2,1,0:T(8,128)}, f32[3,1,4096...) custom-call(f32[3]{0:T(128)} %bitcast.61, f32[3,64,4096]{2,1,0:T(8,128)} %bitcast.44, f32[6,3]{1,0:T(8,128)} %bitcast.58, ...), custom_call_target="tpu_custom_call" | custom-call | tf_op jit(solution)/shard_map/pallas_call | solution.py:325
  56.2 3.5 %collective-permute-start.4 = (f32[1,3,1,4096]{3,2,1,0:T(1,128)}, f32[1,3,1,4096]{3,2,1,0:T(1,128)S(1)}, u32[]{:S(2)}, u32[]{:S(2)}) collective-permute-start(f32[1,3,1,4096]{3,2,1,0:T(1,128)} %bitcast.57), channel_id=1, source_target_pairs={{4,0},{8,4},{12,8},{16,12},{20,16},{24,20},{28,24},{5,1},{9,5},{13... | collective-permute-start | bytes 147464 | tf_op jit(solution)/shard_map/ppermute | solution.py:28
  59.8 2.3 %collective-permute-start.5 = (f32[1,3,1,4096]{3,2,1,0:T(1,128)}, f32[1,3,1,4096]{3,2,1,0:T(1,128)S(1)}, u32[]{:S(2)}, u32[]{:S(2)}) collective-permute-start(f32[1,3,1,4096]{3,2,1,0:T(1,128)} %bitcast.56), channel_id=1, source_target_pairs={{0,4},{4,8},{8,12},{12,16},{16,20},{20,24},{24,28},{1,5},{5,9},{9,... | collective-permute-start | bytes 147464 | tf_op jit(solution)/shard_map/ppermute | solution.py:28
  62.1 0.1 collective-permute-start.6
  62.2 1.7 %collective-permute-start.7 = (f32[1,3,1,64,64]{4,3,1,2,0:T(8,128)}, f32[1,3,1,64,64]{4,3,1,2,0:T(8,128)S(1)}, u32[]{:S(2)}, u32[]{:S(2)}) collective-permute-start(f32[1,3,1,64,64]{4,3,1,2,0:T(8,128)} %bitcast.50), channel_id=1, source_target_pairs={{0,3},{1,0},{2,1},{3,2},{4,7},{5,4},{6,5},{7,6},{8,11},{9,8},{10,9... | collective-permute-start | bytes 147464 | tf_op jit(solution)/shard_map/ppermute | solution.py:33
  63.9 0.0 collective-permute-done.4
  63.9 0.1 reduce.2
  64.0 0.1 reshape_squeeze.14
  64.1 2.7 %collective-permute-done.5 = f32[1,3,1,4096]{3,2,1,0:T(1,128)S(1)} collective-permute-done((f32[1,3,1,4096]{3,2,1,0:T(1,128)}, f32[1,3,1,4096]{3,2,1,0:T(1,128)S(1)}, u32[]{:S(2)}, u32[]{:S(2)}) %collective-permute-start.5) | collective-permute-done | bytes 49184 | tf_op jit(solution)/shard_map/ppermute | solution.py:28
  66.8 0.1 reduce.3
  67.0 0.1 reshape_squeeze.15
  67.1 0.1 rev.33
  67.3 0.1 rev.31
  67.4 0.7 squeeze_broadcast_in_dim_reshape.15.refs_11_
  68.1 0.7 squeeze_broadcast_in_dim_reshape.14.refs_10_
  68.9 0.0 collective-permute-done.6
  68.9 0.0 copy-start.2
  68.9 0.0 collective-permute-done.7
  68.9 0.0 copy-start.3
  68.9 0.6 copy-done.2
  69.5 0.0 copy-done.3
  69.5 21.4 %shard_map.174 = f32[3,64,4096]{2,1,0:T(8,128)} custom-call(f32[3]{0:T(128)} %bitcast.62, f32[3,64,4096]{2,1,0:T(8,128)} %bitcast.45, f32[6,3]{1,0:T(8,128)} %bitcast.59, f32[3,1,4096]{2,1,0:T(1,128)} %get-tuple-element.20.refs_3_, f32[3,1,4096]{2,1,0:T(1,128)} %get-tuple-element.21.refs_4_, f32[3,64,128]{2,1,0:T(8,128)} %get-tuple-element.22.refs_5_, ...), custom_call_target="tpu_custom_call" | custom-call | tf_op jit(solution)/shard_map/pallas_call | solution.py:325
  (18 shorter events, 0.2 us)
Async XLA Ops:
  21.5 7.3 %collective-permute-start.1 = (f32[1,3,1,4224]{3,2,1,0:T(1,128)}, f32[1,3,1,4224]{3,2,1,0:T(1,128)S(1)}, u32[]{:S(2)}, u32[]{:S(2)}) collective-permute-start(f32[1,3,1,4224]{3,2,1,0:T(1,128)} %bitcast.54), channel_id=1, source_target_pairs={{0,4},{4,8},{8,12},{12,16},{16,20},{20,24},{24,28},{1,5},{5,9},{9,... | collective-permute-start | bytes 152072 | tf_op jit(solution)/shard_map/ppermute | solution.py:28
  24.9 6.2 %collective-permute-start = (f32[1,3,1,4224]{3,2,1,0:T(1,128)}, f32[1,3,1,4224]{3,2,1,0:T(1,128)S(1)}, u32[]{:S(2)}, u32[]{:S(2)}) collective-permute-start(f32[1,3,1,4224]{3,2,1,0:T(1,128)} %bitcast.55), channel_id=1, source_target_pairs={{4,0},{8,4},{12,8},{16,12},{20,16},{24,20},{28,24},{5,1},{9,5},{13... | collective-permute-start | bytes 152072 | tf_op jit(solution)/shard_map/ppermute | solution.py:28
  28.2 4.9 %collective-permute-start.3 = (f32[1,3,1,72,64]{4,3,1,2,0:T(8,128)}, f32[1,3,1,72,64]{4,3,1,2,0:T(8,128)S(1)}, u32[]{:S(2)}, u32[]{:S(2)}) collective-permute-start(f32[1,3,1,72,64]{4,3,1,2,0:T(8,128)} %bitcast.48), channel_id=1, source_target_pairs={{0,3},{1,0},{2,1},{3,2},{4,7},{5,4},{6,5},{7,6},{8,11},{9,8},{10,9... | collective-permute-start | bytes 165896 | tf_op jit(solution)/shard_map/ppermute | solution.py:33
  28.7 5.3 %collective-permute-start.2 = (f32[1,3,1,72,64]{4,3,1,2,0:T(8,128)}, f32[1,3,1,72,64]{4,3,1,2,0:T(8,128)S(1)}, u32[]{:S(2)}, u32[]{:S(2)}) collective-permute-start(f32[1,3,1,72,64]{4,3,1,2,0:T(8,128)} %bitcast.49), channel_id=1, source_target_pairs={{0,1},{1,2},{2,3},{3,0},{4,5},{5,6},{6,7},{7,4},{8,9},{9,10},{10,1... | collective-permute-start | bytes 165896 | tf_op jit(solution)/shard_map/ppermute | solution.py:33
  33.2 1.6 %copy-start = (f32[1,3,1,72,64]{4,3,1,2,0:T(8,128)}, f32[1,3,1,72,64]{4,3,1,2,0:T(8,128)S(1)}, u32[]{:S(2)}) copy-start(f32[1,3,1,72,64]{4,3,1,2,0:T(8,128)S(1)} %collective-permute-done.3) | copy-start | bytes 165892
  33.9 0.8 copy-start.1
  56.2 7.7 %collective-permute-start.4 = (f32[1,3,1,4096]{3,2,1,0:T(1,128)}, f32[1,3,1,4096]{3,2,1,0:T(1,128)S(1)}, u32[]{:S(2)}, u32[]{:S(2)}) collective-permute-start(f32[1,3,1,4096]{3,2,1,0:T(1,128)} %bitcast.57), channel_id=1, source_target_pairs={{4,0},{8,4},{12,8},{16,12},{20,16},{24,20},{28,24},{5,1},{9,5},{13... | collective-permute-start | bytes 147464 | tf_op jit(solution)/shard_map/ppermute | solution.py:28
  59.8 7.1 %collective-permute-start.5 = (f32[1,3,1,4096]{3,2,1,0:T(1,128)}, f32[1,3,1,4096]{3,2,1,0:T(1,128)S(1)}, u32[]{:S(2)}, u32[]{:S(2)}) collective-permute-start(f32[1,3,1,4096]{3,2,1,0:T(1,128)} %bitcast.56), channel_id=1, source_target_pairs={{0,4},{4,8},{8,12},{12,16},{16,20},{20,24},{24,28},{1,5},{5,9},{9,... | collective-permute-start | bytes 147464 | tf_op jit(solution)/shard_map/ppermute | solution.py:28
  62.1 6.8 %collective-permute-start.6 = (f32[1,3,1,64,64]{4,3,1,2,0:T(8,128)}, f32[1,3,1,64,64]{4,3,1,2,0:T(8,128)S(1)}, u32[]{:S(2)}, u32[]{:S(2)}) collective-permute-start(f32[1,3,1,64,64]{4,3,1,2,0:T(8,128)} %bitcast.51), channel_id=1, source_target_pairs={{0,1},{1,2},{2,3},{3,0},{4,5},{5,6},{6,7},{7,4},{8,9},{9,10},{10,1... | collective-permute-start | bytes 147464 | tf_op jit(solution)/shard_map/ppermute | solution.py:33
  62.2 6.7 %collective-permute-start.7 = (f32[1,3,1,64,64]{4,3,1,2,0:T(8,128)}, f32[1,3,1,64,64]{4,3,1,2,0:T(8,128)S(1)}, u32[]{:S(2)}, u32[]{:S(2)}) collective-permute-start(f32[1,3,1,64,64]{4,3,1,2,0:T(8,128)} %bitcast.50), channel_id=1, source_target_pairs={{0,3},{1,0},{2,1},{3,2},{4,7},{5,4},{6,5},{7,6},{8,11},{9,8},{10,9... | collective-permute-start | bytes 147464 | tf_op jit(solution)/shard_map/ppermute | solution.py:33
  68.9 0.6 copy-start.2
  68.9 0.7 copy-start.3

commit v14 on v13

--- a/solution.py
+++ b/solution.py
@@ -208,8 +208,8 @@
         xlo_face = (xd + omega * smooth(res, lane_x, nn)) * has_dn
         ly = 0.0 if zero_lam else ly_ref[0]
         lo = lane_y < n
-        recv = jnp.concatenate([ryp_ref[0, 0, 0:n], ryn_ref[0, 0, 0:n]], 1)
-        own = jnp.concatenate([sylo_ref[0, 0, 0:n], syhi_ref[0, 0, 0:n]], 1)
+        recv = jnp.concatenate([ryp_ref[0, 0:n], ryn_ref[0, 0:n]], 1)
+        own = jnp.concatenate([sylo_ref[0, 0:n], syhi_ref[0, 0:n]], 1)
         res = (own + recv) / (m + jnp.where(lo, m_prev, m_next)) - ly
         yadd = ly + omega * smooth(res, lane_y, w2)
         if nlx_ref is not None:
@@ -281,11 +281,11 @@
         c_lo2 = u[:, w2:2 * w2]
         s_lo = m * c_lo + 0.5 * slope(c_lo, pltpu.roll(c_lo, n, 1), c_lo2, pltpu.roll(c_lo2, n, 1))
         lane_s = lax.broadcasted_iota(jnp.int32, (n, w2), 1)
-        ylo_ref[0, 0, 0:n] = s_lo[:, :n]
-        yhi_ref[0, 0, 0:n] = pltpu.roll(s_hi, n, 1)[:, :n]
+        ylo_ref[0, 0:n] = s_lo[:, :n]
+        yhi_ref[0, 0:n] = pltpu.roll(s_hi, n, 1)[:, :n]
         if meta:
-            ylo_ref[0, 0, n:n + 8] = jnp.full((8, n), m, f32)
-            yhi_ref[0, 0, n:n + 8] = jnp.full((8, n), m, f32)
+            ylo_ref[0, n:n + 8] = jnp.full((8, n), m, f32)
+            yhi_ref[0, n:n + 8] = jnp.full((8, n), m, f32)
 
 
 def kernel_sweep(rhs, moduli, code, state=None, emit_u=True, emit_sides=False, omega=0.0, meta=False):
@@ -313,9 +313,9 @@
         out_shape.append(jax.ShapeDtypeStruct(rhs.shape, f32))
     if emit_sides:
         wx, ry = (nn + 2 * n, n + 8) if meta else (nn, n)
-        out_specs += [comp3((1, wx)), comp3((1, wx)), comp3((1, ry, n)), comp3((1, ry, n))]
+        out_specs += [comp3((1, wx)), comp3((1, wx)), comp3((ry, n)), comp3((ry, n))]
         out_shape += [jax.ShapeDtypeStruct((ncomp, 1, wx), f32), jax.ShapeDtypeStruct((ncomp, 1, wx), f32),
-                      jax.ShapeDtypeStruct((ncomp, 1, ry, n), f32), jax.ShapeDtypeStruct((ncomp, 1, ry, n), f32)]
+                      jax.ShapeDtypeStruct((ncomp, ry, n), f32), jax.ShapeDtypeStruct((ncomp, ry, n), f32)]
         if state is not None:
             out_specs += [comp3((1, nn)), comp3((1, nn)), comp3((n, 2 * n))]
             out_shape += [jax.ShapeDtypeStruct((ncomp, 1, nn), f32), jax.ShapeDtypeStruct((ncomp, 1, nn), f32),
@@ -441,7 +441,7 @@
         if sweep == 0:
             codes_down = lower[:, 0, 0, flat + extent].astype(jnp.int32)
             neighbour_moduli = jnp.stack(
-                [upper[:, :, 0, flat], lower[:, :, 0, flat], prv[:, :, 0, extent, 0], nxt[:, :, 0, extent, 0],
+                [upper[:, :, 0, flat], lower[:, :, 0, flat], prv[:, :, extent, 0], nxt[:, :, extent, 0],
                  has_up, has_down], 1
             )
         up_sum = orient(upper[:, :, 0, :flat], codes_here, extent)[:, :, None]

time: 91.8 us -> 91.8 us (level)
  no operation moved by 1% of the time
where the time goes in v14:
time: 91.8 us; the launch traced here: 91.1 us
  Pallas kernels  63.8 us (69%)
  starting transfers between devices  14.9 us (16%)
  local copies, waits for them, and re-layouts  6.1 us (7%)
  waiting for transfers between devices  4.25 us (5%)
  between operations  1.7 us (2%)
    pallas_call x3, Pallas kernels, kernel_sweep(): pl.pallas_call(kernel, grid=(ncomp,), in_specs=in_specs, out_specs=out_sp...  63.8 us
    ppermute x4, starting transfers between devices, shifted(): return lax.ppermute(shard, axis, pairs)  12.6 us
    ppermute x4, waiting for transfers between devices, shifted(): return lax.ppermute(shard, axis, pairs)  3.51 us
    ppermute x4, starting transfers between devices, shifted_2(): lax.ppermute(shard, axis, [(i, (i + by) % length) for i in range(length)])  2.35 us
  transfers between devices with their start and end apart: 8, of which 3 were waited for; matrix products, arithmetic and copies ran while one was open for 6% of the time, Pallas kernels for 0%

profile of v14, /device:TPU:24, one launch (start us, length us, event | category | flops | bytes accessed | tf_op | source)
XLA Modules:
  0.0 91.1 jit_solution(6825650425392004993)
XLA Ops:
  0.7 20.8 %shard_map.172 = (f32[3,1,4224]{2,1,0:T(1,128)}, f32[3,1,4224]{2,1,0:T(1,128)}, f32[3,72,64]{2,1,0:T(8,128)}, f32[3,72,64]{2,1,0:T(8,128)}) custom-call(f32[3]{0:T(128)} %bitcast.60, f32[3,64,4096]{2,1,0:T(8,128)} %bitcast.43, bf16[64,256]{1,0:T(8,128)(2,1)} %constant.77.clone.refs_2_.refs_11_.refs_14_, ...), custom_call_target="tpu_custom_call" | custom-call | tf_op jit(solution)/shard_map/pallas_call | solution.py:325
  21.5 3.4 %collective-permute-start.1 = (f32[1,3,1,4224]{3,2,1,0:T(1,128)}, f32[1,3,1,4224]{3,2,1,0:T(1,128)S(1)}, u32[]{:S(2)}, u32[]{:S(2)}) collective-permute-start(f32[1,3,1,4224]{3,2,1,0:T(1,128)} %bitcast.54), channel_id=1, source_target_pairs={{0,4},{4,8},{8,12},{12,16},{16,20},{20,24},{24,28},{1,5},{5,9},{9,... | collective-permute-start | bytes 152072 | tf_op jit(solution)/shard_map/ppermute | solution.py:28
  24.9 3.3 %collective-permute-start = (f32[1,3,1,4224]{3,2,1,0:T(1,128)}, f32[1,3,1,4224]{3,2,1,0:T(1,128)S(1)}, u32[]{:S(2)}, u32[]{:S(2)}) collective-permute-start(f32[1,3,1,4224]{3,2,1,0:T(1,128)} %bitcast.55), channel_id=1, source_target_pairs={{4,0},{8,4},{12,8},{16,12},{20,16},{24,20},{28,24},{5,1},{9,5},{13... | collective-permute-start | bytes 152072 | tf_op jit(solution)/shard_map/ppermute | solution.py:28
  28.2 0.4 collective-permute-start.3
  28.7 0.1 collective-permute-start.2
  28.8 0.0 collective-permute-done.1
  28.8 0.1 slice_reduce_fusion
  29.0 0.6 slice.33
  30.2 0.1 reshape_squeeze.13
  30.3 0.8 collective-permute-done
  31.1 0.1 slice_reduce_fusion.1
  31.3 0.1 reshape_squeeze.12
  31.4 0.1 rev.27
  31.6 0.1 rev.29
  31.7 0.7 squeeze_broadcast_in_dim_reshape.12.refs_7_
  32.5 0.7 squeeze_broadcast_in_dim_reshape.13.refs_8_
  33.2 0.0 collective-permute-done.3
  33.2 0.0 copy-start
  33.2 0.7 collective-permute-done.2
  33.9 0.0 copy-start.1
  33.9 0.1 stack.31
  34.0 0.7 copy.31
  34.7 0.0 copy-done
  34.7 0.0 copy-done.1
  34.7 21.5 %shard_map.173 = (f32[3,1,4096]{2,1,0:T(1,128)}, f32[3,1,4096]{2,1,0:T(1,128)}, f32[3,64,64]{2,1,0:T(8,128)}, f32[3,64,64]{2,1,0:T(8,128)}, f32[3,1,4096]{2,1,0:...) custom-call(f32[3]{0:T(128)} %bitcast.61, f32[3,64,4096]{2,1,0:T(8,128)} %bitcast.44, f32[6,3]{1,0:T(8,128)} %bitcast.58, ...), custom_call_target="tpu_custom_call" | custom-call | tf_op jit(solution)/shard_map/pallas_call | solution.py:325
  56.2 3.5 %collective-permute-start.4 = (f32[1,3,1,4096]{3,2,1,0:T(1,128)}, f32[1,3,1,4096]{3,2,1,0:T(1,128)S(1)}, u32[]{:S(2)}, u32[]{:S(2)}) collective-permute-start(f32[1,3,1,4096]{3,2,1,0:T(1,128)} %bitcast.57), channel_id=1, source_target_pairs={{4,0},{8,4},{12,8},{16,12},{20,16},{24,20},{28,24},{5,1},{9,5},{13... | collective-permute-start | bytes 147464 | tf_op jit(solution)/shard_map/ppermute | solution.py:28
  59.8 2.3 %collective-permute-start.5 = (f32[1,3,1,4096]{3,2,1,0:T(1,128)}, f32[1,3,1,4096]{3,2,1,0:T(1,128)S(1)}, u32[]{:S(2)}, u32[]{:S(2)}) collective-permute-start(f32[1,3,1,4096]{3,2,1,0:T(1,128)} %bitcast.56), channel_id=1, source_target_pairs={{0,4},{4,8},{8,12},{12,16},{16,20},{20,24},{24,28},{1,5},{5,9},{9,... | collective-permute-start | bytes 147464 | tf_op jit(solution)/shard_map/ppermute | solution.py:28
  62.1 0.1 collective-permute-start.6
  62.2 1.7 %collective-permute-start.7 = (f32[1,3,64,64]{3,2,1,0:T(8,128)}, f32[1,3,64,64]{3,2,1,0:T(8,128)S(1)}, u32[]{:S(2)}, u32[]{:S(2)}) collective-permute-start(f32[1,3,64,64]{3,2,1,0:T(8,128)} %bitcast.50), channel_id=1, source_target_pairs={{0,3},{1,0},{2,1},{3,2},{4,7},{5,4},{6,5},{7,6},{8,11},{9,8},{10,9... | collective-permute-start | bytes 147464 | tf_op jit(solution)/shard_map/ppermute | solution.py:33
  63.9 0.0 collective-permute-done.4
  63.9 0.1 reduce.2
  64.0 0.1 reshape_squeeze.14
  64.1 2.7 %collective-permute-done.5 = f32[1,3,1,4096]{3,2,1,0:T(1,128)S(1)} collective-permute-done((f32[1,3,1,4096]{3,2,1,0:T(1,128)}, f32[1,3,1,4096]{3,2,1,0:T(1,128)S(1)}, u32[]{:S(2)}, u32[]{:S(2)}) %collective-permute-start.5) | collective-permute-done | bytes 49184 | tf_op jit(solution)/shard_map/ppermute | solution.py:28
  66.8 0.1 reduce.3
  67.0 0.1 reshape_squeeze.15
  67.1 0.1 rev.33
  67.3 0.1 rev.31
  67.4 0.7 squeeze_broadcast_in_dim_reshape.15.refs_11_
  68.1 0.7 squeeze_broadcast_in_dim_reshape.14.refs_10_
  68.9 0.0 collective-permute-done.6
  68.9 0.0 copy-start.2
  68.9 0.0 collective-permute-done.7
  68.9 0.0 copy-start.3
  68.9 0.6 copy-done.2
  69.5 0.0 copy-done.3
  69.5 21.4 %shard_map.174 = f32[3,64,4096]{2,1,0:T(8,128)} custom-call(f32[3]{0:T(128)} %bitcast.62, f32[3,64,4096]{2,1,0:T(8,128)} %bitcast.45, f32[6,3]{1,0:T(8,128)} %bitcast.59, f32[3,1,4096]{2,1,0:T(1,128)} %get-tuple-element.20.refs_3_, f32[3,1,4096]{2,1,0:T(1,128)} %get-tuple-element.21.refs_4_, f32[3,64,128]{2,1,0:T(8,128)} %get-tuple-element.22.refs_5_, ...), custom_call_target="tpu_custom_call" | custom-call | tf_op jit(solution)/shard_map/pallas_call | solution.py:325
  (18 shorter events, 0.2 us)
Async XLA Ops:
  21.5 7.3 %collective-permute-start.1 = (f32[1,3,1,4224]{3,2,1,0:T(1,128)}, f32[1,3,1,4224]{3,2,1,0:T(1,128)S(1)}, u32[]{:S(2)}, u32[]{:S(2)}) collective-permute-start(f32[1,3,1,4224]{3,2,1,0:T(1,128)} %bitcast.54), channel_id=1, source_target_pairs={{0,4},{4,8},{8,12},{12,16},{16,20},{20,24},{24,28},{1,5},{5,9},{9,... | collective-permute-start | bytes 152072 | tf_op jit(solution)/shard_map/ppermute | solution.py:28
  24.9 6.2 %collective-permute-start = (f32[1,3,1,4224]{3,2,1,0:T(1,128)}, f32[1,3,1,4224]{3,2,1,0:T(1,128)S(1)}, u32[]{:S(2)}, u32[]{:S(2)}) collective-permute-start(f32[1,3,1,4224]{3,2,1,0:T(1,128)} %bitcast.55), channel_id=1, source_target_pairs={{4,0},{8,4},{12,8},{16,12},{20,16},{24,20},{28,24},{5,1},{9,5},{13... | collective-permute-start | bytes 152072 | tf_op jit(solution)/shard_map/ppermute | solution.py:28
  28.2 4.9 %collective-permute-start.3 = (f32[1,3,72,64]{3,2,1,0:T(8,128)}, f32[1,3,72,64]{3,2,1,0:T(8,128)S(1)}, u32[]{:S(2)}, u32[]{:S(2)}) collective-permute-start(f32[1,3,72,64]{3,2,1,0:T(8,128)} %bitcast.48), channel_id=1, source_target_pairs={{0,3},{1,0},{2,1},{3,2},{4,7},{5,4},{6,5},{7,6},{8,11},{9,8},{10,9... | collective-permute-start | bytes 165896 | tf_op jit(solution)/shard_map/ppermute | solution.py:33
  28.7 5.3 %collective-permute-start.2 = (f32[1,3,72,64]{3,2,1,0:T(8,128)}, f32[1,3,72,64]{3,2,1,0:T(8,128)S(1)}, u32[]{:S(2)}, u32[]{:S(2)}) collective-permute-start(f32[1,3,72,64]{3,2,1,0:T(8,128)} %bitcast.49), channel_id=1, source_target_pairs={{0,1},{1,2},{2,3},{3,0},{4,5},{5,6},{6,7},{7,4},{8,9},{9,10},{10,1... | collective-permute-start | bytes 165896 | tf_op jit(solution)/shard_map/ppermute | solution.py:33
  33.2 1.6 %copy-start = (f32[1,3,72,64]{3,2,1,0:T(8,128)}, f32[1,3,72,64]{3,2,1,0:T(8,128)S(1)}, u32[]{:S(2)}) copy-start(f32[1,3,72,64]{3,2,1,0:T(8,128)S(1)} %collective-permute-done.3) | copy-start | bytes 165892
  33.9 0.8 copy-start.1
  56.2 7.7 %collective-permute-start.4 = (f32[1,3,1,4096]{3,2,1,0:T(1,128)}, f32[1,3,1,4096]{3,2,1,0:T(1,128)S(1)}, u32[]{:S(2)}, u32[]{:S(2)}) collective-permute-start(f32[1,3,1,4096]{3,2,1,0:T(1,128)} %bitcast.57), channel_id=1, source_target_pairs={{4,0},{8,4},{12,8},{16,12},{20,16},{24,20},{28,24},{5,1},{9,5},{13... | collective-permute-start | bytes 147464 | tf_op jit(solution)/shard_map/ppermute | solution.py:28
  59.8 7.1 %collective-permute-start.5 = (f32[1,3,1,4096]{3,2,1,0:T(1,128)}, f32[1,3,1,4096]{3,2,1,0:T(1,128)S(1)}, u32[]{:S(2)}, u32[]{:S(2)}) collective-permute-start(f32[1,3,1,4096]{3,2,1,0:T(1,128)} %bitcast.56), channel_id=1, source_target_pairs={{0,4},{4,8},{8,12},{12,16},{16,20},{20,24},{24,28},{1,5},{5,9},{9,... | collective-permute-start | bytes 147464 | tf_op jit(solution)/shard_map/ppermute | solution.py:28
  62.1 6.8 %collective-permute-start.6 = (f32[1,3,64,64]{3,2,1,0:T(8,128)}, f32[1,3,64,64]{3,2,1,0:T(8,128)S(1)}, u32[]{:S(2)}, u32[]{:S(2)}) collective-permute-start(f32[1,3,64,64]{3,2,1,0:T(8,128)} %bitcast.51), channel_id=1, source_target_pairs={{0,1},{1,2},{2,3},{3,0},{4,5},{5,6},{6,7},{7,4},{8,9},{9,10},{10,1... | collective-permute-start | bytes 147464 | tf_op jit(solution)/shard_map/ppermute | solution.py:33
  62.2 6.7 %collective-permute-start.7 = (f32[1,3,64,64]{3,2,1,0:T(8,128)}, f32[1,3,64,64]{3,2,1,0:T(8,128)S(1)}, u32[]{:S(2)}, u32[]{:S(2)}) collective-permute-start(f32[1,3,64,64]{3,2,1,0:T(8,128)} %bitcast.50), channel_id=1, source_target_pairs={{0,3},{1,0},{2,1},{3,2},{4,7},{5,4},{6,5},{7,6},{8,11},{9,8},{10,9... | collective-permute-start | bytes 147464 | tf_op jit(solution)/shard_map/ppermute | solution.py:33
  68.9 0.6 copy-start.2
  68.9 0.7 copy-start.3

commit v15 on v13

--- a/solution.py
+++ b/solution.py
@@ -434,8 +434,11 @@
         xh, xl, ylo, yhi = (jnp.stack([o[k] for o in outs], 0) for k in range(4))
         if sweep > 0:
             lam_x_up, lam_x_down, lam_y = (jnp.stack([o[k] for o in outs], 0) for k in range(4, 7))
+        high_sum = orient(xh[:, :, 0, :flat], codes_here, extent)[:, :, None]
+        if sweep == 0:
+            high_sum = jnp.concatenate([high_sum, xh[:, :, :, flat:]], -1)
         upper = shifted(xl, "blk", -1)
-        lower = shifted(xh, "blk", 1)
+        lower = shifted(high_sum, "blk", 1)
         nxt = jnp.concatenate([ylo[1:], shifted_2(ylo[:1], "face", -1)], 0)
         prv = jnp.concatenate([shifted_2(yhi[-1:], "face", 1), yhi[:-1]], 0)
         if sweep == 0:
@@ -445,7 +448,7 @@
                  has_up, has_down], 1
             )
         up_sum = orient(upper[:, :, 0, :flat], codes_here, extent)[:, :, None]
-        down_sum = orient(lower[:, :, 0, :flat], codes_down, extent)[:, :, None]
+        down_sum = lower[:, :, :, :flat]
         state = [
             (neighbour_moduli[b], lam_x_up[b], lam_x_down[b], lam_y[b], xh[b], xl[b], ylo[b], yhi[b],
              up_sum[b], down_sum[b], prv[b], nxt[b])

time: 91.8 us -> 95.1 us (1.036)
  waiting for transfers between devices: 4.25 us -> 7.32 us
    ppermute x4, waiting for transfers between devices: 3.51 us -> 7.31 us  [shifted(): return lax.ppermute(shard, axis, pairs)]
    another operation x2, local copies, waits for them, and re-layouts: 1.45 us -> 0.22 us  [shards(): high_sum = orient(xh[:, :, 0, :flat], codes_here, extent)[:, :, None]]
  transfers between devices with their start and end apart: 8 -> 8, of which waited for: 3 -> 2; matrix products, arithmetic and copies ran while one was open for 6% -> 7% of each run, Pallas kernels for 0% -> 0%
where the time goes in v15:
time: 95.1 us; the launch traced here: 94.2 us
  Pallas kernels  63.8 us (67%)
  starting transfers between devices  14.4 us (15%)
  waiting for transfers between devices  7.32 us (8%)
  local copies, waits for them, and re-layouts  6.34 us (7%)
  other arithmetic  1.22 us (1%)
  between operations  1.11 us (1%)
    pallas_call x3, Pallas kernels, kernel_sweep(): pl.pallas_call(kernel, grid=(ncomp,), in_specs=in_specs, out_specs=out_sp...  63.8 us
    ppermute x4, starting transfers between devices, shifted(): return lax.ppermute(shard, axis, pairs)  12 us
    ppermute x4, waiting for transfers between devices, shifted(): return lax.ppermute(shard, axis, pairs)  7.31 us
    ppermute x4, starting transfers between devices, shifted_2(): lax.ppermute(shard, axis, [(i, (i + by) % length) for i in range(length)])  2.35 us
  transfers between devices with their start and end apart: 8, of which 2 were waited for; matrix products, arithmetic and copies ran while one was open for 7% of the time, Pallas kernels for 0%

profile of v15, /device:TPU:24, one launch (start us, length us, event | category | flops | bytes accessed | tf_op | source)
XLA Modules:
  0.0 94.2 jit_solution(9666607942155921610)
XLA Ops:
  0.7 20.8 %shard_map.172 = (f32[3,1,4224]{2,1,0:T(1,128)}, f32[3,1,4224]{2,1,0:T(1,128)}, f32[3,1,72,64]{3,2,1,0:T(8,128)}, f32[3,1,72,64]{3,2,1,0:T(8,128)}) custom-call(f32[3]{0:T(128)} %bitcast.60, f32[3,64,4096]{2,1,0:T(8,128)} %bitcast.42, bf16[64,256]{1,0:T(8,128)(2,1)} %constant.68.clone.refs_2_.refs_11_.refs_14_, ...), custom_call_target="tpu_custom_call" | custom-call | tf_op jit(solution)/shard_map/pallas_call | solution.py:325
  21.5 3.3 %collective-permute-start = (f32[1,3,1,4224]{3,2,1,0:T(1,128)}, f32[1,3,1,4224]{3,2,1,0:T(1,128)S(1)}, u32[]{:S(2)}, u32[]{:S(2)}) collective-permute-start(f32[1,3,1,4224]{3,2,1,0:T(1,128)} %bitcast.55), channel_id=1, source_target_pairs={{4,0},{8,4},{12,8},{16,12},{20,16},{24,20},{28,24},{5,1},{9,5},{13... | collective-permute-start | bytes 152072 | tf_op jit(solution)/shard_map/ppermute | solution.py:28
  24.8 0.7 slice.34
  25.5 0.9 slice_reduce_fusion.1
  26.5 0.1 reshape_squeeze.9
  26.6 0.1 rev.27
  26.8 0.1 broadcast_in_dim_reshape.6
  26.9 2.5 %collective-permute-start.1 = (f32[1,3,1,4224]{3,2,1,0:T(1,128)S(1)}, f32[1,3,1,4224]{3,2,1,0:T(1,128)S(1)}, u32[]{:S(2)}, u32[]{:S(2)}) collective-permute-start(f32[1,3,1,4224]{3,2,1,0:T(1,128)S(1)} %pad_maximum_fusion), channel_id=1, source_target_pairs={{0,4},{4,8},{8,12},{12,16},{16,20},{20,24},{24,28},{1,5},{5,9},{9,... | collective-permute-start | bytes 152072 | tf_op jit(solution)/shard_map/ppermute | solution.py:28
  29.4 0.4 collective-permute-start.3
  29.9 0.1 collective-permute-start.2
  30.0 0.0 collective-permute-done
  30.0 0.1 slice_reduce_fusion
  30.2 0.1 reshape_squeeze.10
  30.3 0.1 rev.29
  30.4 3.4 %collective-permute-done.1 = f32[1,3,1,4224]{3,2,1,0:T(1,128)S(1)} collective-permute-done((f32[1,3,1,4224]{3,2,1,0:T(1,128)S(1)}, f32[1,3,1,4224]{3,2,1,0:T(1,128)S(1)}, u32[]{:S(2)}, u32[]{:S(2)}) %collective-permute-start.1) | collective-permute-done | bytes 50720 | tf_op jit(solution)/shard_map/ppermute | solution.py:28
  33.8 0.6 slice_bitcast_fusion.refs_8_
  34.5 0.7 squeeze_broadcast_in_dim_reshape.6.refs_7_
  35.2 0.0 collective-permute-done.3
  35.2 0.0 copy-start
  35.2 0.0 collective-permute-done.2
  35.2 0.0 copy-start.1
  35.3 0.1 stack.28
  35.4 0.7 copy.31
  36.0 0.0 copy-done
  36.0 0.0 copy-done.1
  36.0 21.5 %shard_map.173 = (f32[3,1,4096]{2,1,0:T(1,128)}, f32[3,1,4096]{2,1,0:T(1,128)}, f32[3,1,64,64]{3,2,1,0:T(8,128)}, f32[3,1,64,64]{3,2,1,0:T(8,128)}, f32[3,1,4096...) custom-call(f32[3]{0:T(128)} %bitcast.61, f32[3,64,4096]{2,1,0:T(8,128)} %bitcast.43, f32[6,3]{1,0:T(8,128)} %bitcast.58, ...), custom_call_target="tpu_custom_call" | custom-call | tf_op jit(solution)/shard_map/pallas_call | solution.py:325
  57.5 4.1 %collective-permute-start.4 = (f32[1,3,1,4096]{3,2,1,0:T(1,128)}, f32[1,3,1,4096]{3,2,1,0:T(1,128)S(1)}, u32[]{:S(2)}, u32[]{:S(2)}) collective-permute-start(f32[1,3,1,4096]{3,2,1,0:T(1,128)} %bitcast.56), channel_id=1, source_target_pairs={{4,0},{8,4},{12,8},{16,12},{20,16},{24,20},{28,24},{5,1},{9,5},{13... | collective-permute-start | bytes 147464 | tf_op jit(solution)/shard_map/ppermute | solution.py:28
  61.7 0.9 reduce.3
  62.6 0.1 reshape_squeeze_stack.3
  62.7 0.1 collective-permute-start.6
  62.8 1.7 %collective-permute-start.7 = (f32[1,3,1,64,64]{4,3,1,2,0:T(8,128)}, f32[1,3,1,64,64]{4,3,1,2,0:T(8,128)S(1)}, u32[]{:S(2)}, u32[]{:S(2)}) collective-permute-start(f32[1,3,1,64,64]{4,3,1,2,0:T(8,128)} %bitcast.51), channel_id=1, source_target_pairs={{0,3},{1,0},{2,1},{3,2},{4,7},{5,4},{6,5},{7,6},{8,11},{9,8},{10,9... | collective-permute-start | bytes 147464 | tf_op jit(solution)/shard_map/ppermute | solution.py:33
  64.5 0.0 collective-permute-done.4
  64.5 0.1 reduce.2
  64.7 0.1 reshape_squeeze.11
  64.8 0.1 rev.33
  64.9 0.1 broadcast_in_dim_reshape.7
  65.1 2.1 %collective-permute-start.5 = (f32[1,3,1,4096]{3,2,1,0:T(1,128)S(1)}, f32[1,3,1,4096]{3,2,1,0:T(1,128)S(1)}, u32[]{:S(2)}, u32[]{:S(2)}) collective-permute-start(f32[1,3,1,4096]{3,2,1,0:T(1,128)S(1)} %broadcast_in_dim_reshape.7), channel_id=1, source_target_pairs={{0,4},{4,8},{8,12},{12,16},{16,20},{20,24},{24,28},{1,5},{5,9},{9,... | collective-permute-start | bytes 147464 | tf_op jit(solution)/shard_map/ppermute | solution.py:28
  67.2 0.1 rev.31
  67.3 0.7 squeeze_broadcast_in_dim_reshape.7.refs_10_
  68.0 0.0 collective-permute-done.6
  68.0 0.0 copy-start.2
  68.0 0.0 collective-permute-done.7
  68.0 0.0 copy-start.3
  68.0 3.9 %collective-permute-done.5 = f32[1,3,1,4096]{3,2,1,0:T(1,128)S(1)} collective-permute-done((f32[1,3,1,4096]{3,2,1,0:T(1,128)S(1)}, f32[1,3,1,4096]{3,2,1,0:T(1,128)S(1)}, u32[]{:S(2)}, u32[]{:S(2)}) %collective-permute-start.5) | collective-permute-done | bytes 49184 | tf_op jit(solution)/shard_map/ppermute | solution.py:28
  71.9 0.0 copy-start.4
  71.9 0.0 copy-done.2
  72.0 0.0 copy-done.3
  72.0 0.6 copy-done.4
  72.6 21.4 %shard_map.174 = f32[3,64,4096]{2,1,0:T(8,128)} custom-call(f32[3]{0:T(128)} %bitcast.62, f32[3,64,4096]{2,1,0:T(8,128)} %bitcast.44, f32[6,3]{1,0:T(8,128)} %bitcast.59, f32[3,1,4096]{2,1,0:T(1,128)} %get-tuple-element.20.refs_3_, f32[3,1,4096]{2,1,0:T(1,128)} %get-tuple-element.21.refs_4_, f32[3,64,128]{2,1,0:T(8,128)} %get-tuple-element.22.refs_5_, ...), custom_call_target="tpu_custom_call" | custom-call | tf_op jit(solution)/shard_map/pallas_call | solution.py:325
  (18 shorter events, 0.2 us)
Async XLA Ops:
  21.5 8.5 %collective-permute-start = (f32[1,3,1,4224]{3,2,1,0:T(1,128)}, f32[1,3,1,4224]{3,2,1,0:T(1,128)S(1)}, u32[]{:S(2)}, u32[]{:S(2)}) collective-permute-start(f32[1,3,1,4224]{3,2,1,0:T(1,128)} %bitcast.55), channel_id=1, source_target_pairs={{4,0},{8,4},{12,8},{16,12},{20,16},{24,20},{28,24},{5,1},{9,5},{13... | collective-permute-start | bytes 152072 | tf_op jit(solution)/shard_map/ppermute | solution.py:28
  26.9 6.9 %collective-permute-start.1 = (f32[1,3,1,4224]{3,2,1,0:T(1,128)S(1)}, f32[1,3,1,4224]{3,2,1,0:T(1,128)S(1)}, u32[]{:S(2)}, u32[]{:S(2)}) collective-permute-start(f32[1,3,1,4224]{3,2,1,0:T(1,128)S(1)} %pad_maximum_fusion), channel_id=1, source_target_pairs={{0,4},{4,8},{8,12},{12,16},{16,20},{20,24},{24,28},{1,5},{5,9},{9,... | collective-permute-start | bytes 152072 | tf_op jit(solution)/shard_map/ppermute | solution.py:28
  29.4 5.7 %collective-permute-start.3 = (f32[1,3,1,72,64]{4,3,1,2,0:T(8,128)}, f32[1,3,1,72,64]{4,3,1,2,0:T(8,128)S(1)}, u32[]{:S(2)}, u32[]{:S(2)}) collective-permute-start(f32[1,3,1,72,64]{4,3,1,2,0:T(8,128)} %bitcast.49), channel_id=1, source_target_pairs={{0,3},{1,0},{2,1},{3,2},{4,7},{5,4},{6,5},{7,6},{8,11},{9,8},{10,9... | collective-permute-start | bytes 165896 | tf_op jit(solution)/shard_map/ppermute | solution.py:33
  29.9 5.3 %collective-permute-start.2 = (f32[1,3,1,72,64]{4,3,1,2,0:T(8,128)}, f32[1,3,1,72,64]{4,3,1,2,0:T(8,128)S(1)}, u32[]{:S(2)}, u32[]{:S(2)}) collective-permute-start(f32[1,3,1,72,64]{4,3,1,2,0:T(8,128)} %bitcast.50), channel_id=1, source_target_pairs={{0,1},{1,2},{2,3},{3,0},{4,5},{5,6},{6,7},{7,4},{8,9},{9,10},{10,1... | collective-permute-start | bytes 165896 | tf_op jit(solution)/shard_map/ppermute | solution.py:33
  35.2 0.9 copy-start
  35.2 0.8 copy-start.1
  57.5 7.0 %collective-permute-start.4 = (f32[1,3,1,4096]{3,2,1,0:T(1,128)}, f32[1,3,1,4096]{3,2,1,0:T(1,128)S(1)}, u32[]{:S(2)}, u32[]{:S(2)}) collective-permute-start(f32[1,3,1,4096]{3,2,1,0:T(1,128)} %bitcast.56), channel_id=1, source_target_pairs={{4,0},{8,4},{12,8},{16,12},{20,16},{24,20},{28,24},{5,1},{9,5},{13... | collective-permute-start | bytes 147464 | tf_op jit(solution)/shard_map/ppermute | solution.py:28
  62.7 5.3 %collective-permute-start.6 = (f32[1,3,1,64,64]{4,3,1,2,0:T(8,128)}, f32[1,3,1,64,64]{4,3,1,2,0:T(8,128)S(1)}, u32[]{:S(2)}, u32[]{:S(2)}) collective-permute-start(f32[1,3,1,64,64]{4,3,1,2,0:T(8,128)} %bitcast.52), channel_id=1, source_target_pairs={{0,1},{1,2},{2,3},{3,0},{4,5},{5,6},{6,7},{7,4},{8,9},{9,10},{10,1... | collective-permute-start | bytes 147464 | tf_op jit(solution)/shard_map/ppermute | solution.py:33
  62.8 5.2 %collective-permute-start.7 = (f32[1,3,1,64,64]{4,3,1,2,0:T(8,128)}, f32[1,3,1,64,64]{4,3,1,2,0:T(8,128)S(1)}, u32[]{:S(2)}, u32[]{:S(2)}) collective-permute-start(f32[1,3,1,64,64]{4,3,1,2,0:T(8,128)} %bitcast.51), channel_id=1, source_target_pairs={{0,3},{1,0},{2,1},{3,2},{4,7},{5,4},{6,5},{7,6},{8,11},{9,8},{10,9... | collective-permute-start | bytes 147464 | tf_op jit(solution)/shard_map/ppermute | solution.py:33
  65.1 6.9 %collective-permute-start.5 = (f32[1,3,1,4096]{3,2,1,0:T(1,128)S(1)}, f32[1,3,1,4096]{3,2,1,0:T(1,128)S(1)}, u32[]{:S(2)}, u32[]{:S(2)}) collective-permute-start(f32[1,3,1,4096]{3,2,1,0:T(1,128)S(1)} %broadcast_in_dim_reshape.7), channel_id=1, source_target_pairs={{0,4},{4,8},{8,12},{12,16},{16,20},{20,24},{24,28},{1,5},{5,9},{9,... | collective-permute-start | bytes 147464 | tf_op jit(solution)/shard_map/ppermute | solution.py:28
  68.0 3.9 %copy-start.2 = (f32[1,3,1,64,64]{4,3,1,2,0:T(8,128)}, f32[1,3,1,64,64]{4,3,1,2,0:T(8,128)S(1)}, u32[]{:S(2)}) copy-start(f32[1,3,1,64,64]{4,3,1,2,0:T(8,128)S(1)} %collective-permute-done.6) | copy-start | bytes 147460
  68.0 3.9 %copy-start.3 = (f32[1,3,1,64,64]{4,3,1,2,0:T(8,128)}, f32[1,3,1,64,64]{4,3,1,2,0:T(8,128)S(1)}, u32[]{:S(2)}) copy-start(f32[1,3,1,64,64]{4,3,1,2,0:T(8,128)S(1)} %collective-permute-done.7) | copy-start | bytes 147460
  71.9 0.6 copy-start.4

commit v16 on v13

--- a/solution.py
+++ b/solution.py
@@ -444,8 +444,13 @@
                 [upper[:, :, 0, flat], lower[:, :, 0, flat], prv[:, :, 0, extent, 0], nxt[:, :, 0, extent, 0],
                  has_up, has_down], 1
             )
-        up_sum = orient(upper[:, :, 0, :flat], codes_here, extent)[:, :, None]
-        down_sum = orient(lower[:, :, 0, :flat], codes_down, extent)[:, :, None]
+        both = orient(
+            jnp.stack([upper[:, :, 0, :flat], lower[:, :, 0, :flat]], 0),
+            jnp.stack([codes_here, codes_down], 0),
+            extent,
+        )
+        up_sum = both[0][:, :, None]
+        down_sum = both[1][:, :, None]
         state = [
             (neighbour_moduli[b], lam_x_up[b], lam_x_down[b], lam_y[b], xh[b], xl[b], ylo[b], yhi[b],
              up_sum[b], down_sum[b], prv[b], nxt[b])

time: 91.8 us -> 91.8 us (level)
  no operation moved by 1% of the time
where the time goes in v16:
time: 91.8 us; the launch traced here: 91.3 us
  Pallas kernels  63.8 us (69%)
  starting transfers between devices  14.9 us (16%)
  local copies, waits for them, and re-layouts  6.08 us (7%)
  waiting for transfers between devices  4.17 us (5%)
  between operations  1.64 us (2%)
    pallas_call x3, Pallas kernels, kernel_sweep(): pl.pallas_call(kernel, grid=(ncomp,), in_specs=in_specs, out_specs=out_sp...  63.8 us
    ppermute x4, starting transfers between devices, shifted(): return lax.ppermute(shard, axis, pairs)  12.6 us
    ppermute x4, waiting for transfers between devices, shifted(): return lax.ppermute(shard, axis, pairs)  3.53 us
    ppermute x4, starting transfers between devices, shifted_2(): lax.ppermute(shard, axis, [(i, (i + by) % length) for i in range(length)])  2.35 us
  transfers between devices with their start and end apart: 8, of which 3 were waited for; matrix products, arithmetic and copies ran while one was open for 6% of the time, Pallas kernels for 0%

profile of v16, /device:TPU:24, one launch (start us, length us, event | category | flops | bytes accessed | tf_op | source)
XLA Modules:
  0.0 91.3 jit_solution(18057371628439097551)
XLA Ops:
  0.7 20.9 %shard_map.172 = (f32[3,1,4224]{2,1,0:T(1,128)}, f32[3,1,4224]{2,1,0:T(1,128)}, f32[3,1,72,64]{3,2,1,0:T(8,128)}, f32[3,1,72,64]{3,2,1,0:T(8,128)}) custom-call(f32[3]{0:T(128)} %bitcast.53, f32[3,64,4096]{2,1,0:T(8,128)} %bitcast.36, bf16[64,256]{1,0:T(8,128)(2,1)} %constant.51.clone.refs_2_.refs_11_.refs_14_, ...), custom_call_target="tpu_custom_call" | custom-call | tf_op jit(solution)/shard_map/pallas_call | solution.py:325
  21.5 3.4 %collective-permute-start.1 = (f32[1,3,1,4224]{3,2,1,0:T(1,128)}, f32[1,3,1,4224]{3,2,1,0:T(1,128)S(1)}, u32[]{:S(2)}, u32[]{:S(2)}) collective-permute-start(f32[1,3,1,4224]{3,2,1,0:T(1,128)} %bitcast.47), channel_id=1, source_target_pairs={{0,4},{4,8},{8,12},{12,16},{16,20},{20,24},{24,28},{1,5},{5,9},{9,... | collective-permute-start | bytes 152072 | tf_op jit(solution)/shard_map/ppermute | solution.py:28
  24.9 3.3 %collective-permute-start = (f32[1,3,1,4224]{3,2,1,0:T(1,128)}, f32[1,3,1,4224]{3,2,1,0:T(1,128)S(1)}, u32[]{:S(2)}, u32[]{:S(2)}) collective-permute-start(f32[1,3,1,4224]{3,2,1,0:T(1,128)} %bitcast.48), channel_id=1, source_target_pairs={{4,0},{8,4},{12,8},{16,12},{20,16},{24,20},{28,24},{5,1},{9,5},{13... | collective-permute-start | bytes 152072 | tf_op jit(solution)/shard_map/ppermute | solution.py:28
  28.3 0.4 collective-permute-start.3
  28.7 0.1 collective-permute-start.2
  28.8 0.0 collective-permute-done.1
  28.8 0.6 slice.52
  30.1 0.1 fusion.1
  30.2 0.1 slice_reduce_fusion
  30.3 0.1 stack.54
  30.4 0.7 collective-permute-done
  31.1 0.1 slice_reduce_fusion.1
  31.3 0.1 stack.53
  31.5 0.1 broadcast_select_fusion.1
  31.5 0.1 rev.15
  31.7 0.1 broadcast_select_fusion.3
  31.8 0.7 squeeze_broadcast_in_dim_squeeze.13.refs_8_
  32.5 0.7 squeeze_broadcast_in_dim_squeeze.12.refs_7_
  33.3 0.0 collective-permute-done.3
  33.3 0.0 copy-start
  33.3 0.6 collective-permute-done.2
  33.9 0.0 copy-start.1
  33.9 0.1 stack.51
  34.0 0.7 copy.31
  34.7 0.0 copy-done
  34.7 0.0 copy-done.1
  34.7 21.5 %shard_map.173 = (f32[3,1,4096]{2,1,0:T(1,128)}, f32[3,1,4096]{2,1,0:T(1,128)}, f32[3,1,64,64]{3,2,1,0:T(8,128)}, f32[3,1,64,64]{3,2,1,0:T(8,128)}, f32[3,1,4096...) custom-call(f32[3]{0:T(128)} %bitcast.54, f32[3,64,4096]{2,1,0:T(8,128)} %bitcast.37, f32[6,3]{1,0:T(8,128)} %bitcast.51, ...), custom_call_target="tpu_custom_call" | custom-call | tf_op jit(solution)/shard_map/pallas_call | solution.py:325
  56.2 3.6 %collective-permute-start.4 = (f32[1,3,1,4096]{3,2,1,0:T(1,128)}, f32[1,3,1,4096]{3,2,1,0:T(1,128)S(1)}, u32[]{:S(2)}, u32[]{:S(2)}) collective-permute-start(f32[1,3,1,4096]{3,2,1,0:T(1,128)} %bitcast.50), channel_id=1, source_target_pairs={{4,0},{8,4},{12,8},{16,12},{20,16},{24,20},{28,24},{5,1},{9,5},{13... | collective-permute-start | bytes 147464 | tf_op jit(solution)/shard_map/ppermute | solution.py:28
  59.9 2.2 %collective-permute-start.5 = (f32[1,3,1,4096]{3,2,1,0:T(1,128)}, f32[1,3,1,4096]{3,2,1,0:T(1,128)S(1)}, u32[]{:S(2)}, u32[]{:S(2)}) collective-permute-start(f32[1,3,1,4096]{3,2,1,0:T(1,128)} %bitcast.49), channel_id=1, source_target_pairs={{0,4},{4,8},{8,12},{12,16},{16,20},{20,24},{24,28},{1,5},{5,9},{9,... | collective-permute-start | bytes 147464 | tf_op jit(solution)/shard_map/ppermute | solution.py:28
  62.1 0.1 collective-permute-start.6
  62.2 1.7 %collective-permute-start.7 = (f32[1,3,1,64,64]{4,3,1,2,0:T(8,128)}, f32[1,3,1,64,64]{4,3,1,2,0:T(8,128)S(1)}, u32[]{:S(2)}, u32[]{:S(2)}) collective-permute-start(f32[1,3,1,64,64]{4,3,1,2,0:T(8,128)} %bitcast.43), channel_id=1, source_target_pairs={{0,3},{1,0},{2,1},{3,2},{4,7},{5,4},{6,5},{7,6},{8,11},{9,8},{10,9... | collective-permute-start | bytes 147464 | tf_op jit(solution)/shard_map/ppermute | solution.py:33
  63.9 0.0 collective-permute-done.4
  63.9 0.1 reduce.2
  64.0 0.1 stack.57
  64.1 2.8 %collective-permute-done.5 = f32[1,3,1,4096]{3,2,1,0:T(1,128)S(1)} collective-permute-done((f32[1,3,1,4096]{3,2,1,0:T(1,128)}, f32[1,3,1,4096]{3,2,1,0:T(1,128)S(1)}, u32[]{:S(2)}, u32[]{:S(2)}) %collective-permute-start.5) | collective-permute-done | bytes 49184 | tf_op jit(solution)/shard_map/ppermute | solution.py:28
  67.0 0.1 reduce.3
  67.1 0.1 stack.59
  67.3 0.1 broadcast_select_fusion
  67.4 0.1 rev.17
  67.5 0.1 broadcast_select_fusion.2
  67.6 0.7 squeeze_broadcast_in_dim_squeeze.15.refs_11_
  68.3 0.7 squeeze_broadcast_in_dim_squeeze.14.refs_10_
  69.0 0.0 collective-permute-done.6
  69.0 0.0 copy-start.2
  69.0 0.0 collective-permute-done.7
  69.1 0.0 copy-start.3
  69.1 0.6 copy-done.2
  69.7 0.0 copy-done.3
  69.7 21.4 %shard_map.174 = f32[3,64,4096]{2,1,0:T(8,128)} custom-call(f32[3]{0:T(128)} %bitcast.55, f32[3,64,4096]{2,1,0:T(8,128)} %bitcast.38, f32[6,3]{1,0:T(8,128)} %bitcast.52, f32[3,1,4096]{2,1,0:T(1,128)} %get-tuple-element.20.refs_3_, f32[3,1,4096]{2,1,0:T(1,128)} %get-tuple-element.21.refs_4_, f32[3,64,128]{2,1,0:T(8,128)} %get-tuple-element.22.refs_5_, ...), custom_call_target="tpu_custom_call" | custom-call | tf_op jit(solution)/shard_map/pallas_call | solution.py:325
  (15 shorter events, 0.1 us)
Async XLA Ops:
  21.5 7.3 %collective-permute-start.1 = (f32[1,3,1,4224]{3,2,1,0:T(1,128)}, f32[1,3,1,4224]{3,2,1,0:T(1,128)S(1)}, u32[]{:S(2)}, u32[]{:S(2)}) collective-permute-start(f32[1,3,1,4224]{3,2,1,0:T(1,128)} %bitcast.47), channel_id=1, source_target_pairs={{0,4},{4,8},{8,12},{12,16},{16,20},{20,24},{24,28},{1,5},{5,9},{9,... | collective-permute-start | bytes 152072 | tf_op jit(solution)/shard_map/ppermute | solution.py:28
  24.9 6.2 %collective-permute-start = (f32[1,3,1,4224]{3,2,1,0:T(1,128)}, f32[1,3,1,4224]{3,2,1,0:T(1,128)S(1)}, u32[]{:S(2)}, u32[]{:S(2)}) collective-permute-start(f32[1,3,1,4224]{3,2,1,0:T(1,128)} %bitcast.48), channel_id=1, source_target_pairs={{4,0},{8,4},{12,8},{16,12},{20,16},{24,20},{28,24},{5,1},{9,5},{13... | collective-permute-start | bytes 152072 | tf_op jit(solution)/shard_map/ppermute | solution.py:28
  28.3 5.0 %collective-permute-start.3 = (f32[1,3,1,72,64]{4,3,1,2,0:T(8,128)}, f32[1,3,1,72,64]{4,3,1,2,0:T(8,128)S(1)}, u32[]{:S(2)}, u32[]{:S(2)}) collective-permute-start(f32[1,3,1,72,64]{4,3,1,2,0:T(8,128)} %bitcast.41), channel_id=1, source_target_pairs={{0,3},{1,0},{2,1},{3,2},{4,7},{5,4},{6,5},{7,6},{8,11},{9,8},{10,9... | collective-permute-start | bytes 165896 | tf_op jit(solution)/shard_map/ppermute | solution.py:33
  28.7 5.2 %collective-permute-start.2 = (f32[1,3,1,72,64]{4,3,1,2,0:T(8,128)}, f32[1,3,1,72,64]{4,3,1,2,0:T(8,128)S(1)}, u32[]{:S(2)}, u32[]{:S(2)}) collective-permute-start(f32[1,3,1,72,64]{4,3,1,2,0:T(8,128)} %bitcast.42), channel_id=1, source_target_pairs={{0,1},{1,2},{2,3},{3,0},{4,5},{5,6},{6,7},{7,4},{8,9},{9,10},{10,1... | collective-permute-start | bytes 165896 | tf_op jit(solution)/shard_map/ppermute | solution.py:33
  33.3 1.5 %copy-start = (f32[1,3,1,72,64]{4,3,1,2,0:T(8,128)}, f32[1,3,1,72,64]{4,3,1,2,0:T(8,128)S(1)}, u32[]{:S(2)}) copy-start(f32[1,3,1,72,64]{4,3,1,2,0:T(8,128)S(1)} %collective-permute-done.3) | copy-start | bytes 165892
  33.9 0.8 copy-start.1
  56.2 7.7 %collective-permute-start.4 = (f32[1,3,1,4096]{3,2,1,0:T(1,128)}, f32[1,3,1,4096]{3,2,1,0:T(1,128)S(1)}, u32[]{:S(2)}, u32[]{:S(2)}) collective-permute-start(f32[1,3,1,4096]{3,2,1,0:T(1,128)} %bitcast.50), channel_id=1, source_target_pairs={{4,0},{8,4},{12,8},{16,12},{20,16},{24,20},{28,24},{5,1},{9,5},{13... | collective-permute-start | bytes 147464 | tf_op jit(solution)/shard_map/ppermute | solution.py:28
  59.9 7.1 %collective-permute-start.5 = (f32[1,3,1,4096]{3,2,1,0:T(1,128)}, f32[1,3,1,4096]{3,2,1,0:T(1,128)S(1)}, u32[]{:S(2)}, u32[]{:S(2)}) collective-permute-start(f32[1,3,1,4096]{3,2,1,0:T(1,128)} %bitcast.49), channel_id=1, source_target_pairs={{0,4},{4,8},{8,12},{12,16},{16,20},{20,24},{24,28},{1,5},{5,9},{9,... | collective-permute-start | bytes 147464 | tf_op jit(solution)/shard_map/ppermute | solution.py:28
  62.1 6.9 %collective-permute-start.6 = (f32[1,3,1,64,64]{4,3,1,2,0:T(8,128)}, f32[1,3,1,64,64]{4,3,1,2,0:T(8,128)S(1)}, u32[]{:S(2)}, u32[]{:S(2)}) collective-permute-start(f32[1,3,1,64,64]{4,3,1,2,0:T(8,128)} %bitcast.44), channel_id=1, source_target_pairs={{0,1},{1,2},{2,3},{3,0},{4,5},{5,6},{6,7},{7,4},{8,9},{9,10},{10,1... | collective-permute-start | bytes 147464 | tf_op jit(solution)/shard_map/ppermute | solution.py:33
  62.2 6.9 %collective-permute-start.7 = (f32[1,3,1,64,64]{4,3,1,2,0:T(8,128)}, f32[1,3,1,64,64]{4,3,1,2,0:T(8,128)S(1)}, u32[]{:S(2)}, u32[]{:S(2)}) collective-permute-start(f32[1,3,1,64,64]{4,3,1,2,0:T(8,128)} %bitcast.43), channel_id=1, source_target_pairs={{0,3},{1,0},{2,1},{3,2},{4,7},{5,4},{6,5},{7,6},{8,11},{9,8},{10,9... | collective-permute-start | bytes 147464 | tf_op jit(solution)/shard_map/ppermute | solution.py:33
  69.0 0.6 copy-start.2
  69.1 0.7 copy-start.3

commit v17 on v13

--- a/solution.py
+++ b/solution.py
@@ -253,7 +253,7 @@
             for xl in range(XG):
                 s_ref[pl.ds(g * XG + xl, h, stride=n), :] = tb[xl * h:(xl + 1) * h]
         return carry
-    lax.fori_loop(0, n // (XG * GPI), body, 0)
+    lax.fori_loop(0, n // (XG * GPI), body, 0, unroll=True)
     for cp in range(npair):
         z_ref[cp * n:(cp + 1) * n, :] = jnp.concatenate(
             [s_ref[(2 * cp) * n:(2 * cp + 1) * n, :], s_ref[(2 * cp + 1) * n:(2 * cp + 2) * n, :]], 1)

time: 91.8 us -> 88.3 us (0.962)
  Pallas kernels: 63.8 us -> 60.4 us
    pallas_call x3, Pallas kernels: 63.8 us -> 60.4 us  [kernel_sweep(): pl.pallas_call(kernel, grid=(ncomp,), in_specs=in_specs, out_specs=out_sp...]
where the time goes in v17:
time: 88.3 us; the launch traced here: 87.7 us
  Pallas kernels  60.4 us (68%)
  starting transfers between devices  14.9 us (17%)
  local copies, waits for them, and re-layouts  6.1 us (7%)
  waiting for transfers between devices  4.25 us (5%)
  between operations  1.7 us (2%)
    pallas_call x3, Pallas kernels, kernel_sweep(): pl.pallas_call(kernel, grid=(ncomp,), in_specs=in_specs, out_specs=out_sp...  60.4 us
    ppermute x4, starting transfers between devices, shifted(): return lax.ppermute(shard, axis, pairs)  12.6 us
    ppermute x4, waiting for transfers between devices, shifted(): return lax.ppermute(shard, axis, pairs)  3.51 us
    ppermute x4, starting transfers between devices, shifted_2(): lax.ppermute(shard, axis, [(i, (i + by) % length) for i in range(length)])  2.35 us
  transfers between devices with their start and end apart: 8, of which 3 were waited for; matrix products, arithmetic and copies ran while one was open for 6% of the time, Pallas kernels for 0%

profile of v17, /device:TPU:24, one launch (start us, length us, event | category | flops | bytes accessed | tf_op | source)
XLA Modules:
  0.0 87.7 jit_solution(7362180937177903656)
XLA Ops:
  0.7 19.6 %shard_map.172 = (f32[3,1,4224]{2,1,0:T(1,128)}, f32[3,1,4224]{2,1,0:T(1,128)}, f32[3,1,72,64]{3,2,1,0:T(8,128)}, f32[3,1,72,64]{3,2,1,0:T(8,128)}) custom-call(f32[3]{0:T(128)} %bitcast.60, f32[3,64,4096]{2,1,0:T(8,128)} %bitcast.43, bf16[64,256]{1,0:T(8,128)(2,1)} %constant.77.clone.refs_2_.refs_11_.refs_14_, ...), custom_call_target="tpu_custom_call" | custom-call | tf_op jit(solution)/shard_map/pallas_call | solution.py:325
  20.3 3.4 %collective-permute-start.1 = (f32[1,3,1,4224]{3,2,1,0:T(1,128)}, f32[1,3,1,4224]{3,2,1,0:T(1,128)S(1)}, u32[]{:S(2)}, u32[]{:S(2)}) collective-permute-start(f32[1,3,1,4224]{3,2,1,0:T(1,128)} %bitcast.54), channel_id=1, source_target_pairs={{0,4},{4,8},{8,12},{12,16},{16,20},{20,24},{24,28},{1,5},{5,9},{9,... | collective-permute-start | bytes 152072 | tf_op jit(solution)/shard_map/ppermute | solution.py:28
  23.7 3.3 %collective-permute-start = (f32[1,3,1,4224]{3,2,1,0:T(1,128)}, f32[1,3,1,4224]{3,2,1,0:T(1,128)S(1)}, u32[]{:S(2)}, u32[]{:S(2)}) collective-permute-start(f32[1,3,1,4224]{3,2,1,0:T(1,128)} %bitcast.55), channel_id=1, source_target_pairs={{4,0},{8,4},{12,8},{16,12},{20,16},{24,20},{28,24},{5,1},{9,5},{13... | collective-permute-start | bytes 152072 | tf_op jit(solution)/shard_map/ppermute | solution.py:28
  27.0 0.4 collective-permute-start.3
  27.4 0.1 collective-permute-start.2
  27.6 0.0 collective-permute-done.1
  27.6 0.1 slice_reduce_fusion
  27.7 0.6 slice.33
  29.0 0.1 reshape_squeeze.13
  29.1 0.8 collective-permute-done
  29.9 0.1 slice_reduce_fusion.1
  30.0 0.1 reshape_squeeze.12
  30.2 0.1 rev.27
  30.3 0.1 rev.29
  30.5 0.7 squeeze_broadcast_in_dim_reshape.12.refs_7_
  31.2 0.7 squeeze_broadcast_in_dim_reshape.13.refs_8_
  31.9 0.0 collective-permute-done.3
  31.9 0.0 copy-start
  31.9 0.7 collective-permute-done.2
  32.7 0.0 copy-start.1
  32.7 0.1 stack.31
  32.8 0.7 copy.31
  33.5 0.0 copy-done
  33.5 0.0 copy-done.1
  33.5 20.4 %shard_map.173 = (f32[3,1,4096]{2,1,0:T(1,128)}, f32[3,1,4096]{2,1,0:T(1,128)}, f32[3,1,64,64]{3,2,1,0:T(8,128)}, f32[3,1,64,64]{3,2,1,0:T(8,128)}, f32[3,1,4096...) custom-call(f32[3]{0:T(128)} %bitcast.61, f32[3,64,4096]{2,1,0:T(8,128)} %bitcast.44, f32[6,3]{1,0:T(8,128)} %bitcast.58, ...), custom_call_target="tpu_custom_call" | custom-call | tf_op jit(solution)/shard_map/pallas_call | solution.py:325
  53.9 3.5 %collective-permute-start.4 = (f32[1,3,1,4096]{3,2,1,0:T(1,128)}, f32[1,3,1,4096]{3,2,1,0:T(1,128)S(1)}, u32[]{:S(2)}, u32[]{:S(2)}) collective-permute-start(f32[1,3,1,4096]{3,2,1,0:T(1,128)} %bitcast.57), channel_id=1, source_target_pairs={{4,0},{8,4},{12,8},{16,12},{20,16},{24,20},{28,24},{5,1},{9,5},{13... | collective-permute-start | bytes 147464 | tf_op jit(solution)/shard_map/ppermute | solution.py:28
  57.4 2.3 %collective-permute-start.5 = (f32[1,3,1,4096]{3,2,1,0:T(1,128)}, f32[1,3,1,4096]{3,2,1,0:T(1,128)S(1)}, u32[]{:S(2)}, u32[]{:S(2)}) collective-permute-start(f32[1,3,1,4096]{3,2,1,0:T(1,128)} %bitcast.56), channel_id=1, source_target_pairs={{0,4},{4,8},{8,12},{12,16},{16,20},{20,24},{24,28},{1,5},{5,9},{9,... | collective-permute-start | bytes 147464 | tf_op jit(solution)/shard_map/ppermute | solution.py:28
  59.7 0.1 collective-permute-start.6
  59.8 1.7 %collective-permute-start.7 = (f32[1,3,1,64,64]{4,3,1,2,0:T(8,128)}, f32[1,3,1,64,64]{4,3,1,2,0:T(8,128)S(1)}, u32[]{:S(2)}, u32[]{:S(2)}) collective-permute-start(f32[1,3,1,64,64]{4,3,1,2,0:T(8,128)} %bitcast.50), channel_id=1, source_target_pairs={{0,3},{1,0},{2,1},{3,2},{4,7},{5,4},{6,5},{7,6},{8,11},{9,8},{10,9... | collective-permute-start | bytes 147464 | tf_op jit(solution)/shard_map/ppermute | solution.py:33
  61.5 0.0 collective-permute-done.4
  61.5 0.1 reduce.2
  61.7 0.1 reshape_squeeze.14
  61.8 2.7 %collective-permute-done.5 = f32[1,3,1,4096]{3,2,1,0:T(1,128)S(1)} collective-permute-done((f32[1,3,1,4096]{3,2,1,0:T(1,128)}, f32[1,3,1,4096]{3,2,1,0:T(1,128)S(1)}, u32[]{:S(2)}, u32[]{:S(2)}) %collective-permute-start.5) | collective-permute-done | bytes 49184 | tf_op jit(solution)/shard_map/ppermute | solution.py:28
  64.5 0.1 reduce.3
  64.6 0.1 reshape_squeeze.15
  64.8 0.1 rev.33
  65.0 0.1 rev.31
  65.1 0.7 squeeze_broadcast_in_dim_reshape.15.refs_11_
  65.8 0.7 squeeze_broadcast_in_dim_reshape.14.refs_10_
  66.5 0.0 collective-permute-done.6
  66.5 0.0 copy-start.2
  66.5 0.0 collective-permute-done.7
  66.5 0.0 copy-start.3
  66.5 0.6 copy-done.2
  67.2 0.0 copy-done.3
  67.2 20.4 %shard_map.174 = f32[3,64,4096]{2,1,0:T(8,128)} custom-call(f32[3]{0:T(128)} %bitcast.62, f32[3,64,4096]{2,1,0:T(8,128)} %bitcast.45, f32[6,3]{1,0:T(8,128)} %bitcast.59, f32[3,1,4096]{2,1,0:T(1,128)} %get-tuple-element.20.refs_3_, f32[3,1,4096]{2,1,0:T(1,128)} %get-tuple-element.21.refs_4_, f32[3,64,128]{2,1,0:T(8,128)} %get-tuple-element.22.refs_5_, ...), custom_call_target="tpu_custom_call" | custom-call | tf_op jit(solution)/shard_map/pallas_call | solution.py:325
  (18 shorter events, 0.2 us)
Async XLA Ops:
  20.3 7.3 %collective-permute-start.1 = (f32[1,3,1,4224]{3,2,1,0:T(1,128)}, f32[1,3,1,4224]{3,2,1,0:T(1,128)S(1)}, u32[]{:S(2)}, u32[]{:S(2)}) collective-permute-start(f32[1,3,1,4224]{3,2,1,0:T(1,128)} %bitcast.54), channel_id=1, source_target_pairs={{0,4},{4,8},{8,12},{12,16},{16,20},{20,24},{24,28},{1,5},{5,9},{9,... | collective-permute-start | bytes 152072 | tf_op jit(solution)/shard_map/ppermute | solution.py:28
  23.7 6.2 %collective-permute-start = (f32[1,3,1,4224]{3,2,1,0:T(1,128)}, f32[1,3,1,4224]{3,2,1,0:T(1,128)S(1)}, u32[]{:S(2)}, u32[]{:S(2)}) collective-permute-start(f32[1,3,1,4224]{3,2,1,0:T(1,128)} %bitcast.55), channel_id=1, source_target_pairs={{4,0},{8,4},{12,8},{16,12},{20,16},{24,20},{28,24},{5,1},{9,5},{13... | collective-permute-start | bytes 152072 | tf_op jit(solution)/shard_map/ppermute | solution.py:28
  27.0 4.9 %collective-permute-start.3 = (f32[1,3,1,72,64]{4,3,1,2,0:T(8,128)}, f32[1,3,1,72,64]{4,3,1,2,0:T(8,128)S(1)}, u32[]{:S(2)}, u32[]{:S(2)}) collective-permute-start(f32[1,3,1,72,64]{4,3,1,2,0:T(8,128)} %bitcast.48), channel_id=1, source_target_pairs={{0,3},{1,0},{2,1},{3,2},{4,7},{5,4},{6,5},{7,6},{8,11},{9,8},{10,9... | collective-permute-start | bytes 165896 | tf_op jit(solution)/shard_map/ppermute | solution.py:33
  27.4 5.2 %collective-permute-start.2 = (f32[1,3,1,72,64]{4,3,1,2,0:T(8,128)}, f32[1,3,1,72,64]{4,3,1,2,0:T(8,128)S(1)}, u32[]{:S(2)}, u32[]{:S(2)}) collective-permute-start(f32[1,3,1,72,64]{4,3,1,2,0:T(8,128)} %bitcast.49), channel_id=1, source_target_pairs={{0,1},{1,2},{2,3},{3,0},{4,5},{5,6},{6,7},{7,4},{8,9},{9,10},{10,1... | collective-permute-start | bytes 165896 | tf_op jit(solution)/shard_map/ppermute | solution.py:33
  31.9 1.5 %copy-start = (f32[1,3,1,72,64]{4,3,1,2,0:T(8,128)}, f32[1,3,1,72,64]{4,3,1,2,0:T(8,128)S(1)}, u32[]{:S(2)}) copy-start(f32[1,3,1,72,64]{4,3,1,2,0:T(8,128)S(1)} %collective-permute-done.3) | copy-start | bytes 165892
  32.7 0.8 copy-start.1
  53.9 7.7 %collective-permute-start.4 = (f32[1,3,1,4096]{3,2,1,0:T(1,128)}, f32[1,3,1,4096]{3,2,1,0:T(1,128)S(1)}, u32[]{:S(2)}, u32[]{:S(2)}) collective-permute-start(f32[1,3,1,4096]{3,2,1,0:T(1,128)} %bitcast.57), channel_id=1, source_target_pairs={{4,0},{8,4},{12,8},{16,12},{20,16},{24,20},{28,24},{5,1},{9,5},{13... | collective-permute-start | bytes 147464 | tf_op jit(solution)/shard_map/ppermute | solution.py:28
  57.4 7.1 %collective-permute-start.5 = (f32[1,3,1,4096]{3,2,1,0:T(1,128)}, f32[1,3,1,4096]{3,2,1,0:T(1,128)S(1)}, u32[]{:S(2)}, u32[]{:S(2)}) collective-permute-start(f32[1,3,1,4096]{3,2,1,0:T(1,128)} %bitcast.56), channel_id=1, source_target_pairs={{0,4},{4,8},{8,12},{12,16},{16,20},{20,24},{24,28},{1,5},{5,9},{9,... | collective-permute-start | bytes 147464 | tf_op jit(solution)/shard_map/ppermute | solution.py:28
  59.7 6.8 %collective-permute-start.6 = (f32[1,3,1,64,64]{4,3,1,2,0:T(8,128)}, f32[1,3,1,64,64]{4,3,1,2,0:T(8,128)S(1)}, u32[]{:S(2)}, u32[]{:S(2)}) collective-permute-start(f32[1,3,1,64,64]{4,3,1,2,0:T(8,128)} %bitcast.51), channel_id=1, source_target_pairs={{0,1},{1,2},{2,3},{3,0},{4,5},{5,6},{6,7},{7,4},{8,9},{9,10},{10,1... | collective-permute-start | bytes 147464 | tf_op jit(solution)/shard_map/ppermute | solution.py:33
  59.8 6.7 %collective-permute-start.7 = (f32[1,3,1,64,64]{4,3,1,2,0:T(8,128)}, f32[1,3,1,64,64]{4,3,1,2,0:T(8,128)S(1)}, u32[]{:S(2)}, u32[]{:S(2)}) collective-permute-start(f32[1,3,1,64,64]{4,3,1,2,0:T(8,128)} %bitcast.50), channel_id=1, source_target_pairs={{0,3},{1,0},{2,1},{3,2},{4,7},{5,4},{6,5},{7,6},{8,11},{9,8},{10,9... | collective-permute-start | bytes 147464 | tf_op jit(solution)/shard_map/ppermute | solution.py:33
  66.5 0.6 copy-start.2
  66.5 0.7 copy-start.3

commit v18 on v17

--- a/solution.py
+++ b/solution.py
@@ -233,7 +233,7 @@
     wy = wy_ref[...]
     ez = ez_ref[...]
     XG = 4
-    GPI = 8
+    GPI = 4
 
     def body(it_, carry):
         lhs = []

time: 88.3 us -> 89.3 us (1.011)
  Pallas kernels: 60.4 us -> 61.3 us
    pallas_call x3, Pallas kernels: 60.4 us -> 61.3 us  [kernel_sweep(): pl.pallas_call(kernel, grid=(ncomp,), in_specs=in_specs, out_specs=out_sp...]
where the time goes in v18:
time: 89.3 us; the launch traced here: 88.7 us
  Pallas kernels  61.3 us (69%)
  starting transfers between devices  14.9 us (17%)
  local copies, waits for them, and re-layouts  6.1 us (7%)
  waiting for transfers between devices  4.23 us (5%)
  between operations  1.7 us (2%)
    pallas_call x3, Pallas kernels, kernel_sweep(): pl.pallas_call(kernel, grid=(ncomp,), in_specs=in_specs, out_specs=out_sp...  61.3 us
    ppermute x4, starting transfers between devices, shifted(): return lax.ppermute(shard, axis, pairs)  12.6 us
    ppermute x4, waiting for transfers between devices, shifted(): return lax.ppermute(shard, axis, pairs)  3.49 us
    ppermute x4, starting transfers between devices, shifted_2(): lax.ppermute(shard, axis, [(i, (i + by) % length) for i in range(length)])  2.35 us
  transfers between devices with their start and end apart: 8, of which 3 were waited for; matrix products, arithmetic and copies ran while one was open for 6% of the time, Pallas kernels for 0%

profile of v18, /device:TPU:24, one launch (start us, length us, event | category | flops | bytes accessed | tf_op | source)
XLA Modules:
  0.0 88.7 jit_solution(1025949386289492097)
XLA Ops:
  0.7 19.9 %shard_map.172 = (f32[3,1,4224]{2,1,0:T(1,128)}, f32[3,1,4224]{2,1,0:T(1,128)}, f32[3,1,72,64]{3,2,1,0:T(8,128)}, f32[3,1,72,64]{3,2,1,0:T(8,128)}) custom-call(f32[3]{0:T(128)} %bitcast.60, f32[3,64,4096]{2,1,0:T(8,128)} %bitcast.43, bf16[64,256]{1,0:T(8,128)(2,1)} %constant.77.clone.refs_2_.refs_11_.refs_14_, ...), custom_call_target="tpu_custom_call" | custom-call | tf_op jit(solution)/shard_map/pallas_call | solution.py:325
  20.6 3.4 %collective-permute-start.1 = (f32[1,3,1,4224]{3,2,1,0:T(1,128)}, f32[1,3,1,4224]{3,2,1,0:T(1,128)S(1)}, u32[]{:S(2)}, u32[]{:S(2)}) collective-permute-start(f32[1,3,1,4224]{3,2,1,0:T(1,128)} %bitcast.54), channel_id=1, source_target_pairs={{0,4},{4,8},{8,12},{12,16},{16,20},{20,24},{24,28},{1,5},{5,9},{9,... | collective-permute-start | bytes 152072 | tf_op jit(solution)/shard_map/ppermute | solution.py:28
  24.0 3.3 %collective-permute-start = (f32[1,3,1,4224]{3,2,1,0:T(1,128)}, f32[1,3,1,4224]{3,2,1,0:T(1,128)S(1)}, u32[]{:S(2)}, u32[]{:S(2)}) collective-permute-start(f32[1,3,1,4224]{3,2,1,0:T(1,128)} %bitcast.55), channel_id=1, source_target_pairs={{4,0},{8,4},{12,8},{16,12},{20,16},{24,20},{28,24},{5,1},{9,5},{13... | collective-permute-start | bytes 152072 | tf_op jit(solution)/shard_map/ppermute | solution.py:28
  27.3 0.4 collective-permute-start.3
  27.7 0.1 collective-permute-start.2
  27.9 0.0 collective-permute-done.1
  27.9 0.1 slice_reduce_fusion
  28.0 0.6 slice.33
  29.3 0.1 reshape_squeeze.13
  29.4 0.8 collective-permute-done
  30.2 0.1 slice_reduce_fusion.1
  30.4 0.1 reshape_squeeze.12
  30.5 0.1 rev.27
  30.6 0.1 rev.29
  30.8 0.7 squeeze_broadcast_in_dim_reshape.12.refs_7_
  31.5 0.7 squeeze_broadcast_in_dim_reshape.13.refs_8_
  32.2 0.0 collective-permute-done.3
  32.3 0.0 copy-start
  32.3 0.7 collective-permute-done.2
  33.0 0.0 copy-start.1
  33.0 0.1 stack.31
  33.1 0.7 copy.31
  33.8 0.0 copy-done
  33.8 0.0 copy-done.1
  33.8 20.7 %shard_map.173 = (f32[3,1,4096]{2,1,0:T(1,128)}, f32[3,1,4096]{2,1,0:T(1,128)}, f32[3,1,64,64]{3,2,1,0:T(8,128)}, f32[3,1,64,64]{3,2,1,0:T(8,128)}, f32[3,1,4096...) custom-call(f32[3]{0:T(128)} %bitcast.61, f32[3,64,4096]{2,1,0:T(8,128)} %bitcast.44, f32[6,3]{1,0:T(8,128)} %bitcast.58, ...), custom_call_target="tpu_custom_call" | custom-call | tf_op jit(solution)/shard_map/pallas_call | solution.py:325
  54.6 3.5 %collective-permute-start.4 = (f32[1,3,1,4096]{3,2,1,0:T(1,128)}, f32[1,3,1,4096]{3,2,1,0:T(1,128)S(1)}, u32[]{:S(2)}, u32[]{:S(2)}) collective-permute-start(f32[1,3,1,4096]{3,2,1,0:T(1,128)} %bitcast.57), channel_id=1, source_target_pairs={{4,0},{8,4},{12,8},{16,12},{20,16},{24,20},{28,24},{5,1},{9,5},{13... | collective-permute-start | bytes 147464 | tf_op jit(solution)/shard_map/ppermute | solution.py:28
  58.1 2.3 %collective-permute-start.5 = (f32[1,3,1,4096]{3,2,1,0:T(1,128)}, f32[1,3,1,4096]{3,2,1,0:T(1,128)S(1)}, u32[]{:S(2)}, u32[]{:S(2)}) collective-permute-start(f32[1,3,1,4096]{3,2,1,0:T(1,128)} %bitcast.56), channel_id=1, source_target_pairs={{0,4},{4,8},{8,12},{12,16},{16,20},{20,24},{24,28},{1,5},{5,9},{9,... | collective-permute-start | bytes 147464 | tf_op jit(solution)/shard_map/ppermute | solution.py:28
  60.4 0.1 collective-permute-start.6
  60.5 1.7 %collective-permute-start.7 = (f32[1,3,1,64,64]{4,3,1,2,0:T(8,128)}, f32[1,3,1,64,64]{4,3,1,2,0:T(8,128)S(1)}, u32[]{:S(2)}, u32[]{:S(2)}) collective-permute-start(f32[1,3,1,64,64]{4,3,1,2,0:T(8,128)} %bitcast.50), channel_id=1, source_target_pairs={{0,3},{1,0},{2,1},{3,2},{4,7},{5,4},{6,5},{7,6},{8,11},{9,8},{10,9... | collective-permute-start | bytes 147464 | tf_op jit(solution)/shard_map/ppermute | solution.py:33
  62.2 0.0 collective-permute-done.4
  62.2 0.1 reduce.2
  62.3 0.1 reshape_squeeze.14
  62.5 2.7 %collective-permute-done.5 = f32[1,3,1,4096]{3,2,1,0:T(1,128)S(1)} collective-permute-done((f32[1,3,1,4096]{3,2,1,0:T(1,128)}, f32[1,3,1,4096]{3,2,1,0:T(1,128)S(1)}, u32[]{:S(2)}, u32[]{:S(2)}) %collective-permute-start.5) | collective-permute-done | bytes 49184 | tf_op jit(solution)/shard_map/ppermute | solution.py:28
  65.2 0.1 reduce.3
  65.3 0.1 reshape_squeeze.15
  65.4 0.1 rev.33
  65.6 0.1 rev.31
  65.7 0.7 squeeze_broadcast_in_dim_reshape.15.refs_11_
  66.4 0.7 squeeze_broadcast_in_dim_reshape.14.refs_10_
  67.2 0.0 collective-permute-done.6
  67.2 0.0 copy-start.2
  67.2 0.0 collective-permute-done.7
  67.2 0.0 copy-start.3
  67.2 0.6 copy-done.2
  67.8 0.0 copy-done.3
  67.8 20.7 %shard_map.174 = f32[3,64,4096]{2,1,0:T(8,128)} custom-call(f32[3]{0:T(128)} %bitcast.62, f32[3,64,4096]{2,1,0:T(8,128)} %bitcast.45, f32[6,3]{1,0:T(8,128)} %bitcast.59, f32[3,1,4096]{2,1,0:T(1,128)} %get-tuple-element.20.refs_3_, f32[3,1,4096]{2,1,0:T(1,128)} %get-tuple-element.21.refs_4_, f32[3,64,128]{2,1,0:T(8,128)} %get-tuple-element.22.refs_5_, ...), custom_call_target="tpu_custom_call" | custom-call | tf_op jit(solution)/shard_map/pallas_call | solution.py:325
  (18 shorter events, 0.2 us)
Async XLA Ops:
  20.6 7.3 %collective-permute-start.1 = (f32[1,3,1,4224]{3,2,1,0:T(1,128)}, f32[1,3,1,4224]{3,2,1,0:T(1,128)S(1)}, u32[]{:S(2)}, u32[]{:S(2)}) collective-permute-start(f32[1,3,1,4224]{3,2,1,0:T(1,128)} %bitcast.54), channel_id=1, source_target_pairs={{0,4},{4,8},{8,12},{12,16},{16,20},{20,24},{24,28},{1,5},{5,9},{9,... | collective-permute-start | bytes 152072 | tf_op jit(solution)/shard_map/ppermute | solution.py:28
  24.0 6.2 %collective-permute-start = (f32[1,3,1,4224]{3,2,1,0:T(1,128)}, f32[1,3,1,4224]{3,2,1,0:T(1,128)S(1)}, u32[]{:S(2)}, u32[]{:S(2)}) collective-permute-start(f32[1,3,1,4224]{3,2,1,0:T(1,128)} %bitcast.55), channel_id=1, source_target_pairs={{4,0},{8,4},{12,8},{16,12},{20,16},{24,20},{28,24},{5,1},{9,5},{13... | collective-permute-start | bytes 152072 | tf_op jit(solution)/shard_map/ppermute | solution.py:28
  27.3 4.9 %collective-permute-start.3 = (f32[1,3,1,72,64]{4,3,1,2,0:T(8,128)}, f32[1,3,1,72,64]{4,3,1,2,0:T(8,128)S(1)}, u32[]{:S(2)}, u32[]{:S(2)}) collective-permute-start(f32[1,3,1,72,64]{4,3,1,2,0:T(8,128)} %bitcast.48), channel_id=1, source_target_pairs={{0,3},{1,0},{2,1},{3,2},{4,7},{5,4},{6,5},{7,6},{8,11},{9,8},{10,9... | collective-permute-start | bytes 165896 | tf_op jit(solution)/shard_map/ppermute | solution.py:33
  27.7 5.2 %collective-permute-start.2 = (f32[1,3,1,72,64]{4,3,1,2,0:T(8,128)}, f32[1,3,1,72,64]{4,3,1,2,0:T(8,128)S(1)}, u32[]{:S(2)}, u32[]{:S(2)}) collective-permute-start(f32[1,3,1,72,64]{4,3,1,2,0:T(8,128)} %bitcast.49), channel_id=1, source_target_pairs={{0,1},{1,2},{2,3},{3,0},{4,5},{5,6},{6,7},{7,4},{8,9},{9,10},{10,1... | collective-permute-start | bytes 165896 | tf_op jit(solution)/shard_map/ppermute | solution.py:33
  32.3 1.6 %copy-start = (f32[1,3,1,72,64]{4,3,1,2,0:T(8,128)}, f32[1,3,1,72,64]{4,3,1,2,0:T(8,128)S(1)}, u32[]{:S(2)}) copy-start(f32[1,3,1,72,64]{4,3,1,2,0:T(8,128)S(1)} %collective-permute-done.3) | copy-start | bytes 165892
  33.0 0.8 copy-start.1
  54.6 7.7 %collective-permute-start.4 = (f32[1,3,1,4096]{3,2,1,0:T(1,128)}, f32[1,3,1,4096]{3,2,1,0:T(1,128)S(1)}, u32[]{:S(2)}, u32[]{:S(2)}) collective-permute-start(f32[1,3,1,4096]{3,2,1,0:T(1,128)} %bitcast.57), channel_id=1, source_target_pairs={{4,0},{8,4},{12,8},{16,12},{20,16},{24,20},{28,24},{5,1},{9,5},{13... | collective-permute-start | bytes 147464 | tf_op jit(solution)/shard_map/ppermute | solution.py:28
  58.1 7.1 %collective-permute-start.5 = (f32[1,3,1,4096]{3,2,1,0:T(1,128)}, f32[1,3,1,4096]{3,2,1,0:T(1,128)S(1)}, u32[]{:S(2)}, u32[]{:S(2)}) collective-permute-start(f32[1,3,1,4096]{3,2,1,0:T(1,128)} %bitcast.56), channel_id=1, source_target_pairs={{0,4},{4,8},{8,12},{12,16},{16,20},{20,24},{24,28},{1,5},{5,9},{9,... | collective-permute-start | bytes 147464 | tf_op jit(solution)/shard_map/ppermute | solution.py:28
  60.4 6.8 %collective-permute-start.6 = (f32[1,3,1,64,64]{4,3,1,2,0:T(8,128)}, f32[1,3,1,64,64]{4,3,1,2,0:T(8,128)S(1)}, u32[]{:S(2)}, u32[]{:S(2)}) collective-permute-start(f32[1,3,1,64,64]{4,3,1,2,0:T(8,128)} %bitcast.51), channel_id=1, source_target_pairs={{0,1},{1,2},{2,3},{3,0},{4,5},{5,6},{6,7},{7,4},{8,9},{9,10},{10,1... | collective-permute-start | bytes 147464 | tf_op jit(solution)/shard_map/ppermute | solution.py:33
  60.5 6.7 %collective-permute-start.7 = (f32[1,3,1,64,64]{4,3,1,2,0:T(8,128)}, f32[1,3,1,64,64]{4,3,1,2,0:T(8,128)S(1)}, u32[]{:S(2)}, u32[]{:S(2)}) collective-permute-start(f32[1,3,1,64,64]{4,3,1,2,0:T(8,128)} %bitcast.50), channel_id=1, source_target_pairs={{0,3},{1,0},{2,1},{3,2},{4,7},{5,4},{6,5},{7,6},{8,11},{9,8},{10,9... | collective-permute-start | bytes 147464 | tf_op jit(solution)/shard_map/ppermute | solution.py:33
  67.2 0.6 copy-start.2
  67.2 0.7 copy-start.3

commit v19 on v18

--- a/solution.py
+++ b/solution.py
@@ -233,7 +233,7 @@
     wy = wy_ref[...]
     ez = ez_ref[...]
     XG = 4
-    GPI = 4
+    GPI = 16
 
     def body(it_, carry):
         lhs = []

time: 89.3 us -> 92.8 us (1.039)
  Pallas kernels: 61.3 us -> 64.9 us
    pallas_call x3, Pallas kernels: 61.3 us -> 64.9 us  [kernel_sweep(): pl.pallas_call(kernel, grid=(ncomp,), in_specs=in_specs, out_specs=out_sp...]
  transfers between devices with their start and end apart: 8 -> 8, of which waited for: 3 -> 3; matrix products, arithmetic and copies ran while one was open for 6% -> 5% of each run, Pallas kernels for 0% -> 0%
where the time goes in v19:
time: 92.8 us; the launch traced here: 92.2 us
  Pallas kernels  64.9 us (70%)
  starting transfers between devices  14.9 us (16%)
  local copies, waits for them, and re-layouts  6.1 us (7%)
  waiting for transfers between devices  4.24 us (5%)
  between operations  1.7 us (2%)
    pallas_call x3, Pallas kernels, kernel_sweep(): pl.pallas_call(kernel, grid=(ncomp,), in_specs=in_specs, out_specs=out_sp...  64.9 us
    ppermute x4, starting transfers between devices, shifted(): return lax.ppermute(shard, axis, pairs)  12.6 us
    ppermute x4, waiting for transfers between devices, shifted(): return lax.ppermute(shard, axis, pairs)  3.5 us
    ppermute x4, starting transfers between devices, shifted_2(): lax.ppermute(shard, axis, [(i, (i + by) % length) for i in range(length)])  2.35 us
  transfers between devices with their start and end apart: 8, of which 3 were waited for; matrix products, arithmetic and copies ran while one was open for 5% of the time, Pallas kernels for 0%

profile of v19, /device:TPU:24, one launch (start us, length us, event | category | flops | bytes accessed | tf_op | source)
XLA Modules:
  0.0 92.2 jit_solution(9192611853234128052)
XLA Ops:
  0.7 21.1 %shard_map.172 = (f32[3,1,4224]{2,1,0:T(1,128)}, f32[3,1,4224]{2,1,0:T(1,128)}, f32[3,1,72,64]{3,2,1,0:T(8,128)}, f32[3,1,72,64]{3,2,1,0:T(8,128)}) custom-call(f32[3]{0:T(128)} %bitcast.60, f32[3,64,4096]{2,1,0:T(8,128)} %bitcast.43, bf16[64,256]{1,0:T(8,128)(2,1)} %constant.77.clone.refs_2_.refs_11_.refs_14_, ...), custom_call_target="tpu_custom_call" | custom-call | tf_op jit(solution)/shard_map/pallas_call | solution.py:325
  21.7 3.4 %collective-permute-start.1 = (f32[1,3,1,4224]{3,2,1,0:T(1,128)}, f32[1,3,1,4224]{3,2,1,0:T(1,128)S(1)}, u32[]{:S(2)}, u32[]{:S(2)}) collective-permute-start(f32[1,3,1,4224]{3,2,1,0:T(1,128)} %bitcast.54), channel_id=1, source_target_pairs={{0,4},{4,8},{8,12},{12,16},{16,20},{20,24},{24,28},{1,5},{5,9},{9,... | collective-permute-start | bytes 152072 | tf_op jit(solution)/shard_map/ppermute | solution.py:28
  25.2 3.3 %collective-permute-start = (f32[1,3,1,4224]{3,2,1,0:T(1,128)}, f32[1,3,1,4224]{3,2,1,0:T(1,128)S(1)}, u32[]{:S(2)}, u32[]{:S(2)}) collective-permute-start(f32[1,3,1,4224]{3,2,1,0:T(1,128)} %bitcast.55), channel_id=1, source_target_pairs={{4,0},{8,4},{12,8},{16,12},{20,16},{24,20},{28,24},{5,1},{9,5},{13... | collective-permute-start | bytes 152072 | tf_op jit(solution)/shard_map/ppermute | solution.py:28
  28.5 0.4 collective-permute-start.3
  28.9 0.1 collective-permute-start.2
  29.0 0.0 collective-permute-done.1
  29.0 0.1 slice_reduce_fusion
  29.2 0.6 slice.33
  30.5 0.1 reshape_squeeze.13
  30.6 0.8 collective-permute-done
  31.4 0.1 slice_reduce_fusion.1
  31.5 0.1 reshape_squeeze.12
  31.7 0.1 rev.27
  31.8 0.1 rev.29
  32.0 0.7 squeeze_broadcast_in_dim_reshape.12.refs_7_
  32.7 0.7 squeeze_broadcast_in_dim_reshape.13.refs_8_
  33.4 0.0 collective-permute-done.3
  33.4 0.0 copy-start
  33.4 0.7 collective-permute-done.2
  34.1 0.0 copy-start.1
  34.2 0.1 stack.31
  34.3 0.7 copy.31
  35.0 0.0 copy-done
  35.0 0.0 copy-done.1
  35.0 21.9 %shard_map.173 = (f32[3,1,4096]{2,1,0:T(1,128)}, f32[3,1,4096]{2,1,0:T(1,128)}, f32[3,1,64,64]{3,2,1,0:T(8,128)}, f32[3,1,64,64]{3,2,1,0:T(8,128)}, f32[3,1,4096...) custom-call(f32[3]{0:T(128)} %bitcast.61, f32[3,64,4096]{2,1,0:T(8,128)} %bitcast.44, f32[6,3]{1,0:T(8,128)} %bitcast.58, ...), custom_call_target="tpu_custom_call" | custom-call | tf_op jit(solution)/shard_map/pallas_call | solution.py:325
  56.9 3.5 %collective-permute-start.4 = (f32[1,3,1,4096]{3,2,1,0:T(1,128)}, f32[1,3,1,4096]{3,2,1,0:T(1,128)S(1)}, u32[]{:S(2)}, u32[]{:S(2)}) collective-permute-start(f32[1,3,1,4096]{3,2,1,0:T(1,128)} %bitcast.57), channel_id=1, source_target_pairs={{4,0},{8,4},{12,8},{16,12},{20,16},{24,20},{28,24},{5,1},{9,5},{13... | collective-permute-start | bytes 147464 | tf_op jit(solution)/shard_map/ppermute | solution.py:28
  60.4 2.3 %collective-permute-start.5 = (f32[1,3,1,4096]{3,2,1,0:T(1,128)}, f32[1,3,1,4096]{3,2,1,0:T(1,128)S(1)}, u32[]{:S(2)}, u32[]{:S(2)}) collective-permute-start(f32[1,3,1,4096]{3,2,1,0:T(1,128)} %bitcast.56), channel_id=1, source_target_pairs={{0,4},{4,8},{8,12},{12,16},{16,20},{20,24},{24,28},{1,5},{5,9},{9,... | collective-permute-start | bytes 147464 | tf_op jit(solution)/shard_map/ppermute | solution.py:28
  62.7 0.1 collective-permute-start.6
  62.8 1.7 %collective-permute-start.7 = (f32[1,3,1,64,64]{4,3,1,2,0:T(8,128)}, f32[1,3,1,64,64]{4,3,1,2,0:T(8,128)S(1)}, u32[]{:S(2)}, u32[]{:S(2)}) collective-permute-start(f32[1,3,1,64,64]{4,3,1,2,0:T(8,128)} %bitcast.50), channel_id=1, source_target_pairs={{0,3},{1,0},{2,1},{3,2},{4,7},{5,4},{6,5},{7,6},{8,11},{9,8},{10,9... | collective-permute-start | bytes 147464 | tf_op jit(solution)/shard_map/ppermute | solution.py:33
  64.5 0.0 collective-permute-done.4
  64.5 0.1 reduce.2
  64.7 0.1 reshape_squeeze.14
  64.8 2.7 %collective-permute-done.5 = f32[1,3,1,4096]{3,2,1,0:T(1,128)S(1)} collective-permute-done((f32[1,3,1,4096]{3,2,1,0:T(1,128)}, f32[1,3,1,4096]{3,2,1,0:T(1,128)S(1)}, u32[]{:S(2)}, u32[]{:S(2)}) %collective-permute-start.5) | collective-permute-done | bytes 49184 | tf_op jit(solution)/shard_map/ppermute | solution.py:28
  67.5 0.1 reduce.3
  67.6 0.1 reshape_squeeze.15
  67.8 0.1 rev.33
  67.9 0.1 rev.31
  68.1 0.7 squeeze_broadcast_in_dim_reshape.15.refs_11_
  68.8 0.7 squeeze_broadcast_in_dim_reshape.14.refs_10_
  69.5 0.0 collective-permute-done.6
  69.5 0.0 copy-start.2
  69.5 0.0 collective-permute-done.7
  69.5 0.0 copy-start.3
  69.5 0.6 copy-done.2
  70.1 0.0 copy-done.3
  70.2 21.9 %shard_map.174 = f32[3,64,4096]{2,1,0:T(8,128)} custom-call(f32[3]{0:T(128)} %bitcast.62, f32[3,64,4096]{2,1,0:T(8,128)} %bitcast.45, f32[6,3]{1,0:T(8,128)} %bitcast.59, f32[3,1,4096]{2,1,0:T(1,128)} %get-tuple-element.20.refs_3_, f32[3,1,4096]{2,1,0:T(1,128)} %get-tuple-element.21.refs_4_, f32[3,64,128]{2,1,0:T(8,128)} %get-tuple-element.22.refs_5_, ...), custom_call_target="tpu_custom_call" | custom-call | tf_op jit(solution)/shard_map/pallas_call | solution.py:325
  (18 shorter events, 0.2 us)
Async XLA Ops:
  21.7 7.3 %collective-permute-start.1 = (f32[1,3,1,4224]{3,2,1,0:T(1,128)}, f32[1,3,1,4224]{3,2,1,0:T(1,128)S(1)}, u32[]{:S(2)}, u32[]{:S(2)}) collective-permute-start(f32[1,3,1,4224]{3,2,1,0:T(1,128)} %bitcast.54), channel_id=1, source_target_pairs={{0,4},{4,8},{8,12},{12,16},{16,20},{20,24},{24,28},{1,5},{5,9},{9,... | collective-permute-start | bytes 152072 | tf_op jit(solution)/shard_map/ppermute | solution.py:28
  25.2 6.2 %collective-permute-start = (f32[1,3,1,4224]{3,2,1,0:T(1,128)}, f32[1,3,1,4224]{3,2,1,0:T(1,128)S(1)}, u32[]{:S(2)}, u32[]{:S(2)}) collective-permute-start(f32[1,3,1,4224]{3,2,1,0:T(1,128)} %bitcast.55), channel_id=1, source_target_pairs={{4,0},{8,4},{12,8},{16,12},{20,16},{24,20},{28,24},{5,1},{9,5},{13... | collective-permute-start | bytes 152072 | tf_op jit(solution)/shard_map/ppermute | solution.py:28
  28.5 4.9 %collective-permute-start.3 = (f32[1,3,1,72,64]{4,3,1,2,0:T(8,128)}, f32[1,3,1,72,64]{4,3,1,2,0:T(8,128)S(1)}, u32[]{:S(2)}, u32[]{:S(2)}) collective-permute-start(f32[1,3,1,72,64]{4,3,1,2,0:T(8,128)} %bitcast.48), channel_id=1, source_target_pairs={{0,3},{1,0},{2,1},{3,2},{4,7},{5,4},{6,5},{7,6},{8,11},{9,8},{10,9... | collective-permute-start | bytes 165896 | tf_op jit(solution)/shard_map/ppermute | solution.py:33
  28.9 5.2 %collective-permute-start.2 = (f32[1,3,1,72,64]{4,3,1,2,0:T(8,128)}, f32[1,3,1,72,64]{4,3,1,2,0:T(8,128)S(1)}, u32[]{:S(2)}, u32[]{:S(2)}) collective-permute-start(f32[1,3,1,72,64]{4,3,1,2,0:T(8,128)} %bitcast.49), channel_id=1, source_target_pairs={{0,1},{1,2},{2,3},{3,0},{4,5},{5,6},{6,7},{7,4},{8,9},{9,10},{10,1... | collective-permute-start | bytes 165896 | tf_op jit(solution)/shard_map/ppermute | solution.py:33
  33.4 1.5 %copy-start = (f32[1,3,1,72,64]{4,3,1,2,0:T(8,128)}, f32[1,3,1,72,64]{4,3,1,2,0:T(8,128)S(1)}, u32[]{:S(2)}) copy-start(f32[1,3,1,72,64]{4,3,1,2,0:T(8,128)S(1)} %collective-permute-done.3) | copy-start | bytes 165892
  34.1 0.8 copy-start.1
  56.9 7.7 %collective-permute-start.4 = (f32[1,3,1,4096]{3,2,1,0:T(1,128)}, f32[1,3,1,4096]{3,2,1,0:T(1,128)S(1)}, u32[]{:S(2)}, u32[]{:S(2)}) collective-permute-start(f32[1,3,1,4096]{3,2,1,0:T(1,128)} %bitcast.57), channel_id=1, source_target_pairs={{4,0},{8,4},{12,8},{16,12},{20,16},{24,20},{28,24},{5,1},{9,5},{13... | collective-permute-start | bytes 147464 | tf_op jit(solution)/shard_map/ppermute | solution.py:28
  60.4 7.1 %collective-permute-start.5 = (f32[1,3,1,4096]{3,2,1,0:T(1,128)}, f32[1,3,1,4096]{3,2,1,0:T(1,128)S(1)}, u32[]{:S(2)}, u32[]{:S(2)}) collective-permute-start(f32[1,3,1,4096]{3,2,1,0:T(1,128)} %bitcast.56), channel_id=1, source_target_pairs={{0,4},{4,8},{8,12},{12,16},{16,20},{20,24},{24,28},{1,5},{5,9},{9,... | collective-permute-start | bytes 147464 | tf_op jit(solution)/shard_map/ppermute | solution.py:28
  62.7 6.8 %collective-permute-start.6 = (f32[1,3,1,64,64]{4,3,1,2,0:T(8,128)}, f32[1,3,1,64,64]{4,3,1,2,0:T(8,128)S(1)}, u32[]{:S(2)}, u32[]{:S(2)}) collective-permute-start(f32[1,3,1,64,64]{4,3,1,2,0:T(8,128)} %bitcast.51), channel_id=1, source_target_pairs={{0,1},{1,2},{2,3},{3,0},{4,5},{5,6},{6,7},{7,4},{8,9},{9,10},{10,1... | collective-permute-start | bytes 147464 | tf_op jit(solution)/shard_map/ppermute | solution.py:33
  62.8 6.7 %collective-permute-start.7 = (f32[1,3,1,64,64]{4,3,1,2,0:T(8,128)}, f32[1,3,1,64,64]{4,3,1,2,0:T(8,128)S(1)}, u32[]{:S(2)}, u32[]{:S(2)}) collective-permute-start(f32[1,3,1,64,64]{4,3,1,2,0:T(8,128)} %bitcast.50), channel_id=1, source_target_pairs={{0,3},{1,0},{2,1},{3,2},{4,7},{5,4},{6,5},{7,6},{8,11},{9,8},{10,9... | collective-permute-start | bytes 147464 | tf_op jit(solution)/shard_map/ppermute | solution.py:33
  69.5 0.6 copy-start.2
  69.5 0.7 copy-start.3
